TPU v7x, 32 devices: a whole 2x2x4 slice. The times are simulated.
32 devices in a mesh: dimer: 4 (over y, x), grid: 8 (over z, core).
Axes of the slice: x: 2, y: 2, z: 4, core: 2. Of those that a mesh axis runs over, the one named last changes fastest.
Arguments:
- basis_values: bfloat16 [4, 10240, 1024], P('dimer', 'grid'), may hold values from -15 to 15
- aux_values: bfloat16 [4, 10240, 2048], P('dimer', 'grid'), may hold values from -6 to 6
- factors: bfloat16 [4, 512, 128], P('dimer', 'grid'), may hold values from -0.25 to 0.25
- frag_slot: int32 [4], replicated, may hold values from 0 to 3, each once
- dimer_pairs: int32 [4, 2], P('dimer'), may hold values from 0 to 3, as said below
- counts: int32 [4, 8], P('dimer', 'grid'), may hold values from 1 to 1280, 4096 in all within a row
- weights: float32 [4, 10240], P('dimer', 'grid'), may hold values from 0.00078125 to 0.003125
- metric_inv: float32 [4, 2048, 2048], P('dimer', 'grid'), may hold values from -1 to 1, as said below
Outputs:
- frag_fock: float32 [4, 512, 512], P('dimer', 'grid')
- coupling: float32 [4, 512, 512], P('dimer', 'grid')
Inputs may be any that keep to these rules, and one draw needn't show every extreme that they name: `dimer_pairs`: each fragment is named by exactly two dimers, and the two fragments of a dimer differ. For each dimer the 8 counts sum to 4096 and the largest equals 1280. `metric_inv`: each matrix is symmetric.
All inputs are finite; a program needn't handle non-finite values. No bound on the sum of `counts` on one device may be relied on, other than what follows from the above.
Results may differ from a plain program's by a relative error of at most 0.0029.
Values may be sent and summed in bfloat16 or wider, within the bound.
No kernel may reach another device: no remote copies, remote signals or barrier semaphores. Data moves between devices by JAX's collectives and lax.ppermute only.
A program may use at most 64 MiB of HBM per device.

v0:
```python
import jax
import jax.numpy as jnp
from jax import lax
from jax.sharding import PartitionSpec as P

exchange_coeff = 0.9847450218426964


def split_product(vector, matrix, vector_left):
    high_part = vector.astype(jnp.bfloat16)
    high_back = lax.optimization_barrier(high_part).astype(jnp.float32)
    low_part = (vector - high_back).astype(jnp.bfloat16)
    if vector_left:
        return jnp.dot(high_part, matrix, preferred_element_type=jnp.float32) + jnp.dot(
            low_part, matrix, preferred_element_type=jnp.float32
        )
    return jnp.dot(matrix, high_part, preferred_element_type=jnp.float32) + jnp.dot(
        matrix, low_part, preferred_element_type=jnp.float32
    )


def contract(left_side, right_side):
    numbers = (((0,), (0,)), ((), ()))
    return lax.dot_general(left_side, right_side, numbers, preferred_element_type=jnp.float32)


def shards(basis_values, aux_values, factors, frag_slot, dimer_pairs, counts, weights, metric_inv):
    highest = lax.Precision.HIGHEST
    basis_rows = basis_values[0]
    aux_block = aux_values[0]
    points = basis_rows.shape[0]
    frag_basis = basis_rows.shape[1] // 2
    live_count = counts[0, 0]
    position = lax.iota(jnp.int32, points)
    live_weight = jnp.where(position < live_count, weights[0], jnp.zeros((), jnp.float32))
    gathered = lax.all_gather(factors, "dimer", axis=0, tiled=True)
    frag_ids = lax.iota(jnp.int32, frag_slot.shape[0])
    wanted = jnp.sum(
        jnp.where(frag_ids[None, :] == dimer_pairs[0][:, None], frag_slot[None, :], 0), axis=1
    )
    selector = (frag_ids[None, :] == wanted[:, None]).astype(jnp.bfloat16)
    chosen = jnp.einsum(
        "as,srk->ark", selector, gathered, preferred_element_type=jnp.float32
    ).astype(jnp.bfloat16)
    dimer_factors = lax.all_gather(chosen, "grid", axis=1, tiled=True)
    orb_first = jnp.dot(
        basis_rows[:, :frag_basis], dimer_factors[0], preferred_element_type=jnp.float32
    )
    orb_second = jnp.dot(
        basis_rows[:, frag_basis:], dimer_factors[1], preferred_element_type=jnp.float32
    )
    density = (
        jnp.sum(orb_first * orb_first, axis=1) + jnp.sum(orb_second * orb_second, axis=1)
    ) / (2.0 * dimer_factors.shape[2])
    exchange = -exchange_coeff * jnp.cbrt(density)
    weighted_density = live_weight * density
    fitted = lax.psum(split_product(weighted_density, aux_block, True), "grid")
    coef_rows = jnp.dot(metric_inv[0], fitted, precision=highest)
    coefficients = lax.all_gather(coef_rows, "grid", axis=0, tiled=True)
    coulomb = split_product(coefficients, aux_block, False)
    potential_total, weight_sum = lax.psum(
        (jnp.sum(live_weight * (coulomb + exchange)), jnp.sum(live_weight)), "grid"
    )
    average = potential_total / weight_sum
    potential = live_weight * (coulomb + exchange - average)
    weighted_basis = (basis_rows * potential[:, None]).astype(jnp.bfloat16)
    half_rows = frag_basis // lax.axis_size("grid")
    left_first = lax.slice_in_dim(weighted_basis, 0, half_rows * lax.axis_size("grid"), axis=1)
    left_second = lax.dynamic_slice_in_dim(
        weighted_basis, frag_basis, half_rows * lax.axis_size("grid"), 1
    )
    first_first = contract(left_first, basis_rows[:, :frag_basis])
    first_second = contract(left_first, basis_rows[:, frag_basis:])
    second_second = contract(left_second, basis_rows[:, frag_basis:])
    shares = lax.psum_scatter(
        jnp.stack([first_first, first_second, second_second], axis=1),
        "grid",
        scatter_dimension=0,
        tiled=True,
    )
    own_first = shares[:, 0]
    own_cross = shares[:, 1]
    own_second = shares[:, 2]
    is_first = (frag_ids == dimer_pairs[0, 0])[:, None, None]
    is_second = (frag_ids == dimer_pairs[0, 1])[:, None, None]
    fock_terms = jnp.where(is_first, own_first[None], jnp.zeros((), jnp.float32)) + jnp.where(
        is_second, own_second[None], jnp.zeros((), jnp.float32)
    )
    frag_fock = lax.psum_scatter(fock_terms, "dimer", scatter_dimension=0, tiled=True)
    return (frag_fock, own_cross[None])


def solution(mesh):
    placed = (
        P("dimer", "grid", None),
        P("dimer", "grid", None),
        P("dimer", "grid", None),
        P(),
        P("dimer", None),
        P("dimer", "grid"),
        P("dimer", "grid"),
        P("dimer", "grid", None),
    )
    return jax.shard_map(
        shards,
        mesh=mesh,
        in_specs=placed,
        out_specs=(P("dimer", "grid", None), P("dimer", "grid", None)),
        check_vma=False,
    )
```

profile of v0, /device:TPU:0, one launch (start us, length us, event | category | flops | bytes accessed | tf_op | source)
XLA Modules:
  0.0 174.4 jit_solution(8135204329770347919)
XLA Ops:
  7.2 0.0 copy-start
  7.2 0.0 reduce-scatter.5.cloned.1.call-start
  7.2 0.0 copy-start.2
  7.2 10.1 %all_gather.9 = bf16[4,64,128]{2,1,0:T(8,128)(2,1)S(1)} all-gather(bf16[1,64,128]{2,1,0:T(8,128)(2,1)} %param.10), channel_id=1, replica_groups=mesh['dimer'=4,'grid'=8] {'dimer'}, dimensions={0}, use_global_device_ids=true | all-gather | bytes 81920 | tf_op jit(solution)/shard_map/all_gather | solution.py:36
  17.4 0.9 fusion.43
  18.2 0.2 convolution_convert_fusion
  18.5 14.4 %all_gather.10 = bf16[2,512,128]{2,0,1:T(2,128)(2,1)S(1)} all-gather(bf16[2,64,128]{2,0,1:T(2,128)(2,1)S(1)} %convolution_convert_fusion), channel_id=1, replica_groups=mesh['dimer'=4,'grid'=8] {'grid'}, dimensions={1}, use_global_device_ids=true | all-gather | bytes 294912 | tf_op jit(solution)/shard_map/all_gather | solution.py:45
  32.9 0.0 copy-start.4
  32.9 0.4 fusion.47
  33.3 1.9 %fusion.11 = f32[1280]{0:T(1024)S(1)} fusion(bf16[1280,1024]{1,0:T(8,128)(2,1)} %bitcast.66, bf16[1,512,128]{2,0,1:T(2,128)(2,1)S(1)} %get-tuple-element.12), kind=kOutput, calls=%fused_computation.18 | convolution fusion | flops 168098560 | bytes 1446912 | tf_op jit(solution)/shard_map/dot_general | solution.py:46
  35.2 0.0 copy-done.2
  35.2 0.6 fusion.12
  36.4 0.0 copy-done.4
  36.5 0.0 copy-start.1
  36.5 3.4 %fusion.4 = f32[1,2048]{1,0:T(1,128)S(1)} fusion(bf16[1280,1]{0,1:T(2,128)(2,1)S(1)} %reshape.48, bf16[1,1280,2048]{2,1,0:T(8,128)(2,1)} %param.9), kind=kOutput, calls=%fused_computation.4 | convolution fusion | flops 5242880 | bytes 5253632 | tf_op jit(solution)/shard_map/dot_general | solution.py:14
  39.9 0.6 copy-done.1
  40.6 0.8 fusion.6
  41.4 17.2 %psum.21 = f32[2048]{0:T(1024)S(1)} all-reduce(f32[2048]{0:T(1024)S(1)} %add.35), channel_id=1, replica_groups=mesh['dimer'=4,'grid'=8] {'grid'}, use_global_device_ids=true, to_apply=%region_3.4 | all-reduce | flops 2048 | bytes 16384 | tf_op jit(solution)/shard_map/psum | solution.py:57
  58.5 0.0 copy-done
  58.6 1.7 fusion.23
  60.3 8.4 %all-gather = f32[8,1,256]{2,1,0:T(1,128)S(1)} all-gather(f32[1,1,256]{2,1,0:T(1,128)S(1)} %fusion.23), channel_id=1, replica_groups=mesh['dimer'=4,'grid'=8] {'grid'}, dimensions={0}, use_global_device_ids=true | all-gather | bytes 9216 | tf_op jit(solution)/shard_map/all_gather | solution.py:59
  68.8 4.0 %fusion.20 = f32[1280]{0:T(1024)S(1)} fusion(bf16[2048,1]{0,1:T(2,128)(2,1)S(1)} %reshape.54, bf16[1,1280,2048]{2,1,0:T(8,128)(2,1)} %param.9), kind=kOutput, calls=%fused_computation.26 | convolution fusion | flops 5242880 | bytes 5252096 | tf_op jit(solution)/shard_map/dot_general | solution.py:17
  72.7 4.0 %fusion.17 = f32[1280]{0:T(1024)S(1)} fusion(bf16[2048,1]{0,1:T(2,128)(2,1)S(1)} %reshape.52, bf16[1,1280,2048]{2,1,0:T(8,128)(2,1)} %param.9), kind=kOutput, calls=%fused_computation.25 | convolution fusion | flops 5242880 | bytes 5252096 | tf_op jit(solution)/shard_map/dot_general | solution.py:17
  76.7 0.7 fusion.31
  77.4 16.1 %all-reduce.1 = (f32[]{:T(128)}, f32[]{:T(128)}) all-reduce(f32[]{:T(128)} %get-tuple-element.3, f32[]{:T(128)} %get-tuple-element.2), channel_id=1, replica_groups=mesh['dimer'=4,'grid'=8] {'grid'}, use_global_device_ids=true, to_apply=%region_5.6 | all-reduce | flops 2 | bytes 16 | tf_op jit(solution)/shard_map/psum | solution.py:61
  94.8 0.0 copy-start.3
  94.8 2.4 %multiply_convert_fusion = bf16[1280,1024]{1,0:T(8,128)(2,1)S(1)} fusion(f32[1280]{0:T(1024)S(1)} %subtract_multiply_fusion, bf16[1,1280,1024]{2,1,0:T(8,128)(2,1)} %param.8), kind=kLoop, calls=%fused_computation.8 | loop fusion | flops 3932160 | bytes 5248000 | tf_op jit(solution)/shard_map/convert_element_type | solution.py:66
  97.2 0.1 copy-done.3
  97.4 0.9 convolution_bitcast_fusion
  98.2 0.9 convolution_bitcast_fusion.1
  99.1 0.9 convolution_bitcast_fusion.2
  100.0 2.0 %pad_maximum_fusion = f32[512,3,512]{2,0,1:T(8,128)} fusion(f32[512,1,512]{2,0,1:T(8,128)S(1)} %convolution_bitcast_fusion, f32[512,1,512]{2,0,1:T(8,128)S(1)} %convolution_bitcast_fusion.1, f32[512,1,512]{2,0,1:T(8,128)S(1)} %convolution_bitcast_fusion.2), kind=kLoop, calls=%fused_computation.9 | loop fusion | flops 1572864 | bytes 6291456 | tf_op jit(solution)/shard_map/stack | solution.py:76
  102.0 0.0 copy-start.5
  102.0 0.0 reduce-scatter.5.cloned.1.call-update
  102.0 0.0 reduce-scatter.7.cloned.1.call-start
  102.0 0.6 copy-done.5
  102.6 0.6 fusion.48
  103.2 1.3 iota_compare_fusion.1
  104.5 35.2 %reduce-scatter.5.cloned.1.call-done = f32[64,3,512]{2,0,1:T(8,128)} async-done(((f32[512,3,512]{2,0,1:T(8,128)}), f32[64,3,512]{2,0,1:T(8,128)}) %reduce-scatter.5.cloned.1.call-update) | async-done | bytes 393232 | tf_op jit(solution)/shard_map/reduce_scatter | solution.py:75
  139.7 1.7 slice_bitcast_fusion
  141.5 0.9 select_add_fusion
  142.4 0.0 reduce-scatter.7.cloned.1.call-update
  142.4 25.1 %reduce-scatter.7.cloned.1.call-done = f32[1,64,512]{2,1,0:T(8,128)} async-done(((f32[4,64,512]{2,1,0:T(8,128)}), f32[1,64,512]{2,1,0:T(8,128)}) %reduce-scatter.7.cloned.1.call-update) | async-done | bytes 131088
  (10 shorter events, 0.1 us)
Async XLA Ops:
  7.2 51.4 %copy-start = (f32[1,256,2048]{2,1,0:T(8,128)S(1)}, f32[1,256,2048]{2,1,0:T(8,128)}, u32[]{:S(2)}) copy-start(f32[1,256,2048]{2,1,0:T(8,128)} %param.15) | copy-start | bytes 6291460
  7.2 132.6 %reduce-scatter.5.cloned.1.call-start = ((), (), s32[]{:S(2)}) async-start(), calls=%async_computation.2 | async-start | bytes 3538944 | tf_op jit(solution)/shard_map/reduce_scatter | solution.py:75
  7.2 28.0 %copy-start.2 = (bf16[1,1280,1024]{2,1,0:T(8,128)(2,1)S(1)}, bf16[1,1280,1024]{2,1,0:T(8,128)(2,1)}, u32[]{:S(2)}) copy-start(bf16[1,1280,1024]{2,1,0:T(8,128)(2,1)} %param.8) | copy-start | bytes 7864324
  32.9 3.5 %copy-start.4 = (f32[1,1280]{1,0:T(1,128)S(1)}, f32[1,1280]{1,0:T(1,128)}, u32[]{:S(2)}) copy-start(f32[1,1280]{1,0:T(1,128)} %param.14) | copy-start | bytes 15364
  36.5 4.0 %copy-start.1 = (bf16[1,1280,2048]{2,1,0:T(8,128)(2,1)S(1)}, bf16[1,1280,2048]{2,1,0:T(8,128)(2,1)}, u32[]{:S(2)}) copy-start(bf16[1,1280,2048]{2,1,0:T(8,128)(2,1)} %param.9) | copy-start | bytes 15728644
  94.8 2.5 %copy-start.3 = (bf16[1,1280,1024]{2,1,0:T(8,128)(2,1)S(1)}, bf16[1,1280,1024]{2,1,0:T(8,128)(2,1)}, u32[]{:S(2)}) copy-start(bf16[1,1280,1024]{2,1,0:T(8,128)(2,1)} %param.8) | copy-start | bytes 7864324
  102.0 0.7 copy-start.5
  102.0 65.6 %reduce-scatter.7.cloned.1.call-start = ((), (), s32[]{:S(2)}) async-start(), calls=%async_computation.3 | async-start | bytes 655360
Sparse Core Ops, SparseCore 0:
  102.1 37.5 reduce-scatter.4
  143.1 24.3 reduce-scatter.6
where the time goes:
time: 175 us; the launch traced here: 174 us
  blocking collectives  66.4 us (38%)
  waiting for transfers between devices  60.4 us (35%)
  matrix products  19.2 us (11%)
  between operations  16.1 us (9%)
  other arithmetic  8.22 us (5%)
  local copies, waits for them, and re-layouts  4.03 us (2%)
    reduce_scatter x1, waiting for transfers between devices, shards(): lax.psum_scatter(jnp.stack([first_first, first_second, second_second], ax...  35.2 us
    unnamed x3, waiting for transfers between devices  25.2 us
    psum x1, blocking collectives, shards(): fitted = lax.psum(split_product(weighted_density, aux_block, True), 'grid')  17.2 us
    psum x1, blocking collectives, shards(): lax.psum((jnp.sum(live_weight * (coulomb + exchange)), jnp.sum(live_weigh...  16.1 us
    all_gather x1, blocking collectives, shards(): dimer_factors = lax.all_gather(chosen, 'grid', axis=1, tiled=True)  14.4 us
    all_gather x1, blocking collectives, shards(): gathered = lax.all_gather(factors, 'dimer', axis=0, tiled=True)  10.1 us
    all_gather x1, blocking collectives, shards(): coefficients = lax.all_gather(coef_rows, 'grid', axis=0, tiled=True)  8.44 us
    dot_general x1, matrix products, split_product(): jnp.dot(matrix, low_part, preferred_element_type=jnp.float32)  3.96 us
  transfers between devices with their start and end apart: 2, of which 2 were waited for; matrix products, arithmetic and copies ran while one was open for 1% of the time, Pallas kernels for 0%

commit v1 on v0

--- a/solution.py
+++ b/solution.py
@@ -6,17 +6,11 @@
 exchange_coeff = 0.9847450218426964
 
 
-def split_product(vector, matrix, vector_left):
-    high_part = vector.astype(jnp.bfloat16)
+def split_rows(rows):
+    high_part = rows.astype(jnp.bfloat16)
     high_back = lax.optimization_barrier(high_part).astype(jnp.float32)
-    low_part = (vector - high_back).astype(jnp.bfloat16)
-    if vector_left:
-        return jnp.dot(high_part, matrix, preferred_element_type=jnp.float32) + jnp.dot(
-            low_part, matrix, preferred_element_type=jnp.float32
-        )
-    return jnp.dot(matrix, high_part, preferred_element_type=jnp.float32) + jnp.dot(
-        matrix, low_part, preferred_element_type=jnp.float32
-    )
+    low_part = (rows - high_back).astype(jnp.bfloat16)
+    return high_part, low_part
 
 
 def contract(left_side, right_side):
@@ -29,6 +23,7 @@
     basis_rows = basis_values[0]
     aux_block = aux_values[0]
     points = basis_rows.shape[0]
+    naux = aux_block.shape[1]
     frag_basis = basis_rows.shape[1] // 2
     live_count = counts[0, 0]
     position = lax.iota(jnp.int32, points)
@@ -54,13 +49,27 @@
     ) / (2.0 * dimer_factors.shape[2])
     exchange = -exchange_coeff * jnp.cbrt(density)
     weighted_density = live_weight * density
-    fitted = lax.psum(split_product(weighted_density, aux_block, True), "grid")
+    high_rows, low_rows = split_rows(jnp.stack([weighted_density, live_weight]))
+    projections = jnp.dot(
+        jnp.concatenate([high_rows, low_rows]), aux_block, preferred_element_type=jnp.float32
+    )
+    fitted_part = projections[0] + projections[2]
+    weight_part = projections[1] + projections[3]
+    sums_part = jnp.stack([jnp.sum(live_weight * exchange), jnp.sum(live_weight)])
+    payload = jnp.concatenate([fitted_part, weight_part, sums_part])
+    totals = lax.psum(payload, "grid")
+    fitted = totals[:naux]
+    weight_projection = totals[naux : 2 * naux]
+    exchange_total = totals[2 * naux]
+    weight_sum = totals[2 * naux + 1]
     coef_rows = jnp.dot(metric_inv[0], fitted, precision=highest)
     coefficients = lax.all_gather(coef_rows, "grid", axis=0, tiled=True)
-    coulomb = split_product(coefficients, aux_block, False)
-    potential_total, weight_sum = lax.psum(
-        (jnp.sum(live_weight * (coulomb + exchange)), jnp.sum(live_weight)), "grid"
+    coef_high, coef_low = split_rows(coefficients)
+    coulomb_parts = jnp.dot(
+        aux_block, jnp.stack([coef_high, coef_low], axis=1), preferred_element_type=jnp.float32
     )
+    coulomb = coulomb_parts[:, 0] + coulomb_parts[:, 1]
+    potential_total = jnp.dot(coefficients, weight_projection, precision=highest) + exchange_total
     average = potential_total / weight_sum
     potential = live_weight * (coulomb + exchange - average)
     weighted_basis = (basis_rows * potential[:, None]).astype(jnp.bfloat16)
@@ -81,13 +90,22 @@
     own_first = shares[:, 0]
     own_cross = shares[:, 1]
     own_second = shares[:, 2]
-    is_first = (frag_ids == dimer_pairs[0, 0])[:, None, None]
-    is_second = (frag_ids == dimer_pairs[0, 1])[:, None, None]
-    fock_terms = jnp.where(is_first, own_first[None], jnp.zeros((), jnp.float32)) + jnp.where(
-        is_second, own_second[None], jnp.zeros((), jnp.float32)
-    )
-    frag_fock = lax.psum_scatter(fock_terms, "dimer", scatter_dimension=0, tiled=True)
-    return (frag_fock, own_cross[None])
+    groups = lax.axis_size("dimer")
+    me = lax.axis_index("dimer")
+    zero = jnp.zeros((), jnp.float32)
+
+    def piece(dest):
+        return jnp.where(dimer_pairs[0, 0] == dest, own_first, zero) + jnp.where(
+            dimer_pairs[0, 1] == dest, own_second, zero
+        )
+
+    frag_fock = piece(me)
+    for shift in range(1, groups):
+        sent = piece(lax.rem(me + shift, groups))
+        frag_fock = frag_fock + lax.ppermute(
+            sent, "dimer", [(i, (i + shift) % groups) for i in range(groups)]
+        )
+    return (frag_fock[None], own_cross[None])
 
 
 def solution(mesh):

time: 175 us -> 152 us (0.87)
  waiting for transfers between devices: 60.4 us -> 36.6 us
  between operations: 16.1 us -> 21.6 us
  matrix products: 19.2 us -> 14.4 us
  starting transfers between devices: 0.08 us -> 4.44 us
  blocking collectives: 66.4 us -> 62.1 us
    unnamed x3 -> x1, waiting for transfers between devices: 25.2 us -> 0.02 us
    dot_general x4 -> x2, matrix products: 12.1 us -> 7.36 us  [the longest x1 4.09 us: shards(): jnp.dot(aux_block, jnp.stack([coef_high, coef_low], axis=1), preferred_el...]
    ppermute x0 -> x3, starting transfers between devices: none -> 4.4 us  [shards(): lax.ppermute(sent, 'dimer', [(i, (i + shift) % groups) for i in range(gro...]
    psum x2 -> x1, blocking collectives: 33.3 us -> 29.1 us  [shards(): totals = lax.psum(payload, 'grid')]
    ppermute x0 -> x3, waiting for transfers between devices: none -> 2.27 us  [shards(): lax.ppermute(sent, 'dimer', [(i, (i + shift) % groups) for i in range(gro...]
    convert_element_type x1, other arithmetic: 2.38 us -> 0.49 us  [shards(): weighted_basis = (basis_rows * potential[:, None]).astype(jnp.bfloat16)]
  transfers between devices with their start and end apart: 2 -> 4, of which waited for: 2 -> 4; matrix products, arithmetic and copies ran while one was open for 1% -> 0% of each run, Pallas kernels for 0% -> 0%
where the time goes in v1:
time: 152 us; the launch traced here: 151 us
  blocking collectives  62.1 us (41%)
  waiting for transfers between devices  36.6 us (24%)
  between operations  21.6 us (14%)
  matrix products  14.4 us (9%)
  other arithmetic  8.17 us (5%)
  starting transfers between devices  4.44 us (3%)
  local copies, waits for them, and re-layouts  3.69 us (2%)
    reduce_scatter x1, waiting for transfers between devices, shards(): lax.psum_scatter(jnp.stack([first_first, first_second, second_second], ax...  34.3 us
    psum x1, blocking collectives, shards(): totals = lax.psum(payload, 'grid')  29.1 us
    all_gather x1, blocking collectives, shards(): dimer_factors = lax.all_gather(chosen, 'grid', axis=1, tiled=True)  14.4 us
    all_gather x1, blocking collectives, shards(): gathered = lax.all_gather(factors, 'dimer', axis=0, tiled=True)  10.1 us
    all_gather x1, blocking collectives, shards(): coefficients = lax.all_gather(coef_rows, 'grid', axis=0, tiled=True)  8.44 us
    ppermute x3, starting transfers between devices, shards(): lax.ppermute(sent, 'dimer', [(i, (i + shift) % groups) for i in range(gro...  4.4 us
    dot_general x1, matrix products, shards(): jnp.dot(aux_block, jnp.stack([coef_high, coef_low], axis=1), preferred_el...  4.09 us
    dot_general x1, matrix products, shards(): jnp.dot(jnp.concatenate([high_rows, low_rows]), aux_block, preferred_elem...  3.28 us
  transfers between devices with their start and end apart: 4, of which 4 were waited for; matrix products, arithmetic and copies ran while one was open for 0% of the time, Pallas kernels for 0%

profile of v1, /device:TPU:0, one launch (start us, length us, event | category | flops | bytes accessed | tf_op | source)
XLA Modules:
  0.0 151.1 jit_solution(14757088467848177024)
XLA Ops:
  7.2 0.0 copy-start
  7.2 0.0 reduce-scatter.2.cloned.1.call-start
  7.2 0.0 copy-start.1
  7.2 10.1 %all_gather.9 = bf16[4,64,128]{2,1,0:T(8,128)(2,1)S(1)} all-gather(bf16[1,64,128]{2,1,0:T(8,128)(2,1)} %param.10), channel_id=1, replica_groups=mesh['dimer'=4,'grid'=8] {'dimer'}, dimensions={0}, use_global_device_ids=true | all-gather | bytes 81920 | tf_op jit(solution)/shard_map/all_gather | solution.py:31
  17.4 0.9 fusion.41
  18.2 0.2 convolution_convert_fusion
  18.5 14.4 %all_gather.10 = bf16[2,512,128]{2,0,1:T(2,128)(2,1)S(1)} all-gather(bf16[2,64,128]{2,0,1:T(2,128)(2,1)S(1)} %convolution_convert_fusion), channel_id=1, replica_groups=mesh['dimer'=4,'grid'=8] {'grid'}, dimensions={1}, use_global_device_ids=true | all-gather | bytes 294912 | tf_op jit(solution)/shard_map/all_gather | solution.py:40
  32.9 0.0 copy-start.3
  32.9 0.4 fusion.46
  33.3 1.9 %fusion.10 = f32[1280]{0:T(1024)S(1)} fusion(bf16[1280,1024]{1,0:T(8,128)(2,1)} %bitcast.73, bf16[1,512,128]{2,0,1:T(2,128)(2,1)S(1)} %get-tuple-element.12), kind=kOutput, calls=%fused_computation.15 | convolution fusion | flops 168098560 | bytes 1446912 | tf_op jit(solution)/shard_map/dot_general | solution.py:41
  35.2 0.0 copy-done.1
  35.2 0.6 fusion.11
  36.4 0.0 copy-done.3
  36.5 0.7 fusion.34
  37.2 3.3 %fusion.2 = f32[4,2048]{1,0:T(4,128)S(1)} fusion(bf16[1,1280,2048]{2,1,0:T(8,128)(2,1)} %param.9, bf16[2,1280]{1,0:T(2,128)(2,1)S(1)} %subtract_convert_fusion, bf16[2,1280]{1,0:T(2,128)(2,1)S(1)} %fusion.38), kind=kOutput, calls=%fused_computation.2 | convolution fusion | flops 20992000 | bytes 5285888 | tf_op jit(solution)/shard_map/dot_general | solution.py:53
  40.5 1.4 concatenate.7
  42.0 29.1 %psum.7 = f32[4098]{0:T(1024)S(1)} all-reduce(f32[4098]{0:T(1024)S(1)} %concatenate.7), channel_id=1, replica_groups=mesh['dimer'=4,'grid'=8] {'grid'}, use_global_device_ids=true, to_apply=%region_5.6 | all-reduce | flops 4098 | bytes 32784 | tf_op jit(solution)/shard_map/psum | solution.py:60
  71.1 0.7 fusion.47
  71.7 0.0 copy-done
  71.7 1.7 %fusion.16 = f32[1,1,256]{2,1,0:T(1,128)S(1)} fusion(f32[2048,1]{0,1:T(1,128)S(1)} %bitcast.80, f32[1,256,2048]{2,1,0:T(8,128)S(1)} %copy-done), kind=kOutput, calls=%fused_computation.22 | convolution fusion | flops 6291456 | bytes 2106368 | tf_op jit(solution)/shard_map/dot_general | solution.py:65
  73.5 8.4 %all-gather = f32[8,1,256]{2,1,0:T(1,128)S(1)} all-gather(f32[1,1,256]{2,1,0:T(1,128)S(1)} %fusion.16), channel_id=1, replica_groups=mesh['dimer'=4,'grid'=8] {'grid'}, dimensions={0}, use_global_device_ids=true | all-gather | bytes 9216 | tf_op jit(solution)/shard_map/all_gather | solution.py:66
  81.9 0.6 fusion.29
  84.5 0.0 copy-start.2
  84.5 4.1 %fusion.4 = f32[1280,2]{0,1:T(2,128)S(1)} fusion(bf16[1,1280,2048]{2,1,0:T(8,128)(2,1)} %param.9, bf16[2048,1]{0,1:T(2,128)(2,1)S(1)} %stack.36, bf16[2048,1]{0,1:T(2,128)(2,1)S(1)} %stack.35), kind=kOutput, calls=%fused_computation.8 | convolution fusion | flops 10502144 | bytes 5261312 | tf_op jit(solution)/shard_map/dot_general | solution.py:68
  88.6 0.0 copy-done.2
  88.7 0.5 multiply_convert_fusion
  89.1 0.9 convolution_bitcast_fusion
  90.0 0.9 convolution_bitcast_fusion.1
  90.9 0.9 convolution_bitcast_fusion.2
  91.8 2.0 %pad_maximum_fusion = f32[512,3,512]{2,0,1:T(8,128)} fusion(f32[512,1,512]{2,0,1:T(8,128)S(1)} %convolution_bitcast_fusion, f32[512,1,512]{2,0,1:T(8,128)S(1)} %convolution_bitcast_fusion.1, f32[512,1,512]{2,0,1:T(8,128)S(1)} %convolution_bitcast_fusion.2), kind=kLoop, calls=%fused_computation.5 | loop fusion | flops 1572864 | bytes 6291456 | tf_op jit(solution)/shard_map/stack | solution.py:85
  93.8 0.0 copy-start.4
  93.8 0.0 reduce-scatter.2.cloned.1.call-update
  93.8 0.6 copy-done.4
  94.4 0.6 fusion.48
  98.6 34.3 %reduce-scatter.2.cloned.1.call-done = f32[64,3,512]{2,0,1:T(8,128)} async-done(((f32[512,3,512]{2,0,1:T(8,128)}), f32[64,3,512]{2,0,1:T(8,128)}) %reduce-scatter.2.cloned.1.call-update) | async-done | bytes 393232 | tf_op jit(solution)/shard_map/reduce_scatter | solution.py:84
  133.0 1.7 %slice_bitcast_fusion = (f32[1,64,512]{2,1,0:T(8,128)}, f32[64,512]{1,0:T(8,128)S(1)}, f32[64,512]{1,0:T(8,128)S(1)}, f32[64,512]{1,0:T(8,128)S(1)}) fusion(f32[64,3,512]{2,0,1:T(8,128)} %reduce-scatter.2.cloned.1.call-done, pred[]{:T(512)S(6)} %eq.64, pred[]{:T(512)S(6)} %eq.63, pred[]{:T(512)S(6)} %eq.66, pred[]{:T(512)S(6)} %eq.65, pred[]{:T(512)S(6)} %eq.62, ...), kind=kLoop, calls=%fused_computation.26 | loop fusion | flops 294912 | bytes 917510 | tf_op jit(solution)/shard_map/broadcast_in_dim;squeeze | solution.py:108
  134.7 1.5 collective-permute-start
  136.2 1.5 collective-permute-start.1
  137.6 1.5 collective-permute-start.2
  140.3 0.3 collective-permute-done
  140.6 1.3 collective-permute-done.1
  142.0 0.6 collective-permute-done.2
  142.6 1.7 %fusion.24 = f32[1,64,512]{2,1,0:T(8,128)} fusion(f32[64,512]{1,0:T(8,128)S(1)} %collective-permute-done.2, f32[64,512]{1,0:T(8,128)S(1)} %collective-permute-done.1, f32[64,512]{1,0:T(8,128)S(1)} %collective-permute-done, f32[64,3,512]{2,0,1:T(8,128)} %reduce-scatter.2.cloned.1.call-done, pred[]{:T(512)S(6)} %eq.60, pred[]{:T(512)S(6)} %eq.52), kind=kLoop, calls=%fused_computation.32 | loop fusion | flops 196608 | bytes 786434 | tf_op jit(solution)/shard_map/broadcast_in_dim | solution.py:108
  (11 shorter events, 0.2 us)
Async XLA Ops:
  7.2 64.6 %copy-start = (f32[1,256,2048]{2,1,0:T(8,128)S(1)}, f32[1,256,2048]{2,1,0:T(8,128)}, u32[]{:S(2)}) copy-start(f32[1,256,2048]{2,1,0:T(8,128)} %param.15) | copy-start | bytes 6291460
  7.2 125.8 %reduce-scatter.2.cloned.1.call-start = ((), (), s32[]{:S(2)}) async-start(), calls=%async_computation.1 | async-start | bytes 3538944 | tf_op jit(solution)/shard_map/reduce_scatter | solution.py:84
  7.2 28.0 %copy-start.1 = (bf16[1,1280,1024]{2,1,0:T(8,128)(2,1)S(1)}, bf16[1,1280,1024]{2,1,0:T(8,128)(2,1)}, u32[]{:S(2)}) copy-start(bf16[1,1280,1024]{2,1,0:T(8,128)(2,1)} %param.8) | copy-start | bytes 7864324
  32.9 3.5 %copy-start.3 = (f32[1,1280]{1,0:T(1,128)S(1)}, f32[1,1280]{1,0:T(1,128)}, u32[]{:S(2)}) copy-start(f32[1,1280]{1,0:T(1,128)} %param.14) | copy-start | bytes 15364
  84.5 4.2 %copy-start.2 = (bf16[1,1280,1024]{2,1,0:T(8,128)(2,1)S(1)}, bf16[1,1280,1024]{2,1,0:T(8,128)(2,1)}, u32[]{:S(2)}) copy-start(bf16[1,1280,1024]{2,1,0:T(8,128)(2,1)} %param.8) | copy-start | bytes 7864324
  93.8 0.7 copy-start.4
  134.7 6.0 %collective-permute-start = (f32[64,512]{1,0:T(8,128)S(1)}, f32[64,512]{1,0:T(8,128)S(1)}, u32[]{:S(2)}, u32[]{:S(2)}) collective-permute-start(f32[64,512]{1,0:T(8,128)S(1)} %get-tuple-element.10), channel_id=1, source_target_pairs={{0,8},{8,16},{16,24},{24,0},{1,9},{9,17},{17,25},{25,1},{2,10},{10... | collective-permute-start | bytes 393224 | tf_op jit(solution)/shard_map/ppermute | solution.py:105
  136.2 5.8 %collective-permute-start.1 = (f32[64,512]{1,0:T(8,128)S(1)}, f32[64,512]{1,0:T(8,128)S(1)}, u32[]{:S(2)}, u32[]{:S(2)}) collective-permute-start(f32[64,512]{1,0:T(8,128)S(1)} %get-tuple-element.8), channel_id=1, source_target_pairs={{0,16},{8,24},{16,0},{24,8},{1,17},{9,25},{17,1},{25,9},{2,18},{10... | collective-permute-start | bytes 393224 | tf_op jit(solution)/shard_map/ppermute | solution.py:105
  137.6 5.0 %collective-permute-start.2 = (f32[64,512]{1,0:T(8,128)S(1)}, f32[64,512]{1,0:T(8,128)S(1)}, u32[]{:S(2)}, u32[]{:S(2)}) collective-permute-start(f32[64,512]{1,0:T(8,128)S(1)} %get-tuple-element.9), channel_id=1, source_target_pairs={{0,24},{8,0},{16,8},{24,16},{1,25},{9,1},{17,9},{25,17},{2,26},{10... | collective-permute-start | bytes 393224 | tf_op jit(solution)/shard_map/ppermute | solution.py:105
Sparse Core Ops, SparseCore 0:
  93.9 39.0 reduce-scatter.1

commit v2 on v1

--- a/solution.py
+++ b/solution.py
@@ -18,6 +18,34 @@
     return lax.dot_general(left_side, right_side, numbers, preferred_element_type=jnp.float32)
 
 
+def xor_sum(value, axis):
+    size = lax.axis_size(axis)
+    if size & (size - 1):
+        return lax.psum(value, axis)
+    step = 1
+    while step < size:
+        value = value + lax.ppermute(value, axis, [(i, i ^ step) for i in range(size)])
+        step *= 2
+    return value
+
+
+def xor_gather(value, axis, dim):
+    size = lax.axis_size(axis)
+    if size & (size - 1):
+        return lax.all_gather(value, axis, axis=dim, tiled=True)
+    me = lax.axis_index(axis)
+    step = 1
+    while step < size:
+        other = lax.ppermute(value, axis, [(i, i ^ step) for i in range(size)])
+        value = jnp.where(
+            (me & step) == 0,
+            jnp.concatenate([value, other], axis=dim),
+            jnp.concatenate([other, value], axis=dim),
+        )
+        step *= 2
+    return value
+
+
 def shards(basis_values, aux_values, factors, frag_slot, dimer_pairs, counts, weights, metric_inv):
     highest = lax.Precision.HIGHEST
     basis_rows = basis_values[0]
@@ -28,7 +56,7 @@
     live_count = counts[0, 0]
     position = lax.iota(jnp.int32, points)
     live_weight = jnp.where(position < live_count, weights[0], jnp.zeros((), jnp.float32))
-    gathered = lax.all_gather(factors, "dimer", axis=0, tiled=True)
+    gathered = xor_gather(factors, "dimer", 0)
     frag_ids = lax.iota(jnp.int32, frag_slot.shape[0])
     wanted = jnp.sum(
         jnp.where(frag_ids[None, :] == dimer_pairs[0][:, None], frag_slot[None, :], 0), axis=1
@@ -37,7 +65,7 @@
     chosen = jnp.einsum(
         "as,srk->ark", selector, gathered, preferred_element_type=jnp.float32
     ).astype(jnp.bfloat16)
-    dimer_factors = lax.all_gather(chosen, "grid", axis=1, tiled=True)
+    dimer_factors = xor_gather(chosen, "grid", 1)
     orb_first = jnp.dot(
         basis_rows[:, :frag_basis], dimer_factors[0], preferred_element_type=jnp.float32
     )
@@ -57,7 +85,7 @@
     weight_part = projections[1] + projections[3]
     sums_part = jnp.stack([jnp.sum(live_weight * exchange), jnp.sum(live_weight)])
     payload = jnp.concatenate([fitted_part, weight_part, sums_part])
-    totals = lax.psum(payload, "grid")
+    totals = xor_sum(payload, "grid")
     fitted = totals[:naux]
     weight_projection = totals[naux : 2 * naux]
     exchange_total = totals[2 * naux]

time: 152 us -> 133 us (0.88)
  blocking collectives: 62.1 us -> 11.6 us
  waiting for transfers between devices: 36.6 us -> 56.5 us
  starting transfers between devices: 4.44 us -> 15.9 us
  other arithmetic: 8.17 us -> 10.6 us
    psum x1 -> x0, blocking collectives: 29.1 us -> none  [shards(): totals = lax.psum(payload, 'grid')]
    all_gather x2 -> x0, blocking collectives: 24.6 us -> none  [the longest x1 14.4 us: shards(): dimer_factors = lax.all_gather(chosen, 'grid', axis=1, tiled=True)]
    ppermute x0 -> x8, waiting for transfers between devices: none -> 18.6 us  [the longest x5 11 us: xor_gather(): other = lax.ppermute(value, axis, [(i, i ^ step) for i in range(size)])]
    ppermute x0 -> x8, starting transfers between devices: none -> 12.3 us  [the longest x5 10.2 us: xor_gather(): other = lax.ppermute(value, axis, [(i, i ^ step) for i in range(size)])]
    all_gather x1, blocking collectives: 8.44 us -> 11.6 us  [shards(): coefficients = lax.all_gather(coef_rows, 'grid', axis=0, tiled=True)]
    dot_general x1, matrix products: 3.28 us -> 0.79 us  [shards(): jnp.dot(jnp.concatenate([high_rows, low_rows]), aux_block, preferred_elem...]
    select_n x0 -> x5, other arithmetic: none -> 1.83 us  [xor_gather(): jnp.where(me & step == 0, jnp.concatenate([value, other], axis=dim), jnp....]
    ppermute x3, waiting for transfers between devices: 2.27 us -> 4.03 us  [shards(): lax.ppermute(sent, 'dimer', [(i, (i + shift) % groups) for i in range(gro...]
  transfers between devices with their start and end apart: 4 -> 12, of which waited for: 4 -> 12; matrix products, arithmetic and copies ran while one was open for 0% -> 2% of each run, Pallas kernels for 0% -> 0%
where the time goes in v2:
time: 133 us
  waiting for transfers between devices  56.5 us (42%)
  between operations  21.6 us (16%)
  starting transfers between devices  15.9 us (12%)
  matrix products  13.4 us (10%)
  blocking collectives  11.6 us (9%)
  other arithmetic  10.6 us (8%)
  local copies, waits for them, and re-layouts  3.46 us (3%)
    reduce_scatter x1, waiting for transfers between devices, shards(): lax.psum_scatter(jnp.stack([first_first, first_second, second_second], ax...  33.9 us
    all_gather x1, blocking collectives, shards(): coefficients = lax.all_gather(coef_rows, 'grid', axis=0, tiled=True)  11.6 us
    ppermute x5, waiting for transfers between devices, xor_gather(): other = lax.ppermute(value, axis, [(i, i ^ step) for i in range(size)])  11 us
    ppermute x5, starting transfers between devices, xor_gather(): other = lax.ppermute(value, axis, [(i, i ^ step) for i in range(size)])  10.2 us
    ppermute x3, waiting for transfers between devices, xor_sum(): lax.ppermute(value, axis, [(i, i ^ step) for i in range(size)])  7.51 us
    dot_general x1, matrix products, shards(): jnp.dot(aux_block, jnp.stack([coef_high, coef_low], axis=1), preferred_el...  4.09 us
    ppermute x3, waiting for transfers between devices, shards(): lax.ppermute(sent, 'dimer', [(i, (i + shift) % groups) for i in range(gro...  4.03 us
    ppermute x3, starting transfers between devices, shards(): lax.ppermute(sent, 'dimer', [(i, (i + shift) % groups) for i in range(gro...  3.49 us
  transfers between devices with their start and end apart: 12, of which 12 were waited for; matrix products, arithmetic and copies ran while one was open for 2% of the time, Pallas kernels for 0%

profile of v2, /device:TPU:0, one launch (start us, length us, event | category | flops | bytes accessed | tf_op | source)
XLA Modules:
  0.0 133.1 jit_solution(3173696769242370758)
XLA Ops:
  7.2 3.0 %collective-permute-start = (bf16[1,64,128]{2,1,0:T(8,128)(2,1)}, bf16[1,64,128]{2,1,0:T(8,128)(2,1)S(1)}, u32[]{:S(2)}, u32[]{:S(2)}) collective-permute-start(bf16[1,64,128]{2,1,0:T(8,128)(2,1)} %param.10), channel_id=1, source_target_pairs={{0,8},{8,0},{16,24},{24,16},{1,9},{9,1},{17,25},{25,17},{2,10},{10... | collective-permute-start | bytes 49160 | tf_op jit(solution)/shard_map/ppermute | solution.py:39
  10.3 1.9 %collective-permute-done = bf16[1,64,128]{2,1,0:T(8,128)(2,1)S(1)} collective-permute-done((bf16[1,64,128]{2,1,0:T(8,128)(2,1)}, bf16[1,64,128]{2,1,0:T(8,128)(2,1)S(1)}, u32[]{:S(2)}, u32[]{:S(2)}) %collective-permute-start) | collective-permute-done | bytes 16416 | tf_op jit(solution)/shard_map/ppermute | solution.py:39
  12.2 0.8 maximum_select_fusion.1
  13.0 2.0 %collective-permute-start.1 = (bf16[2,64,128]{2,1,0:T(8,128)(2,1)S(1)}, bf16[2,64,128]{2,1,0:T(8,128)(2,1)S(1)}, u32[]{:S(2)}, u32[]{:S(2)}) collective-permute-start(bf16[2,64,128]{2,1,0:T(8,128)(2,1)S(1)} %maximum_select_fusion.1), channel_id=1, source_target_pairs={{0,16},{8,24},{16,0},{24,8},{1,17},{9,25},{17,1},{25,9},{2,18},{10... | collective-permute-start | bytes 98312 | tf_op jit(solution)/shard_map/ppermute | solution.py:39
  15.0 0.9 fusion.45
  15.9 1.0 collective-permute-done.1
  16.9 0.2 convolution_convert_fusion
  17.2 0.1 collective-permute-start.2
  17.3 1.2 collective-permute-done.2
  18.4 0.1 broadcast_select_fusion.2
  18.6 2.1 %collective-permute-start.3 = (bf16[2,128,128]{2,0,1:T(2,128)(2,1)S(1)}, bf16[2,128,128]{2,0,1:T(2,128)(2,1)S(1)}, u32[]{:S(2)}, u32[]{:S(2)}) collective-permute-start(bf16[2,128,128]{2,0,1:T(2,128)(2,1)S(1)} %broadcast_select_fusion.2), channel_id=1, source_target_pairs={{0,2},{1,3},{2,0},{3,1},{4,6},{5,7},{6,4},{7,5},{8,10},{9,11},{10,... | collective-permute-start | bytes 196616 | tf_op jit(solution)/shard_map/ppermute | solution.py:39
  20.7 2.4 %collective-permute-done.3 = bf16[2,128,128]{2,0,1:T(2,128)(2,1)S(1)} collective-permute-done((bf16[2,128,128]{2,0,1:T(2,128)(2,1)S(1)}, bf16[2,128,128]{2,0,1:T(2,128)(2,1)S(1)}, u32[]{:S(2)}, u32[]{:S(2)}) %collective-permute-start.3) | collective-permute-done | bytes 65568 | tf_op jit(solution)/shard_map/ppermute | solution.py:39
  23.2 0.3 broadcast_select_fusion.1
  23.5 2.9 %collective-permute-start.4 = (bf16[2,256,128]{2,0,1:T(2,128)(2,1)S(1)}, bf16[2,256,128]{2,0,1:T(2,128)(2,1)S(1)}, u32[]{:S(2)}, u32[]{:S(2)}) collective-permute-start(bf16[2,256,128]{2,0,1:T(2,128)(2,1)S(1)} %broadcast_select_fusion.1), channel_id=1, source_target_pairs={{0,4},{1,5},{2,6},{3,7},{4,0},{5,1},{6,2},{7,3},{8,12},{9,13},{10,... | collective-permute-start | bytes 393224 | tf_op jit(solution)/shard_map/ppermute | solution.py:39
  27.0 0.7 reduce.3
  27.8 4.5 %collective-permute-done.4 = bf16[2,256,128]{2,0,1:T(2,128)(2,1)S(1)} collective-permute-done((bf16[2,256,128]{2,0,1:T(2,128)(2,1)S(1)}, bf16[2,256,128]{2,0,1:T(2,128)(2,1)S(1)}, u32[]{:S(2)}, u32[]{:S(2)}) %collective-permute-start.4) | collective-permute-done | bytes 131104 | tf_op jit(solution)/shard_map/ppermute | solution.py:39
  32.2 0.6 broadcast_select_fusion
  32.8 0.4 fusion.50
  33.2 2.1 %fusion.10 = f32[1280]{0:T(1024)S(1)} fusion(bf16[1280,1024]{1,0:T(8,128)(2,1)} %bitcast.73, bf16[1,512,128]{2,0,1:T(2,128)(2,1)S(1)} %get-tuple-element.12), kind=kOutput, calls=%fused_computation.15 | convolution fusion | flops 168098560 | bytes 1446912 | tf_op jit(solution)/shard_map/dot_general | solution.py:69
  35.3 1.9 %fusion.11 = f32[1280]{0:T(1024)S(1)} fusion(bf16[1280,1024]{1,0:T(8,128)(2,1)} %bitcast.74, bf16[1,512,128]{2,0,1:T(2,128)(2,1)S(1)} %get-tuple-element.11), kind=kOutput, calls=%fused_computation.16 | convolution fusion | flops 168098560 | bytes 1446912 | tf_op jit(solution)/shard_map/dot_general | solution.py:72
  37.2 0.6 fusion.38
  37.9 0.8 fusion.2
  38.7 1.3 concatenate.47
  40.0 1.2 collective-permute-done.5
  41.2 0.4 collective-permute-start.6
  41.6 3.4 %collective-permute-done.6 = f32[4098]{0:T(1024)S(1)} collective-permute-done((f32[4098]{0:T(1024)S(1)}, f32[4098]{0:T(1024)S(1)}, u32[]{:S(2)}, u32[]{:S(2)}) %collective-permute-start.6) | collective-permute-done | bytes 16424 | tf_op jit(solution)/shard_map/ppermute | solution.py:27
  45.0 1.7 %collective-permute-start.7 = (f32[4098]{0:T(1024)S(1)}, f32[4098]{0:T(1024)S(1)}, u32[]{:S(2)}, u32[]{:S(2)}) collective-permute-start(f32[4098]{0:T(1024)S(1)} %add.101), channel_id=1, source_target_pairs={{0,4},{1,5},{2,6},{3,7},{4,0},{5,1},{6,2},{7,3},{8,12},{9,13},{10,... | collective-permute-start | bytes 49184 | tf_op jit(solution)/shard_map/ppermute | solution.py:27
  46.7 2.9 %collective-permute-done.7 = f32[4098]{0:T(1024)S(1)} collective-permute-done((f32[4098]{0:T(1024)S(1)}, f32[4098]{0:T(1024)S(1)}, u32[]{:S(2)}, u32[]{:S(2)}) %collective-permute-start.7) | collective-permute-done | bytes 16424 | tf_op jit(solution)/shard_map/ppermute | solution.py:27
  49.7 0.6 fusion.51
  50.2 1.7 %fusion.16 = f32[1,1,256]{2,1,0:T(1,128)S(1)} fusion(f32[2048,1]{0,1:T(1,128)S(1)} %bitcast.80, f32[1,256,2048]{2,1,0:T(8,128)S(1)} %copy-done), kind=kOutput, calls=%fused_computation.22 | convolution fusion | flops 6291456 | bytes 2106368 | tf_op jit(solution)/shard_map/dot_general | solution.py:93
  52.0 11.6 %all-gather = f32[8,1,256]{2,1,0:T(1,128)S(1)} all-gather(f32[1,1,256]{2,1,0:T(1,128)S(1)} %fusion.16), channel_id=1, replica_groups=mesh['dimer'=4,'grid'=8] {'grid'}, dimensions={0}, use_global_device_ids=true | all-gather | bytes 9216 | tf_op jit(solution)/shard_map/all_gather | solution.py:94
  63.6 0.6 fusion.33
  66.1 4.1 %fusion.4 = f32[1280,2]{0,1:T(2,128)S(1)} fusion(bf16[1,1280,2048]{2,1,0:T(8,128)(2,1)} %param.9, bf16[2048,1]{0,1:T(2,128)(2,1)S(1)} %stack.36, bf16[2048,1]{0,1:T(2,128)(2,1)S(1)} %stack.35), kind=kOutput, calls=%fused_computation.8 | convolution fusion | flops 10502144 | bytes 5261312 | tf_op jit(solution)/shard_map/dot_general | solution.py:96
  70.2 0.5 multiply_convert_fusion
  70.7 0.9 convolution_bitcast_fusion
  71.6 0.9 convolution_bitcast_fusion.1
  72.5 0.9 convolution_bitcast_fusion.2
  73.4 2.0 %pad_maximum_fusion = f32[512,3,512]{2,0,1:T(8,128)} fusion(f32[512,1,512]{2,0,1:T(8,128)S(1)} %convolution_bitcast_fusion, f32[512,1,512]{2,0,1:T(8,128)S(1)} %convolution_bitcast_fusion.1, f32[512,1,512]{2,0,1:T(8,128)S(1)} %convolution_bitcast_fusion.2), kind=kLoop, calls=%fused_computation.5 | loop fusion | flops 1572864 | bytes 6291456 | tf_op jit(solution)/shard_map/stack | solution.py:113
  75.4 0.6 copy-done.4
  76.0 0.6 fusion.52
  80.2 33.9 %reduce-scatter.2.cloned.1.call-done = f32[64,3,512]{2,0,1:T(8,128)} async-done(((f32[512,3,512]{2,0,1:T(8,128)}), f32[64,3,512]{2,0,1:T(8,128)}) %reduce-scatter.2.cloned.1.call-update) | async-done | bytes 393232 | tf_op jit(solution)/shard_map/reduce_scatter | solution.py:112
  114.1 1.7 %slice_bitcast_fusion = (f32[1,64,512]{2,1,0:T(8,128)}, f32[64,512]{1,0:T(8,128)S(1)}, f32[64,512]{1,0:T(8,128)S(1)}, f32[64,512]{1,0:T(8,128)S(1)}) fusion(f32[64,3,512]{2,0,1:T(8,128)} %reduce-scatter.2.cloned.1.call-done, pred[]{:T(512)S(6)} %eq.84, pred[]{:T(512)S(6)} %eq.83, pred[]{:T(512)S(6)} %eq.86, pred[]{:T(512)S(6)} %eq.85, pred[]{:T(512)S(6)} %eq.82, ...), kind=kLoop, calls=%fused_computation.28 | loop fusion | flops 294912 | bytes 917510 | tf_op jit(solution)/shard_map/broadcast_in_dim;squeeze | solution.py:136
  115.8 2.4 %collective-permute-start.10 = (f32[64,512]{1,0:T(8,128)S(1)}, f32[64,512]{1,0:T(8,128)S(1)}, u32[]{:S(2)}, u32[]{:S(2)}) collective-permute-start(f32[64,512]{1,0:T(8,128)S(1)} %get-tuple-element.9), channel_id=1, source_target_pairs={{0,24},{8,0},{16,8},{24,16},{1,25},{9,1},{17,9},{25,17},{2,26},{10... | collective-permute-start | bytes 393224 | tf_op jit(solution)/shard_map/ppermute | solution.py:133
  118.2 1.1 collective-permute-start.9
  120.5 0.4 collective-permute-done.10
  120.9 3.3 %collective-permute-done.8 = f32[64,512]{1,0:T(8,128)S(1)} collective-permute-done((f32[64,512]{1,0:T(8,128)S(1)}, f32[64,512]{1,0:T(8,128)S(1)}, u32[]{:S(2)}, u32[]{:S(2)}) %collective-permute-start.8) | collective-permute-done | bytes 131104 | tf_op jit(solution)/shard_map/ppermute | solution.py:133
  124.1 0.4 collective-permute-done.9
  124.5 1.7 %fusion.28 = f32[1,64,512]{2,1,0:T(8,128)} fusion(f32[64,512]{1,0:T(8,128)S(1)} %collective-permute-done.10, f32[64,512]{1,0:T(8,128)S(1)} %collective-permute-done.9, f32[64,512]{1,0:T(8,128)S(1)} %collective-permute-done.8, f32[64,3,512]{2,0,1:T(8,128)} %reduce-scatter.2.cloned.1.call-done, pred[]{:T(512)S(6)} %eq.80, pred[]{:T(512)S(6)} %eq.67), kind=kLoop, calls=%fused_computation.36 | loop fusion | flops 196608 | bytes 786434 | tf_op jit(solution)/shard_map/broadcast_in_dim | solution.py:136
  (27 shorter events, 0.3 us)
Async XLA Ops:
  7.2 43.1 %copy-start = (f32[1,256,2048]{2,1,0:T(8,128)S(1)}, f32[1,256,2048]{2,1,0:T(8,128)}, u32[]{:S(2)}) copy-start(f32[1,256,2048]{2,1,0:T(8,128)} %param.15) | copy-start | bytes 6291460
  7.2 106.9 %reduce-scatter.2.cloned.1.call-start = ((), (), s32[]{:S(2)}) async-start(), calls=%async_computation.1 | async-start | bytes 3538944 | tf_op jit(solution)/shard_map/reduce_scatter | solution.py:112
  7.2 5.0 %collective-permute-start = (bf16[1,64,128]{2,1,0:T(8,128)(2,1)}, bf16[1,64,128]{2,1,0:T(8,128)(2,1)S(1)}, u32[]{:S(2)}, u32[]{:S(2)}) collective-permute-start(bf16[1,64,128]{2,1,0:T(8,128)(2,1)} %param.10), channel_id=1, source_target_pairs={{0,8},{8,0},{16,24},{24,16},{1,9},{9,1},{17,25},{25,17},{2,10},{10... | collective-permute-start | bytes 49160 | tf_op jit(solution)/shard_map/ppermute | solution.py:39
  13.0 3.9 %collective-permute-start.1 = (bf16[2,64,128]{2,1,0:T(8,128)(2,1)S(1)}, bf16[2,64,128]{2,1,0:T(8,128)(2,1)S(1)}, u32[]{:S(2)}, u32[]{:S(2)}) collective-permute-start(bf16[2,64,128]{2,1,0:T(8,128)(2,1)S(1)} %maximum_select_fusion.1), channel_id=1, source_target_pairs={{0,16},{8,24},{16,0},{24,8},{1,17},{9,25},{17,1},{25,9},{2,18},{10... | collective-permute-start | bytes 98312 | tf_op jit(solution)/shard_map/ppermute | solution.py:39
  17.2 1.3 collective-permute-start.2
  18.6 4.6 %collective-permute-start.3 = (bf16[2,128,128]{2,0,1:T(2,128)(2,1)S(1)}, bf16[2,128,128]{2,0,1:T(2,128)(2,1)S(1)}, u32[]{:S(2)}, u32[]{:S(2)}) collective-permute-start(bf16[2,128,128]{2,0,1:T(2,128)(2,1)S(1)} %broadcast_select_fusion.2), channel_id=1, source_target_pairs={{0,2},{1,3},{2,0},{3,1},{4,6},{5,7},{6,4},{7,5},{8,10},{9,11},{10,... | collective-permute-start | bytes 196616 | tf_op jit(solution)/shard_map/ppermute | solution.py:39
  23.5 8.8 %collective-permute-start.4 = (bf16[2,256,128]{2,0,1:T(2,128)(2,1)S(1)}, bf16[2,256,128]{2,0,1:T(2,128)(2,1)S(1)}, u32[]{:S(2)}, u32[]{:S(2)}) collective-permute-start(bf16[2,256,128]{2,0,1:T(2,128)(2,1)S(1)} %broadcast_select_fusion.1), channel_id=1, source_target_pairs={{0,4},{1,5},{2,6},{3,7},{4,0},{5,1},{6,2},{7,3},{8,12},{9,13},{10,... | collective-permute-start | bytes 393224 | tf_op jit(solution)/shard_map/ppermute | solution.py:39
  32.8 5.0 %copy-start.3 = (f32[1,1280]{1,0:T(1,128)S(1)}, f32[1,1280]{1,0:T(1,128)}, u32[]{:S(2)}) copy-start(f32[1,1280]{1,0:T(1,128)} %param.14) | copy-start | bytes 15364
  32.8 5.1 %copy-start.1 = (bf16[1,1280,2048]{2,1,0:T(8,128)(2,1)S(1)}, bf16[1,1280,2048]{2,1,0:T(8,128)(2,1)}, u32[]{:S(2)}) copy-start(bf16[1,1280,2048]{2,1,0:T(8,128)(2,1)} %param.9) | copy-start | bytes 15728644
  40.0 1.2 collective-permute-start.5
  41.2 3.8 %collective-permute-start.6 = (f32[4098]{0:T(1024)S(1)}, f32[4098]{0:T(1024)S(1)}, u32[]{:S(2)}, u32[]{:S(2)}) collective-permute-start(f32[4098]{0:T(1024)S(1)} %add.100), channel_id=1, source_target_pairs={{0,2},{1,3},{2,0},{3,1},{4,6},{5,7},{6,4},{7,5},{8,10},{9,11},{10,... | collective-permute-start | bytes 49184 | tf_op jit(solution)/shard_map/ppermute | solution.py:27
  45.0 4.7 %collective-permute-start.7 = (f32[4098]{0:T(1024)S(1)}, f32[4098]{0:T(1024)S(1)}, u32[]{:S(2)}, u32[]{:S(2)}) collective-permute-start(f32[4098]{0:T(1024)S(1)} %add.101), channel_id=1, source_target_pairs={{0,4},{1,5},{2,6},{3,7},{4,0},{5,1},{6,2},{7,3},{8,12},{9,13},{10,... | collective-permute-start | bytes 49184 | tf_op jit(solution)/shard_map/ppermute | solution.py:27
  66.1 4.2 %copy-start.2 = (bf16[1,1280,1024]{2,1,0:T(8,128)(2,1)S(1)}, bf16[1,1280,1024]{2,1,0:T(8,128)(2,1)}, u32[]{:S(2)}) copy-start(bf16[1,1280,1024]{2,1,0:T(8,128)(2,1)} %param.8) | copy-start | bytes 7864324
  75.3 0.7 copy-start.4
  115.8 5.1 %collective-permute-start.10 = (f32[64,512]{1,0:T(8,128)S(1)}, f32[64,512]{1,0:T(8,128)S(1)}, u32[]{:S(2)}, u32[]{:S(2)}) collective-permute-start(f32[64,512]{1,0:T(8,128)S(1)} %get-tuple-element.9), channel_id=1, source_target_pairs={{0,24},{8,0},{16,8},{24,16},{1,25},{9,1},{17,9},{25,17},{2,26},{10... | collective-permute-start | bytes 393224 | tf_op jit(solution)/shard_map/ppermute | solution.py:133
  118.2 6.0 %collective-permute-start.8 = (f32[64,512]{1,0:T(8,128)S(1)}, f32[64,512]{1,0:T(8,128)S(1)}, u32[]{:S(2)}, u32[]{:S(2)}) collective-permute-start(f32[64,512]{1,0:T(8,128)S(1)} %get-tuple-element.10), channel_id=1, source_target_pairs={{0,8},{8,16},{16,24},{24,0},{1,9},{9,17},{17,25},{25,1},{2,10},{10... | collective-permute-start | bytes 393224 | tf_op jit(solution)/shard_map/ppermute | solution.py:133
  118.2 6.4 %collective-permute-start.9 = (f32[64,512]{1,0:T(8,128)S(1)}, f32[64,512]{1,0:T(8,128)S(1)}, u32[]{:S(2)}, u32[]{:S(2)}) collective-permute-start(f32[64,512]{1,0:T(8,128)S(1)} %get-tuple-element.8), channel_id=1, source_target_pairs={{0,16},{8,24},{16,0},{24,8},{1,17},{9,25},{17,1},{25,9},{2,18},{10... | collective-permute-start | bytes 393224 | tf_op jit(solution)/shard_map/ppermute | solution.py:133
Sparse Core Ops, SparseCore 0:
  75.5 38.5 reduce-scatter.1

commit v3 on v2

--- a/solution.py
+++ b/solution.py
@@ -91,12 +91,15 @@
     exchange_total = totals[2 * naux]
     weight_sum = totals[2 * naux + 1]
     coef_rows = jnp.dot(metric_inv[0], fitted, precision=highest)
-    coefficients = lax.all_gather(coef_rows, "grid", axis=0, tiled=True)
+    coefficients = xor_gather(coef_rows, "grid", 0)
     coef_high, coef_low = split_rows(coefficients)
-    coulomb_parts = jnp.dot(
-        aux_block, jnp.stack([coef_high, coef_low], axis=1), preferred_element_type=jnp.float32
+    coulomb_parts = lax.dot_general(
+        jnp.stack([coef_high, coef_low]),
+        aux_block,
+        (((1,), (1,)), ((), ())),
+        preferred_element_type=jnp.float32,
     )
-    coulomb = coulomb_parts[:, 0] + coulomb_parts[:, 1]
+    coulomb = coulomb_parts[0] + coulomb_parts[1]
     potential_total = jnp.dot(coefficients, weight_projection, precision=highest) + exchange_total
     average = potential_total / weight_sum
     potential = live_weight * (coulomb + exchange - average)
@@ -109,15 +112,12 @@
     first_first = contract(left_first, basis_rows[:, :frag_basis])
     first_second = contract(left_first, basis_rows[:, frag_basis:])
     second_second = contract(left_second, basis_rows[:, frag_basis:])
-    shares = lax.psum_scatter(
-        jnp.stack([first_first, first_second, second_second], axis=1),
-        "grid",
-        scatter_dimension=0,
-        tiled=True,
+    diagonal = lax.psum_scatter(
+        jnp.stack([first_first, second_second], axis=1), "grid", scatter_dimension=0, tiled=True
     )
-    own_first = shares[:, 0]
-    own_cross = shares[:, 1]
-    own_second = shares[:, 2]
+    own_cross = lax.psum_scatter(first_second, "grid", scatter_dimension=0, tiled=True)
+    own_first = diagonal[:, 0]
+    own_second = diagonal[:, 1]
     groups = lax.axis_size("dimer")
     me = lax.axis_index("dimer")
     zero = jnp.zeros((), jnp.float32)

time: 133 us -> 152 us (1.14)
  waiting for transfers between devices: 56.5 us -> 79.4 us
  blocking collectives: 11.6 us -> 0 us
  starting transfers between devices: 15.9 us -> 19.3 us
  matrix products: 13.4 us -> 16 us
    reduce_scatter x1 -> x2, waiting for transfers between devices: 33.9 us -> 52.2 us  [the longest x1 28.9 us: shards(): lax.psum_scatter(jnp.stack([first_first, second_second], axis=1), 'grid',...]
    all_gather x1 -> x0, blocking collectives: 11.6 us -> none  [shards(): coefficients = lax.all_gather(coef_rows, 'grid', axis=0, tiled=True)]
    ppermute x5 -> x8, waiting for transfers between devices: 11 us -> 17.2 us  [xor_gather(): other = lax.ppermute(value, axis, [(i, i ^ step) for i in range(size)])]
    dot_general x3, matrix products: 2.62 us -> 5.39 us  [contract(): lax.dot_general(left_side, right_side, numbers, preferred_element_type=jn...]
    ppermute x5 -> x8, starting transfers between devices: 10.2 us -> 12.8 us  [xor_gather(): other = lax.ppermute(value, axis, [(i, i ^ step) for i in range(size)])]
    another operation x2 -> x1, other arithmetic: 3.69 us -> 1.5 us  [shards(): jnp.stack([first_first, second_second], axis=1)]
    convert_element_type x1, other arithmetic: 0.49 us -> 2.38 us  [shards(): weighted_basis = (basis_rows * potential[:, None]).astype(jnp.bfloat16)]
  transfers between devices with their start and end apart: 12 -> 16, of which waited for: 12 -> 16; matrix products, arithmetic and copies ran while one was open for 2% -> 6% of each run, Pallas kernels for 0% -> 0%
where the time goes in v3:
time: 152 us
  waiting for transfers between devices  79.4 us (52%)
  between operations  21.9 us (14%)
  starting transfers between devices  19.3 us (13%)
  matrix products  16 us (11%)
  other arithmetic  11.4 us (8%)
  local copies, waits for them, and re-layouts  3.69 us (2%)
    reduce_scatter x1, waiting for transfers between devices, shards(): lax.psum_scatter(jnp.stack([first_first, second_second], axis=1), 'grid',...  28.9 us
    reduce_scatter x1, waiting for transfers between devices, shards(): lax.psum_scatter(first_second, 'grid', scatter_dimension=0, tiled=True)  23.3 us
    ppermute x8, waiting for transfers between devices, xor_gather(): other = lax.ppermute(value, axis, [(i, i ^ step) for i in range(size)])  17.2 us
    ppermute x8, starting transfers between devices, xor_gather(): other = lax.ppermute(value, axis, [(i, i ^ step) for i in range(size)])  12.8 us
    ppermute x3, waiting for transfers between devices, xor_sum(): lax.ppermute(value, axis, [(i, i ^ step) for i in range(size)])  7.54 us
    dot_general x3, matrix products, contract(): lax.dot_general(left_side, right_side, numbers, preferred_element_type=jn...  5.39 us
    ppermute x3, starting transfers between devices, shards(): lax.ppermute(sent, 'dimer', [(i, (i + shift) % groups) for i in range(gro...  4.29 us
    dot_general x1, matrix products, shards(): lax.dot_general(jnp.stack([coef_high, coef_low]), aux_block, (((1,), (1,)...  3.94 us
  transfers between devices with their start and end apart: 16, of which 16 were waited for; matrix products, arithmetic and copies ran while one was open for 6% of the time, Pallas kernels for 0%

profile of v3, /device:TPU:0, one launch (start us, length us, event | category | flops | bytes accessed | tf_op | source)
XLA Modules:
  0.0 151.7 jit_solution(9521772793374325933)
XLA Ops:
  7.2 3.0 %collective-permute-start = (bf16[1,64,128]{2,1,0:T(8,128)(2,1)}, bf16[1,64,128]{2,1,0:T(8,128)(2,1)S(1)}, u32[]{:S(2)}, u32[]{:S(2)}) collective-permute-start(bf16[1,64,128]{2,1,0:T(8,128)(2,1)} %param.10), channel_id=1, source_target_pairs={{0,8},{8,0},{16,24},{24,16},{1,9},{9,1},{17,25},{25,17},{2,10},{10... | collective-permute-start | bytes 49160 | tf_op jit(solution)/shard_map/ppermute | solution.py:39
  10.3 1.9 %collective-permute-done = bf16[1,64,128]{2,1,0:T(8,128)(2,1)S(1)} collective-permute-done((bf16[1,64,128]{2,1,0:T(8,128)(2,1)}, bf16[1,64,128]{2,1,0:T(8,128)(2,1)S(1)}, u32[]{:S(2)}, u32[]{:S(2)}) %collective-permute-start) | collective-permute-done | bytes 16416 | tf_op jit(solution)/shard_map/ppermute | solution.py:39
  12.2 0.8 maximum_select_fusion.1
  13.0 2.0 %collective-permute-start.1 = (bf16[2,64,128]{2,1,0:T(8,128)(2,1)S(1)}, bf16[2,64,128]{2,1,0:T(8,128)(2,1)S(1)}, u32[]{:S(2)}, u32[]{:S(2)}) collective-permute-start(bf16[2,64,128]{2,1,0:T(8,128)(2,1)S(1)} %maximum_select_fusion.1), channel_id=1, source_target_pairs={{0,16},{8,24},{16,0},{24,8},{1,17},{9,25},{17,1},{25,9},{2,18},{10... | collective-permute-start | bytes 98312 | tf_op jit(solution)/shard_map/ppermute | solution.py:39
  15.0 0.9 fusion.39
  15.9 1.0 collective-permute-done.1
  17.3 1.2 collective-permute-done.2
  18.6 2.1 %collective-permute-start.3 = (bf16[2,128,128]{2,0,1:T(2,128)(2,1)S(1)}, bf16[2,128,128]{2,0,1:T(2,128)(2,1)S(1)}, u32[]{:S(2)}, u32[]{:S(2)}) collective-permute-start(bf16[2,128,128]{2,0,1:T(2,128)(2,1)S(1)} %broadcast_select_fusion.2), channel_id=1, source_target_pairs={{0,2},{1,3},{2,0},{3,1},{4,6},{5,7},{6,4},{7,5},{8,10},{9,11},{10,... | collective-permute-start | bytes 196616 | tf_op jit(solution)/shard_map/ppermute | solution.py:39
  20.7 2.4 %collective-permute-done.3 = bf16[2,128,128]{2,0,1:T(2,128)(2,1)S(1)} collective-permute-done((bf16[2,128,128]{2,0,1:T(2,128)(2,1)S(1)}, bf16[2,128,128]{2,0,1:T(2,128)(2,1)S(1)}, u32[]{:S(2)}, u32[]{:S(2)}) %collective-permute-start.3) | collective-permute-done | bytes 65568 | tf_op jit(solution)/shard_map/ppermute | solution.py:39
  23.5 2.9 %collective-permute-start.4 = (bf16[2,256,128]{2,0,1:T(2,128)(2,1)S(1)}, bf16[2,256,128]{2,0,1:T(2,128)(2,1)S(1)}, u32[]{:S(2)}, u32[]{:S(2)}) collective-permute-start(bf16[2,256,128]{2,0,1:T(2,128)(2,1)S(1)} %broadcast_select_fusion.1), channel_id=1, source_target_pairs={{0,4},{1,5},{2,6},{3,7},{4,0},{5,1},{6,2},{7,3},{8,12},{9,13},{10,... | collective-permute-start | bytes 393224 | tf_op jit(solution)/shard_map/ppermute | solution.py:39
  27.0 0.7 reduce.3
  27.8 4.5 %collective-permute-done.4 = bf16[2,256,128]{2,0,1:T(2,128)(2,1)S(1)} collective-permute-done((bf16[2,256,128]{2,0,1:T(2,128)(2,1)S(1)}, bf16[2,256,128]{2,0,1:T(2,128)(2,1)S(1)}, u32[]{:S(2)}, u32[]{:S(2)}) %collective-permute-start.4) | collective-permute-done | bytes 131104 | tf_op jit(solution)/shard_map/ppermute | solution.py:39
  32.2 0.6 broadcast_select_fusion
  33.2 2.1 %fusion.8 = f32[1280]{0:T(1024)S(1)} fusion(bf16[1280,1024]{1,0:T(8,128)(2,1)} %bitcast.58, bf16[1,512,128]{2,0,1:T(2,128)(2,1)S(1)} %get-tuple-element.10), kind=kOutput, calls=%fused_computation.14 | convolution fusion | flops 168098560 | bytes 1446912 | tf_op jit(solution)/shard_map/dot_general | solution.py:72
  35.3 1.9 %fusion.7 = f32[1280]{0:T(1024)S(1)} fusion(bf16[1280,1024]{1,0:T(8,128)(2,1)} %bitcast.59, bf16[1,512,128]{2,0,1:T(2,128)(2,1)S(1)} %get-tuple-element.11), kind=kOutput, calls=%fused_computation.13 | convolution fusion | flops 168098560 | bytes 1446912 | tf_op jit(solution)/shard_map/dot_general | solution.py:69
  37.2 0.6 fusion.34
  37.9 0.8 fusion.2
  38.7 1.3 concatenate.105
  40.1 1.2 collective-permute-done.5
  41.6 3.4 %collective-permute-done.6 = f32[4098]{0:T(1024)S(1)} collective-permute-done((f32[4098]{0:T(1024)S(1)}, f32[4098]{0:T(1024)S(1)}, u32[]{:S(2)}, u32[]{:S(2)}) %collective-permute-start.6) | collective-permute-done | bytes 16424 | tf_op jit(solution)/shard_map/ppermute | solution.py:27
  45.1 1.7 %collective-permute-start.7 = (f32[4098]{0:T(1024)S(1)}, f32[4098]{0:T(1024)S(1)}, u32[]{:S(2)}, u32[]{:S(2)}) collective-permute-start(f32[4098]{0:T(1024)S(1)} %add.108), channel_id=1, source_target_pairs={{0,4},{1,5},{2,6},{3,7},{4,0},{5,1},{6,2},{7,3},{8,12},{9,13},{10,... | collective-permute-start | bytes 49184 | tf_op jit(solution)/shard_map/ppermute | solution.py:27
  46.8 2.9 %collective-permute-done.7 = f32[4098]{0:T(1024)S(1)} collective-permute-done((f32[4098]{0:T(1024)S(1)}, f32[4098]{0:T(1024)S(1)}, u32[]{:S(2)}, u32[]{:S(2)}) %collective-permute-start.7) | collective-permute-done | bytes 16424 | tf_op jit(solution)/shard_map/ppermute | solution.py:27
  49.7 1.7 %fusion.4 = f32[1,256]{1,0:T(1,128)S(1)} fusion(f32[2048,1]{0,1:T(1,128)S(1)} %bitcast.65, f32[1,256,2048]{2,1,0:T(8,128)S(1)} %copy-done), kind=kOutput, calls=%fused_computation.8 | convolution fusion | flops 6291456 | bytes 2106368 | tf_op jit(solution)/shard_map/dot_general | solution.py:93
  51.5 1.2 collective-permute-done.8
  52.7 0.8 collective-permute-start.9
  53.5 2.8 %collective-permute-done.9 = f32[512]{0:T(512)S(1)} collective-permute-done((f32[512]{0:T(512)S(1)}, f32[512]{0:T(512)S(1)}, u32[]{:S(2)}, u32[]{:S(2)}) %collective-permute-start.9) | collective-permute-done | bytes 2080 | tf_op jit(solution)/shard_map/ppermute | solution.py:39
  56.2 1.7 %collective-permute-start.10 = (f32[1024]{0:T(1024)S(1)}, f32[1024]{0:T(1024)S(1)}, u32[]{:S(2)}, u32[]{:S(2)}) collective-permute-start(f32[1024]{0:T(1024)S(1)} %maximum_select_fusion.3), channel_id=1, source_target_pairs={{0,4},{1,5},{2,6},{3,7},{4,0},{5,1},{6,2},{7,3},{8,12},{9,13},{10,... | collective-permute-start | bytes 12296 | tf_op jit(solution)/shard_map/ppermute | solution.py:39
  58.0 0.6 fusion.46
  58.6 2.2 %collective-permute-done.10 = f32[1024]{0:T(1024)S(1)} collective-permute-done((f32[1024]{0:T(1024)S(1)}, f32[1024]{0:T(1024)S(1)}, u32[]{:S(2)}, u32[]{:S(2)}) %collective-permute-start.10) | collective-permute-done | bytes 4128 | tf_op jit(solution)/shard_map/ppermute | solution.py:39
  60.8 0.6 fusion.29
  61.4 3.9 %fusion = f32[2,1280]{1,0:T(2,128)S(1)} fusion(bf16[1,1280,2048]{2,1,0:T(8,128)(2,1)} %param.9, bf16[1,2048]{1,0:T(2,128)(2,1)S(1)} %stack.30, bf16[1,2048]{1,0:T(2,128)(2,1)S(1)} %fusion.28), kind=kOutput, calls=%fused_computation | convolution fusion | flops 10502144 | bytes 5261312 | tf_op jit(solution)/shard_map/dot_general | solution.py:96
  67.3 2.4 %multiply_convert_fusion = bf16[1280,1024]{1,0:T(8,128)(2,1)S(1)} fusion(f32[1280]{0:T(1024)S(1)} %subtract_multiply_fusion, bf16[1,1280,1024]{2,1,0:T(8,128)(2,1)} %param.8), kind=kLoop, calls=%fused_computation.4 | loop fusion | flops 3932160 | bytes 5248000 | tf_op jit(solution)/shard_map/convert_element_type | solution.py:106
  69.8 0.9 convolution_bitcast_fusion
  70.7 0.6 copy-done.3
  71.3 0.9 convolution_bitcast_fusion.1
  72.2 1.5 pad_maximum_fusion
  73.8 3.6 %fusion.9 = f32[512,512]{1,0:T(8,128)} fusion(bf16[1280,1024]{1,0:T(8,128)(2,1)} %copy-done.3, bf16[1280,1024]{1,0:T(8,128)(2,1)} %bitcast.60), kind=kOutput, calls=%fused_computation.15 | convolution fusion | flops 671088640 | bytes 3670016 | tf_op jit(solution)/shard_map/dot_general | solution.py:18
  77.4 0.6 fusion.47
  81.8 28.9 %reduce-scatter.3.cloned.1.call-done = f32[64,2,512]{2,0,1:T(8,128)} async-done(((f32[512,2,512]{2,0,1:T(8,128)}), f32[64,2,512]{2,0,1:T(8,128)}) %reduce-scatter.3.cloned.1.call-update) | async-done | bytes 262160 | tf_op jit(solution)/shard_map/reduce_scatter | solution.py:115
  110.7 1.0 add_bitcast_fusion.2
  111.7 1.6 %collective-permute-start.11 = (f32[64,512]{1,0:T(8,128)S(1)}, f32[64,512]{1,0:T(8,128)S(1)}, u32[]{:S(2)}, u32[]{:S(2)}) collective-permute-start(f32[64,512]{1,0:T(8,128)S(1)} %get-tuple-element.7), channel_id=1, source_target_pairs={{0,8},{8,16},{16,24},{24,0},{1,9},{9,17},{17,25},{25,1},{2,10},{10... | collective-permute-start | bytes 393224 | tf_op jit(solution)/shard_map/ppermute | solution.py:133
  113.3 1.5 %collective-permute-start.12 = (f32[64,512]{1,0:T(8,128)S(1)}, f32[64,512]{1,0:T(8,128)S(1)}, u32[]{:S(2)}, u32[]{:S(2)}) collective-permute-start(f32[64,512]{1,0:T(8,128)S(1)} %get-tuple-element.8), channel_id=1, source_target_pairs={{0,16},{8,24},{16,0},{24,8},{1,17},{9,25},{17,1},{25,9},{2,18},{10... | collective-permute-start | bytes 393224 | tf_op jit(solution)/shard_map/ppermute | solution.py:133
  114.8 1.2 collective-permute-start.13
  117.3 0.4 collective-permute-done.11
  117.7 1.3 collective-permute-done.12
  119.1 0.7 collective-permute-done.13
  119.8 1.7 %fusion.23 = f32[1,64,512]{2,1,0:T(8,128)} fusion(f32[64,512]{1,0:T(8,128)S(1)} %collective-permute-done.13, f32[64,512]{1,0:T(8,128)S(1)} %collective-permute-done.12, f32[64,512]{1,0:T(8,128)S(1)} %collective-permute-done.11, f32[64,2,512]{2,0,1:T(8,128)} %reduce-scatter.3.cloned.1.call-done, pred[]{:T(512)S(6)} %eq.83, pred[]{:T(512)S(6)} %eq.70), kind=kLoop, calls=%fused_computation.33 | loop fusion | flops 196608 | bytes 786434 | tf_op jit(solution)/shard_map/broadcast_in_dim | solution.py:136
  121.5 23.3 %reduce-scatter.5.cloned.1.call-done = f32[64,512]{1,0:T(8,128)} async-done(((f32[512,512]{1,0:T(8,128)}), f32[64,512]{1,0:T(8,128)}) %reduce-scatter.5.cloned.1.call-update) | async-done | bytes 131088 | tf_op jit(solution)/shard_map/reduce_scatter | solution.py:118
  (39 shorter events, 2.0 us)
Async XLA Ops:
  7.2 42.6 %copy-start = (f32[1,256,2048]{2,1,0:T(8,128)S(1)}, f32[1,256,2048]{2,1,0:T(8,128)}, u32[]{:S(2)}) copy-start(f32[1,256,2048]{2,1,0:T(8,128)} %param.15) | copy-start | bytes 6291460
  7.2 103.5 %reduce-scatter.3.cloned.1.call-start = ((), (), s32[]{:S(2)}) async-start(), calls=%async_computation.2 | async-start | bytes 2359296 | tf_op jit(solution)/shard_map/reduce_scatter | solution.py:115
  7.2 5.0 %collective-permute-start = (bf16[1,64,128]{2,1,0:T(8,128)(2,1)}, bf16[1,64,128]{2,1,0:T(8,128)(2,1)S(1)}, u32[]{:S(2)}, u32[]{:S(2)}) collective-permute-start(bf16[1,64,128]{2,1,0:T(8,128)(2,1)} %param.10), channel_id=1, source_target_pairs={{0,8},{8,0},{16,24},{24,16},{1,9},{9,1},{17,25},{25,17},{2,10},{10... | collective-permute-start | bytes 49160 | tf_op jit(solution)/shard_map/ppermute | solution.py:39
  13.0 3.9 %collective-permute-start.1 = (bf16[2,64,128]{2,1,0:T(8,128)(2,1)S(1)}, bf16[2,64,128]{2,1,0:T(8,128)(2,1)S(1)}, u32[]{:S(2)}, u32[]{:S(2)}) collective-permute-start(bf16[2,64,128]{2,1,0:T(8,128)(2,1)S(1)} %maximum_select_fusion.1), channel_id=1, source_target_pairs={{0,16},{8,24},{16,0},{24,8},{1,17},{9,25},{17,1},{25,9},{2,18},{10... | collective-permute-start | bytes 98312 | tf_op jit(solution)/shard_map/ppermute | solution.py:39
  17.2 1.3 collective-permute-start.2
  18.6 4.6 %collective-permute-start.3 = (bf16[2,128,128]{2,0,1:T(2,128)(2,1)S(1)}, bf16[2,128,128]{2,0,1:T(2,128)(2,1)S(1)}, u32[]{:S(2)}, u32[]{:S(2)}) collective-permute-start(bf16[2,128,128]{2,0,1:T(2,128)(2,1)S(1)} %broadcast_select_fusion.2), channel_id=1, source_target_pairs={{0,2},{1,3},{2,0},{3,1},{4,6},{5,7},{6,4},{7,5},{8,10},{9,11},{10,... | collective-permute-start | bytes 196616 | tf_op jit(solution)/shard_map/ppermute | solution.py:39
  23.5 8.8 %collective-permute-start.4 = (bf16[2,256,128]{2,0,1:T(2,128)(2,1)S(1)}, bf16[2,256,128]{2,0,1:T(2,128)(2,1)S(1)}, u32[]{:S(2)}, u32[]{:S(2)}) collective-permute-start(bf16[2,256,128]{2,0,1:T(2,128)(2,1)S(1)} %broadcast_select_fusion.1), channel_id=1, source_target_pairs={{0,4},{1,5},{2,6},{3,7},{4,0},{5,1},{6,2},{7,3},{8,12},{9,13},{10,... | collective-permute-start | bytes 393224 | tf_op jit(solution)/shard_map/ppermute | solution.py:39
  32.8 5.0 %copy-start.4 = (f32[1,1280]{1,0:T(1,128)S(1)}, f32[1,1280]{1,0:T(1,128)}, u32[]{:S(2)}) copy-start(f32[1,1280]{1,0:T(1,128)} %param.14) | copy-start | bytes 15364
  32.8 5.1 %copy-start.1 = (bf16[1,1280,2048]{2,1,0:T(8,128)(2,1)S(1)}, bf16[1,1280,2048]{2,1,0:T(8,128)(2,1)}, u32[]{:S(2)}) copy-start(bf16[1,1280,2048]{2,1,0:T(8,128)(2,1)} %param.9) | copy-start | bytes 15728644
  40.1 1.2 collective-permute-start.5
  41.3 3.8 %collective-permute-start.6 = (f32[4098]{0:T(1024)S(1)}, f32[4098]{0:T(1024)S(1)}, u32[]{:S(2)}, u32[]{:S(2)}) collective-permute-start(f32[4098]{0:T(1024)S(1)} %add.107), channel_id=1, source_target_pairs={{0,2},{1,3},{2,0},{3,1},{4,6},{5,7},{6,4},{7,5},{8,10},{9,11},{10,... | collective-permute-start | bytes 49184 | tf_op jit(solution)/shard_map/ppermute | solution.py:27
  45.1 4.7 %collective-permute-start.7 = (f32[4098]{0:T(1024)S(1)}, f32[4098]{0:T(1024)S(1)}, u32[]{:S(2)}, u32[]{:S(2)}) collective-permute-start(f32[4098]{0:T(1024)S(1)} %add.108), channel_id=1, source_target_pairs={{0,4},{1,5},{2,6},{3,7},{4,0},{5,1},{6,2},{7,3},{8,12},{9,13},{10,... | collective-permute-start | bytes 49184 | tf_op jit(solution)/shard_map/ppermute | solution.py:27
  51.5 1.2 collective-permute-start.8
  52.7 3.6 %collective-permute-start.9 = (f32[512]{0:T(512)S(1)}, f32[512]{0:T(512)S(1)}, u32[]{:S(2)}, u32[]{:S(2)}) collective-permute-start(f32[512]{0:T(512)S(1)} %maximum_select_fusion.4), channel_id=1, source_target_pairs={{0,2},{1,3},{2,0},{3,1},{4,6},{5,7},{6,4},{7,5},{8,10},{9,11},{10,... | collective-permute-start | bytes 6152 | tf_op jit(solution)/shard_map/ppermute | solution.py:39
  56.2 4.5 %collective-permute-start.10 = (f32[1024]{0:T(1024)S(1)}, f32[1024]{0:T(1024)S(1)}, u32[]{:S(2)}, u32[]{:S(2)}) collective-permute-start(f32[1024]{0:T(1024)S(1)} %maximum_select_fusion.3), channel_id=1, source_target_pairs={{0,4},{1,5},{2,6},{3,7},{4,0},{5,1},{6,2},{7,3},{8,12},{9,13},{10,... | collective-permute-start | bytes 12296 | tf_op jit(solution)/shard_map/ppermute | solution.py:39
  67.3 2.5 %copy-start.2 = (bf16[1,1280,1024]{2,1,0:T(8,128)(2,1)S(1)}, bf16[1,1280,1024]{2,1,0:T(8,128)(2,1)}, u32[]{:S(2)}) copy-start(bf16[1,1280,1024]{2,1,0:T(8,128)(2,1)} %param.8) | copy-start | bytes 7864324
  69.8 1.5 copy-start.3
  73.7 3.7 %copy-start.5 = (s32[1,2]{1,0:T(1,128)S(1)}, s32[1,2]{1,0:T(1,128)}, u32[]{:S(2)}) copy-start(s32[1,2]{1,0:T(1,128)} %param.12) | copy-start | bytes 28
  73.7 71.1 %reduce-scatter.5.cloned.1.call-start = ((), (), s32[]{:S(2)}) async-start(), calls=%async_computation.3 | async-start | bytes 1179648 | tf_op jit(solution)/shard_map/reduce_scatter | solution.py:118
  111.7 6.0 %collective-permute-start.11 = (f32[64,512]{1,0:T(8,128)S(1)}, f32[64,512]{1,0:T(8,128)S(1)}, u32[]{:S(2)}, u32[]{:S(2)}) collective-permute-start(f32[64,512]{1,0:T(8,128)S(1)} %get-tuple-element.7), channel_id=1, source_target_pairs={{0,8},{8,16},{16,24},{24,0},{1,9},{9,17},{17,25},{25,1},{2,10},{10... | collective-permute-start | bytes 393224 | tf_op jit(solution)/shard_map/ppermute | solution.py:133
  113.3 5.8 %collective-permute-start.12 = (f32[64,512]{1,0:T(8,128)S(1)}, f32[64,512]{1,0:T(8,128)S(1)}, u32[]{:S(2)}, u32[]{:S(2)}) collective-permute-start(f32[64,512]{1,0:T(8,128)S(1)} %get-tuple-element.8), channel_id=1, source_target_pairs={{0,16},{8,24},{16,0},{24,8},{1,17},{9,25},{17,1},{25,9},{2,18},{10... | collective-permute-start | bytes 393224 | tf_op jit(solution)/shard_map/ppermute | solution.py:133
  114.8 5.0 %collective-permute-start.13 = (f32[64,512]{1,0:T(8,128)S(1)}, f32[64,512]{1,0:T(8,128)S(1)}, u32[]{:S(2)}, u32[]{:S(2)}) collective-permute-start(f32[64,512]{1,0:T(8,128)S(1)} %get-tuple-element.9), channel_id=1, source_target_pairs={{0,24},{8,0},{16,8},{24,16},{1,25},{9,1},{17,9},{25,17},{2,26},{10... | collective-permute-start | bytes 393224 | tf_op jit(solution)/shard_map/ppermute | solution.py:133
Sparse Core Ops, SparseCore 0:
  73.8 36.8 reduce-scatter.2
  113.6 31.2 reduce-scatter.4

commit v4 on v2

--- a/solution.py
+++ b/solution.py
@@ -46,6 +46,23 @@
     return value
 
 
+def xor_scatter(value, axis):
+    size = lax.axis_size(axis)
+    if size & (size - 1):
+        return lax.psum_scatter(value, axis, scatter_dimension=0, tiled=True)
+    me = lax.axis_index(axis)
+    value = value.reshape((size, value.shape[0] // size) + value.shape[1:])
+    bit = 0
+    while (1 << bit) < size:
+        pairs = value.reshape((value.shape[0] // 2, 2) + value.shape[1:])
+        mine = (me >> bit) & 1
+        keep = lax.dynamic_index_in_dim(pairs, mine, axis=1, keepdims=False)
+        send = lax.dynamic_index_in_dim(pairs, 1 - mine, axis=1, keepdims=False)
+        value = keep + lax.ppermute(send, axis, [(i, i ^ (1 << bit)) for i in range(size)])
+        bit += 1
+    return value[0]
+
+
 def shards(basis_values, aux_values, factors, frag_slot, dimer_pairs, counts, weights, metric_inv):
     highest = lax.Precision.HIGHEST
     basis_rows = basis_values[0]
@@ -91,7 +108,7 @@
     exchange_total = totals[2 * naux]
     weight_sum = totals[2 * naux + 1]
     coef_rows = jnp.dot(metric_inv[0], fitted, precision=highest)
-    coefficients = lax.all_gather(coef_rows, "grid", axis=0, tiled=True)
+    coefficients = xor_gather(coef_rows, "grid", 0)
     coef_high, coef_low = split_rows(coefficients)
     coulomb_parts = jnp.dot(
         aux_block, jnp.stack([coef_high, coef_low], axis=1), preferred_element_type=jnp.float32
@@ -109,12 +126,7 @@
     first_first = contract(left_first, basis_rows[:, :frag_basis])
     first_second = contract(left_first, basis_rows[:, frag_basis:])
     second_second = contract(left_second, basis_rows[:, frag_basis:])
-    shares = lax.psum_scatter(
-        jnp.stack([first_first, first_second, second_second], axis=1),
-        "grid",
-        scatter_dimension=0,
-        tiled=True,
-    )
+    shares = xor_scatter(jnp.stack([first_first, first_second, second_second], axis=1), "grid")
     own_first = shares[:, 0]
     own_cross = shares[:, 1]
     own_second = shares[:, 2]

time: 133 us -> 127 us (0.955)
  between operations: 21.6 us -> 8.42 us
  blocking collectives: 11.6 us -> 0 us
  waiting for transfers between devices: 56.5 us -> 63.6 us
  starting transfers between devices: 15.9 us -> 22 us
  local copies, waits for them, and re-layouts: 3.46 us -> 7.05 us
    ppermute x0 -> x3, waiting for transfers between devices: none -> 36.1 us  [xor_scatter(): lax.ppermute(send, axis, [(i, i ^ 1 << bit) for i in range(size)])]
    reduce_scatter x1 -> x0, waiting for transfers between devices: 33.9 us -> none  [shards(): lax.psum_scatter(jnp.stack([first_first, first_second, second_second], ax...]
    all_gather x1 -> x0, blocking collectives: 11.6 us -> none  [shards(): coefficients = lax.all_gather(coef_rows, 'grid', axis=0, tiled=True)]
    ppermute x5 -> x8, waiting for transfers between devices: 11 us -> 17.1 us  [xor_gather(): other = lax.ppermute(value, axis, [(i, i ^ step) for i in range(size)])]
    add x0 -> x2, other arithmetic: none -> 3.74 us  [xor_scatter(): keep + lax.ppermute(send, axis, [(i, i ^ 1 << bit) for i in range(size)])]
    ppermute x0 -> x3, starting transfers between devices: none -> 2.99 us  [xor_scatter(): lax.ppermute(send, axis, [(i, i ^ 1 << bit) for i in range(size)])]
    dynamic_slice x0 -> x2, local copies, waits for them, and re-layouts: none -> 2.77 us  [the longest x1 1.49 us: xor_scatter(): keep = lax.dynamic_index_in_dim(pairs, mine, axis=1, keepdims=False)]
    ppermute x5 -> x8, starting transfers between devices: 10.2 us -> 12.8 us  [xor_gather(): other = lax.ppermute(value, axis, [(i, i ^ step) for i in range(size)])]
  transfers between devices with their start and end apart: 12 -> 17, of which waited for: 12 -> 16; matrix products, arithmetic and copies ran while one was open for 2% -> 2% of each run, Pallas kernels for 0% -> 0%
where the time goes in v4:
time: 127 us; the launch traced here: 126 us
  waiting for transfers between devices  63.6 us (50%)
  starting transfers between devices  22 us (17%)
  matrix products  13.4 us (11%)
  other arithmetic  11.9 us (9%)
  between operations  8.42 us (7%)
  local copies, waits for them, and re-layouts  7.05 us (6%)
    ppermute x3, waiting for transfers between devices, xor_scatter(): lax.ppermute(send, axis, [(i, i ^ 1 << bit) for i in range(size)])  36.1 us
    ppermute x8, waiting for transfers between devices, xor_gather(): other = lax.ppermute(value, axis, [(i, i ^ step) for i in range(size)])  17.1 us
    ppermute x8, starting transfers between devices, xor_gather(): other = lax.ppermute(value, axis, [(i, i ^ step) for i in range(size)])  12.8 us
    ppermute x3, waiting for transfers between devices, xor_sum(): lax.ppermute(value, axis, [(i, i ^ step) for i in range(size)])  7.54 us
    ppermute x3, starting transfers between devices, shards(): lax.ppermute(sent, 'dimer', [(i, (i + shift) % groups) for i in range(gro...  4.14 us
    dot_general x1, matrix products, shards(): jnp.dot(aux_block, jnp.stack([coef_high, coef_low], axis=1), preferred_el...  4.09 us
    add x2, other arithmetic, xor_scatter(): keep + lax.ppermute(send, axis, [(i, i ^ 1 << bit) for i in range(size)])  3.74 us
    ppermute x3, starting transfers between devices, xor_scatter(): lax.ppermute(send, axis, [(i, i ^ 1 << bit) for i in range(size)])  2.99 us
  transfers between devices with their start and end apart: 17, of which 16 were waited for; matrix products, arithmetic and copies ran while one was open for 2% of the time, Pallas kernels for 0%

profile of v4, /device:TPU:0, one launch (start us, length us, event | category | flops | bytes accessed | tf_op | source)
XLA Modules:
  0.0 126.4 jit_solution(11738893888732505061)
XLA Ops:
  0.6 3.0 %collective-permute-start = (bf16[1,64,128]{2,1,0:T(8,128)(2,1)}, bf16[1,64,128]{2,1,0:T(8,128)(2,1)S(1)}, u32[]{:S(2)}, u32[]{:S(2)}) collective-permute-start(bf16[1,64,128]{2,1,0:T(8,128)(2,1)} %param.10), channel_id=1, source_target_pairs={{0,8},{8,0},{16,24},{24,16},{1,9},{9,1},{17,25},{25,17},{2,10},{10... | collective-permute-start | bytes 49160 | tf_op jit(solution)/shard_map/ppermute | solution.py:39
  3.7 1.9 %collective-permute-done = bf16[1,64,128]{2,1,0:T(8,128)(2,1)S(1)} collective-permute-done((bf16[1,64,128]{2,1,0:T(8,128)(2,1)}, bf16[1,64,128]{2,1,0:T(8,128)(2,1)S(1)}, u32[]{:S(2)}, u32[]{:S(2)}) %collective-permute-start) | collective-permute-done | bytes 16416 | tf_op jit(solution)/shard_map/ppermute | solution.py:39
  5.6 0.8 maximum_select_fusion.1
  6.4 2.0 %collective-permute-start.1 = (bf16[2,64,128]{2,1,0:T(8,128)(2,1)S(1)}, bf16[2,64,128]{2,1,0:T(8,128)(2,1)S(1)}, u32[]{:S(2)}, u32[]{:S(2)}) collective-permute-start(bf16[2,64,128]{2,1,0:T(8,128)(2,1)S(1)} %maximum_select_fusion.1), channel_id=1, source_target_pairs={{0,16},{8,24},{16,0},{24,8},{1,17},{9,25},{17,1},{25,9},{2,18},{10... | collective-permute-start | bytes 98312 | tf_op jit(solution)/shard_map/ppermute | solution.py:39
  8.5 0.9 fusion.46
  9.3 1.0 collective-permute-done.1
  10.7 1.2 collective-permute-done.2
  12.0 2.1 %collective-permute-start.3 = (bf16[2,128,128]{2,0,1:T(2,128)(2,1)S(1)}, bf16[2,128,128]{2,0,1:T(2,128)(2,1)S(1)}, u32[]{:S(2)}, u32[]{:S(2)}) collective-permute-start(bf16[2,128,128]{2,0,1:T(2,128)(2,1)S(1)} %broadcast_select_fusion.2), channel_id=1, source_target_pairs={{0,2},{1,3},{2,0},{3,1},{4,6},{5,7},{6,4},{7,5},{8,10},{9,11},{10,... | collective-permute-start | bytes 196616 | tf_op jit(solution)/shard_map/ppermute | solution.py:39
  14.2 2.4 %collective-permute-done.3 = bf16[2,128,128]{2,0,1:T(2,128)(2,1)S(1)} collective-permute-done((bf16[2,128,128]{2,0,1:T(2,128)(2,1)S(1)}, bf16[2,128,128]{2,0,1:T(2,128)(2,1)S(1)}, u32[]{:S(2)}, u32[]{:S(2)}) %collective-permute-start.3) | collective-permute-done | bytes 65568 | tf_op jit(solution)/shard_map/ppermute | solution.py:39
  16.9 2.9 %collective-permute-start.4 = (bf16[2,256,128]{2,0,1:T(2,128)(2,1)S(1)}, bf16[2,256,128]{2,0,1:T(2,128)(2,1)S(1)}, u32[]{:S(2)}, u32[]{:S(2)}) collective-permute-start(bf16[2,256,128]{2,0,1:T(2,128)(2,1)S(1)} %broadcast_select_fusion.1), channel_id=1, source_target_pairs={{0,4},{1,5},{2,6},{3,7},{4,0},{5,1},{6,2},{7,3},{8,12},{9,13},{10,... | collective-permute-start | bytes 393224 | tf_op jit(solution)/shard_map/ppermute | solution.py:39
  20.5 0.7 reduce.3
  21.2 4.5 %collective-permute-done.4 = bf16[2,256,128]{2,0,1:T(2,128)(2,1)S(1)} collective-permute-done((bf16[2,256,128]{2,0,1:T(2,128)(2,1)S(1)}, bf16[2,256,128]{2,0,1:T(2,128)(2,1)S(1)}, u32[]{:S(2)}, u32[]{:S(2)}) %collective-permute-start.4) | collective-permute-done | bytes 131104 | tf_op jit(solution)/shard_map/ppermute | solution.py:39
  26.6 2.1 %fusion.11 = f32[1280]{0:T(1024)S(1)} fusion(bf16[1280,1024]{1,0:T(8,128)(2,1)} %bitcast.80, bf16[1,512,128]{2,0,1:T(2,128)(2,1)S(1)} %get-tuple-element.14), kind=kOutput, calls=%fused_computation.15 | convolution fusion | flops 168098560 | bytes 1446912 | tf_op jit(solution)/shard_map/dot_general | solution.py:86
  28.7 1.9 %fusion.12 = f32[1280]{0:T(1024)S(1)} fusion(bf16[1280,1024]{1,0:T(8,128)(2,1)} %bitcast.81, bf16[1,512,128]{2,0,1:T(2,128)(2,1)S(1)} %get-tuple-element.13), kind=kOutput, calls=%fused_computation.16 | convolution fusion | flops 168098560 | bytes 1446912 | tf_op jit(solution)/shard_map/dot_general | solution.py:89
  30.6 0.7 fusion.39
  31.4 0.8 fusion.2
  32.2 1.4 %concatenate.106 = f32[4098]{0:T(1024)S(1)} concatenate(f32[2048]{0:T(1024)S(1)} %bitcast.92, f32[2048]{0:T(1024)S(1)} %bitcast.91, f32[1]{0:T(128)} %bitcast.9, f32[1]{0:T(128)} %bitcast.10), dimensions={0} | concatenate | bytes 32784 | tf_op jit(solution)/shard_map/concatenate | solution.py:104
  33.6 1.2 collective-permute-done.5
  35.2 3.4 %collective-permute-done.6 = f32[4098]{0:T(1024)S(1)} collective-permute-done((f32[4098]{0:T(1024)S(1)}, f32[4098]{0:T(1024)S(1)}, u32[]{:S(2)}, u32[]{:S(2)}) %collective-permute-start.6) | collective-permute-done | bytes 16424 | tf_op jit(solution)/shard_map/ppermute | solution.py:27
  38.6 1.7 %collective-permute-start.7 = (f32[4098]{0:T(1024)S(1)}, f32[4098]{0:T(1024)S(1)}, u32[]{:S(2)}, u32[]{:S(2)}) collective-permute-start(f32[4098]{0:T(1024)S(1)} %add.132), channel_id=1, source_target_pairs={{0,4},{1,5},{2,6},{3,7},{4,0},{5,1},{6,2},{7,3},{8,12},{9,13},{10,... | collective-permute-start | bytes 49184 | tf_op jit(solution)/shard_map/ppermute | solution.py:27
  40.3 2.9 %collective-permute-done.7 = f32[4098]{0:T(1024)S(1)} collective-permute-done((f32[4098]{0:T(1024)S(1)}, f32[4098]{0:T(1024)S(1)}, u32[]{:S(2)}, u32[]{:S(2)}) %collective-permute-start.7) | collective-permute-done | bytes 16424 | tf_op jit(solution)/shard_map/ppermute | solution.py:27
  43.3 1.7 %fusion.7 = f32[1,256]{1,0:T(1,128)S(1)} fusion(f32[2048,1]{0,1:T(1,128)S(1)} %bitcast.90, f32[1,256,2048]{2,1,0:T(8,128)S(1)} %copy-done), kind=kOutput, calls=%fused_computation.9 | convolution fusion | flops 6291456 | bytes 2106368 | tf_op jit(solution)/shard_map/dot_general | solution.py:110
  45.0 1.2 collective-permute-done.8
  46.2 0.8 collective-permute-start.9
  47.1 2.7 %collective-permute-done.9 = f32[512]{0:T(512)S(1)} collective-permute-done((f32[512]{0:T(512)S(1)}, f32[512]{0:T(512)S(1)}, u32[]{:S(2)}, u32[]{:S(2)}) %collective-permute-start.9) | collective-permute-done | bytes 2080 | tf_op jit(solution)/shard_map/ppermute | solution.py:39
  49.8 1.7 %collective-permute-start.10 = (f32[1024]{0:T(1024)S(1)}, f32[1024]{0:T(1024)S(1)}, u32[]{:S(2)}, u32[]{:S(2)}) collective-permute-start(f32[1024]{0:T(1024)S(1)} %maximum_select_fusion.3), channel_id=1, source_target_pairs={{0,4},{1,5},{2,6},{3,7},{4,0},{5,1},{6,2},{7,3},{8,12},{9,13},{10,... | collective-permute-start | bytes 12296 | tf_op jit(solution)/shard_map/ppermute | solution.py:39
  52.2 2.1 %collective-permute-done.10 = f32[1024]{0:T(1024)S(1)} collective-permute-done((f32[1024]{0:T(1024)S(1)}, f32[1024]{0:T(1024)S(1)}, u32[]{:S(2)}, u32[]{:S(2)}) %collective-permute-start.10) | collective-permute-done | bytes 4128 | tf_op jit(solution)/shard_map/ppermute | solution.py:39
  56.9 4.1 %fusion.4 = f32[1280,2]{0,1:T(2,128)S(1)} fusion(bf16[1,1280,2048]{2,1,0:T(8,128)(2,1)} %param.9, bf16[2048,1]{0,1:T(2,128)(2,1)S(1)} %stack.33, bf16[2048,1]{0,1:T(2,128)(2,1)S(1)} %fusion.33), kind=kOutput, calls=%fused_computation.8 | convolution fusion | flops 10502144 | bytes 5261312 | tf_op jit(solution)/shard_map/dot_general | solution.py:113
  61.6 0.9 fusion.15
  62.5 0.9 fusion.13
  63.3 0.9 fusion.9
  64.6 1.5 %constant_dynamic-slice_fusion.2 = (f32[4,1,64,3,512]{4,2,1,0,3:T(8,128)}, f32[4,1,64,3,512]{4,2,1,0,3:T(8,128)S(1)}) fusion(f32[4,2,64,3,512]{4,2,1,0,3:T(8,128)S(1)} %pad_maximum_fusion, s32[]{:T(128)S(6)} %select_n.207, s32[]{:T(128)S(6)} %select_n.208), kind=kLoop, calls=%fused_computation.85 | loop fusion | bytes 6291464 | tf_op jit(solution)/shard_map/jit(dynamic_index_in_dim)/dynamic_slice | solution.py:59
  66.1 1.3 %copy.33 = f32[4,1,64,3,512]{4,2,3,0,1:T(8,128)} copy(f32[4,1,64,3,512]{4,2,1,0,3:T(8,128)S(1)} %get-tuple-element.8) | data formatting | bytes 3145728 | tf_op jit(solution)/shard_map/jit(dynamic_index_in_dim)/dynamic_slice | solution.py:60
  67.4 3.7 %collective-permute-done.11 = f32[4,64,3,512]{3,1,2,0:T(8,128)} collective-permute-done((f32[4,64,3,512]{3,1,2,0:T(8,128)}, f32[4,64,3,512]{3,1,2,0:T(8,128)}, u32[]{:S(2)}, u32[]{:S(2)}) %collective-permute-start.11) | collective-permute-done | bytes 1572896 | tf_op jit(solution)/shard_map/ppermute | solution.py:61
  71.1 2.2 %bitcast_add_fusion = f32[4,64,3,512]{3,1,2,0:T(8,128)S(1)} fusion(f32[4,64,3,512]{3,1,2,0:T(8,128)} %collective-permute-done.11, f32[4,1,64,3,512]{4,2,1,0,3:T(8,128)} %get-tuple-element.7), kind=kLoop, calls=%fused_computation.11 | loop fusion | flops 393216 | bytes 4718592 | tf_op jit(solution)/shard_map/add | solution.py:61
  73.4 1.1 copy-done.2
  74.6 0.9 collective-permute-start.12
  75.5 18.8 %collective-permute-done.12 = f32[2,64,3,512]{3,1,2,0:T(8,128)} collective-permute-done((f32[2,64,3,512]{3,1,2,0:T(8,128)S(1)}, f32[2,64,3,512]{3,1,2,0:T(8,128)}, u32[]{:S(2)}, u32[]{:S(2)}) %collective-permute-start.12) | collective-permute-done | bytes 786464 | tf_op jit(solution)/shard_map/ppermute | solution.py:61
  94.3 1.5 %bitcast_add_fusion.1 = f32[2,64,3,512]{3,1,2,0:T(8,128)S(1)} fusion(f32[2,64,3,512]{3,1,2,0:T(8,128)} %collective-permute-done.12, f32[2,2,64,3,512]{4,2,3,1,0:T(8,128)} %bitcast.79, s32[]{:T(128)S(6)} %select_n.209), kind=kLoop, calls=%fused_computation.27 | loop fusion | flops 196608 | bytes 2359300 | tf_op jit(solution)/shard_map/add | solution.py:61
  95.9 2.1 %collective-permute-start.13 = (f32[1,64,3,512]{3,1,2,0:T(8,128)S(1)}, f32[1,64,3,512]{3,1,2,0:T(8,128)}, u32[]{:S(2)}, u32[]{:S(2)}) collective-permute-start(f32[1,64,3,512]{3,1,2,0:T(8,128)S(1)} %constant_dynamic-slice_fusion), channel_id=1, source_target_pairs={{0,4},{1,5},{2,6},{3,7},{4,0},{5,1},{6,2},{7,3},{8,12},{9,13},{10,... | collective-permute-start | bytes 1179656 | tf_op jit(solution)/shard_map/ppermute | solution.py:61
  102.2 13.5 %collective-permute-done.13 = f32[1,64,3,512]{3,1,2,0:T(8,128)} collective-permute-done((f32[1,64,3,512]{3,1,2,0:T(8,128)S(1)}, f32[1,64,3,512]{3,1,2,0:T(8,128)}, u32[]{:S(2)}, u32[]{:S(2)}) %collective-permute-start.13) | collective-permute-done | bytes 393248 | tf_op jit(solution)/shard_map/ppermute | solution.py:61
  115.7 1.0 add_bitcast_fusion
  117.4 1.2 collective-permute-start.14
  118.6 1.5 %collective-permute-start.15 = (f32[64,512]{1,0:T(8,128)S(1)}, f32[64,512]{1,0:T(8,128)S(1)}, u32[]{:S(2)}, u32[]{:S(2)}) collective-permute-start(f32[64,512]{1,0:T(8,128)S(1)} %get-tuple-element.10), channel_id=1, source_target_pairs={{0,16},{8,24},{16,0},{24,8},{1,17},{9,25},{17,1},{25,9},{2,18},{10... | collective-permute-start | bytes 393224 | tf_op jit(solution)/shard_map/ppermute | solution.py:145
  120.1 1.4 %collective-permute-start.16 = (f32[64,512]{1,0:T(8,128)S(1)}, f32[64,512]{1,0:T(8,128)S(1)}, u32[]{:S(2)}, u32[]{:S(2)}) collective-permute-start(f32[64,512]{1,0:T(8,128)S(1)} %get-tuple-element.11), channel_id=1, source_target_pairs={{0,24},{8,0},{16,8},{24,16},{1,25},{9,1},{17,9},{25,17},{2,26},{10... | collective-permute-start | bytes 393224 | tf_op jit(solution)/shard_map/ppermute | solution.py:145
  122.8 1.9 %collective-permute-done.14 = f32[64,512]{1,0:T(8,128)S(1)} collective-permute-done((f32[64,512]{1,0:T(8,128)S(1)}, f32[64,512]{1,0:T(8,128)S(1)}, u32[]{:S(2)}, u32[]{:S(2)}) %collective-permute-start.14) | collective-permute-done | bytes 131104 | tf_op jit(solution)/shard_map/ppermute | solution.py:145
  124.6 1.1 collective-permute-done.15
  125.7 0.7 fusion.28
  (46 shorter events, 5.8 us)
Async XLA Ops:
  0.6 42.7 %copy-start = (f32[1,256,2048]{2,1,0:T(8,128)S(1)}, f32[1,256,2048]{2,1,0:T(8,128)}, u32[]{:S(2)}) copy-start(f32[1,256,2048]{2,1,0:T(8,128)} %param.15) | copy-start | bytes 6291460
  0.6 5.0 %collective-permute-start = (bf16[1,64,128]{2,1,0:T(8,128)(2,1)}, bf16[1,64,128]{2,1,0:T(8,128)(2,1)S(1)}, u32[]{:S(2)}, u32[]{:S(2)}) collective-permute-start(bf16[1,64,128]{2,1,0:T(8,128)(2,1)} %param.10), channel_id=1, source_target_pairs={{0,8},{8,0},{16,24},{24,16},{1,9},{9,1},{17,25},{25,17},{2,10},{10... | collective-permute-start | bytes 49160 | tf_op jit(solution)/shard_map/ppermute | solution.py:39
  6.4 3.9 %collective-permute-start.1 = (bf16[2,64,128]{2,1,0:T(8,128)(2,1)S(1)}, bf16[2,64,128]{2,1,0:T(8,128)(2,1)S(1)}, u32[]{:S(2)}, u32[]{:S(2)}) collective-permute-start(bf16[2,64,128]{2,1,0:T(8,128)(2,1)S(1)} %maximum_select_fusion.1), channel_id=1, source_target_pairs={{0,16},{8,24},{16,0},{24,8},{1,17},{9,25},{17,1},{25,9},{2,18},{10... | collective-permute-start | bytes 98312 | tf_op jit(solution)/shard_map/ppermute | solution.py:39
  10.6 1.3 %collective-permute-start.2 = (bf16[2,64,128]{2,0,1:T(2,128)(2,1)S(1)}, bf16[2,64,128]{2,0,1:T(2,128)(2,1)S(1)}, u32[]{:S(2)}, u32[]{:S(2)}) collective-permute-start(bf16[2,64,128]{2,0,1:T(2,128)(2,1)S(1)} %convolution_convert_fusion), channel_id=1, source_target_pairs={{0,1},{1,0},{2,3},{3,2},{4,5},{5,4},{6,7},{7,6},{8,9},{9,8},{10,11... | collective-permute-start | bytes 98312 | tf_op jit(solution)/shard_map/ppermute | solution.py:39
  12.0 4.6 %collective-permute-start.3 = (bf16[2,128,128]{2,0,1:T(2,128)(2,1)S(1)}, bf16[2,128,128]{2,0,1:T(2,128)(2,1)S(1)}, u32[]{:S(2)}, u32[]{:S(2)}) collective-permute-start(bf16[2,128,128]{2,0,1:T(2,128)(2,1)S(1)} %broadcast_select_fusion.2), channel_id=1, source_target_pairs={{0,2},{1,3},{2,0},{3,1},{4,6},{5,7},{6,4},{7,5},{8,10},{9,11},{10,... | collective-permute-start | bytes 196616 | tf_op jit(solution)/shard_map/ppermute | solution.py:39
  16.9 8.8 %collective-permute-start.4 = (bf16[2,256,128]{2,0,1:T(2,128)(2,1)S(1)}, bf16[2,256,128]{2,0,1:T(2,128)(2,1)S(1)}, u32[]{:S(2)}, u32[]{:S(2)}) collective-permute-start(bf16[2,256,128]{2,0,1:T(2,128)(2,1)S(1)} %broadcast_select_fusion.1), channel_id=1, source_target_pairs={{0,4},{1,5},{2,6},{3,7},{4,0},{5,1},{6,2},{7,3},{8,12},{9,13},{10,... | collective-permute-start | bytes 393224 | tf_op jit(solution)/shard_map/ppermute | solution.py:39
  26.2 5.1 %copy-start.4 = (f32[1,1280]{1,0:T(1,128)S(1)}, f32[1,1280]{1,0:T(1,128)}, u32[]{:S(2)}) copy-start(f32[1,1280]{1,0:T(1,128)} %param.14) | copy-start | bytes 15364
  26.2 5.1 %copy-start.1 = (bf16[1,1280,2048]{2,1,0:T(8,128)(2,1)S(1)}, bf16[1,1280,2048]{2,1,0:T(8,128)(2,1)}, u32[]{:S(2)}) copy-start(bf16[1,1280,2048]{2,1,0:T(8,128)(2,1)} %param.9) | copy-start | bytes 15728644
  33.6 1.2 collective-permute-start.5
  34.8 3.8 %collective-permute-start.6 = (f32[4098]{0:T(1024)S(1)}, f32[4098]{0:T(1024)S(1)}, u32[]{:S(2)}, u32[]{:S(2)}) collective-permute-start(f32[4098]{0:T(1024)S(1)} %add.131), channel_id=1, source_target_pairs={{0,2},{1,3},{2,0},{3,1},{4,6},{5,7},{6,4},{7,5},{8,10},{9,11},{10,... | collective-permute-start | bytes 49184 | tf_op jit(solution)/shard_map/ppermute | solution.py:27
  38.6 4.7 %collective-permute-start.7 = (f32[4098]{0:T(1024)S(1)}, f32[4098]{0:T(1024)S(1)}, u32[]{:S(2)}, u32[]{:S(2)}) collective-permute-start(f32[4098]{0:T(1024)S(1)} %add.132), channel_id=1, source_target_pairs={{0,4},{1,5},{2,6},{3,7},{4,0},{5,1},{6,2},{7,3},{8,12},{9,13},{10,... | collective-permute-start | bytes 49184 | tf_op jit(solution)/shard_map/ppermute | solution.py:27
  45.0 1.2 collective-permute-start.8
  46.2 3.6 %collective-permute-start.9 = (f32[512]{0:T(512)S(1)}, f32[512]{0:T(512)S(1)}, u32[]{:S(2)}, u32[]{:S(2)}) collective-permute-start(f32[512]{0:T(512)S(1)} %maximum_select_fusion.4), channel_id=1, source_target_pairs={{0,2},{1,3},{2,0},{3,1},{4,6},{5,7},{6,4},{7,5},{8,10},{9,11},{10,... | collective-permute-start | bytes 6152 | tf_op jit(solution)/shard_map/ppermute | solution.py:39
  49.8 4.5 %collective-permute-start.10 = (f32[1024]{0:T(1024)S(1)}, f32[1024]{0:T(1024)S(1)}, u32[]{:S(2)}, u32[]{:S(2)}) collective-permute-start(f32[1024]{0:T(1024)S(1)} %maximum_select_fusion.3), channel_id=1, source_target_pairs={{0,4},{1,5},{2,6},{3,7},{4,0},{5,1},{6,2},{7,3},{8,12},{9,13},{10,... | collective-permute-start | bytes 12296 | tf_op jit(solution)/shard_map/ppermute | solution.py:39
  56.9 4.2 %copy-start.3 = (bf16[1,1280,1024]{2,1,0:T(8,128)(2,1)S(1)}, bf16[1,1280,1024]{2,1,0:T(8,128)(2,1)}, u32[]{:S(2)}) copy-start(bf16[1,1280,1024]{2,1,0:T(8,128)(2,1)} %param.8) | copy-start | bytes 7864324
  67.4 3.8 %collective-permute-start.11 = (f32[4,64,3,512]{3,1,2,0:T(8,128)}, f32[4,64,3,512]{3,1,2,0:T(8,128)}, u32[]{:S(2)}, u32[]{:S(2)}) collective-permute-start(f32[4,64,3,512]{3,1,2,0:T(8,128)} %bitcast.74), channel_id=1, source_target_pairs={{0,1},{1,0},{2,3},{3,2},{4,5},{5,4},{6,7},{7,6},{8,9},{9,8},{10,11... | collective-permute-start | bytes 4718600 | tf_op jit(solution)/shard_map/ppermute | solution.py:61
  73.3 1.1 copy-start.2
  73.4 24.6 %copy-start.5 = (s32[1,2]{1,0:T(1,128)S(1)}, s32[1,2]{1,0:T(1,128)}, u32[]{:S(2)}) copy-start(s32[1,2]{1,0:T(1,128)} %param.12) | copy-start | bytes 28
  74.6 19.8 %collective-permute-start.12 = (f32[2,64,3,512]{3,1,2,0:T(8,128)S(1)}, f32[2,64,3,512]{3,1,2,0:T(8,128)}, u32[]{:S(2)}, u32[]{:S(2)}) collective-permute-start(f32[2,64,3,512]{3,1,2,0:T(8,128)S(1)} %dynamic-slice_bitcast_fusion), channel_id=1, source_target_pairs={{0,2},{1,3},{2,0},{3,1},{4,6},{5,7},{6,4},{7,5},{8,10},{9,11},{10,... | collective-permute-start | bytes 2359304 | tf_op jit(solution)/shard_map/ppermute | solution.py:61
  95.9 19.8 %collective-permute-start.13 = (f32[1,64,3,512]{3,1,2,0:T(8,128)S(1)}, f32[1,64,3,512]{3,1,2,0:T(8,128)}, u32[]{:S(2)}, u32[]{:S(2)}) collective-permute-start(f32[1,64,3,512]{3,1,2,0:T(8,128)S(1)} %constant_dynamic-slice_fusion), channel_id=1, source_target_pairs={{0,4},{1,5},{2,6},{3,7},{4,0},{5,1},{6,2},{7,3},{8,12},{9,13},{10,... | collective-permute-start | bytes 1179656 | tf_op jit(solution)/shard_map/ppermute | solution.py:61
  117.4 7.2 %collective-permute-start.14 = (f32[64,512]{1,0:T(8,128)S(1)}, f32[64,512]{1,0:T(8,128)S(1)}, u32[]{:S(2)}, u32[]{:S(2)}) collective-permute-start(f32[64,512]{1,0:T(8,128)S(1)} %get-tuple-element.12), channel_id=1, source_target_pairs={{0,8},{8,16},{16,24},{24,0},{1,9},{9,17},{17,25},{25,1},{2,10},{10... | collective-permute-start | bytes 393224 | tf_op jit(solution)/shard_map/ppermute | solution.py:145
  118.6 7.1 %collective-permute-start.15 = (f32[64,512]{1,0:T(8,128)S(1)}, f32[64,512]{1,0:T(8,128)S(1)}, u32[]{:S(2)}, u32[]{:S(2)}) collective-permute-start(f32[64,512]{1,0:T(8,128)S(1)} %get-tuple-element.10), channel_id=1, source_target_pairs={{0,16},{8,24},{16,0},{24,8},{1,17},{9,25},{17,1},{25,9},{2,18},{10... | collective-permute-start | bytes 393224 | tf_op jit(solution)/shard_map/ppermute | solution.py:145
  120.1 5.6 %collective-permute-start.16 = (f32[64,512]{1,0:T(8,128)S(1)}, f32[64,512]{1,0:T(8,128)S(1)}, u32[]{:S(2)}, u32[]{:S(2)}) collective-permute-start(f32[64,512]{1,0:T(8,128)S(1)} %get-tuple-element.11), channel_id=1, source_target_pairs={{0,24},{8,0},{16,8},{24,16},{1,25},{9,1},{17,9},{25,17},{2,26},{10... | collective-permute-start | bytes 393224 | tf_op jit(solution)/shard_map/ppermute | solution.py:145

commit v5 on v4

--- a/solution.py
+++ b/solution.py
@@ -46,21 +46,36 @@
     return value
 
 
-def xor_scatter(value, axis):
+def scatter_chunks(value, axis):
+    size = lax.axis_size(axis)
+    return value.reshape((size, value.shape[0] // size) + value.shape[1:])
+
+
+def scatter_step(value, axis, bit):
+    size = lax.axis_size(axis)
+    mine = (lax.axis_index(axis) >> bit) & 1
+    pairs = value.reshape((value.shape[0] // 2, 2) + value.shape[1:])
+    keep = lax.dynamic_index_in_dim(pairs, mine, axis=1, keepdims=False)
+    send = lax.dynamic_index_in_dim(pairs, 1 - mine, axis=1, keepdims=False)
+    return keep + lax.ppermute(send, axis, [(i, i ^ (1 << bit)) for i in range(size)])
+
+
+def paired_scatter(lead, follow, axis):
     size = lax.axis_size(axis)
     if size & (size - 1):
-        return lax.psum_scatter(value, axis, scatter_dimension=0, tiled=True)
-    me = lax.axis_index(axis)
-    value = value.reshape((size, value.shape[0] // size) + value.shape[1:])
+        return (
+            lax.psum_scatter(lead, axis, scatter_dimension=0, tiled=True),
+            lax.psum_scatter(follow, axis, scatter_dimension=0, tiled=True),
+        )
+    lead = scatter_chunks(lead, axis)
+    follow = scatter_chunks(follow, axis)
     bit = 0
     while (1 << bit) < size:
-        pairs = value.reshape((value.shape[0] // 2, 2) + value.shape[1:])
-        mine = (me >> bit) & 1
-        keep = lax.dynamic_index_in_dim(pairs, mine, axis=1, keepdims=False)
-        send = lax.dynamic_index_in_dim(pairs, 1 - mine, axis=1, keepdims=False)
-        value = keep + lax.ppermute(send, axis, [(i, i ^ (1 << bit)) for i in range(size)])
+        lead = scatter_step(lead, axis, bit)
+        follow, _ = lax.optimization_barrier((follow, lead))
+        follow = scatter_step(follow, axis, bit)
         bit += 1
-    return value[0]
+    return lead[0], follow[0]
 
 
 def shards(basis_values, aux_values, factors, frag_slot, dimer_pairs, counts, weights, metric_inv):
@@ -126,10 +141,11 @@
     first_first = contract(left_first, basis_rows[:, :frag_basis])
     first_second = contract(left_first, basis_rows[:, frag_basis:])
     second_second = contract(left_second, basis_rows[:, frag_basis:])
-    shares = xor_scatter(jnp.stack([first_first, first_second, second_second], axis=1), "grid")
-    own_first = shares[:, 0]
-    own_cross = shares[:, 1]
-    own_second = shares[:, 2]
+    diagonal, own_cross = paired_scatter(
+        jnp.stack([first_first, second_second], axis=1), first_second, "grid"
+    )
+    own_first = diagonal[:, 0]
+    own_second = diagonal[:, 1]
     groups = lax.axis_size("dimer")
     me = lax.axis_index("dimer")
     zero = jnp.zeros((), jnp.float32)

time: 127 us -> 111 us (0.87)
  waiting for transfers between devices: 63.6 us -> 46.3 us
  starting transfers between devices: 22 us -> 24.5 us
  local copies, waits for them, and re-layouts: 7.05 us -> 5.74 us
    ppermute x3 -> x6, waiting for transfers between devices: 36.1 us -> 21.1 us  [scatter_step(): lax.ppermute(send, axis, [(i, i ^ 1 << bit) for i in range(size)])]
    dynamic_slice x2 -> x1, local copies, waits for them, and re-layouts: 2.77 us -> 0.07 us  [scatter_step(): send = lax.dynamic_index_in_dim(pairs, 1 - mine, axis=1, keepdims=False)]
    squeeze x2 -> x5, local copies, waits for them, and re-layouts: 0.11 us -> 2.7 us  [scatter_step(): send = lax.dynamic_index_in_dim(pairs, 1 - mine, axis=1, keepdims=False)]
    ppermute x3, waiting for transfers between devices: 2.93 us -> 0.53 us  [shards(): lax.ppermute(sent, 'dimer', [(i, (i + shift) % groups) for i in range(gro...]
    add x2 -> x7, other arithmetic: 3.74 us -> 6.1 us  [the longest x6 6.05 us: scatter_step(): keep + lax.ppermute(send, axis, [(i, i ^ 1 << bit) for i in range(size)])]
    ppermute x3 -> x6, starting transfers between devices: 2.99 us -> 5.01 us  [scatter_step(): lax.ppermute(send, axis, [(i, i ^ 1 << bit) for i in range(size)])]
  transfers between devices with their start and end apart: 17 -> 20, of which waited for: 16 -> 18; matrix products, arithmetic and copies ran while one was open for 2% -> 8% of each run, Pallas kernels for 0% -> 0%
where the time goes in v5:
time: 111 us
  waiting for transfers between devices  46.3 us (42%)
  starting transfers between devices  24.5 us (22%)
  matrix products  13.4 us (12%)
  other arithmetic  12.4 us (11%)
  between operations  8.65 us (8%)
  local copies, waits for them, and re-layouts  5.74 us (5%)
    ppermute x6, waiting for transfers between devices, scatter_step(): lax.ppermute(send, axis, [(i, i ^ 1 << bit) for i in range(size)])  21.1 us
    ppermute x8, waiting for transfers between devices, xor_gather(): other = lax.ppermute(value, axis, [(i, i ^ step) for i in range(size)])  17.1 us
    ppermute x8, starting transfers between devices, xor_gather(): other = lax.ppermute(value, axis, [(i, i ^ step) for i in range(size)])  12.8 us
    ppermute x3, waiting for transfers between devices, xor_sum(): lax.ppermute(value, axis, [(i, i ^ step) for i in range(size)])  7.53 us
    add x6, other arithmetic, scatter_step(): keep + lax.ppermute(send, axis, [(i, i ^ 1 << bit) for i in range(size)])  6.05 us
    ppermute x6, starting transfers between devices, scatter_step(): lax.ppermute(send, axis, [(i, i ^ 1 << bit) for i in range(size)])  5.01 us
    ppermute x3, starting transfers between devices, shards(): lax.ppermute(sent, 'dimer', [(i, (i + shift) % groups) for i in range(gro...  4.59 us
    dot_general x1, matrix products, shards(): jnp.dot(aux_block, jnp.stack([coef_high, coef_low], axis=1), preferred_el...  4.09 us
  transfers between devices with their start and end apart: 20, of which 18 were waited for; matrix products, arithmetic and copies ran while one was open for 8% of the time, Pallas kernels for 0%

profile of v5, /device:TPU:0, one launch (start us, length us, event | category | flops | bytes accessed | tf_op | source)
XLA Modules:
  0.0 110.9 jit_solution(18061460688477271932)
XLA Ops:
  0.6 3.0 %collective-permute-start = (bf16[1,64,128]{2,1,0:T(8,128)(2,1)}, bf16[1,64,128]{2,1,0:T(8,128)(2,1)S(1)}, u32[]{:S(2)}, u32[]{:S(2)}) collective-permute-start(bf16[1,64,128]{2,1,0:T(8,128)(2,1)} %param.10), channel_id=1, source_target_pairs={{0,8},{8,0},{16,24},{24,16},{1,9},{9,1},{17,25},{25,17},{2,10},{10... | collective-permute-start | bytes 49160 | tf_op jit(solution)/shard_map/ppermute | solution.py:39
  3.7 1.9 %collective-permute-done = bf16[1,64,128]{2,1,0:T(8,128)(2,1)S(1)} collective-permute-done((bf16[1,64,128]{2,1,0:T(8,128)(2,1)}, bf16[1,64,128]{2,1,0:T(8,128)(2,1)S(1)}, u32[]{:S(2)}, u32[]{:S(2)}) %collective-permute-start) | collective-permute-done | bytes 16416 | tf_op jit(solution)/shard_map/ppermute | solution.py:39
  5.6 0.8 maximum_select_fusion.1
  6.4 2.0 %collective-permute-start.1 = (bf16[2,64,128]{2,1,0:T(8,128)(2,1)S(1)}, bf16[2,64,128]{2,1,0:T(8,128)(2,1)S(1)}, u32[]{:S(2)}, u32[]{:S(2)}) collective-permute-start(bf16[2,64,128]{2,1,0:T(8,128)(2,1)S(1)} %maximum_select_fusion.1), channel_id=1, source_target_pairs={{0,16},{8,24},{16,0},{24,8},{1,17},{9,25},{17,1},{25,9},{2,18},{10... | collective-permute-start | bytes 98312 | tf_op jit(solution)/shard_map/ppermute | solution.py:39
  8.5 0.9 fusion.48
  9.3 1.0 collective-permute-done.1
  10.7 1.2 %collective-permute-done.2 = bf16[2,64,128]{2,0,1:T(2,128)(2,1)S(1)} collective-permute-done((bf16[2,64,128]{2,0,1:T(2,128)(2,1)S(1)}, bf16[2,64,128]{2,0,1:T(2,128)(2,1)S(1)}, u32[]{:S(2)}, u32[]{:S(2)}) %collective-permute-start.2) | collective-permute-done | bytes 32800 | tf_op jit(solution)/shard_map/ppermute | solution.py:39
  12.0 2.1 %collective-permute-start.3 = (bf16[2,128,128]{2,0,1:T(2,128)(2,1)S(1)}, bf16[2,128,128]{2,0,1:T(2,128)(2,1)S(1)}, u32[]{:S(2)}, u32[]{:S(2)}) collective-permute-start(bf16[2,128,128]{2,0,1:T(2,128)(2,1)S(1)} %broadcast_select_fusion.2), channel_id=1, source_target_pairs={{0,2},{1,3},{2,0},{3,1},{4,6},{5,7},{6,4},{7,5},{8,10},{9,11},{10,... | collective-permute-start | bytes 196616 | tf_op jit(solution)/shard_map/ppermute | solution.py:39
  14.2 2.4 %collective-permute-done.3 = bf16[2,128,128]{2,0,1:T(2,128)(2,1)S(1)} collective-permute-done((bf16[2,128,128]{2,0,1:T(2,128)(2,1)S(1)}, bf16[2,128,128]{2,0,1:T(2,128)(2,1)S(1)}, u32[]{:S(2)}, u32[]{:S(2)}) %collective-permute-start.3) | collective-permute-done | bytes 65568 | tf_op jit(solution)/shard_map/ppermute | solution.py:39
  16.9 2.9 %collective-permute-start.4 = (bf16[2,256,128]{2,0,1:T(2,128)(2,1)S(1)}, bf16[2,256,128]{2,0,1:T(2,128)(2,1)S(1)}, u32[]{:S(2)}, u32[]{:S(2)}) collective-permute-start(bf16[2,256,128]{2,0,1:T(2,128)(2,1)S(1)} %broadcast_select_fusion.1), channel_id=1, source_target_pairs={{0,4},{1,5},{2,6},{3,7},{4,0},{5,1},{6,2},{7,3},{8,12},{9,13},{10,... | collective-permute-start | bytes 393224 | tf_op jit(solution)/shard_map/ppermute | solution.py:39
  20.5 0.7 reduce.3
  21.2 4.5 %collective-permute-done.4 = bf16[2,256,128]{2,0,1:T(2,128)(2,1)S(1)} collective-permute-done((bf16[2,256,128]{2,0,1:T(2,128)(2,1)S(1)}, bf16[2,256,128]{2,0,1:T(2,128)(2,1)S(1)}, u32[]{:S(2)}, u32[]{:S(2)}) %collective-permute-start.4) | collective-permute-done | bytes 131104 | tf_op jit(solution)/shard_map/ppermute | solution.py:39
  26.6 2.1 %fusion.12 = f32[1280]{0:T(1024)S(1)} fusion(bf16[1280,1024]{1,0:T(8,128)(2,1)} %bitcast.91, bf16[1,512,128]{2,0,1:T(2,128)(2,1)S(1)} %get-tuple-element.18), kind=kOutput, calls=%fused_computation.17 | convolution fusion | flops 168098560 | bytes 1446912 | tf_op jit(solution)/shard_map/dot_general | solution.py:104
  28.7 1.9 %fusion.11 = f32[1280]{0:T(1024)S(1)} fusion(bf16[1280,1024]{1,0:T(8,128)(2,1)} %bitcast.92, bf16[1,512,128]{2,0,1:T(2,128)(2,1)S(1)} %get-tuple-element.19), kind=kOutput, calls=%fused_computation.16 | convolution fusion | flops 168098560 | bytes 1446912 | tf_op jit(solution)/shard_map/dot_general | solution.py:101
  31.3 0.8 fusion.2
  32.2 1.4 %concatenate.106 = f32[4098]{0:T(1024)S(1)} concatenate(f32[2048]{0:T(1024)S(1)} %bitcast.109, f32[2048]{0:T(1024)S(1)} %bitcast.108, f32[1]{0:T(128)} %bitcast.9, f32[1]{0:T(128)} %bitcast.10), dimensions={0} | concatenate | bytes 32784 | tf_op jit(solution)/shard_map/concatenate | solution.py:119
  33.5 1.2 %collective-permute-done.5 = f32[4098]{0:T(1024)S(1)} collective-permute-done((f32[4098]{0:T(1024)S(1)}, f32[4098]{0:T(1024)S(1)}, u32[]{:S(2)}, u32[]{:S(2)}) %collective-permute-start.5) | collective-permute-done | bytes 16424 | tf_op jit(solution)/shard_map/ppermute | solution.py:27
  35.1 3.4 %collective-permute-done.6 = f32[4098]{0:T(1024)S(1)} collective-permute-done((f32[4098]{0:T(1024)S(1)}, f32[4098]{0:T(1024)S(1)}, u32[]{:S(2)}, u32[]{:S(2)}) %collective-permute-start.6) | collective-permute-done | bytes 16424 | tf_op jit(solution)/shard_map/ppermute | solution.py:27
  38.5 1.7 %collective-permute-start.7 = (f32[4098]{0:T(1024)S(1)}, f32[4098]{0:T(1024)S(1)}, u32[]{:S(2)}, u32[]{:S(2)}) collective-permute-start(f32[4098]{0:T(1024)S(1)} %add.150), channel_id=1, source_target_pairs={{0,4},{1,5},{2,6},{3,7},{4,0},{5,1},{6,2},{7,3},{8,12},{9,13},{10,... | collective-permute-start | bytes 49184 | tf_op jit(solution)/shard_map/ppermute | solution.py:27
  40.2 2.9 %collective-permute-done.7 = f32[4098]{0:T(1024)S(1)} collective-permute-done((f32[4098]{0:T(1024)S(1)}, f32[4098]{0:T(1024)S(1)}, u32[]{:S(2)}, u32[]{:S(2)}) %collective-permute-start.7) | collective-permute-done | bytes 16424 | tf_op jit(solution)/shard_map/ppermute | solution.py:27
  43.2 1.7 %fusion.7 = f32[1,256]{1,0:T(1,128)S(1)} fusion(f32[2048,1]{0,1:T(1,128)S(1)} %bitcast.107, f32[1,256,2048]{2,1,0:T(8,128)S(1)} %copy-done), kind=kOutput, calls=%fused_computation.12 | convolution fusion | flops 6291456 | bytes 2106368 | tf_op jit(solution)/shard_map/dot_general | solution.py:125
  44.9 1.2 %collective-permute-done.8 = f32[256]{0:T(256)S(1)} collective-permute-done((f32[256]{0:T(256)S(1)}, f32[256]{0:T(256)S(1)}, u32[]{:S(2)}, u32[]{:S(2)}) %collective-permute-start.8) | collective-permute-done | bytes 1056 | tf_op jit(solution)/shard_map/ppermute | solution.py:39
  46.1 0.8 collective-permute-start.9
  47.0 2.7 %collective-permute-done.9 = f32[512]{0:T(512)S(1)} collective-permute-done((f32[512]{0:T(512)S(1)}, f32[512]{0:T(512)S(1)}, u32[]{:S(2)}, u32[]{:S(2)}) %collective-permute-start.9) | collective-permute-done | bytes 2080 | tf_op jit(solution)/shard_map/ppermute | solution.py:39
  49.7 1.7 %collective-permute-start.10 = (f32[1024]{0:T(1024)S(1)}, f32[1024]{0:T(1024)S(1)}, u32[]{:S(2)}, u32[]{:S(2)}) collective-permute-start(f32[1024]{0:T(1024)S(1)} %maximum_select_fusion.3), channel_id=1, source_target_pairs={{0,4},{1,5},{2,6},{3,7},{4,0},{5,1},{6,2},{7,3},{8,12},{9,13},{10,... | collective-permute-start | bytes 12296 | tf_op jit(solution)/shard_map/ppermute | solution.py:39
  52.0 2.2 %collective-permute-done.10 = f32[1024]{0:T(1024)S(1)} collective-permute-done((f32[1024]{0:T(1024)S(1)}, f32[1024]{0:T(1024)S(1)}, u32[]{:S(2)}, u32[]{:S(2)}) %collective-permute-start.10) | collective-permute-done | bytes 4128 | tf_op jit(solution)/shard_map/ppermute | solution.py:39
  56.7 4.1 %fusion.4 = f32[1280,2]{0,1:T(2,128)S(1)} fusion(bf16[1,1280,2048]{2,1,0:T(8,128)(2,1)} %param.9, bf16[2048,1]{0,1:T(2,128)(2,1)S(1)} %stack.30, bf16[2048,1]{0,1:T(2,128)(2,1)S(1)} %fusion.35), kind=kOutput, calls=%fused_computation.11 | convolution fusion | flops 10502144 | bytes 5261312 | tf_op jit(solution)/shard_map/dot_general | solution.py:128
  61.4 0.9 fusion.9
  62.3 0.9 fusion.15
  63.5 0.9 fusion.13
  64.4 1.8 %collective-permute-done.11 = f32[4,64,2,512]{3,1,2,0:T(8,128)S(1)} collective-permute-done((f32[4,64,2,512]{3,1,2,0:T(8,128)S(1)}, f32[4,64,2,512]{3,1,2,0:T(8,128)S(1)}, u32[]{:S(2)}, u32[]{:S(2)}) %collective-permute-start.11) | collective-permute-done | bytes 1048608 | tf_op jit(solution)/shard_map/ppermute | solution.py:60
  66.4 0.9 dynamic-slice_bitcast_fusion
  67.4 0.8 dynamic-slice_bitcast_fusion.1
  68.3 0.8 collective-permute-start.12
  69.5 1.3 %bitcast_add_fusion.1 = f32[4,64,512]{2,1,0:T(8,128)S(1)} fusion(f32[4,64,512]{2,1,0:T(8,128)} %collective-permute-done.17, f32[4,2,64,512]{3,2,1,0:T(8,128)} %bitcast.104, s32[]{:T(128)S(6)} %select_n.216), kind=kLoop, calls=%fused_computation.32 | loop fusion | flops 131072 | bytes 1572868 | tf_op jit(solution)/shard_map/add | solution.py:60
  70.8 12.0 %collective-permute-done.12 = f32[2,64,2,512]{3,1,2,0:T(8,128)} collective-permute-done((f32[2,64,2,512]{3,1,2,0:T(8,128)}, f32[2,64,2,512]{3,1,2,0:T(8,128)}, u32[]{:S(2)}, u32[]{:S(2)}) %collective-permute-start.12) | collective-permute-done | bytes 524320 | tf_op jit(solution)/shard_map/ppermute | solution.py:60
  82.8 1.9 %bitcast_add_fusion.2 = f32[2,64,2,512]{3,1,2,0:T(8,128)} fusion(f32[2,64,2,512]{3,1,2,0:T(8,128)} %collective-permute-done.12, f32[2,2,64,2,512]{4,2,3,1,0:T(8,128)S(1)} %bitcast.90, s32[]{:T(128)S(6)} %select_n.218), kind=kLoop, calls=%fused_computation.33 | loop fusion | flops 131072 | bytes 1572868 | tf_op jit(solution)/shard_map/add | solution.py:60
  84.7 0.9 collective-permute-start.18
  85.6 1.0 constant_dynamic-slice_fusion.1
  86.6 3.0 %collective-permute-start.13 = (f32[1,64,2,512]{3,1,2,0:T(8,128)S(1)}, f32[1,64,2,512]{3,1,2,0:T(8,128)S(1)}, u32[]{:S(2)}, u32[]{:S(2)}) collective-permute-start(f32[1,64,2,512]{3,1,2,0:T(8,128)S(1)} %constant_dynamic-slice_fusion.1), channel_id=1, source_target_pairs={{0,4},{1,5},{2,6},{3,7},{4,0},{5,1},{6,2},{7,3},{8,12},{9,13},{10,... | collective-permute-start | bytes 786440 | tf_op jit(solution)/shard_map/ppermute | solution.py:60
  95.3 1.8 %collective-permute-done.18 = f32[2,64,512]{2,1,0:T(8,128)S(1)} collective-permute-done((f32[2,64,512]{2,1,0:T(8,128)S(1)}, f32[2,64,512]{2,1,0:T(8,128)S(1)}, u32[]{:S(2)}, u32[]{:S(2)}) %collective-permute-start.18) | collective-permute-done | bytes 262176 | tf_op jit(solution)/shard_map/ppermute | solution.py:60
  97.1 1.0 bitcast_add_fusion.3
  98.1 2.8 %collective-permute-done.13 = f32[1,64,2,512]{3,1,2,0:T(8,128)S(1)} collective-permute-done((f32[1,64,2,512]{3,1,2,0:T(8,128)S(1)}, f32[1,64,2,512]{3,1,2,0:T(8,128)S(1)}, u32[]{:S(2)}, u32[]{:S(2)}) %collective-permute-start.13) | collective-permute-done | bytes 262176 | tf_op jit(solution)/shard_map/ppermute | solution.py:60
  100.9 1.0 dynamic-slice_add_fusion
  102.1 1.6 %collective-permute-start.14 = (f32[64,512]{1,0:T(8,128)S(1)}, f32[64,512]{1,0:T(8,128)S(1)}, u32[]{:S(2)}, u32[]{:S(2)}) collective-permute-start(f32[64,512]{1,0:T(8,128)S(1)} %get-tuple-element.15), channel_id=1, source_target_pairs={{0,8},{8,16},{16,24},{24,0},{1,9},{9,17},{17,25},{25,1},{2,10},{10... | collective-permute-start | bytes 393224 | tf_op jit(solution)/shard_map/ppermute | solution.py:161
  103.7 1.5 %collective-permute-start.15 = (f32[64,512]{1,0:T(8,128)S(1)}, f32[64,512]{1,0:T(8,128)S(1)}, u32[]{:S(2)}, u32[]{:S(2)}) collective-permute-start(f32[64,512]{1,0:T(8,128)S(1)} %get-tuple-element.16), channel_id=1, source_target_pairs={{0,16},{8,24},{16,0},{24,8},{1,17},{9,25},{17,1},{25,9},{2,18},{10... | collective-permute-start | bytes 393224 | tf_op jit(solution)/shard_map/ppermute | solution.py:161
  105.2 1.4 %collective-permute-start.16 = (f32[64,512]{1,0:T(8,128)S(1)}, f32[64,512]{1,0:T(8,128)S(1)}, u32[]{:S(2)}, u32[]{:S(2)}) collective-permute-start(f32[64,512]{1,0:T(8,128)S(1)} %get-tuple-element.17), channel_id=1, source_target_pairs={{0,24},{8,0},{16,8},{24,16},{1,25},{9,1},{17,9},{25,17},{2,26},{10... | collective-permute-start | bytes 393224 | tf_op jit(solution)/shard_map/ppermute | solution.py:161
  106.7 2.3 %collective-permute-done.19 = f32[1,64,512]{2,1,0:T(8,128)S(1)} collective-permute-done((f32[1,64,512]{2,1,0:T(8,128)S(1)}, f32[1,64,512]{2,1,0:T(8,128)S(1)}, u32[]{:S(2)}, u32[]{:S(2)}) %collective-permute-start.19) | collective-permute-done | bytes 131104 | tf_op jit(solution)/shard_map/ppermute | solution.py:60
  (59 shorter events, 8.5 us)
Async XLA Ops:
  0.6 42.6 %copy-start = (f32[1,256,2048]{2,1,0:T(8,128)S(1)}, f32[1,256,2048]{2,1,0:T(8,128)}, u32[]{:S(2)}) copy-start(f32[1,256,2048]{2,1,0:T(8,128)} %param.15) | copy-start | bytes 6291460
  0.6 5.0 %collective-permute-start = (bf16[1,64,128]{2,1,0:T(8,128)(2,1)}, bf16[1,64,128]{2,1,0:T(8,128)(2,1)S(1)}, u32[]{:S(2)}, u32[]{:S(2)}) collective-permute-start(bf16[1,64,128]{2,1,0:T(8,128)(2,1)} %param.10), channel_id=1, source_target_pairs={{0,8},{8,0},{16,24},{24,16},{1,9},{9,1},{17,25},{25,17},{2,10},{10... | collective-permute-start | bytes 49160 | tf_op jit(solution)/shard_map/ppermute | solution.py:39
  6.4 3.9 %collective-permute-start.1 = (bf16[2,64,128]{2,1,0:T(8,128)(2,1)S(1)}, bf16[2,64,128]{2,1,0:T(8,128)(2,1)S(1)}, u32[]{:S(2)}, u32[]{:S(2)}) collective-permute-start(bf16[2,64,128]{2,1,0:T(8,128)(2,1)S(1)} %maximum_select_fusion.1), channel_id=1, source_target_pairs={{0,16},{8,24},{16,0},{24,8},{1,17},{9,25},{17,1},{25,9},{2,18},{10... | collective-permute-start | bytes 98312 | tf_op jit(solution)/shard_map/ppermute | solution.py:39
  10.6 1.3 %collective-permute-start.2 = (bf16[2,64,128]{2,0,1:T(2,128)(2,1)S(1)}, bf16[2,64,128]{2,0,1:T(2,128)(2,1)S(1)}, u32[]{:S(2)}, u32[]{:S(2)}) collective-permute-start(bf16[2,64,128]{2,0,1:T(2,128)(2,1)S(1)} %convolution_convert_fusion), channel_id=1, source_target_pairs={{0,1},{1,0},{2,3},{3,2},{4,5},{5,4},{6,7},{7,6},{8,9},{9,8},{10,11... | collective-permute-start | bytes 98312 | tf_op jit(solution)/shard_map/ppermute | solution.py:39
  12.0 4.6 %collective-permute-start.3 = (bf16[2,128,128]{2,0,1:T(2,128)(2,1)S(1)}, bf16[2,128,128]{2,0,1:T(2,128)(2,1)S(1)}, u32[]{:S(2)}, u32[]{:S(2)}) collective-permute-start(bf16[2,128,128]{2,0,1:T(2,128)(2,1)S(1)} %broadcast_select_fusion.2), channel_id=1, source_target_pairs={{0,2},{1,3},{2,0},{3,1},{4,6},{5,7},{6,4},{7,5},{8,10},{9,11},{10,... | collective-permute-start | bytes 196616 | tf_op jit(solution)/shard_map/ppermute | solution.py:39
  16.9 8.8 %collective-permute-start.4 = (bf16[2,256,128]{2,0,1:T(2,128)(2,1)S(1)}, bf16[2,256,128]{2,0,1:T(2,128)(2,1)S(1)}, u32[]{:S(2)}, u32[]{:S(2)}) collective-permute-start(bf16[2,256,128]{2,0,1:T(2,128)(2,1)S(1)} %broadcast_select_fusion.1), channel_id=1, source_target_pairs={{0,4},{1,5},{2,6},{3,7},{4,0},{5,1},{6,2},{7,3},{8,12},{9,13},{10,... | collective-permute-start | bytes 393224 | tf_op jit(solution)/shard_map/ppermute | solution.py:39
  26.2 5.0 %copy-start.5 = (f32[1,1280]{1,0:T(1,128)S(1)}, f32[1,1280]{1,0:T(1,128)}, u32[]{:S(2)}) copy-start(f32[1,1280]{1,0:T(1,128)} %param.14) | copy-start | bytes 15364
  26.2 5.1 %copy-start.1 = (bf16[1,1280,2048]{2,1,0:T(8,128)(2,1)S(1)}, bf16[1,1280,2048]{2,1,0:T(8,128)(2,1)}, u32[]{:S(2)}) copy-start(bf16[1,1280,2048]{2,1,0:T(8,128)(2,1)} %param.9) | copy-start | bytes 15728644
  33.5 1.2 %collective-permute-start.5 = (f32[4098]{0:T(1024)S(1)}, f32[4098]{0:T(1024)S(1)}, u32[]{:S(2)}, u32[]{:S(2)}) collective-permute-start(f32[4098]{0:T(1024)S(1)} %concatenate.106), channel_id=1, source_target_pairs={{0,1},{1,0},{2,3},{3,2},{4,5},{5,4},{6,7},{7,6},{8,9},{9,8},{10,11... | collective-permute-start | bytes 49184 | tf_op jit(solution)/shard_map/ppermute | solution.py:27
  34.7 3.8 %collective-permute-start.6 = (f32[4098]{0:T(1024)S(1)}, f32[4098]{0:T(1024)S(1)}, u32[]{:S(2)}, u32[]{:S(2)}) collective-permute-start(f32[4098]{0:T(1024)S(1)} %add.149), channel_id=1, source_target_pairs={{0,2},{1,3},{2,0},{3,1},{4,6},{5,7},{6,4},{7,5},{8,10},{9,11},{10,... | collective-permute-start | bytes 49184 | tf_op jit(solution)/shard_map/ppermute | solution.py:27
  38.5 4.7 %collective-permute-start.7 = (f32[4098]{0:T(1024)S(1)}, f32[4098]{0:T(1024)S(1)}, u32[]{:S(2)}, u32[]{:S(2)}) collective-permute-start(f32[4098]{0:T(1024)S(1)} %add.150), channel_id=1, source_target_pairs={{0,4},{1,5},{2,6},{3,7},{4,0},{5,1},{6,2},{7,3},{8,12},{9,13},{10,... | collective-permute-start | bytes 49184 | tf_op jit(solution)/shard_map/ppermute | solution.py:27
  44.9 1.2 %collective-permute-start.8 = (f32[256]{0:T(256)S(1)}, f32[256]{0:T(256)S(1)}, u32[]{:S(2)}, u32[]{:S(2)}) collective-permute-start(f32[256]{0:T(256)S(1)} %bitcast.110), channel_id=1, source_target_pairs={{0,1},{1,0},{2,3},{3,2},{4,5},{5,4},{6,7},{7,6},{8,9},{9,8},{10,11... | collective-permute-start | bytes 3080 | tf_op jit(solution)/shard_map/ppermute | solution.py:39
  46.1 3.6 %collective-permute-start.9 = (f32[512]{0:T(512)S(1)}, f32[512]{0:T(512)S(1)}, u32[]{:S(2)}, u32[]{:S(2)}) collective-permute-start(f32[512]{0:T(512)S(1)} %maximum_select_fusion.4), channel_id=1, source_target_pairs={{0,2},{1,3},{2,0},{3,1},{4,6},{5,7},{6,4},{7,5},{8,10},{9,11},{10,... | collective-permute-start | bytes 6152 | tf_op jit(solution)/shard_map/ppermute | solution.py:39
  49.7 4.5 %collective-permute-start.10 = (f32[1024]{0:T(1024)S(1)}, f32[1024]{0:T(1024)S(1)}, u32[]{:S(2)}, u32[]{:S(2)}) collective-permute-start(f32[1024]{0:T(1024)S(1)} %maximum_select_fusion.3), channel_id=1, source_target_pairs={{0,4},{1,5},{2,6},{3,7},{4,0},{5,1},{6,2},{7,3},{8,12},{9,13},{10,... | collective-permute-start | bytes 12296 | tf_op jit(solution)/shard_map/ppermute | solution.py:39
  56.7 4.2 %copy-start.2 = (bf16[1,1280,1024]{2,1,0:T(8,128)(2,1)S(1)}, bf16[1,1280,1024]{2,1,0:T(8,128)(2,1)}, u32[]{:S(2)}) copy-start(bf16[1,1280,1024]{2,1,0:T(8,128)(2,1)} %param.8) | copy-start | bytes 7864324
  63.5 2.7 %collective-permute-start.11 = (f32[4,64,2,512]{3,1,2,0:T(8,128)S(1)}, f32[4,64,2,512]{3,1,2,0:T(8,128)S(1)}, u32[]{:S(2)}, u32[]{:S(2)}) collective-permute-start(f32[4,64,2,512]{3,1,2,0:T(8,128)S(1)} %bitcast.102), channel_id=1, source_target_pairs={{0,1},{1,0},{2,3},{3,2},{4,5},{5,4},{6,7},{7,6},{8,9},{9,8},{10,11... | collective-permute-start | bytes 3145736 | tf_op jit(solution)/shard_map/ppermute | solution.py:60
  64.4 2.0 %copy-start.4 = (f32[512,512]{1,0:T(8,128)}, f32[512,512]{1,0:T(8,128)S(1)}, u32[]{:S(2)}) copy-start(f32[512,512]{1,0:T(8,128)S(1)} %fusion.13) | copy-start | bytes 3145732
  67.3 2.3 %collective-permute-start.17 = (f32[4,64,512]{2,1,0:T(8,128)}, f32[4,64,512]{2,1,0:T(8,128)}, u32[]{:S(2)}, u32[]{:S(2)}) collective-permute-start(f32[4,64,512]{2,1,0:T(8,128)} %dynamic-slice_bitcast_fusion), channel_id=1, source_target_pairs={{0,1},{1,0},{2,3},{3,2},{4,5},{5,4},{6,7},{7,6},{8,9},{9,8},{10,11... | collective-permute-start | bytes 1572872 | tf_op jit(solution)/shard_map/ppermute | solution.py:60
  67.4 22.2 %copy-start.6 = (s32[1,2]{1,0:T(1,128)S(1)}, s32[1,2]{1,0:T(1,128)}, u32[]{:S(2)}) copy-start(s32[1,2]{1,0:T(1,128)} %param.12) | copy-start | bytes 28
  68.3 14.5 %collective-permute-start.12 = (f32[2,64,2,512]{3,1,2,0:T(8,128)}, f32[2,64,2,512]{3,1,2,0:T(8,128)}, u32[]{:S(2)}, u32[]{:S(2)}) collective-permute-start(f32[2,64,2,512]{3,1,2,0:T(8,128)} %dynamic-slice_bitcast_fusion.1), channel_id=1, source_target_pairs={{0,2},{1,3},{2,0},{3,1},{4,6},{5,7},{6,4},{7,5},{8,10},{9,11},{10,... | collective-permute-start | bytes 1572872 | tf_op jit(solution)/shard_map/ppermute | solution.py:60
  70.8 13.9 %copy-start.3 = (f32[4,64,512]{2,1,0:T(8,128)}, f32[4,64,512]{2,1,0:T(8,128)S(1)}, u32[]{:S(2)}) copy-start(f32[4,64,512]{2,1,0:T(8,128)S(1)} %bitcast_add_fusion.1) | copy-start | bytes 1572868
  84.7 12.4 %collective-permute-start.18 = (f32[2,64,512]{2,1,0:T(8,128)S(1)}, f32[2,64,512]{2,1,0:T(8,128)S(1)}, u32[]{:S(2)}, u32[]{:S(2)}) collective-permute-start(f32[2,64,512]{2,1,0:T(8,128)S(1)} %dynamic-slice_bitcast_fusion.2), channel_id=1, source_target_pairs={{0,2},{1,3},{2,0},{3,1},{4,6},{5,7},{6,4},{7,5},{8,10},{9,11},{10,... | collective-permute-start | bytes 786440 | tf_op jit(solution)/shard_map/ppermute | solution.py:60
  86.6 14.4 %collective-permute-start.13 = (f32[1,64,2,512]{3,1,2,0:T(8,128)S(1)}, f32[1,64,2,512]{3,1,2,0:T(8,128)S(1)}, u32[]{:S(2)}, u32[]{:S(2)}) collective-permute-start(f32[1,64,2,512]{3,1,2,0:T(8,128)S(1)} %constant_dynamic-slice_fusion.1), channel_id=1, source_target_pairs={{0,4},{1,5},{2,6},{3,7},{4,0},{5,1},{6,2},{7,3},{8,12},{9,13},{10,... | collective-permute-start | bytes 786440 | tf_op jit(solution)/shard_map/ppermute | solution.py:60
  102.0 7.0 %collective-permute-start.19 = (f32[1,64,512]{2,1,0:T(8,128)S(1)}, f32[1,64,512]{2,1,0:T(8,128)S(1)}, u32[]{:S(2)}, u32[]{:S(2)}) collective-permute-start(f32[1,64,512]{2,1,0:T(8,128)S(1)} %constant_dynamic-slice_fusion), channel_id=1, source_target_pairs={{0,4},{1,5},{2,6},{3,7},{4,0},{5,1},{6,2},{7,3},{8,12},{9,13},{10,... | collective-permute-start | bytes 393224 | tf_op jit(solution)/shard_map/ppermute | solution.py:60
  102.1 7.6 %collective-permute-start.14 = (f32[64,512]{1,0:T(8,128)S(1)}, f32[64,512]{1,0:T(8,128)S(1)}, u32[]{:S(2)}, u32[]{:S(2)}) collective-permute-start(f32[64,512]{1,0:T(8,128)S(1)} %get-tuple-element.15), channel_id=1, source_target_pairs={{0,8},{8,16},{16,24},{24,0},{1,9},{9,17},{17,25},{25,1},{2,10},{10... | collective-permute-start | bytes 393224 | tf_op jit(solution)/shard_map/ppermute | solution.py:161
  103.7 6.0 %collective-permute-start.15 = (f32[64,512]{1,0:T(8,128)S(1)}, f32[64,512]{1,0:T(8,128)S(1)}, u32[]{:S(2)}, u32[]{:S(2)}) collective-permute-start(f32[64,512]{1,0:T(8,128)S(1)} %get-tuple-element.16), channel_id=1, source_target_pairs={{0,16},{8,24},{16,0},{24,8},{1,17},{9,25},{17,1},{25,9},{2,18},{10... | collective-permute-start | bytes 393224 | tf_op jit(solution)/shard_map/ppermute | solution.py:161
  105.2 5.0 %collective-permute-start.16 = (f32[64,512]{1,0:T(8,128)S(1)}, f32[64,512]{1,0:T(8,128)S(1)}, u32[]{:S(2)}, u32[]{:S(2)}) collective-permute-start(f32[64,512]{1,0:T(8,128)S(1)} %get-tuple-element.17), channel_id=1, source_target_pairs={{0,24},{8,0},{16,8},{24,16},{1,25},{9,1},{17,9},{25,17},{2,26},{10... | collective-permute-start | bytes 393224 | tf_op jit(solution)/shard_map/ppermute | solution.py:161

commit v6 on v5

--- a/solution.py
+++ b/solution.py
@@ -32,18 +32,24 @@
 def xor_gather(value, axis, dim):
     size = lax.axis_size(axis)
     if size & (size - 1):
-        return lax.all_gather(value, axis, axis=dim, tiled=True)
+        plain = jnp.arange(size, dtype=jnp.int32)
+        return lax.all_gather(value, axis, axis=dim, tiled=True), plain, plain
     me = lax.axis_index(axis)
-    step = 1
-    while step < size:
-        other = lax.ppermute(value, axis, [(i, i ^ step) for i in range(size)])
-        value = jnp.where(
-            (me & step) == 0,
-            jnp.concatenate([value, other], axis=dim),
-            jnp.concatenate([other, value], axis=dim),
-        )
-        step *= 2
-    return value
+    bits = size.bit_length() - 1
+    for bit in reversed(range(bits)):
+        other = lax.ppermute(value, axis, [(i, i ^ (1 << bit)) for i in range(size)])
+        value = jnp.concatenate([value, other], axis=dim)
+    flip = [sum(((p >> b) & 1) << (bits - 1 - b) for b in range(bits)) for p in range(size)]
+    flipped_me = sum(((me >> b) & 1) << (bits - 1 - b) for b in range(bits))
+    table = jnp.array(flip, jnp.int32)
+    return value, jnp.bitwise_xor(table, me), jnp.bitwise_xor(table, flipped_me)
+
+
+def in_order(value, holder, place, dim):
+    size = holder.shape[0]
+    shape = value.shape
+    blocks = value.reshape(shape[:dim] + (size, shape[dim] // size) + shape[dim + 1 :])
+    return jnp.take(blocks, place, axis=dim).reshape(shape)
 
 
 def scatter_chunks(value, axis):
@@ -88,16 +94,16 @@
     live_count = counts[0, 0]
     position = lax.iota(jnp.int32, points)
     live_weight = jnp.where(position < live_count, weights[0], jnp.zeros((), jnp.float32))
-    gathered = xor_gather(factors, "dimer", 0)
+    gathered, slot_held, _ = xor_gather(factors, "dimer", 0)
     frag_ids = lax.iota(jnp.int32, frag_slot.shape[0])
     wanted = jnp.sum(
         jnp.where(frag_ids[None, :] == dimer_pairs[0][:, None], frag_slot[None, :], 0), axis=1
     )
-    selector = (frag_ids[None, :] == wanted[:, None]).astype(jnp.bfloat16)
+    selector = (slot_held[None, :] == wanted[:, None]).astype(jnp.bfloat16)
     chosen = jnp.einsum(
         "as,srk->ark", selector, gathered, preferred_element_type=jnp.float32
     ).astype(jnp.bfloat16)
-    dimer_factors = xor_gather(chosen, "grid", 1)
+    dimer_factors = in_order(*xor_gather(chosen, "grid", 1), 1)
     orb_first = jnp.dot(
         basis_rows[:, :frag_basis], dimer_factors[0], preferred_element_type=jnp.float32
     )
@@ -113,17 +119,18 @@
     projections = jnp.dot(
         jnp.concatenate([high_rows, low_rows]), aux_block, preferred_element_type=jnp.float32
     )
-    fitted_part = projections[0] + projections[2]
-    weight_part = projections[1] + projections[3]
     sums_part = jnp.stack([jnp.sum(live_weight * exchange), jnp.sum(live_weight)])
-    payload = jnp.concatenate([fitted_part, weight_part, sums_part])
+    first_lane = lax.broadcasted_iota(jnp.int32, (2, 128), 1) == 0
+    payload = jnp.concatenate(
+        [projections[:2] + projections[2:], jnp.where(first_lane, sums_part[:, None], 0.0)], axis=1
+    )
     totals = xor_sum(payload, "grid")
-    fitted = totals[:naux]
-    weight_projection = totals[naux : 2 * naux]
-    exchange_total = totals[2 * naux]
-    weight_sum = totals[2 * naux + 1]
+    fitted = totals[0, :naux]
+    weight_projection = totals[1, :naux]
+    exchange_total = totals[0, naux]
+    weight_sum = totals[1, naux]
     coef_rows = jnp.dot(metric_inv[0], fitted, precision=highest)
-    coefficients = xor_gather(coef_rows, "grid", 0)
+    coefficients = in_order(*xor_gather(coef_rows, "grid", 0), 0)
     coef_high, coef_low = split_rows(coefficients)
     coulomb_parts = jnp.dot(
         aux_block, jnp.stack([coef_high, coef_low], axis=1), preferred_element_type=jnp.float32

time: 111 us -> 110 us (level)
  waiting for transfers between devices: 46.3 us -> 35.5 us
  starting transfers between devices: 24.5 us -> 31.8 us
  other arithmetic: 12.4 us -> 14.3 us
    ppermute x8, waiting for transfers between devices: 17.1 us -> 10.1 us  [xor_gather(): other = lax.ppermute(value, axis, [(i, i ^ 1 << bit) for i in range(size)])]
    ppermute x3, starting transfers between devices: 2.11 us -> 5.48 us  [xor_sum(): lax.ppermute(value, axis, [(i, i ^ step) for i in range(size)])]
    ppermute x3, waiting for transfers between devices: 7.53 us -> 4.51 us  [xor_sum(): lax.ppermute(value, axis, [(i, i ^ step) for i in range(size)])]
    ppermute x8, starting transfers between devices: 12.8 us -> 14.9 us  [xor_gather(): other = lax.ppermute(value, axis, [(i, i ^ 1 << bit) for i in range(size)])]
    ppermute x6, starting transfers between devices: 5.01 us -> 6.96 us  [scatter_step(): lax.ppermute(send, axis, [(i, i ^ 1 << bit) for i in range(size)])]
    select_n x7 -> x2, other arithmetic: 1.85 us -> 0.17 us  [the longest x1 0.09 us: in_order(): return jnp.take(blocks, place, axis=dim).reshape(shape)]
    concatenate x1 -> x0, local copies, waits for them, and re-layouts: 1.36 us -> none  [shards(): payload = jnp.concatenate([fitted_part, weight_part, sums_part])]
    another operation x0 -> x1, other arithmetic: none -> 1.36 us  [shards(): jnp.stack([jnp.sum(live_weight * exchange), jnp.sum(live_weight)])]
  transfers between devices with their start and end apart: 20 -> 20, of which waited for: 18 -> 17; matrix products, arithmetic and copies ran while one was open for 8% -> 9% of each run, Pallas kernels for 0% -> 0%
where the time goes in v6:
time: 110 us
  waiting for transfers between devices  35.5 us (32%)
  starting transfers between devices  31.8 us (29%)
  other arithmetic  14.3 us (13%)
  matrix products  13.4 us (12%)
  between operations  8.69 us (8%)
  local copies, waits for them, and re-layouts  6.09 us (6%)
    ppermute x6, waiting for transfers between devices, scatter_step(): lax.ppermute(send, axis, [(i, i ^ 1 << bit) for i in range(size)])  19.8 us
    ppermute x8, starting transfers between devices, xor_gather(): other = lax.ppermute(value, axis, [(i, i ^ 1 << bit) for i in range(size)])  14.9 us
    ppermute x8, waiting for transfers between devices, xor_gather(): other = lax.ppermute(value, axis, [(i, i ^ 1 << bit) for i in range(size)])  10.1 us
    ppermute x6, starting transfers between devices, scatter_step(): lax.ppermute(send, axis, [(i, i ^ 1 << bit) for i in range(size)])  6.96 us
    add x6, other arithmetic, scatter_step(): keep + lax.ppermute(send, axis, [(i, i ^ 1 << bit) for i in range(size)])  6.05 us
    ppermute x3, starting transfers between devices, xor_sum(): lax.ppermute(value, axis, [(i, i ^ step) for i in range(size)])  5.48 us
    ppermute x3, waiting for transfers between devices, xor_sum(): lax.ppermute(value, axis, [(i, i ^ step) for i in range(size)])  4.51 us
    ppermute x3, starting transfers between devices, shards(): lax.ppermute(sent, 'dimer', [(i, (i + shift) % groups) for i in range(gro...  4.49 us
  transfers between devices with their start and end apart: 20, of which 17 were waited for; matrix products, arithmetic and copies ran while one was open for 9% of the time, Pallas kernels for 0%

profile of v6, /device:TPU:0, one launch (start us, length us, event | category | flops | bytes accessed | tf_op | source)
XLA Modules:
  0.0 109.8 jit_solution(16415980992204687390)
XLA Ops:
  0.6 0.9 copy.33
  1.5 3.1 %collective-permute-start = (bf16[1,64,128]{2,0,1:T(2,128)(2,1)S(1)}, bf16[1,64,128]{2,0,1:T(2,128)(2,1)S(1)}, u32[]{:S(2)}, u32[]{:S(2)}) collective-permute-start(bf16[1,64,128]{2,0,1:T(2,128)(2,1)S(1)} %copy.33), channel_id=1, source_target_pairs={{0,16},{8,24},{16,0},{24,8},{1,17},{9,25},{17,1},{25,9},{2,18},{10... | collective-permute-start | bytes 49160 | tf_op jit(solution)/shard_map/ppermute | solution.py:40
  5.3 1.2 %collective-permute-done = bf16[1,64,128]{2,0,1:T(2,128)(2,1)S(1)} collective-permute-done((bf16[1,64,128]{2,0,1:T(2,128)(2,1)S(1)}, bf16[1,64,128]{2,0,1:T(2,128)(2,1)S(1)}, u32[]{:S(2)}, u32[]{:S(2)}) %collective-permute-start) | collective-permute-done | bytes 16416 | tf_op jit(solution)/shard_map/ppermute | solution.py:40
  6.6 2.1 %collective-permute-start.1 = (bf16[2,64,128]{2,0,1:T(2,128)(2,1)S(1)}, bf16[2,64,128]{2,0,1:T(2,128)(2,1)S(1)}, u32[]{:S(2)}, u32[]{:S(2)}) collective-permute-start(bf16[2,64,128]{2,0,1:T(2,128)(2,1)S(1)} %pad_maximum_fusion.5), channel_id=1, source_target_pairs={{0,8},{8,0},{16,24},{24,16},{1,9},{9,1},{17,25},{25,17},{2,10},{10... | collective-permute-start | bytes 98312 | tf_op jit(solution)/shard_map/ppermute | solution.py:40
  8.6 0.9 fusion.45
  9.5 1.1 collective-permute-done.1
  10.8 3.2 %collective-permute-start.2 = (bf16[2,64,128]{2,0,1:T(2,128)(2,1)S(1)}, bf16[2,64,128]{2,0,1:T(2,128)(2,1)S(1)}, u32[]{:S(2)}, u32[]{:S(2)}) collective-permute-start(bf16[2,64,128]{2,0,1:T(2,128)(2,1)S(1)} %convolution_convert_fusion), channel_id=1, source_target_pairs={{0,4},{1,5},{2,6},{3,7},{4,0},{5,1},{6,2},{7,3},{8,12},{9,13},{10,... | collective-permute-start | bytes 98312 | tf_op jit(solution)/shard_map/ppermute | solution.py:40
  14.0 2.0 %collective-permute-done.2 = bf16[2,64,128]{2,0,1:T(2,128)(2,1)S(1)} collective-permute-done((bf16[2,64,128]{2,0,1:T(2,128)(2,1)S(1)}, bf16[2,64,128]{2,0,1:T(2,128)(2,1)S(1)}, u32[]{:S(2)}, u32[]{:S(2)}) %collective-permute-start.2) | collective-permute-done | bytes 32800 | tf_op jit(solution)/shard_map/ppermute | solution.py:40
  16.0 1.9 %collective-permute-start.3 = (bf16[2,128,128]{2,0,1:T(2,128)(2,1)S(1)}, bf16[2,128,128]{2,0,1:T(2,128)(2,1)S(1)}, u32[]{:S(2)}, u32[]{:S(2)}) collective-permute-start(bf16[2,128,128]{2,0,1:T(2,128)(2,1)S(1)} %pad_maximum_fusion.4), channel_id=1, source_target_pairs={{0,2},{1,3},{2,0},{3,1},{4,6},{5,7},{6,4},{7,5},{8,10},{9,11},{10,... | collective-permute-start | bytes 196616 | tf_op jit(solution)/shard_map/ppermute | solution.py:40
  18.6 1.8 %collective-permute-done.3 = bf16[2,128,128]{2,0,1:T(2,128)(2,1)S(1)} collective-permute-done((bf16[2,128,128]{2,0,1:T(2,128)(2,1)S(1)}, bf16[2,128,128]{2,0,1:T(2,128)(2,1)S(1)}, u32[]{:S(2)}, u32[]{:S(2)}) %collective-permute-start.3) | collective-permute-done | bytes 65568 | tf_op jit(solution)/shard_map/ppermute | solution.py:40
  21.3 0.7 reduce.3
  23.2 2.0 %fusion.12 = f32[1280]{0:T(1024)S(1)} fusion(bf16[512,128]{1,0:T(8,128)(2,1)S(1)} %bitcast.115, bf16[1280,1024]{1,0:T(8,128)(2,1)} %bitcast.99), kind=kOutput, calls=%fused_computation.19 | convolution fusion | flops 168098560 | bytes 1446912 | tf_op jit(solution)/shard_map/dot_general | solution.py:110
  25.3 1.9 %fusion.11 = f32[1280]{0:T(1024)S(1)} fusion(bf16[512,128]{1,0:T(8,128)(2,1)S(1)} %bitcast.114, bf16[1280,1024]{1,0:T(8,128)(2,1)} %bitcast.100), kind=kOutput, calls=%fused_computation.18 | convolution fusion | flops 168098560 | bytes 1446912 | tf_op jit(solution)/shard_map/dot_general | solution.py:107
  27.9 0.8 fusion.2
  28.7 1.4 %pad_maximum_fusion.11 = f32[2]{0:T(128)S(1)} fusion(f32[1]{0:T(128)} %bitcast.12, f32[1]{0:T(128)} %bitcast.11), kind=kLoop, calls=%fused_computation.101 | loop fusion | flops 2 | bytes 16 | tf_op jit(solution)/shard_map/stack | solution.py:122
  30.7 0.8 collective-permute-done.5
  31.6 1.9 %collective-permute-start.6 = (f32[2,2176]{1,0:T(2,128)S(1)}, f32[2,2176]{1,0:T(2,128)S(1)}, u32[]{:S(2)}, u32[]{:S(2)}) collective-permute-start(f32[2,2176]{1,0:T(2,128)S(1)} %fusion.51), channel_id=1, source_target_pairs={{0,2},{1,3},{2,0},{3,1},{4,6},{5,7},{6,4},{7,5},{8,10},{9,11},{10,... | collective-permute-start | bytes 52232 | tf_op jit(solution)/shard_map/ppermute | solution.py:27
  33.4 1.9 %collective-permute-done.6 = f32[2,2176]{1,0:T(2,128)S(1)} collective-permute-done((f32[2,2176]{1,0:T(2,128)S(1)}, f32[2,2176]{1,0:T(2,128)S(1)}, u32[]{:S(2)}, u32[]{:S(2)}) %collective-permute-start.6) | collective-permute-done | bytes 17440 | tf_op jit(solution)/shard_map/ppermute | solution.py:27
  35.4 3.1 %collective-permute-start.7 = (f32[2,2176]{1,0:T(2,128)S(1)}, f32[2,2176]{1,0:T(2,128)S(1)}, u32[]{:S(2)}, u32[]{:S(2)}) collective-permute-start(f32[2,2176]{1,0:T(2,128)S(1)} %add.158), channel_id=1, source_target_pairs={{0,4},{1,5},{2,6},{3,7},{4,0},{5,1},{6,2},{7,3},{8,12},{9,13},{10,... | collective-permute-start | bytes 52232 | tf_op jit(solution)/shard_map/ppermute | solution.py:27
  38.4 1.7 %collective-permute-done.7 = f32[2,2176]{1,0:T(2,128)S(1)} collective-permute-done((f32[2,2176]{1,0:T(2,128)S(1)}, f32[2,2176]{1,0:T(2,128)S(1)}, u32[]{:S(2)}, u32[]{:S(2)}) %collective-permute-start.7) | collective-permute-done | bytes 17440 | tf_op jit(solution)/shard_map/ppermute | solution.py:27
  40.2 1.7 %fusion.7 = f32[1,256]{1,0:T(1,128)S(1)} fusion(f32[1,256,2048]{2,1,0:T(8,128)S(1)} %copy-done, f32[2,2176]{1,0:T(2,128)S(1)} %add.159), kind=kOutput, calls=%fused_computation.14 | convolution fusion | flops 6291456 | bytes 2106368 | tf_op jit(solution)/shard_map/dot_general | solution.py:132
  41.9 2.9 %collective-permute-start.8 = (f32[256]{0:T(256)S(1)}, f32[256]{0:T(256)S(1)}, u32[]{:S(2)}, u32[]{:S(2)}) collective-permute-start(f32[256]{0:T(256)S(1)} %bitcast.120), channel_id=1, source_target_pairs={{0,4},{1,5},{2,6},{3,7},{4,0},{5,1},{6,2},{7,3},{8,12},{9,13},{10,... | collective-permute-start | bytes 3080 | tf_op jit(solution)/shard_map/ppermute | solution.py:40
  44.9 1.6 %collective-permute-done.8 = f32[256]{0:T(256)S(1)} collective-permute-done((f32[256]{0:T(256)S(1)}, f32[256]{0:T(256)S(1)}, u32[]{:S(2)}, u32[]{:S(2)}) %collective-permute-start.8) | collective-permute-done | bytes 1056 | tf_op jit(solution)/shard_map/ppermute | solution.py:40
  46.4 1.7 %collective-permute-start.9 = (f32[512]{0:T(512)S(1)}, f32[512]{0:T(512)S(1)}, u32[]{:S(2)}, u32[]{:S(2)}) collective-permute-start(f32[512]{0:T(512)S(1)} %pad_maximum_fusion.10), channel_id=1, source_target_pairs={{0,2},{1,3},{2,0},{3,1},{4,6},{5,7},{6,4},{7,5},{8,10},{9,11},{10,... | collective-permute-start | bytes 6152 | tf_op jit(solution)/shard_map/ppermute | solution.py:40
  48.2 1.8 %collective-permute-done.9 = f32[512]{0:T(512)S(1)} collective-permute-done((f32[512]{0:T(512)S(1)}, f32[512]{0:T(512)S(1)}, u32[]{:S(2)}, u32[]{:S(2)}) %collective-permute-start.9) | collective-permute-done | bytes 2080 | tf_op jit(solution)/shard_map/ppermute | solution.py:40
  54.4 4.1 %fusion.4 = f32[1280,2]{0,1:T(2,128)S(1)} fusion(bf16[1,1280,2048]{2,1,0:T(8,128)(2,1)} %param.12, bf16[2048,1]{0,1:T(2,128)(2,1)S(1)} %stack.34, bf16[2048,1]{0,1:T(2,128)(2,1)S(1)} %bitcast.118), kind=kOutput, calls=%fused_computation.13 | convolution fusion | flops 10502144 | bytes 5261312 | tf_op jit(solution)/shard_map/dot_general | solution.py:135
  59.1 0.9 fusion.9
  60.0 0.9 fusion.15
  61.4 0.9 fusion.13
  62.3 1.6 %collective-permute-done.11 = f32[4,64,2,512]{3,1,2,0:T(8,128)S(1)} collective-permute-done((f32[4,64,2,512]{3,1,2,0:T(8,128)S(1)}, f32[4,64,2,512]{3,1,2,0:T(8,128)S(1)}, u32[]{:S(2)}, u32[]{:S(2)}) %collective-permute-start.11) | collective-permute-done | bytes 1048608 | tf_op jit(solution)/shard_map/ppermute | solution.py:66
  64.1 0.9 dynamic-slice_bitcast_fusion
  65.1 0.8 dynamic-slice_bitcast_fusion.1
  66.0 1.7 %collective-permute-start.12 = (f32[2,64,2,512]{3,1,2,0:T(8,128)}, f32[2,64,2,512]{3,1,2,0:T(8,128)}, u32[]{:S(2)}, u32[]{:S(2)}) collective-permute-start(f32[2,64,2,512]{3,1,2,0:T(8,128)} %dynamic-slice_bitcast_fusion.1), channel_id=1, source_target_pairs={{0,2},{1,3},{2,0},{3,1},{4,6},{5,7},{6,4},{7,5},{8,10},{9,11},{10,... | collective-permute-start | bytes 1572872 | tf_op jit(solution)/shard_map/ppermute | solution.py:66
  67.7 1.3 %bitcast_add_fusion.1 = f32[4,64,512]{2,1,0:T(8,128)S(1)} fusion(f32[4,64,512]{2,1,0:T(8,128)} %collective-permute-done.17, f32[4,2,64,512]{3,2,1,0:T(8,128)} %bitcast.113, s32[]{:T(128)S(6)} %select_n.160), kind=kLoop, calls=%fused_computation.34 | loop fusion | flops 131072 | bytes 1572868 | tf_op jit(solution)/shard_map/add | solution.py:66
  69.0 11.5 %collective-permute-done.12 = f32[2,64,2,512]{3,1,2,0:T(8,128)} collective-permute-done((f32[2,64,2,512]{3,1,2,0:T(8,128)}, f32[2,64,2,512]{3,1,2,0:T(8,128)}, u32[]{:S(2)}, u32[]{:S(2)}) %collective-permute-start.12) | collective-permute-done | bytes 524320 | tf_op jit(solution)/shard_map/ppermute | solution.py:66
  80.5 1.9 %bitcast_add_fusion.2 = f32[2,64,2,512]{3,1,2,0:T(8,128)} fusion(f32[2,64,2,512]{3,1,2,0:T(8,128)} %collective-permute-done.12, f32[2,2,64,2,512]{4,2,3,1,0:T(8,128)S(1)} %bitcast.98, s32[]{:T(128)S(6)} %select_n.162), kind=kLoop, calls=%fused_computation.35 | loop fusion | flops 131072 | bytes 1572868 | tf_op jit(solution)/shard_map/add | solution.py:66
  82.4 1.8 %collective-permute-start.18 = (f32[2,64,512]{2,1,0:T(8,128)S(1)}, f32[2,64,512]{2,1,0:T(8,128)S(1)}, u32[]{:S(2)}, u32[]{:S(2)}) collective-permute-start(f32[2,64,512]{2,1,0:T(8,128)S(1)} %dynamic-slice_bitcast_fusion.2), channel_id=1, source_target_pairs={{0,2},{1,3},{2,0},{3,1},{4,6},{5,7},{6,4},{7,5},{8,10},{9,11},{10,... | collective-permute-start | bytes 786440 | tf_op jit(solution)/shard_map/ppermute | solution.py:66
  84.2 1.0 constant_dynamic-slice_fusion.1
  85.2 3.0 %collective-permute-start.13 = (f32[1,64,2,512]{3,1,2,0:T(8,128)S(1)}, f32[1,64,2,512]{3,1,2,0:T(8,128)S(1)}, u32[]{:S(2)}, u32[]{:S(2)}) collective-permute-start(f32[1,64,2,512]{3,1,2,0:T(8,128)S(1)} %constant_dynamic-slice_fusion.1), channel_id=1, source_target_pairs={{0,4},{1,5},{2,6},{3,7},{4,0},{5,1},{6,2},{7,3},{8,12},{9,13},{10,... | collective-permute-start | bytes 786440 | tf_op jit(solution)/shard_map/ppermute | solution.py:66
  94.6 1.0 bitcast_add_fusion.3
  95.6 4.3 %collective-permute-done.13 = f32[1,64,2,512]{3,1,2,0:T(8,128)S(1)} collective-permute-done((f32[1,64,2,512]{3,1,2,0:T(8,128)S(1)}, f32[1,64,2,512]{3,1,2,0:T(8,128)S(1)}, u32[]{:S(2)}, u32[]{:S(2)}) %collective-permute-start.13) | collective-permute-done | bytes 262176 | tf_op jit(solution)/shard_map/ppermute | solution.py:66
  99.9 1.0 dynamic-slice_add_fusion
  101.1 1.5 %collective-permute-start.14 = (f32[64,512]{1,0:T(8,128)S(1)}, f32[64,512]{1,0:T(8,128)S(1)}, u32[]{:S(2)}, u32[]{:S(2)}) collective-permute-start(f32[64,512]{1,0:T(8,128)S(1)} %get-tuple-element.17), channel_id=1, source_target_pairs={{0,8},{8,16},{16,24},{24,0},{1,9},{9,17},{17,25},{25,1},{2,10},{10... | collective-permute-start | bytes 393224 | tf_op jit(solution)/shard_map/ppermute | solution.py:168
  102.6 1.5 %collective-permute-start.15 = (f32[64,512]{1,0:T(8,128)S(1)}, f32[64,512]{1,0:T(8,128)S(1)}, u32[]{:S(2)}, u32[]{:S(2)}) collective-permute-start(f32[64,512]{1,0:T(8,128)S(1)} %get-tuple-element.18), channel_id=1, source_target_pairs={{0,16},{8,24},{16,0},{24,8},{1,17},{9,25},{17,1},{25,9},{2,18},{10... | collective-permute-start | bytes 393224 | tf_op jit(solution)/shard_map/ppermute | solution.py:168
  104.1 1.4 %collective-permute-start.16 = (f32[64,512]{1,0:T(8,128)S(1)}, f32[64,512]{1,0:T(8,128)S(1)}, u32[]{:S(2)}, u32[]{:S(2)}) collective-permute-start(f32[64,512]{1,0:T(8,128)S(1)} %get-tuple-element.19), channel_id=1, source_target_pairs={{0,24},{8,0},{16,8},{24,16},{1,25},{9,1},{17,9},{25,17},{2,26},{10... | collective-permute-start | bytes 393224 | tf_op jit(solution)/shard_map/ppermute | solution.py:168
  105.6 1.8 %collective-permute-done.19 = f32[1,64,512]{2,1,0:T(8,128)S(1)} collective-permute-done((f32[1,64,512]{2,1,0:T(8,128)S(1)}, f32[1,64,512]{2,1,0:T(8,128)S(1)}, u32[]{:S(2)}, u32[]{:S(2)}) %collective-permute-start.19) | collective-permute-done | bytes 131104 | tf_op jit(solution)/shard_map/ppermute | solution.py:66
  108.4 0.7 collective-permute-done.16
  109.1 0.7 fusion.26
  (74 shorter events, 11.0 us)
Async XLA Ops:
  0.6 39.6 %copy-start = (f32[1,256,2048]{2,1,0:T(8,128)S(1)}, f32[1,256,2048]{2,1,0:T(8,128)}, u32[]{:S(2)}) copy-start(f32[1,256,2048]{2,1,0:T(8,128)} %param.18) | copy-start | bytes 6291460
  1.5 5.0 %collective-permute-start = (bf16[1,64,128]{2,0,1:T(2,128)(2,1)S(1)}, bf16[1,64,128]{2,0,1:T(2,128)(2,1)S(1)}, u32[]{:S(2)}, u32[]{:S(2)}) collective-permute-start(bf16[1,64,128]{2,0,1:T(2,128)(2,1)S(1)} %copy.33), channel_id=1, source_target_pairs={{0,16},{8,24},{16,0},{24,8},{1,17},{9,25},{17,1},{25,9},{2,18},{10... | collective-permute-start | bytes 49160 | tf_op jit(solution)/shard_map/ppermute | solution.py:40
  6.6 4.0 %collective-permute-start.1 = (bf16[2,64,128]{2,0,1:T(2,128)(2,1)S(1)}, bf16[2,64,128]{2,0,1:T(2,128)(2,1)S(1)}, u32[]{:S(2)}, u32[]{:S(2)}) collective-permute-start(bf16[2,64,128]{2,0,1:T(2,128)(2,1)S(1)} %pad_maximum_fusion.5), channel_id=1, source_target_pairs={{0,8},{8,0},{16,24},{24,16},{1,9},{9,1},{17,25},{25,17},{2,10},{10... | collective-permute-start | bytes 98312 | tf_op jit(solution)/shard_map/ppermute | solution.py:40
  10.8 5.2 %collective-permute-start.2 = (bf16[2,64,128]{2,0,1:T(2,128)(2,1)S(1)}, bf16[2,64,128]{2,0,1:T(2,128)(2,1)S(1)}, u32[]{:S(2)}, u32[]{:S(2)}) collective-permute-start(bf16[2,64,128]{2,0,1:T(2,128)(2,1)S(1)} %convolution_convert_fusion), channel_id=1, source_target_pairs={{0,4},{1,5},{2,6},{3,7},{4,0},{5,1},{6,2},{7,3},{8,12},{9,13},{10,... | collective-permute-start | bytes 98312 | tf_op jit(solution)/shard_map/ppermute | solution.py:40
  16.0 4.3 %collective-permute-start.3 = (bf16[2,128,128]{2,0,1:T(2,128)(2,1)S(1)}, bf16[2,128,128]{2,0,1:T(2,128)(2,1)S(1)}, u32[]{:S(2)}, u32[]{:S(2)}) collective-permute-start(bf16[2,128,128]{2,0,1:T(2,128)(2,1)S(1)} %pad_maximum_fusion.4), channel_id=1, source_target_pairs={{0,2},{1,3},{2,0},{3,1},{4,6},{5,7},{6,4},{7,5},{8,10},{9,11},{10,... | collective-permute-start | bytes 196616 | tf_op jit(solution)/shard_map/ppermute | solution.py:40
  20.6 1.5 %collective-permute-start.4 = (bf16[2,256,128]{2,0,1:T(2,128)(2,1)S(1)}, bf16[2,256,128]{2,0,1:T(2,128)(2,1)S(1)}, u32[]{:S(2)}, u32[]{:S(2)}) collective-permute-start(bf16[2,256,128]{2,0,1:T(2,128)(2,1)S(1)} %pad_maximum_fusion.1), channel_id=1, source_target_pairs={{0,1},{1,0},{2,3},{3,2},{4,5},{5,4},{6,7},{7,6},{8,9},{9,8},{10,11... | collective-permute-start | bytes 393224 | tf_op jit(solution)/shard_map/ppermute | solution.py:40
  23.1 4.8 %copy-start.5 = (f32[1,1280]{1,0:T(1,128)S(1)}, f32[1,1280]{1,0:T(1,128)}, u32[]{:S(2)}) copy-start(f32[1,1280]{1,0:T(1,128)} %param.17) | copy-start | bytes 15364
  23.1 4.8 %copy-start.1 = (bf16[1,1280,2048]{2,1,0:T(8,128)(2,1)S(1)}, bf16[1,1280,2048]{2,1,0:T(8,128)(2,1)}, u32[]{:S(2)}) copy-start(bf16[1,1280,2048]{2,1,0:T(8,128)(2,1)} %param.12) | copy-start | bytes 15728644
  30.2 1.4 %collective-permute-start.5 = (f32[2,2176]{1,0:T(2,128)S(1)}, f32[2,2176]{1,0:T(2,128)S(1)}, u32[]{:S(2)}, u32[]{:S(2)}) collective-permute-start(f32[2,2176]{1,0:T(2,128)S(1)} %pad_maximum_fusion.6), channel_id=1, source_target_pairs={{0,1},{1,0},{2,3},{3,2},{4,5},{5,4},{6,7},{7,6},{8,9},{9,8},{10,11... | collective-permute-start | bytes 52232 | tf_op jit(solution)/shard_map/ppermute | solution.py:27
  31.6 3.8 %collective-permute-start.6 = (f32[2,2176]{1,0:T(2,128)S(1)}, f32[2,2176]{1,0:T(2,128)S(1)}, u32[]{:S(2)}, u32[]{:S(2)}) collective-permute-start(f32[2,2176]{1,0:T(2,128)S(1)} %fusion.51), channel_id=1, source_target_pairs={{0,2},{1,3},{2,0},{3,1},{4,6},{5,7},{6,4},{7,5},{8,10},{9,11},{10,... | collective-permute-start | bytes 52232 | tf_op jit(solution)/shard_map/ppermute | solution.py:27
  35.4 4.8 %collective-permute-start.7 = (f32[2,2176]{1,0:T(2,128)S(1)}, f32[2,2176]{1,0:T(2,128)S(1)}, u32[]{:S(2)}, u32[]{:S(2)}) collective-permute-start(f32[2,2176]{1,0:T(2,128)S(1)} %add.158), channel_id=1, source_target_pairs={{0,4},{1,5},{2,6},{3,7},{4,0},{5,1},{6,2},{7,3},{8,12},{9,13},{10,... | collective-permute-start | bytes 52232 | tf_op jit(solution)/shard_map/ppermute | solution.py:27
  41.9 4.5 %collective-permute-start.8 = (f32[256]{0:T(256)S(1)}, f32[256]{0:T(256)S(1)}, u32[]{:S(2)}, u32[]{:S(2)}) collective-permute-start(f32[256]{0:T(256)S(1)} %bitcast.120), channel_id=1, source_target_pairs={{0,4},{1,5},{2,6},{3,7},{4,0},{5,1},{6,2},{7,3},{8,12},{9,13},{10,... | collective-permute-start | bytes 3080 | tf_op jit(solution)/shard_map/ppermute | solution.py:40
  46.4 3.6 %collective-permute-start.9 = (f32[512]{0:T(512)S(1)}, f32[512]{0:T(512)S(1)}, u32[]{:S(2)}, u32[]{:S(2)}) collective-permute-start(f32[512]{0:T(512)S(1)} %pad_maximum_fusion.10), channel_id=1, source_target_pairs={{0,2},{1,3},{2,0},{3,1},{4,6},{5,7},{6,4},{7,5},{8,10},{9,11},{10,... | collective-permute-start | bytes 6152 | tf_op jit(solution)/shard_map/ppermute | solution.py:40
  50.0 1.2 %collective-permute-start.10 = (f32[1024]{0:T(1024)S(1)}, f32[1024]{0:T(1024)S(1)}, u32[]{:S(2)}, u32[]{:S(2)}) collective-permute-start(f32[1024]{0:T(1024)S(1)} %pad_maximum_fusion.9), channel_id=1, source_target_pairs={{0,1},{1,0},{2,3},{3,2},{4,5},{5,4},{6,7},{7,6},{8,9},{9,8},{10,11... | collective-permute-start | bytes 12296 | tf_op jit(solution)/shard_map/ppermute | solution.py:40
  54.4 4.2 %copy-start.2 = (bf16[1,1280,1024]{2,1,0:T(8,128)(2,1)S(1)}, bf16[1,1280,1024]{2,1,0:T(8,128)(2,1)}, u32[]{:S(2)}) copy-start(bf16[1,1280,1024]{2,1,0:T(8,128)(2,1)} %param.11) | copy-start | bytes 7864324
  61.2 2.7 %collective-permute-start.11 = (f32[4,64,2,512]{3,1,2,0:T(8,128)S(1)}, f32[4,64,2,512]{3,1,2,0:T(8,128)S(1)}, u32[]{:S(2)}, u32[]{:S(2)}) collective-permute-start(f32[4,64,2,512]{3,1,2,0:T(8,128)S(1)} %bitcast.110), channel_id=1, source_target_pairs={{0,1},{1,0},{2,3},{3,2},{4,5},{5,4},{6,7},{7,6},{8,9},{9,8},{10,11... | collective-permute-start | bytes 3145736 | tf_op jit(solution)/shard_map/ppermute | solution.py:66
  62.3 1.8 %copy-start.4 = (f32[512,512]{1,0:T(8,128)}, f32[512,512]{1,0:T(8,128)S(1)}, u32[]{:S(2)}) copy-start(f32[512,512]{1,0:T(8,128)S(1)} %fusion.13) | copy-start | bytes 3145732
  65.0 2.8 %collective-permute-start.17 = (f32[4,64,512]{2,1,0:T(8,128)}, f32[4,64,512]{2,1,0:T(8,128)}, u32[]{:S(2)}, u32[]{:S(2)}) collective-permute-start(f32[4,64,512]{2,1,0:T(8,128)} %dynamic-slice_bitcast_fusion), channel_id=1, source_target_pairs={{0,1},{1,0},{2,3},{3,2},{4,5},{5,4},{6,7},{7,6},{8,9},{9,8},{10,11... | collective-permute-start | bytes 1572872 | tf_op jit(solution)/shard_map/ppermute | solution.py:66
  65.1 23.0 %copy-start.6 = (s32[1,2]{1,0:T(1,128)S(1)}, s32[1,2]{1,0:T(1,128)}, u32[]{:S(2)}) copy-start(s32[1,2]{1,0:T(1,128)} %param.15) | copy-start | bytes 28
  66.0 14.5 %collective-permute-start.12 = (f32[2,64,2,512]{3,1,2,0:T(8,128)}, f32[2,64,2,512]{3,1,2,0:T(8,128)}, u32[]{:S(2)}, u32[]{:S(2)}) collective-permute-start(f32[2,64,2,512]{3,1,2,0:T(8,128)} %dynamic-slice_bitcast_fusion.1), channel_id=1, source_target_pairs={{0,2},{1,3},{2,0},{3,1},{4,6},{5,7},{6,4},{7,5},{8,10},{9,11},{10,... | collective-permute-start | bytes 1572872 | tf_op jit(solution)/shard_map/ppermute | solution.py:66
  69.0 13.4 %copy-start.3 = (f32[4,64,512]{2,1,0:T(8,128)}, f32[4,64,512]{2,1,0:T(8,128)S(1)}, u32[]{:S(2)}) copy-start(f32[4,64,512]{2,1,0:T(8,128)S(1)} %bitcast_add_fusion.1) | copy-start | bytes 1572868
  82.4 12.2 %collective-permute-start.18 = (f32[2,64,512]{2,1,0:T(8,128)S(1)}, f32[2,64,512]{2,1,0:T(8,128)S(1)}, u32[]{:S(2)}, u32[]{:S(2)}) collective-permute-start(f32[2,64,512]{2,1,0:T(8,128)S(1)} %dynamic-slice_bitcast_fusion.2), channel_id=1, source_target_pairs={{0,2},{1,3},{2,0},{3,1},{4,6},{5,7},{6,4},{7,5},{8,10},{9,11},{10,... | collective-permute-start | bytes 786440 | tf_op jit(solution)/shard_map/ppermute | solution.py:66
  85.2 14.7 %collective-permute-start.13 = (f32[1,64,2,512]{3,1,2,0:T(8,128)S(1)}, f32[1,64,2,512]{3,1,2,0:T(8,128)S(1)}, u32[]{:S(2)}, u32[]{:S(2)}) collective-permute-start(f32[1,64,2,512]{3,1,2,0:T(8,128)S(1)} %constant_dynamic-slice_fusion.1), channel_id=1, source_target_pairs={{0,4},{1,5},{2,6},{3,7},{4,0},{5,1},{6,2},{7,3},{8,12},{9,13},{10,... | collective-permute-start | bytes 786440 | tf_op jit(solution)/shard_map/ppermute | solution.py:66
  100.9 6.4 %collective-permute-start.19 = (f32[1,64,512]{2,1,0:T(8,128)S(1)}, f32[1,64,512]{2,1,0:T(8,128)S(1)}, u32[]{:S(2)}, u32[]{:S(2)}) collective-permute-start(f32[1,64,512]{2,1,0:T(8,128)S(1)} %constant_dynamic-slice_fusion), channel_id=1, source_target_pairs={{0,4},{1,5},{2,6},{3,7},{4,0},{5,1},{6,2},{7,3},{8,12},{9,13},{10,... | collective-permute-start | bytes 393224 | tf_op jit(solution)/shard_map/ppermute | solution.py:66
  101.1 6.9 %collective-permute-start.14 = (f32[64,512]{1,0:T(8,128)S(1)}, f32[64,512]{1,0:T(8,128)S(1)}, u32[]{:S(2)}, u32[]{:S(2)}) collective-permute-start(f32[64,512]{1,0:T(8,128)S(1)} %get-tuple-element.17), channel_id=1, source_target_pairs={{0,8},{8,16},{16,24},{24,0},{1,9},{9,17},{17,25},{25,1},{2,10},{10... | collective-permute-start | bytes 393224 | tf_op jit(solution)/shard_map/ppermute | solution.py:168
  102.6 5.8 %collective-permute-start.15 = (f32[64,512]{1,0:T(8,128)S(1)}, f32[64,512]{1,0:T(8,128)S(1)}, u32[]{:S(2)}, u32[]{:S(2)}) collective-permute-start(f32[64,512]{1,0:T(8,128)S(1)} %get-tuple-element.18), channel_id=1, source_target_pairs={{0,16},{8,24},{16,0},{24,8},{1,17},{9,25},{17,1},{25,9},{2,18},{10... | collective-permute-start | bytes 393224 | tf_op jit(solution)/shard_map/ppermute | solution.py:168
  104.1 5.0 %collective-permute-start.16 = (f32[64,512]{1,0:T(8,128)S(1)}, f32[64,512]{1,0:T(8,128)S(1)}, u32[]{:S(2)}, u32[]{:S(2)}) collective-permute-start(f32[64,512]{1,0:T(8,128)S(1)} %get-tuple-element.19), channel_id=1, source_target_pairs={{0,24},{8,0},{16,8},{24,16},{1,25},{9,1},{17,9},{25,17},{2,26},{10... | collective-permute-start | bytes 393224 | tf_op jit(solution)/shard_map/ppermute | solution.py:168

commit v7 on v6

--- a/solution.py
+++ b/solution.py
@@ -52,18 +52,20 @@
     return jnp.take(blocks, place, axis=dim).reshape(shape)
 
 
-def scatter_chunks(value, axis):
+def send_order(axis):
     size = lax.axis_size(axis)
-    return value.reshape((size, value.shape[0] // size) + value.shape[1:])
+    if size & (size - 1):
+        return jnp.arange(size, dtype=jnp.int32)
+    bits = size.bit_length() - 1
+    flip = [sum(((p >> b) & 1) << (bits - 1 - b) for b in range(bits)) for p in range(size)]
+    return jnp.bitwise_xor(jnp.array(flip, jnp.int32), lax.axis_index(axis))
 
 
-def scatter_step(value, axis, bit):
+def half_step(value, axis, bit):
     size = lax.axis_size(axis)
-    mine = (lax.axis_index(axis) >> bit) & 1
-    pairs = value.reshape((value.shape[0] // 2, 2) + value.shape[1:])
-    keep = lax.dynamic_index_in_dim(pairs, mine, axis=1, keepdims=False)
-    send = lax.dynamic_index_in_dim(pairs, 1 - mine, axis=1, keepdims=False)
-    return keep + lax.ppermute(send, axis, [(i, i ^ (1 << bit)) for i in range(size)])
+    half = value.shape[0] // 2
+    sent = lax.ppermute(value[half:], axis, [(i, i ^ (1 << bit)) for i in range(size)])
+    return value[:half] + sent
 
 
 def paired_scatter(lead, follow, axis):
@@ -73,15 +75,13 @@
             lax.psum_scatter(lead, axis, scatter_dimension=0, tiled=True),
             lax.psum_scatter(follow, axis, scatter_dimension=0, tiled=True),
         )
-    lead = scatter_chunks(lead, axis)
-    follow = scatter_chunks(follow, axis)
     bit = 0
     while (1 << bit) < size:
-        lead = scatter_step(lead, axis, bit)
+        lead = half_step(lead, axis, bit)
         follow, _ = lax.optimization_barrier((follow, lead))
-        follow = scatter_step(follow, axis, bit)
+        follow = half_step(follow, axis, bit)
         bit += 1
-    return lead[0], follow[0]
+    return lead, follow
 
 
 def shards(basis_values, aux_values, factors, frag_slot, dimer_pairs, counts, weights, metric_inv):
@@ -139,12 +139,13 @@
     potential_total = jnp.dot(coefficients, weight_projection, precision=highest) + exchange_total
     average = potential_total / weight_sum
     potential = live_weight * (coulomb + exchange - average)
-    weighted_basis = (basis_rows * potential[:, None]).astype(jnp.bfloat16)
-    half_rows = frag_basis // lax.axis_size("grid")
-    left_first = lax.slice_in_dim(weighted_basis, 0, half_rows * lax.axis_size("grid"), axis=1)
-    left_second = lax.dynamic_slice_in_dim(
-        weighted_basis, frag_basis, half_rows * lax.axis_size("grid"), 1
-    )
+    grid_size = lax.axis_size("grid")
+    order = send_order("grid")
+    blocked = basis_rows.reshape(points, 2, grid_size, frag_basis // grid_size)
+    permuted_basis = jnp.take(blocked, order, axis=2).reshape(points, 2 * frag_basis)
+    weighted_basis = (permuted_basis * potential[:, None]).astype(jnp.bfloat16)
+    left_first = weighted_basis[:, :frag_basis]
+    left_second = weighted_basis[:, frag_basis:]
     first_first = contract(left_first, basis_rows[:, :frag_basis])
     first_second = contract(left_first, basis_rows[:, frag_basis:])
     second_second = contract(left_second, basis_rows[:, frag_basis:])

time: 110 us -> 117 us (1.064)
  local copies, waits for them, and re-layouts: 6.09 us -> 17.9 us
  other arithmetic: 14.3 us -> 10.3 us
  starting transfers between devices: 31.8 us -> 30.5 us
    gather x0 -> x2, local copies, waits for them, and re-layouts: none -> 7.46 us  [shards(): jnp.take(blocked, order, axis=2).reshape(points, 2 * frag_basis)]
    unnamed x17 -> x16, local copies, waits for them, and re-layouts: 0.95 us -> 6.38 us
    add x6 -> x5, other arithmetic: 6.05 us -> 1.39 us  [half_step(): return value[:half] + sent]
    squeeze x5 -> x0, local copies, waits for them, and re-layouts: 2.7 us -> none  [scatter_step(): send = lax.dynamic_index_in_dim(pairs, 1 - mine, axis=1, keepdims=False)]
    ppermute x6, waiting for transfers between devices: 19.8 us -> 21.5 us  [half_step(): lax.ppermute(value[half:], axis, [(i, i ^ 1 << bit) for i in range(size)])]
    slice x0 -> x5, local copies, waits for them, and re-layouts: none -> 1.52 us  [half_step(): value[half:]]
    ppermute x8, waiting for transfers between devices: 10.1 us -> 8.56 us  [xor_gather(): other = lax.ppermute(value, axis, [(i, i ^ 1 << bit) for i in range(size)])]
    ppermute x6, starting transfers between devices: 6.96 us -> 5.64 us  [half_step(): lax.ppermute(value[half:], axis, [(i, i ^ 1 << bit) for i in range(size)])]
  transfers between devices with their start and end apart: 20 -> 20, of which waited for: 17 -> 15; matrix products, arithmetic and copies ran while one was open for 9% -> 17% of each run, Pallas kernels for 0% -> 0%
where the time goes in v7:
time: 117 us; the launch traced here: 116 us
  waiting for transfers between devices  35.7 us (31%)
  starting transfers between devices  30.5 us (26%)
  local copies, waits for them, and re-layouts  17.9 us (15%)
  matrix products  13.3 us (11%)
  other arithmetic  10.3 us (9%)
  between operations  8.7 us (7%)
    ppermute x6, waiting for transfers between devices, half_step(): lax.ppermute(value[half:], axis, [(i, i ^ 1 << bit) for i in range(size)])  21.5 us
    ppermute x8, starting transfers between devices, xor_gather(): other = lax.ppermute(value, axis, [(i, i ^ 1 << bit) for i in range(size)])  14.9 us
    ppermute x8, waiting for transfers between devices, xor_gather(): other = lax.ppermute(value, axis, [(i, i ^ 1 << bit) for i in range(size)])  8.56 us
    gather x2, local copies, waits for them, and re-layouts, shards(): jnp.take(blocked, order, axis=2).reshape(points, 2 * frag_basis)  7.46 us
    unnamed x16, local copies, waits for them, and re-layouts  6.38 us
    ppermute x6, starting transfers between devices, half_step(): lax.ppermute(value[half:], axis, [(i, i ^ 1 << bit) for i in range(size)])  5.64 us
    ppermute x3, starting transfers between devices, xor_sum(): lax.ppermute(value, axis, [(i, i ^ step) for i in range(size)])  5.49 us
    ppermute x3, waiting for transfers between devices, xor_sum(): lax.ppermute(value, axis, [(i, i ^ step) for i in range(size)])  4.51 us
  transfers between devices with their start and end apart: 20, of which 15 were waited for; matrix products, arithmetic and copies ran while one was open for 17% of the time, Pallas kernels for 0%

profile of v7, /device:TPU:0, one launch (start us, length us, event | category | flops | bytes accessed | tf_op | source)
XLA Modules:
  0.0 116.5 jit_solution(7388669860188904175)
XLA Ops:
  0.6 0.9 copy.32
  1.5 3.1 %collective-permute-start = (bf16[1,64,128]{2,0,1:T(2,128)(2,1)S(1)}, bf16[1,64,128]{2,0,1:T(2,128)(2,1)S(1)}, u32[]{:S(2)}, u32[]{:S(2)}) collective-permute-start(bf16[1,64,128]{2,0,1:T(2,128)(2,1)S(1)} %copy.32), channel_id=1, source_target_pairs={{0,16},{8,24},{16,0},{24,8},{1,17},{9,25},{17,1},{25,9},{2,18},{10... | collective-permute-start | bytes 49160 | tf_op jit(solution)/shard_map/ppermute | solution.py:40
  5.3 1.2 %collective-permute-done = bf16[1,64,128]{2,0,1:T(2,128)(2,1)S(1)} collective-permute-done((bf16[1,64,128]{2,0,1:T(2,128)(2,1)S(1)}, bf16[1,64,128]{2,0,1:T(2,128)(2,1)S(1)}, u32[]{:S(2)}, u32[]{:S(2)}) %collective-permute-start) | collective-permute-done | bytes 16416 | tf_op jit(solution)/shard_map/ppermute | solution.py:40
  6.6 2.1 %collective-permute-start.1 = (bf16[2,64,128]{2,0,1:T(2,128)(2,1)S(1)}, bf16[2,64,128]{2,0,1:T(2,128)(2,1)S(1)}, u32[]{:S(2)}, u32[]{:S(2)}) collective-permute-start(bf16[2,64,128]{2,0,1:T(2,128)(2,1)S(1)} %pad_maximum_fusion.6), channel_id=1, source_target_pairs={{0,8},{8,0},{16,24},{24,16},{1,9},{9,1},{17,25},{25,17},{2,10},{10... | collective-permute-start | bytes 98312 | tf_op jit(solution)/shard_map/ppermute | solution.py:40
  8.6 0.9 fusion.43
  9.5 1.1 collective-permute-done.1
  10.8 3.2 %collective-permute-start.2 = (bf16[2,64,128]{2,0,1:T(2,128)(2,1)S(1)}, bf16[2,64,128]{2,0,1:T(2,128)(2,1)S(1)}, u32[]{:S(2)}, u32[]{:S(2)}) collective-permute-start(bf16[2,64,128]{2,0,1:T(2,128)(2,1)S(1)} %convolution_convert_fusion), channel_id=1, source_target_pairs={{0,4},{1,5},{2,6},{3,7},{4,0},{5,1},{6,2},{7,3},{8,12},{9,13},{10,... | collective-permute-start | bytes 98312 | tf_op jit(solution)/shard_map/ppermute | solution.py:40
  14.0 2.0 %collective-permute-done.2 = bf16[2,64,128]{2,0,1:T(2,128)(2,1)S(1)} collective-permute-done((bf16[2,64,128]{2,0,1:T(2,128)(2,1)S(1)}, bf16[2,64,128]{2,0,1:T(2,128)(2,1)S(1)}, u32[]{:S(2)}, u32[]{:S(2)}) %collective-permute-start.2) | collective-permute-done | bytes 32800 | tf_op jit(solution)/shard_map/ppermute | solution.py:40
  16.0 1.9 %collective-permute-start.3 = (bf16[2,128,128]{2,0,1:T(2,128)(2,1)S(1)}, bf16[2,128,128]{2,0,1:T(2,128)(2,1)S(1)}, u32[]{:S(2)}, u32[]{:S(2)}) collective-permute-start(bf16[2,128,128]{2,0,1:T(2,128)(2,1)S(1)} %pad_maximum_fusion.5), channel_id=1, source_target_pairs={{0,2},{1,3},{2,0},{3,1},{4,6},{5,7},{6,4},{7,5},{8,10},{9,11},{10,... | collective-permute-start | bytes 196616 | tf_op jit(solution)/shard_map/ppermute | solution.py:40
  18.6 1.8 %collective-permute-done.3 = bf16[2,128,128]{2,0,1:T(2,128)(2,1)S(1)} collective-permute-done((bf16[2,128,128]{2,0,1:T(2,128)(2,1)S(1)}, bf16[2,128,128]{2,0,1:T(2,128)(2,1)S(1)}, u32[]{:S(2)}, u32[]{:S(2)}) %collective-permute-start.3) | collective-permute-done | bytes 65568 | tf_op jit(solution)/shard_map/ppermute | solution.py:40
  21.3 0.7 reduce.3
  23.2 2.0 %fusion.11 = f32[1280]{0:T(1024)S(1)} fusion(bf16[512,128]{1,0:T(8,128)(2,1)S(1)} %bitcast.89, bf16[1280,1024]{1,0:T(8,128)(2,1)} %bitcast.82), kind=kOutput, calls=%fused_computation.20 | convolution fusion | flops 168098560 | bytes 1446912 | tf_op jit(solution)/shard_map/dot_general | solution.py:110
  25.3 1.9 %fusion.10 = f32[1280]{0:T(1024)S(1)} fusion(bf16[512,128]{1,0:T(8,128)(2,1)S(1)} %bitcast.88, bf16[1280,1024]{1,0:T(8,128)(2,1)} %bitcast.83), kind=kOutput, calls=%fused_computation.19 | convolution fusion | flops 168098560 | bytes 1446912 | tf_op jit(solution)/shard_map/dot_general | solution.py:107
  27.2 0.7 multiply_reduce_fusion.1
  27.9 0.8 fusion.2
  28.8 1.3 %pad_maximum_fusion.12 = f32[2]{0:T(128)S(1)} fusion(f32[1]{0:T(128)} %bitcast.15, f32[1]{0:T(128)} %bitcast.14), kind=kLoop, calls=%fused_computation.98 | loop fusion | flops 2 | bytes 16 | tf_op jit(solution)/shard_map/stack | solution.py:122
  30.7 0.8 collective-permute-done.5
  31.6 1.9 %collective-permute-start.6 = (f32[2,2176]{1,0:T(2,128)S(1)}, f32[2,2176]{1,0:T(2,128)S(1)}, u32[]{:S(2)}, u32[]{:S(2)}) collective-permute-start(f32[2,2176]{1,0:T(2,128)S(1)} %fusion.49), channel_id=1, source_target_pairs={{0,2},{1,3},{2,0},{3,1},{4,6},{5,7},{6,4},{7,5},{8,10},{9,11},{10,... | collective-permute-start | bytes 52232 | tf_op jit(solution)/shard_map/ppermute | solution.py:27
  33.5 1.9 %collective-permute-done.6 = f32[2,2176]{1,0:T(2,128)S(1)} collective-permute-done((f32[2,2176]{1,0:T(2,128)S(1)}, f32[2,2176]{1,0:T(2,128)S(1)}, u32[]{:S(2)}, u32[]{:S(2)}) %collective-permute-start.6) | collective-permute-done | bytes 17440 | tf_op jit(solution)/shard_map/ppermute | solution.py:27
  35.4 3.1 %collective-permute-start.7 = (f32[2,2176]{1,0:T(2,128)S(1)}, f32[2,2176]{1,0:T(2,128)S(1)}, u32[]{:S(2)}, u32[]{:S(2)}) collective-permute-start(f32[2,2176]{1,0:T(2,128)S(1)} %add.130), channel_id=1, source_target_pairs={{0,4},{1,5},{2,6},{3,7},{4,0},{5,1},{6,2},{7,3},{8,12},{9,13},{10,... | collective-permute-start | bytes 52232 | tf_op jit(solution)/shard_map/ppermute | solution.py:27
  38.5 1.7 %collective-permute-done.7 = f32[2,2176]{1,0:T(2,128)S(1)} collective-permute-done((f32[2,2176]{1,0:T(2,128)S(1)}, f32[2,2176]{1,0:T(2,128)S(1)}, u32[]{:S(2)}, u32[]{:S(2)}) %collective-permute-start.7) | collective-permute-done | bytes 17440 | tf_op jit(solution)/shard_map/ppermute | solution.py:27
  40.2 1.7 %fusion.7 = f32[1,256]{1,0:T(1,128)S(1)} fusion(f32[1,256,2048]{2,1,0:T(8,128)S(1)} %copy-done, f32[2,2176]{1,0:T(2,128)S(1)} %add.131), kind=kOutput, calls=%fused_computation.14 | convolution fusion | flops 6291456 | bytes 2106368 | tf_op jit(solution)/shard_map/dot_general | solution.py:132
  42.0 2.9 %collective-permute-start.8 = (f32[256]{0:T(256)S(1)}, f32[256]{0:T(256)S(1)}, u32[]{:S(2)}, u32[]{:S(2)}) collective-permute-start(f32[256]{0:T(256)S(1)} %bitcast.94), channel_id=1, source_target_pairs={{0,4},{1,5},{2,6},{3,7},{4,0},{5,1},{6,2},{7,3},{8,12},{9,13},{10,... | collective-permute-start | bytes 3080 | tf_op jit(solution)/shard_map/ppermute | solution.py:40
  44.9 4.4 %copy.28 = bf16[1,1280,1024]{1,2,0:T(8,128)(2,1)} copy(bf16[1,1280,1024]{2,1,0:T(8,128)(2,1)} %param.12) | data formatting | bytes 5242880 | tf_op args[0]
  49.5 4.0 %gather_fusion = bf16[8,1280,2,64]{1,3,2,0:T(8,128)(2,1)} fusion(bf16[1280,2,8,64]{0,3,2,1:T(8,128)(2,1)} %bitcast.80, s32[1024]{0:T(1024)S(1)} %get-tuple-element.31), kind=kCustom, calls=%fused_computation | custom fusion | bytes 5242912 | tf_op jit(solution)/shard_map/jit(_take)/gather | solution.py:145
  53.4 3.5 %copy.29 = bf16[1280,2,8,64]{0,3,2,1:T(8,128)(2,1)} copy(bf16[1280,2,8,64]{0,3,1,2:T(8,128)(2,1)} %bitcast.81) | data formatting | bytes 5242880 | tf_op jit(solution)/shard_map/jit(_take)/gather | solution.py:145
  56.9 1.8 %collective-permute-start.9 = (f32[512]{0:T(512)S(1)}, f32[512]{0:T(512)S(1)}, u32[]{:S(2)}, u32[]{:S(2)}) collective-permute-start(f32[512]{0:T(512)S(1)} %pad_maximum_fusion.11), channel_id=1, source_target_pairs={{0,2},{1,3},{2,0},{3,1},{4,6},{5,7},{6,4},{7,5},{8,10},{9,11},{10,... | collective-permute-start | bytes 6152 | tf_op jit(solution)/shard_map/ppermute | solution.py:40
  58.7 1.9 %collective-permute-done.9 = f32[512]{0:T(512)S(1)} collective-permute-done((f32[512]{0:T(512)S(1)}, f32[512]{0:T(512)S(1)}, u32[]{:S(2)}, u32[]{:S(2)}) %collective-permute-start.9) | collective-permute-done | bytes 2080 | tf_op jit(solution)/shard_map/ppermute | solution.py:40
  65.0 4.1 %fusion.4 = f32[1280,2]{0,1:T(2,128)S(1)} fusion(bf16[1,1280,2048]{2,1,0:T(8,128)(2,1)} %param.13, bf16[2048,1]{0,1:T(2,128)(2,1)S(1)} %stack.34, bf16[2048,1]{0,1:T(2,128)(2,1)S(1)} %bitcast.92), kind=kOutput, calls=%fused_computation.11 | convolution fusion | flops 10502144 | bytes 5261312 | tf_op jit(solution)/shard_map/dot_general | solution.py:135
  69.2 0.7 multiply_convert_fusion
  69.9 1.0 copy-done.3
  70.9 0.8 convolution_bitcast_fusion
  71.8 0.8 convolution_bitcast_fusion.1
  72.9 2.5 %collective-permute-done.11 = f32[256,2,512]{2,0,1:T(8,128)S(1)} collective-permute-done((f32[256,2,512]{2,0,1:T(8,128)S(1)}, f32[256,2,512]{2,0,1:T(8,128)S(1)}, u32[]{:S(2)}, u32[]{:S(2)}) %collective-permute-start.11) | collective-permute-done | bytes 1048608 | tf_op jit(solution)/shard_map/ppermute | solution.py:67
  75.7 1.8 %collective-permute-start.12 = (f32[128,2,512]{2,0,1:T(8,128)S(1)}, f32[128,2,512]{2,0,1:T(8,128)S(1)}, u32[]{:S(2)}, u32[]{:S(2)}) collective-permute-start(f32[128,2,512]{2,0,1:T(8,128)S(1)} %slice.154), channel_id=1, source_target_pairs={{0,2},{1,3},{2,0},{3,1},{4,6},{5,7},{6,4},{7,5},{8,10},{9,11},{10,... | collective-permute-start | bytes 1572872 | tf_op jit(solution)/shard_map/ppermute | solution.py:67
  77.4 0.8 fusion.12
  78.4 11.3 %collective-permute-done.12 = f32[128,2,512]{2,0,1:T(8,128)S(1)} collective-permute-done((f32[128,2,512]{2,0,1:T(8,128)S(1)}, f32[128,2,512]{2,0,1:T(8,128)S(1)}, u32[]{:S(2)}, u32[]{:S(2)}) %collective-permute-start.12) | collective-permute-done | bytes 524320 | tf_op jit(solution)/shard_map/ppermute | solution.py:67
  89.8 0.7 slice.156
  90.6 0.7 slice.128
  91.3 1.7 %collective-permute-start.18 = (f32[128,512]{1,0:T(8,128)}, f32[128,512]{1,0:T(8,128)}, u32[]{:S(2)}, u32[]{:S(2)}) collective-permute-start(f32[128,512]{1,0:T(8,128)} %slice.128), channel_id=1, source_target_pairs={{0,2},{1,3},{2,0},{3,1},{4,6},{5,7},{6,4},{7,5},{8,10},{9,11},{10,... | collective-permute-start | bytes 786440 | tf_op jit(solution)/shard_map/ppermute | solution.py:67
  98.8 6.0 %collective-permute-done.13 = f32[64,2,512]{2,0,1:T(8,128)S(1)} collective-permute-done((f32[64,2,512]{2,0,1:T(8,128)}, f32[64,2,512]{2,0,1:T(8,128)S(1)}, u32[]{:S(2)}, u32[]{:S(2)}) %collective-permute-start.13) | collective-permute-done | bytes 262176 | tf_op jit(solution)/shard_map/ppermute | solution.py:67
  104.9 1.0 slice_add_fusion.3
  105.9 1.8 %collective-permute-start.19 = (f32[64,512]{1,0:T(8,128)S(1)}, f32[64,512]{1,0:T(8,128)S(1)}, u32[]{:S(2)}, u32[]{:S(2)}) collective-permute-start(f32[64,512]{1,0:T(8,128)S(1)} %slice.130), channel_id=1, source_target_pairs={{0,4},{1,5},{2,6},{3,7},{4,0},{5,1},{6,2},{7,3},{8,12},{9,13},{10,... | collective-permute-start | bytes 393224 | tf_op jit(solution)/shard_map/ppermute | solution.py:67
  107.8 1.5 %collective-permute-start.14 = (f32[64,512]{1,0:T(8,128)S(1)}, f32[64,512]{1,0:T(8,128)S(1)}, u32[]{:S(2)}, u32[]{:S(2)}) collective-permute-start(f32[64,512]{1,0:T(8,128)S(1)} %get-tuple-element.17), channel_id=1, source_target_pairs={{0,8},{8,16},{16,24},{24,0},{1,9},{9,17},{17,25},{25,1},{2,10},{10... | collective-permute-start | bytes 393224 | tf_op jit(solution)/shard_map/ppermute | solution.py:169
  109.3 1.5 %collective-permute-start.15 = (f32[64,512]{1,0:T(8,128)S(1)}, f32[64,512]{1,0:T(8,128)S(1)}, u32[]{:S(2)}, u32[]{:S(2)}) collective-permute-start(f32[64,512]{1,0:T(8,128)S(1)} %get-tuple-element.18), channel_id=1, source_target_pairs={{0,16},{8,24},{16,0},{24,8},{1,17},{9,25},{17,1},{25,9},{2,18},{10... | collective-permute-start | bytes 393224 | tf_op jit(solution)/shard_map/ppermute | solution.py:169
  110.8 1.4 %collective-permute-start.16 = (f32[64,512]{1,0:T(8,128)S(1)}, f32[64,512]{1,0:T(8,128)S(1)}, u32[]{:S(2)}, u32[]{:S(2)}) collective-permute-start(f32[64,512]{1,0:T(8,128)S(1)} %get-tuple-element.19), channel_id=1, source_target_pairs={{0,24},{8,0},{16,8},{24,16},{1,25},{9,1},{17,9},{25,17},{2,26},{10... | collective-permute-start | bytes 393224 | tf_op jit(solution)/shard_map/ppermute | solution.py:169
  112.2 1.7 %collective-permute-done.19 = f32[64,512]{1,0:T(8,128)S(1)} collective-permute-done((f32[64,512]{1,0:T(8,128)S(1)}, f32[64,512]{1,0:T(8,128)S(1)}, u32[]{:S(2)}, u32[]{:S(2)}) %collective-permute-start.19) | collective-permute-done | bytes 131104 | tf_op jit(solution)/shard_map/ppermute | solution.py:67
  115.8 0.7 fusion.24
  (76 shorter events, 9.9 us)
Async XLA Ops:
  0.6 39.6 %copy-start = (f32[1,256,2048]{2,1,0:T(8,128)S(1)}, f32[1,256,2048]{2,1,0:T(8,128)}, u32[]{:S(2)}) copy-start(f32[1,256,2048]{2,1,0:T(8,128)} %param.19) | copy-start | bytes 6291460
  1.5 5.0 %collective-permute-start = (bf16[1,64,128]{2,0,1:T(2,128)(2,1)S(1)}, bf16[1,64,128]{2,0,1:T(2,128)(2,1)S(1)}, u32[]{:S(2)}, u32[]{:S(2)}) collective-permute-start(bf16[1,64,128]{2,0,1:T(2,128)(2,1)S(1)} %copy.32), channel_id=1, source_target_pairs={{0,16},{8,24},{16,0},{24,8},{1,17},{9,25},{17,1},{25,9},{2,18},{10... | collective-permute-start | bytes 49160 | tf_op jit(solution)/shard_map/ppermute | solution.py:40
  6.6 4.0 %collective-permute-start.1 = (bf16[2,64,128]{2,0,1:T(2,128)(2,1)S(1)}, bf16[2,64,128]{2,0,1:T(2,128)(2,1)S(1)}, u32[]{:S(2)}, u32[]{:S(2)}) collective-permute-start(bf16[2,64,128]{2,0,1:T(2,128)(2,1)S(1)} %pad_maximum_fusion.6), channel_id=1, source_target_pairs={{0,8},{8,0},{16,24},{24,16},{1,9},{9,1},{17,25},{25,17},{2,10},{10... | collective-permute-start | bytes 98312 | tf_op jit(solution)/shard_map/ppermute | solution.py:40
  10.8 5.2 %collective-permute-start.2 = (bf16[2,64,128]{2,0,1:T(2,128)(2,1)S(1)}, bf16[2,64,128]{2,0,1:T(2,128)(2,1)S(1)}, u32[]{:S(2)}, u32[]{:S(2)}) collective-permute-start(bf16[2,64,128]{2,0,1:T(2,128)(2,1)S(1)} %convolution_convert_fusion), channel_id=1, source_target_pairs={{0,4},{1,5},{2,6},{3,7},{4,0},{5,1},{6,2},{7,3},{8,12},{9,13},{10,... | collective-permute-start | bytes 98312 | tf_op jit(solution)/shard_map/ppermute | solution.py:40
  16.0 4.3 %collective-permute-start.3 = (bf16[2,128,128]{2,0,1:T(2,128)(2,1)S(1)}, bf16[2,128,128]{2,0,1:T(2,128)(2,1)S(1)}, u32[]{:S(2)}, u32[]{:S(2)}) collective-permute-start(bf16[2,128,128]{2,0,1:T(2,128)(2,1)S(1)} %pad_maximum_fusion.5), channel_id=1, source_target_pairs={{0,2},{1,3},{2,0},{3,1},{4,6},{5,7},{6,4},{7,5},{8,10},{9,11},{10,... | collective-permute-start | bytes 196616 | tf_op jit(solution)/shard_map/ppermute | solution.py:40
  20.6 1.5 %collective-permute-start.4 = (bf16[2,256,128]{2,0,1:T(2,128)(2,1)S(1)}, bf16[2,256,128]{2,0,1:T(2,128)(2,1)S(1)}, u32[]{:S(2)}, u32[]{:S(2)}) collective-permute-start(bf16[2,256,128]{2,0,1:T(2,128)(2,1)S(1)} %pad_maximum_fusion.2), channel_id=1, source_target_pairs={{0,1},{1,0},{2,3},{3,2},{4,5},{5,4},{6,7},{7,6},{8,9},{9,8},{10,11... | collective-permute-start | bytes 393224 | tf_op jit(solution)/shard_map/ppermute | solution.py:40
  23.1 4.8 %copy-start.4 = (f32[1,1280]{1,0:T(1,128)S(1)}, f32[1,1280]{1,0:T(1,128)}, u32[]{:S(2)}) copy-start(f32[1,1280]{1,0:T(1,128)} %param.18) | copy-start | bytes 15364
  23.1 4.9 %copy-start.1 = (bf16[1,1280,2048]{2,1,0:T(8,128)(2,1)S(1)}, bf16[1,1280,2048]{2,1,0:T(8,128)(2,1)}, u32[]{:S(2)}) copy-start(bf16[1,1280,2048]{2,1,0:T(8,128)(2,1)} %param.13) | copy-start | bytes 15728644
  30.2 1.4 %collective-permute-start.5 = (f32[2,2176]{1,0:T(2,128)S(1)}, f32[2,2176]{1,0:T(2,128)S(1)}, u32[]{:S(2)}, u32[]{:S(2)}) collective-permute-start(f32[2,2176]{1,0:T(2,128)S(1)} %pad_maximum_fusion.7), channel_id=1, source_target_pairs={{0,1},{1,0},{2,3},{3,2},{4,5},{5,4},{6,7},{7,6},{8,9},{9,8},{10,11... | collective-permute-start | bytes 52232 | tf_op jit(solution)/shard_map/ppermute | solution.py:27
  31.6 3.8 %collective-permute-start.6 = (f32[2,2176]{1,0:T(2,128)S(1)}, f32[2,2176]{1,0:T(2,128)S(1)}, u32[]{:S(2)}, u32[]{:S(2)}) collective-permute-start(f32[2,2176]{1,0:T(2,128)S(1)} %fusion.49), channel_id=1, source_target_pairs={{0,2},{1,3},{2,0},{3,1},{4,6},{5,7},{6,4},{7,5},{8,10},{9,11},{10,... | collective-permute-start | bytes 52232 | tf_op jit(solution)/shard_map/ppermute | solution.py:27
  35.4 4.8 %collective-permute-start.7 = (f32[2,2176]{1,0:T(2,128)S(1)}, f32[2,2176]{1,0:T(2,128)S(1)}, u32[]{:S(2)}, u32[]{:S(2)}) collective-permute-start(f32[2,2176]{1,0:T(2,128)S(1)} %add.130), channel_id=1, source_target_pairs={{0,4},{1,5},{2,6},{3,7},{4,0},{5,1},{6,2},{7,3},{8,12},{9,13},{10,... | collective-permute-start | bytes 52232 | tf_op jit(solution)/shard_map/ppermute | solution.py:27
  42.0 15.0 %collective-permute-start.8 = (f32[256]{0:T(256)S(1)}, f32[256]{0:T(256)S(1)}, u32[]{:S(2)}, u32[]{:S(2)}) collective-permute-start(f32[256]{0:T(256)S(1)} %bitcast.94), channel_id=1, source_target_pairs={{0,4},{1,5},{2,6},{3,7},{4,0},{5,1},{6,2},{7,3},{8,12},{9,13},{10,... | collective-permute-start | bytes 3080 | tf_op jit(solution)/shard_map/ppermute | solution.py:40
  56.9 3.7 %collective-permute-start.9 = (f32[512]{0:T(512)S(1)}, f32[512]{0:T(512)S(1)}, u32[]{:S(2)}, u32[]{:S(2)}) collective-permute-start(f32[512]{0:T(512)S(1)} %pad_maximum_fusion.11), channel_id=1, source_target_pairs={{0,2},{1,3},{2,0},{3,1},{4,6},{5,7},{6,4},{7,5},{8,10},{9,11},{10,... | collective-permute-start | bytes 6152 | tf_op jit(solution)/shard_map/ppermute | solution.py:40
  60.6 1.2 %collective-permute-start.10 = (f32[1024]{0:T(1024)S(1)}, f32[1024]{0:T(1024)S(1)}, u32[]{:S(2)}, u32[]{:S(2)}) collective-permute-start(f32[1024]{0:T(1024)S(1)} %pad_maximum_fusion.10), channel_id=1, source_target_pairs={{0,1},{1,0},{2,3},{3,2},{4,5},{5,4},{6,7},{7,6},{8,9},{9,8},{10,11... | collective-permute-start | bytes 12296 | tf_op jit(solution)/shard_map/ppermute | solution.py:40
  65.0 4.2 %copy-start.2 = (bf16[1280,2,8,64]{0,3,2,1:T(8,128)(2,1)S(1)}, bf16[1280,2,8,64]{0,3,2,1:T(8,128)(2,1)}, u32[]{:S(2)}) copy-start(bf16[1280,2,8,64]{0,3,2,1:T(8,128)(2,1)} %copy.29) | copy-start | bytes 7864324
  69.2 1.7 %copy-start.3 = (bf16[1,1280,1024]{2,1,0:T(8,128)(2,1)S(1)}, bf16[1,1280,1024]{2,1,0:T(8,128)(2,1)}, u32[]{:S(2)}) copy-start(bf16[1,1280,1024]{2,1,0:T(8,128)(2,1)} %param.12) | copy-start | bytes 7864324
  72.7 2.7 %collective-permute-start.11 = (f32[256,2,512]{2,0,1:T(8,128)S(1)}, f32[256,2,512]{2,0,1:T(8,128)S(1)}, u32[]{:S(2)}, u32[]{:S(2)}) collective-permute-start(f32[256,2,512]{2,0,1:T(8,128)S(1)} %pad_maximum_fusion), channel_id=1, source_target_pairs={{0,1},{1,0},{2,3},{3,2},{4,5},{5,4},{6,7},{7,6},{8,9},{9,8},{10,11... | collective-permute-start | bytes 3145736 | tf_op jit(solution)/shard_map/ppermute | solution.py:67
  75.7 14.1 %collective-permute-start.12 = (f32[128,2,512]{2,0,1:T(8,128)S(1)}, f32[128,2,512]{2,0,1:T(8,128)S(1)}, u32[]{:S(2)}, u32[]{:S(2)}) collective-permute-start(f32[128,2,512]{2,0,1:T(8,128)S(1)} %slice.154), channel_id=1, source_target_pairs={{0,2},{1,3},{2,0},{3,1},{4,6},{5,7},{6,4},{7,5},{8,10},{9,11},{10,... | collective-permute-start | bytes 1572872 | tf_op jit(solution)/shard_map/ppermute | solution.py:67
  78.3 14.8 %copy-start.5 = (s32[1,2]{1,0:T(1,128)S(1)}, s32[1,2]{1,0:T(1,128)}, u32[]{:S(2)}) copy-start(s32[1,2]{1,0:T(1,128)} %param.16) | copy-start | bytes 28
  78.3 12.2 %collective-permute-start.17 = (f32[256,512]{1,0:T(8,128)S(1)}, f32[256,512]{1,0:T(8,128)S(1)}, u32[]{:S(2)}, u32[]{:S(2)}) collective-permute-start(f32[256,512]{1,0:T(8,128)S(1)} %slice.126), channel_id=1, source_target_pairs={{0,1},{1,0},{2,3},{3,2},{4,5},{5,4},{6,7},{7,6},{8,9},{9,8},{10,11... | collective-permute-start | bytes 1572872 | tf_op jit(solution)/shard_map/ppermute | solution.py:67
  90.5 14.3 %collective-permute-start.13 = (f32[64,2,512]{2,0,1:T(8,128)}, f32[64,2,512]{2,0,1:T(8,128)S(1)}, u32[]{:S(2)}, u32[]{:S(2)}) collective-permute-start(f32[64,2,512]{2,0,1:T(8,128)} %slice.156), channel_id=1, source_target_pairs={{0,4},{1,5},{2,6},{3,7},{4,0},{5,1},{6,2},{7,3},{8,12},{9,13},{10,... | collective-permute-start | bytes 786440 | tf_op jit(solution)/shard_map/ppermute | solution.py:67
  91.3 13.5 %collective-permute-start.18 = (f32[128,512]{1,0:T(8,128)}, f32[128,512]{1,0:T(8,128)}, u32[]{:S(2)}, u32[]{:S(2)}) collective-permute-start(f32[128,512]{1,0:T(8,128)} %slice.128), channel_id=1, source_target_pairs={{0,2},{1,3},{2,0},{3,1},{4,6},{5,7},{6,4},{7,5},{8,10},{9,11},{10,... | collective-permute-start | bytes 786440 | tf_op jit(solution)/shard_map/ppermute | solution.py:67
  105.9 8.1 %collective-permute-start.19 = (f32[64,512]{1,0:T(8,128)S(1)}, f32[64,512]{1,0:T(8,128)S(1)}, u32[]{:S(2)}, u32[]{:S(2)}) collective-permute-start(f32[64,512]{1,0:T(8,128)S(1)} %slice.130), channel_id=1, source_target_pairs={{0,4},{1,5},{2,6},{3,7},{4,0},{5,1},{6,2},{7,3},{8,12},{9,13},{10,... | collective-permute-start | bytes 393224 | tf_op jit(solution)/shard_map/ppermute | solution.py:67
  107.8 6.9 %collective-permute-start.14 = (f32[64,512]{1,0:T(8,128)S(1)}, f32[64,512]{1,0:T(8,128)S(1)}, u32[]{:S(2)}, u32[]{:S(2)}) collective-permute-start(f32[64,512]{1,0:T(8,128)S(1)} %get-tuple-element.17), channel_id=1, source_target_pairs={{0,8},{8,16},{16,24},{24,0},{1,9},{9,17},{17,25},{25,1},{2,10},{10... | collective-permute-start | bytes 393224 | tf_op jit(solution)/shard_map/ppermute | solution.py:169
  109.3 5.9 %collective-permute-start.15 = (f32[64,512]{1,0:T(8,128)S(1)}, f32[64,512]{1,0:T(8,128)S(1)}, u32[]{:S(2)}, u32[]{:S(2)}) collective-permute-start(f32[64,512]{1,0:T(8,128)S(1)} %get-tuple-element.18), channel_id=1, source_target_pairs={{0,16},{8,24},{16,0},{24,8},{1,17},{9,25},{17,1},{25,9},{2,18},{10... | collective-permute-start | bytes 393224 | tf_op jit(solution)/shard_map/ppermute | solution.py:169
  110.8 5.0 %collective-permute-start.16 = (f32[64,512]{1,0:T(8,128)S(1)}, f32[64,512]{1,0:T(8,128)S(1)}, u32[]{:S(2)}, u32[]{:S(2)}) collective-permute-start(f32[64,512]{1,0:T(8,128)S(1)} %get-tuple-element.19), channel_id=1, source_target_pairs={{0,24},{8,0},{16,8},{24,16},{1,25},{9,1},{17,9},{25,17},{2,26},{10... | collective-permute-start | bytes 393224 | tf_op jit(solution)/shard_map/ppermute | solution.py:169

commit v8 on v7

--- a/solution.py
+++ b/solution.py
@@ -139,18 +139,23 @@
     potential_total = jnp.dot(coefficients, weight_projection, precision=highest) + exchange_total
     average = potential_total / weight_sum
     potential = live_weight * (coulomb + exchange - average)
-    grid_size = lax.axis_size("grid")
-    order = send_order("grid")
-    blocked = basis_rows.reshape(points, 2, grid_size, frag_basis // grid_size)
-    permuted_basis = jnp.take(blocked, order, axis=2).reshape(points, 2 * frag_basis)
-    weighted_basis = (permuted_basis * potential[:, None]).astype(jnp.bfloat16)
+    weighted_basis = (basis_rows * potential[:, None]).astype(jnp.bfloat16)
     left_first = weighted_basis[:, :frag_basis]
     left_second = weighted_basis[:, frag_basis:]
     first_first = contract(left_first, basis_rows[:, :frag_basis])
     first_second = contract(left_first, basis_rows[:, frag_basis:])
     second_second = contract(left_second, basis_rows[:, frag_basis:])
+    grid_size = lax.axis_size("grid")
+    order = send_order("grid")
+
+    def in_send_order(rows):
+        blocks = rows.reshape((grid_size, rows.shape[0] // grid_size) + rows.shape[1:])
+        return jnp.take(blocks, order, axis=0).reshape(rows.shape)
+
     diagonal, own_cross = paired_scatter(
-        jnp.stack([first_first, second_second], axis=1), first_second, "grid"
+        in_send_order(jnp.stack([first_first, second_second], axis=1)),
+        in_send_order(first_second),
+        "grid",
     )
     own_first = diagonal[:, 0]
     own_second = diagonal[:, 1]

time: 117 us -> 122 us (1.043)
  other arithmetic: 10.3 us -> 14.8 us
  local copies, waits for them, and re-layouts: 17.9 us -> 14.7 us
  matrix products: 13.3 us -> 16.1 us
  starting transfers between devices: 30.5 us -> 32.3 us
  waiting for transfers between devices: 35.7 us -> 34.2 us
    unnamed x16 -> x15, local copies, waits for them, and re-layouts: 6.38 us -> 1.57 us
    dot_general x3, matrix products: 2.53 us -> 5.34 us  [contract(): lax.dot_general(left_side, right_side, numbers, preferred_element_type=jn...]
    slice x0 -> x2, local copies, waits for them, and re-layouts: none -> 2.52 us  [half_step(): return value[:half] + sent]
    ppermute x6, waiting for transfers between devices: 21.5 us -> 19.1 us  [half_step(): lax.ppermute(value[half:], axis, [(i, i ^ 1 << bit) for i in range(size)])]
    select_n x0 -> x2, other arithmetic: none -> 2.04 us  [in_send_order(): return jnp.take(blocks, order, axis=0).reshape(rows.shape)]
    gather x2, local copies, waits for them, and re-layouts: 7.46 us -> 5.49 us  [in_send_order(): return jnp.take(blocks, order, axis=0).reshape(rows.shape)]
    ppermute x6, starting transfers between devices: 5.64 us -> 7.41 us  [half_step(): lax.ppermute(value[half:], axis, [(i, i ^ 1 << bit) for i in range(size)])]
    ppermute x8, waiting for transfers between devices: 8.56 us -> 10.1 us  [xor_gather(): other = lax.ppermute(value, axis, [(i, i ^ 1 << bit) for i in range(size)])]
  transfers between devices with their start and end apart: 20 -> 20, of which waited for: 15 -> 16; matrix products, arithmetic and copies ran while one was open for 17% -> 11% of each run, Pallas kernels for 0% -> 0%
where the time goes in v8:
time: 122 us; the launch traced here: 121 us
  waiting for transfers between devices  34.2 us (28%)
  starting transfers between devices  32.3 us (26%)
  matrix products  16.1 us (13%)
  other arithmetic  14.8 us (12%)
  local copies, waits for them, and re-layouts  14.7 us (12%)
  between operations  8.72 us (7%)
    ppermute x6, waiting for transfers between devices, half_step(): lax.ppermute(value[half:], axis, [(i, i ^ 1 << bit) for i in range(size)])  19.1 us
    ppermute x8, starting transfers between devices, xor_gather(): other = lax.ppermute(value, axis, [(i, i ^ 1 << bit) for i in range(size)])  14.9 us
    ppermute x8, waiting for transfers between devices, xor_gather(): other = lax.ppermute(value, axis, [(i, i ^ 1 << bit) for i in range(size)])  10.1 us
    ppermute x6, starting transfers between devices, half_step(): lax.ppermute(value[half:], axis, [(i, i ^ 1 << bit) for i in range(size)])  7.41 us
    ppermute x3, starting transfers between devices, xor_sum(): lax.ppermute(value, axis, [(i, i ^ step) for i in range(size)])  5.49 us
    gather x2, local copies, waits for them, and re-layouts, in_send_order(): return jnp.take(blocks, order, axis=0).reshape(rows.shape)  5.49 us
    dot_general x3, matrix products, contract(): lax.dot_general(left_side, right_side, numbers, preferred_element_type=jn...  5.34 us
    ppermute x3, waiting for transfers between devices, xor_sum(): lax.ppermute(value, axis, [(i, i ^ step) for i in range(size)])  4.52 us
  transfers between devices with their start and end apart: 20, of which 16 were waited for; matrix products, arithmetic and copies ran while one was open for 11% of the time, Pallas kernels for 0%

profile of v8, /device:TPU:0, one launch (start us, length us, event | category | flops | bytes accessed | tf_op | source)
XLA Modules:
  0.0 120.9 jit_solution(371010342406575455)
XLA Ops:
  0.6 0.9 copy.32
  1.5 3.1 %collective-permute-start = (bf16[1,64,128]{2,0,1:T(2,128)(2,1)S(1)}, bf16[1,64,128]{2,0,1:T(2,128)(2,1)S(1)}, u32[]{:S(2)}, u32[]{:S(2)}) collective-permute-start(bf16[1,64,128]{2,0,1:T(2,128)(2,1)S(1)} %copy.32), channel_id=1, source_target_pairs={{0,16},{8,24},{16,0},{24,8},{1,17},{9,25},{17,1},{25,9},{2,18},{10... | collective-permute-start | bytes 49160 | tf_op jit(solution)/shard_map/ppermute | solution.py:40
  5.3 1.2 %collective-permute-done = bf16[1,64,128]{2,0,1:T(2,128)(2,1)S(1)} collective-permute-done((bf16[1,64,128]{2,0,1:T(2,128)(2,1)S(1)}, bf16[1,64,128]{2,0,1:T(2,128)(2,1)S(1)}, u32[]{:S(2)}, u32[]{:S(2)}) %collective-permute-start) | collective-permute-done | bytes 16416 | tf_op jit(solution)/shard_map/ppermute | solution.py:40
  6.6 2.1 %collective-permute-start.1 = (bf16[2,64,128]{2,0,1:T(2,128)(2,1)S(1)}, bf16[2,64,128]{2,0,1:T(2,128)(2,1)S(1)}, u32[]{:S(2)}, u32[]{:S(2)}) collective-permute-start(bf16[2,64,128]{2,0,1:T(2,128)(2,1)S(1)} %pad_maximum_fusion.6), channel_id=1, source_target_pairs={{0,8},{8,0},{16,24},{24,16},{1,9},{9,1},{17,25},{25,17},{2,10},{10... | collective-permute-start | bytes 98312 | tf_op jit(solution)/shard_map/ppermute | solution.py:40
  8.6 0.9 fusion.43
  9.5 1.1 collective-permute-done.1
  10.8 3.2 %collective-permute-start.2 = (bf16[2,64,128]{2,0,1:T(2,128)(2,1)S(1)}, bf16[2,64,128]{2,0,1:T(2,128)(2,1)S(1)}, u32[]{:S(2)}, u32[]{:S(2)}) collective-permute-start(bf16[2,64,128]{2,0,1:T(2,128)(2,1)S(1)} %convolution_convert_fusion), channel_id=1, source_target_pairs={{0,4},{1,5},{2,6},{3,7},{4,0},{5,1},{6,2},{7,3},{8,12},{9,13},{10,... | collective-permute-start | bytes 98312 | tf_op jit(solution)/shard_map/ppermute | solution.py:40
  14.0 2.0 %collective-permute-done.2 = bf16[2,64,128]{2,0,1:T(2,128)(2,1)S(1)} collective-permute-done((bf16[2,64,128]{2,0,1:T(2,128)(2,1)S(1)}, bf16[2,64,128]{2,0,1:T(2,128)(2,1)S(1)}, u32[]{:S(2)}, u32[]{:S(2)}) %collective-permute-start.2) | collective-permute-done | bytes 32800 | tf_op jit(solution)/shard_map/ppermute | solution.py:40
  16.0 1.9 %collective-permute-start.3 = (bf16[2,128,128]{2,0,1:T(2,128)(2,1)S(1)}, bf16[2,128,128]{2,0,1:T(2,128)(2,1)S(1)}, u32[]{:S(2)}, u32[]{:S(2)}) collective-permute-start(bf16[2,128,128]{2,0,1:T(2,128)(2,1)S(1)} %pad_maximum_fusion.5), channel_id=1, source_target_pairs={{0,2},{1,3},{2,0},{3,1},{4,6},{5,7},{6,4},{7,5},{8,10},{9,11},{10,... | collective-permute-start | bytes 196616 | tf_op jit(solution)/shard_map/ppermute | solution.py:40
  18.6 1.8 %collective-permute-done.3 = bf16[2,128,128]{2,0,1:T(2,128)(2,1)S(1)} collective-permute-done((bf16[2,128,128]{2,0,1:T(2,128)(2,1)S(1)}, bf16[2,128,128]{2,0,1:T(2,128)(2,1)S(1)}, u32[]{:S(2)}, u32[]{:S(2)}) %collective-permute-start.3) | collective-permute-done | bytes 65568 | tf_op jit(solution)/shard_map/ppermute | solution.py:40
  23.2 2.0 %fusion.12 = f32[1280]{0:T(1024)S(1)} fusion(bf16[512,128]{1,0:T(8,128)(2,1)S(1)} %bitcast.89, bf16[1280,1024]{1,0:T(8,128)(2,1)} %bitcast.79), kind=kOutput, calls=%fused_computation.18 | convolution fusion | flops 168098560 | bytes 1446912 | tf_op jit(solution)/shard_map/dot_general | solution.py:110
  25.3 1.9 %fusion.11 = f32[1280]{0:T(1024)S(1)} fusion(bf16[512,128]{1,0:T(8,128)(2,1)S(1)} %bitcast.88, bf16[1280,1024]{1,0:T(8,128)(2,1)} %bitcast.80), kind=kOutput, calls=%fused_computation.17 | convolution fusion | flops 168098560 | bytes 1446912 | tf_op jit(solution)/shard_map/dot_general | solution.py:107
  27.9 0.8 fusion.2
  28.7 1.4 %pad_maximum_fusion.12 = f32[2]{0:T(128)S(1)} fusion(f32[1]{0:T(128)} %bitcast.12, f32[1]{0:T(128)} %bitcast.11), kind=kLoop, calls=%fused_computation.97 | loop fusion | flops 2 | bytes 16 | tf_op jit(solution)/shard_map/stack | solution.py:122
  30.7 0.8 collective-permute-done.5
  31.6 1.9 %collective-permute-start.6 = (f32[2,2176]{1,0:T(2,128)S(1)}, f32[2,2176]{1,0:T(2,128)S(1)}, u32[]{:S(2)}, u32[]{:S(2)}) collective-permute-start(f32[2,2176]{1,0:T(2,128)S(1)} %fusion.49), channel_id=1, source_target_pairs={{0,2},{1,3},{2,0},{3,1},{4,6},{5,7},{6,4},{7,5},{8,10},{9,11},{10,... | collective-permute-start | bytes 52232 | tf_op jit(solution)/shard_map/ppermute | solution.py:27
  33.4 2.0 %collective-permute-done.6 = f32[2,2176]{1,0:T(2,128)S(1)} collective-permute-done((f32[2,2176]{1,0:T(2,128)S(1)}, f32[2,2176]{1,0:T(2,128)S(1)}, u32[]{:S(2)}, u32[]{:S(2)}) %collective-permute-start.6) | collective-permute-done | bytes 17440 | tf_op jit(solution)/shard_map/ppermute | solution.py:27
  35.4 3.1 %collective-permute-start.7 = (f32[2,2176]{1,0:T(2,128)S(1)}, f32[2,2176]{1,0:T(2,128)S(1)}, u32[]{:S(2)}, u32[]{:S(2)}) collective-permute-start(f32[2,2176]{1,0:T(2,128)S(1)} %add.132), channel_id=1, source_target_pairs={{0,4},{1,5},{2,6},{3,7},{4,0},{5,1},{6,2},{7,3},{8,12},{9,13},{10,... | collective-permute-start | bytes 52232 | tf_op jit(solution)/shard_map/ppermute | solution.py:27
  38.5 1.7 %collective-permute-done.7 = f32[2,2176]{1,0:T(2,128)S(1)} collective-permute-done((f32[2,2176]{1,0:T(2,128)S(1)}, f32[2,2176]{1,0:T(2,128)S(1)}, u32[]{:S(2)}, u32[]{:S(2)}) %collective-permute-start.7) | collective-permute-done | bytes 17440 | tf_op jit(solution)/shard_map/ppermute | solution.py:27
  40.2 1.7 %fusion.7 = f32[1,256]{1,0:T(1,128)S(1)} fusion(f32[1,256,2048]{2,1,0:T(8,128)S(1)} %copy-done, f32[2,2176]{1,0:T(2,128)S(1)} %add.133), kind=kOutput, calls=%fused_computation.13 | convolution fusion | flops 6291456 | bytes 2106368 | tf_op jit(solution)/shard_map/dot_general | solution.py:132
  41.9 2.9 %collective-permute-start.8 = (f32[256]{0:T(256)S(1)}, f32[256]{0:T(256)S(1)}, u32[]{:S(2)}, u32[]{:S(2)}) collective-permute-start(f32[256]{0:T(256)S(1)} %bitcast.94), channel_id=1, source_target_pairs={{0,4},{1,5},{2,6},{3,7},{4,0},{5,1},{6,2},{7,3},{8,12},{9,13},{10,... | collective-permute-start | bytes 3080 | tf_op jit(solution)/shard_map/ppermute | solution.py:40
  44.9 1.6 %collective-permute-done.8 = f32[256]{0:T(256)S(1)} collective-permute-done((f32[256]{0:T(256)S(1)}, f32[256]{0:T(256)S(1)}, u32[]{:S(2)}, u32[]{:S(2)}) %collective-permute-start.8) | collective-permute-done | bytes 1056 | tf_op jit(solution)/shard_map/ppermute | solution.py:40
  46.4 1.7 %collective-permute-start.9 = (f32[512]{0:T(512)S(1)}, f32[512]{0:T(512)S(1)}, u32[]{:S(2)}, u32[]{:S(2)}) collective-permute-start(f32[512]{0:T(512)S(1)} %pad_maximum_fusion.11), channel_id=1, source_target_pairs={{0,2},{1,3},{2,0},{3,1},{4,6},{5,7},{6,4},{7,5},{8,10},{9,11},{10,... | collective-permute-start | bytes 6152 | tf_op jit(solution)/shard_map/ppermute | solution.py:40
  48.2 1.8 %collective-permute-done.9 = f32[512]{0:T(512)S(1)} collective-permute-done((f32[512]{0:T(512)S(1)}, f32[512]{0:T(512)S(1)}, u32[]{:S(2)}, u32[]{:S(2)}) %collective-permute-start.9) | collective-permute-done | bytes 2080 | tf_op jit(solution)/shard_map/ppermute | solution.py:40
  54.5 4.1 %fusion.4 = f32[1280,2]{0,1:T(2,128)S(1)} fusion(bf16[1,1280,2048]{2,1,0:T(8,128)(2,1)} %param.13, bf16[2048,1]{0,1:T(2,128)(2,1)S(1)} %stack.34, bf16[2048,1]{0,1:T(2,128)(2,1)S(1)} %bitcast.92), kind=kOutput, calls=%fused_computation.11 | convolution fusion | flops 10502144 | bytes 5261312 | tf_op jit(solution)/shard_map/dot_general | solution.py:135
  59.1 0.9 fusion.9
  60.6 0.9 fusion.15
  61.5 1.6 %pad_maximum_fusion = f32[8,64,2,512]{3,1,0,2:T(8,128)} fusion(f32[8,64,1,512]{3,1,0,2:T(8,128)S(1)} %bitcast.86, f32[8,64,1,512]{3,1,0,2:T(8,128)S(1)} %bitcast.87), kind=kLoop, calls=%fused_computation.12 | loop fusion | flops 524288 | bytes 4194304 | tf_op jit(solution)/shard_map/stack | solution.py:156
  63.0 3.7 %gather_fusion.2 = f32[8,64,2,512]{3,1,2,0:T(8,128)} fusion(f32[8,64,2,512]{3,1,0,2:T(8,128)} %pad_maximum_fusion, s32[1024]{0:T(1024)S(1)} %get-tuple-element.32), kind=kCustom, calls=%fused_computation.2 | custom fusion | bytes 4194336 | tf_op jit(solution)/shard_map/jit(_take)/gather | solution.py:153
  66.7 1.9 %broadcast_select_fusion = f32[8,64,2,512]{3,1,2,0:T(8,128)S(1)} fusion(f32[8,64,2,512]{3,1,2,0:T(8,128)} %gather_fusion.2, pred[8]{0:T(512)(128)(4,1)S(1)} %get-tuple-element.10), kind=kLoop, calls=%fused_computation.28 | loop fusion | flops 524288 | bytes 4194312 | tf_op jit(solution)/shard_map/jit(_take)/select_n | solution.py:153
  68.6 1.2 fusion.50
  69.8 1.1 copy.35
  71.2 3.6 %fusion.13 = f32[512,512]{1,0:T(8,128)} fusion(bf16[1280,1024]{1,0:T(8,128)(2,1)} %copy-done.3, bf16[1280,1024]{1,0:T(8,128)(2,1)} %bitcast.81), kind=kOutput, calls=%fused_computation.19 | convolution fusion | flops 671088640 | bytes 3670016 | tf_op jit(solution)/shard_map/dot_general | solution.py:18
  74.8 1.8 %gather_fusion.3 = f32[8,64,512]{2,1,0:T(8,128)S(1)} fusion(f32[8,64,512]{2,1,0:T(8,128)} %bitcast.84, s32[1024]{0:T(1024)S(1)} %get-tuple-element.32), kind=kCustom, calls=%fused_computation.3 | custom fusion | bytes 2097184 | tf_op jit(solution)/shard_map/jit(_take)/gather | solution.py:153
  76.7 1.3 %copy.34 = f32[4,64,2,512]{3,1,0,2:T(8,128)S(1)} copy(f32[4,64,2,512]{3,1,2,0:T(8,128)} %get-tuple-element.17) | data formatting | bytes 2097152 | tf_op jit(solution)/shard_map/slice | solution.py:68
  78.0 1.4 %bitcast_add_fusion = f32[256,2,512]{2,0,1:T(8,128)S(1)} fusion(f32[256,2,512]{2,0,1:T(8,128)} %collective-permute-done.11, f32[4,64,2,512]{3,1,0,2:T(8,128)S(1)} %copy.34), kind=kLoop, calls=%fused_computation.27 | loop fusion | flops 262144 | bytes 3145728 | tf_op jit(solution)/shard_map/add | solution.py:68
  79.4 1.8 %collective-permute-start.12 = (f32[128,2,512]{2,0,1:T(8,128)S(1)}, f32[128,2,512]{2,0,1:T(8,128)S(1)}, u32[]{:S(2)}, u32[]{:S(2)}) collective-permute-start(f32[128,2,512]{2,0,1:T(8,128)S(1)} %slice.164), channel_id=1, source_target_pairs={{0,2},{1,3},{2,0},{3,1},{4,6},{5,7},{6,4},{7,5},{8,10},{9,11},{10,... | collective-permute-start | bytes 1572872 | tf_op jit(solution)/shard_map/ppermute | solution.py:67
  81.5 12.1 %collective-permute-done.12 = f32[128,2,512]{2,0,1:T(8,128)S(1)} collective-permute-done((f32[128,2,512]{2,0,1:T(8,128)S(1)}, f32[128,2,512]{2,0,1:T(8,128)S(1)}, u32[]{:S(2)}, u32[]{:S(2)}) %collective-permute-start.12) | collective-permute-done | bytes 524320 | tf_op jit(solution)/shard_map/ppermute | solution.py:67
  94.5 2.9 %collective-permute-start.13 = (f32[64,2,512]{2,0,1:T(8,128)}, f32[64,2,512]{2,0,1:T(8,128)S(1)}, u32[]{:S(2)}, u32[]{:S(2)}) collective-permute-start(f32[64,2,512]{2,0,1:T(8,128)} %slice.166), channel_id=1, source_target_pairs={{0,4},{1,5},{2,6},{3,7},{4,0},{5,1},{6,2},{7,3},{8,12},{9,13},{10,... | collective-permute-start | bytes 786440 | tf_op jit(solution)/shard_map/ppermute | solution.py:67
  98.2 1.7 %collective-permute-start.18 = (f32[128,512]{1,0:T(8,128)}, f32[128,512]{1,0:T(8,128)}, u32[]{:S(2)}, u32[]{:S(2)}) collective-permute-start(f32[128,512]{1,0:T(8,128)} %slice.136), channel_id=1, source_target_pairs={{0,2},{1,3},{2,0},{3,1},{4,6},{5,7},{6,4},{7,5},{8,10},{9,11},{10,... | collective-permute-start | bytes 786440 | tf_op jit(solution)/shard_map/ppermute | solution.py:67
  105.6 3.6 %collective-permute-done.13 = f32[64,2,512]{2,0,1:T(8,128)S(1)} collective-permute-done((f32[64,2,512]{2,0,1:T(8,128)}, f32[64,2,512]{2,0,1:T(8,128)S(1)}, u32[]{:S(2)}, u32[]{:S(2)}) %collective-permute-start.13) | collective-permute-done | bytes 262176 | tf_op jit(solution)/shard_map/ppermute | solution.py:67
  109.3 1.0 collective-permute-done.18
  110.3 1.0 slice_add_fusion.3
  111.3 0.7 collective-permute-start.19
  112.1 1.6 %collective-permute-start.14 = (f32[64,512]{1,0:T(8,128)S(1)}, f32[64,512]{1,0:T(8,128)S(1)}, u32[]{:S(2)}, u32[]{:S(2)}) collective-permute-start(f32[64,512]{1,0:T(8,128)S(1)} %get-tuple-element.19), channel_id=1, source_target_pairs={{0,8},{8,16},{16,24},{24,0},{1,9},{9,17},{17,25},{25,1},{2,10},{10... | collective-permute-start | bytes 393224 | tf_op jit(solution)/shard_map/ppermute | solution.py:174
  113.7 1.5 %collective-permute-start.15 = (f32[64,512]{1,0:T(8,128)S(1)}, f32[64,512]{1,0:T(8,128)S(1)}, u32[]{:S(2)}, u32[]{:S(2)}) collective-permute-start(f32[64,512]{1,0:T(8,128)S(1)} %get-tuple-element.20), channel_id=1, source_target_pairs={{0,16},{8,24},{16,0},{24,8},{1,17},{9,25},{17,1},{25,9},{2,18},{10... | collective-permute-start | bytes 393224 | tf_op jit(solution)/shard_map/ppermute | solution.py:174
  115.2 1.4 %collective-permute-start.16 = (f32[64,512]{1,0:T(8,128)S(1)}, f32[64,512]{1,0:T(8,128)S(1)}, u32[]{:S(2)}, u32[]{:S(2)}) collective-permute-start(f32[64,512]{1,0:T(8,128)S(1)} %get-tuple-element.21), channel_id=1, source_target_pairs={{0,24},{8,0},{16,8},{24,16},{1,25},{9,1},{17,9},{25,17},{2,26},{10... | collective-permute-start | bytes 393224 | tf_op jit(solution)/shard_map/ppermute | solution.py:174
  116.6 2.3 %collective-permute-done.19 = f32[64,512]{1,0:T(8,128)S(1)} collective-permute-done((f32[64,512]{1,0:T(8,128)S(1)}, f32[64,512]{1,0:T(8,128)S(1)}, u32[]{:S(2)}, u32[]{:S(2)}) %collective-permute-start.19) | collective-permute-done | bytes 131104 | tf_op jit(solution)/shard_map/ppermute | solution.py:67
  (80 shorter events, 13.8 us)
Async XLA Ops:
  0.6 39.6 %copy-start = (f32[1,256,2048]{2,1,0:T(8,128)S(1)}, f32[1,256,2048]{2,1,0:T(8,128)}, u32[]{:S(2)}) copy-start(f32[1,256,2048]{2,1,0:T(8,128)} %param.19) | copy-start | bytes 6291460
  1.5 5.0 %collective-permute-start = (bf16[1,64,128]{2,0,1:T(2,128)(2,1)S(1)}, bf16[1,64,128]{2,0,1:T(2,128)(2,1)S(1)}, u32[]{:S(2)}, u32[]{:S(2)}) collective-permute-start(bf16[1,64,128]{2,0,1:T(2,128)(2,1)S(1)} %copy.32), channel_id=1, source_target_pairs={{0,16},{8,24},{16,0},{24,8},{1,17},{9,25},{17,1},{25,9},{2,18},{10... | collective-permute-start | bytes 49160 | tf_op jit(solution)/shard_map/ppermute | solution.py:40
  6.6 4.0 %collective-permute-start.1 = (bf16[2,64,128]{2,0,1:T(2,128)(2,1)S(1)}, bf16[2,64,128]{2,0,1:T(2,128)(2,1)S(1)}, u32[]{:S(2)}, u32[]{:S(2)}) collective-permute-start(bf16[2,64,128]{2,0,1:T(2,128)(2,1)S(1)} %pad_maximum_fusion.6), channel_id=1, source_target_pairs={{0,8},{8,0},{16,24},{24,16},{1,9},{9,1},{17,25},{25,17},{2,10},{10... | collective-permute-start | bytes 98312 | tf_op jit(solution)/shard_map/ppermute | solution.py:40
  10.8 5.2 %collective-permute-start.2 = (bf16[2,64,128]{2,0,1:T(2,128)(2,1)S(1)}, bf16[2,64,128]{2,0,1:T(2,128)(2,1)S(1)}, u32[]{:S(2)}, u32[]{:S(2)}) collective-permute-start(bf16[2,64,128]{2,0,1:T(2,128)(2,1)S(1)} %convolution_convert_fusion), channel_id=1, source_target_pairs={{0,4},{1,5},{2,6},{3,7},{4,0},{5,1},{6,2},{7,3},{8,12},{9,13},{10,... | collective-permute-start | bytes 98312 | tf_op jit(solution)/shard_map/ppermute | solution.py:40
  16.0 4.3 %collective-permute-start.3 = (bf16[2,128,128]{2,0,1:T(2,128)(2,1)S(1)}, bf16[2,128,128]{2,0,1:T(2,128)(2,1)S(1)}, u32[]{:S(2)}, u32[]{:S(2)}) collective-permute-start(bf16[2,128,128]{2,0,1:T(2,128)(2,1)S(1)} %pad_maximum_fusion.5), channel_id=1, source_target_pairs={{0,2},{1,3},{2,0},{3,1},{4,6},{5,7},{6,4},{7,5},{8,10},{9,11},{10,... | collective-permute-start | bytes 196616 | tf_op jit(solution)/shard_map/ppermute | solution.py:40
  20.6 1.5 %collective-permute-start.4 = (bf16[2,256,128]{2,0,1:T(2,128)(2,1)S(1)}, bf16[2,256,128]{2,0,1:T(2,128)(2,1)S(1)}, u32[]{:S(2)}, u32[]{:S(2)}) collective-permute-start(bf16[2,256,128]{2,0,1:T(2,128)(2,1)S(1)} %pad_maximum_fusion.2), channel_id=1, source_target_pairs={{0,1},{1,0},{2,3},{3,2},{4,5},{5,4},{6,7},{7,6},{8,9},{9,8},{10,11... | collective-permute-start | bytes 393224 | tf_op jit(solution)/shard_map/ppermute | solution.py:40
  23.1 4.8 %copy-start.1 = (bf16[1,1280,2048]{2,1,0:T(8,128)(2,1)S(1)}, bf16[1,1280,2048]{2,1,0:T(8,128)(2,1)}, u32[]{:S(2)}) copy-start(bf16[1,1280,2048]{2,1,0:T(8,128)(2,1)} %param.13) | copy-start | bytes 15728644
  23.2 4.6 %copy-start.4 = (f32[1,1280]{1,0:T(1,128)S(1)}, f32[1,1280]{1,0:T(1,128)}, u32[]{:S(2)}) copy-start(f32[1,1280]{1,0:T(1,128)} %param.18) | copy-start | bytes 15364
  30.2 1.4 %collective-permute-start.5 = (f32[2,2176]{1,0:T(2,128)S(1)}, f32[2,2176]{1,0:T(2,128)S(1)}, u32[]{:S(2)}, u32[]{:S(2)}) collective-permute-start(f32[2,2176]{1,0:T(2,128)S(1)} %pad_maximum_fusion.7), channel_id=1, source_target_pairs={{0,1},{1,0},{2,3},{3,2},{4,5},{5,4},{6,7},{7,6},{8,9},{9,8},{10,11... | collective-permute-start | bytes 52232 | tf_op jit(solution)/shard_map/ppermute | solution.py:27
  31.6 3.8 %collective-permute-start.6 = (f32[2,2176]{1,0:T(2,128)S(1)}, f32[2,2176]{1,0:T(2,128)S(1)}, u32[]{:S(2)}, u32[]{:S(2)}) collective-permute-start(f32[2,2176]{1,0:T(2,128)S(1)} %fusion.49), channel_id=1, source_target_pairs={{0,2},{1,3},{2,0},{3,1},{4,6},{5,7},{6,4},{7,5},{8,10},{9,11},{10,... | collective-permute-start | bytes 52232 | tf_op jit(solution)/shard_map/ppermute | solution.py:27
  35.4 4.8 %collective-permute-start.7 = (f32[2,2176]{1,0:T(2,128)S(1)}, f32[2,2176]{1,0:T(2,128)S(1)}, u32[]{:S(2)}, u32[]{:S(2)}) collective-permute-start(f32[2,2176]{1,0:T(2,128)S(1)} %add.132), channel_id=1, source_target_pairs={{0,4},{1,5},{2,6},{3,7},{4,0},{5,1},{6,2},{7,3},{8,12},{9,13},{10,... | collective-permute-start | bytes 52232 | tf_op jit(solution)/shard_map/ppermute | solution.py:27
  41.9 4.5 %collective-permute-start.8 = (f32[256]{0:T(256)S(1)}, f32[256]{0:T(256)S(1)}, u32[]{:S(2)}, u32[]{:S(2)}) collective-permute-start(f32[256]{0:T(256)S(1)} %bitcast.94), channel_id=1, source_target_pairs={{0,4},{1,5},{2,6},{3,7},{4,0},{5,1},{6,2},{7,3},{8,12},{9,13},{10,... | collective-permute-start | bytes 3080 | tf_op jit(solution)/shard_map/ppermute | solution.py:40
  46.4 3.6 %collective-permute-start.9 = (f32[512]{0:T(512)S(1)}, f32[512]{0:T(512)S(1)}, u32[]{:S(2)}, u32[]{:S(2)}) collective-permute-start(f32[512]{0:T(512)S(1)} %pad_maximum_fusion.11), channel_id=1, source_target_pairs={{0,2},{1,3},{2,0},{3,1},{4,6},{5,7},{6,4},{7,5},{8,10},{9,11},{10,... | collective-permute-start | bytes 6152 | tf_op jit(solution)/shard_map/ppermute | solution.py:40
  50.0 1.2 collective-permute-start.10
  54.5 4.2 %copy-start.2 = (bf16[1,1280,1024]{2,1,0:T(8,128)(2,1)S(1)}, bf16[1,1280,1024]{2,1,0:T(8,128)(2,1)}, u32[]{:S(2)}) copy-start(bf16[1,1280,1024]{2,1,0:T(8,128)(2,1)} %param.12) | copy-start | bytes 7864324
  59.1 1.5 %copy-start.3 = (bf16[1280,1024]{1,0:T(8,128)(2,1)}, bf16[1280,1024]{1,0:T(8,128)(2,1)S(1)}, u32[]{:S(2)}) copy-start(bf16[1280,1024]{1,0:T(8,128)(2,1)S(1)} %multiply_convert_fusion) | copy-start | bytes 7864324
  70.9 7.1 %collective-permute-start.11 = (f32[256,2,512]{2,0,1:T(8,128)}, f32[256,2,512]{2,0,1:T(8,128)}, u32[]{:S(2)}, u32[]{:S(2)}) collective-permute-start(f32[256,2,512]{2,0,1:T(8,128)} %bitcast.24), channel_id=1, source_target_pairs={{0,1},{1,0},{2,3},{3,2},{4,5},{5,4},{6,7},{7,6},{8,9},{9,8},{10,11... | collective-permute-start | bytes 3145736 | tf_op jit(solution)/shard_map/ppermute | solution.py:67
  79.4 14.2 %collective-permute-start.12 = (f32[128,2,512]{2,0,1:T(8,128)S(1)}, f32[128,2,512]{2,0,1:T(8,128)S(1)}, u32[]{:S(2)}, u32[]{:S(2)}) collective-permute-start(f32[128,2,512]{2,0,1:T(8,128)S(1)} %slice.164), channel_id=1, source_target_pairs={{0,2},{1,3},{2,0},{3,1},{4,6},{5,7},{6,4},{7,5},{8,10},{9,11},{10,... | collective-permute-start | bytes 1572872 | tf_op jit(solution)/shard_map/ppermute | solution.py:67
  81.4 18.5 %copy-start.5 = (s32[1,2]{1,0:T(1,128)S(1)}, s32[1,2]{1,0:T(1,128)}, u32[]{:S(2)}) copy-start(s32[1,2]{1,0:T(1,128)} %param.16) | copy-start | bytes 28
  81.4 16.0 %collective-permute-start.17 = (f32[256,512]{1,0:T(8,128)S(1)}, f32[256,512]{1,0:T(8,128)S(1)}, u32[]{:S(2)}, u32[]{:S(2)}) collective-permute-start(f32[256,512]{1,0:T(8,128)S(1)} %slice.134), channel_id=1, source_target_pairs={{0,1},{1,0},{2,3},{3,2},{4,5},{5,4},{6,7},{7,6},{8,9},{9,8},{10,11... | collective-permute-start | bytes 1572872 | tf_op jit(solution)/shard_map/ppermute | solution.py:67
  94.5 14.8 %collective-permute-start.13 = (f32[64,2,512]{2,0,1:T(8,128)}, f32[64,2,512]{2,0,1:T(8,128)S(1)}, u32[]{:S(2)}, u32[]{:S(2)}) collective-permute-start(f32[64,2,512]{2,0,1:T(8,128)} %slice.166), channel_id=1, source_target_pairs={{0,4},{1,5},{2,6},{3,7},{4,0},{5,1},{6,2},{7,3},{8,12},{9,13},{10,... | collective-permute-start | bytes 786440 | tf_op jit(solution)/shard_map/ppermute | solution.py:67
  98.2 12.1 %collective-permute-start.18 = (f32[128,512]{1,0:T(8,128)}, f32[128,512]{1,0:T(8,128)}, u32[]{:S(2)}, u32[]{:S(2)}) collective-permute-start(f32[128,512]{1,0:T(8,128)} %slice.136), channel_id=1, source_target_pairs={{0,2},{1,3},{2,0},{3,1},{4,6},{5,7},{6,4},{7,5},{8,10},{9,11},{10,... | collective-permute-start | bytes 786440 | tf_op jit(solution)/shard_map/ppermute | solution.py:67
  111.3 7.6 %collective-permute-start.19 = (f32[64,512]{1,0:T(8,128)S(1)}, f32[64,512]{1,0:T(8,128)S(1)}, u32[]{:S(2)}, u32[]{:S(2)}) collective-permute-start(f32[64,512]{1,0:T(8,128)S(1)} %slice.138), channel_id=1, source_target_pairs={{0,4},{1,5},{2,6},{3,7},{4,0},{5,1},{6,2},{7,3},{8,12},{9,13},{10,... | collective-permute-start | bytes 393224 | tf_op jit(solution)/shard_map/ppermute | solution.py:67
  112.1 7.5 %collective-permute-start.14 = (f32[64,512]{1,0:T(8,128)S(1)}, f32[64,512]{1,0:T(8,128)S(1)}, u32[]{:S(2)}, u32[]{:S(2)}) collective-permute-start(f32[64,512]{1,0:T(8,128)S(1)} %get-tuple-element.19), channel_id=1, source_target_pairs={{0,8},{8,16},{16,24},{24,0},{1,9},{9,17},{17,25},{25,1},{2,10},{10... | collective-permute-start | bytes 393224 | tf_op jit(solution)/shard_map/ppermute | solution.py:174
  113.7 6.2 %collective-permute-start.15 = (f32[64,512]{1,0:T(8,128)S(1)}, f32[64,512]{1,0:T(8,128)S(1)}, u32[]{:S(2)}, u32[]{:S(2)}) collective-permute-start(f32[64,512]{1,0:T(8,128)S(1)} %get-tuple-element.20), channel_id=1, source_target_pairs={{0,16},{8,24},{16,0},{24,8},{1,17},{9,25},{17,1},{25,9},{2,18},{10... | collective-permute-start | bytes 393224 | tf_op jit(solution)/shard_map/ppermute | solution.py:174
  115.2 5.0 %collective-permute-start.16 = (f32[64,512]{1,0:T(8,128)S(1)}, f32[64,512]{1,0:T(8,128)S(1)}, u32[]{:S(2)}, u32[]{:S(2)}) collective-permute-start(f32[64,512]{1,0:T(8,128)S(1)} %get-tuple-element.21), channel_id=1, source_target_pairs={{0,24},{8,0},{16,8},{24,16},{1,25},{9,1},{17,9},{25,17},{2,26},{10... | collective-permute-start | bytes 393224 | tf_op jit(solution)/shard_map/ppermute | solution.py:174

commit v9 on v6

--- a/solution.py
+++ b/solution.py
@@ -104,15 +104,17 @@
         "as,srk->ark", selector, gathered, preferred_element_type=jnp.float32
     ).astype(jnp.bfloat16)
     dimer_factors = in_order(*xor_gather(chosen, "grid", 1), 1)
-    orb_first = jnp.dot(
-        basis_rows[:, :frag_basis], dimer_factors[0], preferred_element_type=jnp.float32
+    nocc = dimer_factors.shape[2]
+    empty = jnp.zeros((frag_basis, nocc), jnp.bfloat16)
+    block_factors = jnp.concatenate(
+        [
+            jnp.concatenate([dimer_factors[0], empty], axis=1),
+            jnp.concatenate([empty, dimer_factors[1]], axis=1),
+        ],
+        axis=0,
     )
-    orb_second = jnp.dot(
-        basis_rows[:, frag_basis:], dimer_factors[1], preferred_element_type=jnp.float32
-    )
-    density = (
-        jnp.sum(orb_first * orb_first, axis=1) + jnp.sum(orb_second * orb_second, axis=1)
-    ) / (2.0 * dimer_factors.shape[2])
+    orbitals = jnp.dot(basis_rows, block_factors, preferred_element_type=jnp.float32)
+    density = jnp.sum(orbitals * orbitals, axis=1) / (2.0 * nocc)
     exchange = -exchange_coeff * jnp.cbrt(density)
     weighted_density = live_weight * density
     high_rows, low_rows = split_rows(jnp.stack([weighted_density, live_weight]))

time: 110 us -> 109 us (level)
    dot_general x2 -> x1, matrix products: 3.94 us -> 2.8 us  [shards(): jnp.dot(basis_rows, block_factors, preferred_element_type=jnp.float32)]
where the time goes in v9:
time: 109 us
  waiting for transfers between devices  35.6 us (33%)
  starting transfers between devices  31.8 us (29%)
  other arithmetic  14.3 us (13%)
  matrix products  12.3 us (11%)
  between operations  8.74 us (8%)
  local copies, waits for them, and re-layouts  6.13 us (6%)
    ppermute x6, waiting for transfers between devices, scatter_step(): lax.ppermute(send, axis, [(i, i ^ 1 << bit) for i in range(size)])  19.8 us
    ppermute x8, starting transfers between devices, xor_gather(): other = lax.ppermute(value, axis, [(i, i ^ 1 << bit) for i in range(size)])  14.9 us
    ppermute x8, waiting for transfers between devices, xor_gather(): other = lax.ppermute(value, axis, [(i, i ^ 1 << bit) for i in range(size)])  10.1 us
    ppermute x6, starting transfers between devices, scatter_step(): lax.ppermute(send, axis, [(i, i ^ 1 << bit) for i in range(size)])  6.94 us
    add x6, other arithmetic, scatter_step(): keep + lax.ppermute(send, axis, [(i, i ^ 1 << bit) for i in range(size)])  6.05 us
    ppermute x3, starting transfers between devices, xor_sum(): lax.ppermute(value, axis, [(i, i ^ step) for i in range(size)])  5.49 us
    ppermute x3, waiting for transfers between devices, xor_sum(): lax.ppermute(value, axis, [(i, i ^ step) for i in range(size)])  4.52 us
    ppermute x3, starting transfers between devices, shards(): lax.ppermute(sent, 'dimer', [(i, (i + shift) % groups) for i in range(gro...  4.49 us
  transfers between devices with their start and end apart: 20, of which 17 were waited for; matrix products, arithmetic and copies ran while one was open for 9% of the time, Pallas kernels for 0%

profile of v9, /device:TPU:0, one launch (start us, length us, event | category | flops | bytes accessed | tf_op | source)
XLA Modules:
  0.0 108.8 jit_solution(16841744803671800)
XLA Ops:
  0.6 0.9 copy.33
  1.5 3.1 %collective-permute-start = (bf16[1,64,128]{2,0,1:T(2,128)(2,1)S(1)}, bf16[1,64,128]{2,0,1:T(2,128)(2,1)S(1)}, u32[]{:S(2)}, u32[]{:S(2)}) collective-permute-start(bf16[1,64,128]{2,0,1:T(2,128)(2,1)S(1)} %copy.33), channel_id=1, source_target_pairs={{0,16},{8,24},{16,0},{24,8},{1,17},{9,25},{17,1},{25,9},{2,18},{10... | collective-permute-start | bytes 49160 | tf_op jit(solution)/shard_map/ppermute | solution.py:40
  5.3 1.2 %collective-permute-done = bf16[1,64,128]{2,0,1:T(2,128)(2,1)S(1)} collective-permute-done((bf16[1,64,128]{2,0,1:T(2,128)(2,1)S(1)}, bf16[1,64,128]{2,0,1:T(2,128)(2,1)S(1)}, u32[]{:S(2)}, u32[]{:S(2)}) %collective-permute-start) | collective-permute-done | bytes 16416 | tf_op jit(solution)/shard_map/ppermute | solution.py:40
  6.6 2.1 %collective-permute-start.1 = (bf16[2,64,128]{2,0,1:T(2,128)(2,1)S(1)}, bf16[2,64,128]{2,0,1:T(2,128)(2,1)S(1)}, u32[]{:S(2)}, u32[]{:S(2)}) collective-permute-start(bf16[2,64,128]{2,0,1:T(2,128)(2,1)S(1)} %pad_maximum_fusion.5), channel_id=1, source_target_pairs={{0,8},{8,0},{16,24},{24,16},{1,9},{9,1},{17,25},{25,17},{2,10},{10... | collective-permute-start | bytes 98312 | tf_op jit(solution)/shard_map/ppermute | solution.py:40
  8.6 0.9 fusion.51
  9.5 1.1 collective-permute-done.1
  10.8 3.2 %collective-permute-start.2 = (bf16[2,64,128]{2,0,1:T(2,128)(2,1)S(1)}, bf16[2,64,128]{2,0,1:T(2,128)(2,1)S(1)}, u32[]{:S(2)}, u32[]{:S(2)}) collective-permute-start(bf16[2,64,128]{2,0,1:T(2,128)(2,1)S(1)} %convolution_convert_fusion), channel_id=1, source_target_pairs={{0,4},{1,5},{2,6},{3,7},{4,0},{5,1},{6,2},{7,3},{8,12},{9,13},{10,... | collective-permute-start | bytes 98312 | tf_op jit(solution)/shard_map/ppermute | solution.py:40
  14.0 2.0 %collective-permute-done.2 = bf16[2,64,128]{2,0,1:T(2,128)(2,1)S(1)} collective-permute-done((bf16[2,64,128]{2,0,1:T(2,128)(2,1)S(1)}, bf16[2,64,128]{2,0,1:T(2,128)(2,1)S(1)}, u32[]{:S(2)}, u32[]{:S(2)}) %collective-permute-start.2) | collective-permute-done | bytes 32800 | tf_op jit(solution)/shard_map/ppermute | solution.py:40
  16.0 1.9 %collective-permute-start.3 = (bf16[2,128,128]{2,0,1:T(2,128)(2,1)S(1)}, bf16[2,128,128]{2,0,1:T(2,128)(2,1)S(1)}, u32[]{:S(2)}, u32[]{:S(2)}) collective-permute-start(bf16[2,128,128]{2,0,1:T(2,128)(2,1)S(1)} %pad_maximum_fusion.4), channel_id=1, source_target_pairs={{0,2},{1,3},{2,0},{3,1},{4,6},{5,7},{6,4},{7,5},{8,10},{9,11},{10,... | collective-permute-start | bytes 196616 | tf_op jit(solution)/shard_map/ppermute | solution.py:40
  18.6 1.8 %collective-permute-done.3 = bf16[2,128,128]{2,0,1:T(2,128)(2,1)S(1)} collective-permute-done((bf16[2,128,128]{2,0,1:T(2,128)(2,1)S(1)}, bf16[2,128,128]{2,0,1:T(2,128)(2,1)S(1)}, u32[]{:S(2)}, u32[]{:S(2)}) %collective-permute-start.3) | collective-permute-done | bytes 65568 | tf_op jit(solution)/shard_map/ppermute | solution.py:40
  21.3 0.7 reduce.2
  23.2 2.8 %fusion.13 = f32[1280]{0:T(1024)S(1)} fusion(bf16[512,128]{1,0:T(8,128)(2,1)S(1)} %bitcast.113, bf16[512,128]{1,0:T(8,128)(2,1)S(1)} %bitcast.112, bf16[1,1280,1024]{2,1,0:T(8,128)(2,1)} %param.11), kind=kOutput, calls=%fused_computation.19 | convolution fusion | flops 673839872 | bytes 2888704 | tf_op jit(solution)/shard_map/dot_general | solution.py:116
  26.0 0.7 multiply_reduce_fusion.1
  26.8 0.8 fusion.2
  27.6 1.3 %pad_maximum_fusion.11 = f32[2]{0:T(128)S(1)} fusion(f32[1]{0:T(128)} %bitcast.12, f32[1]{0:T(128)} %bitcast.11), kind=kLoop, calls=%fused_computation.106 | loop fusion | flops 2 | bytes 16 | tf_op jit(solution)/shard_map/stack | solution.py:124
  29.6 0.8 collective-permute-done.5
  30.5 1.9 %collective-permute-start.6 = (f32[2,2176]{1,0:T(2,128)S(1)}, f32[2,2176]{1,0:T(2,128)S(1)}, u32[]{:S(2)}, u32[]{:S(2)}) collective-permute-start(f32[2,2176]{1,0:T(2,128)S(1)} %fusion.61), channel_id=1, source_target_pairs={{0,2},{1,3},{2,0},{3,1},{4,6},{5,7},{6,4},{7,5},{8,10},{9,11},{10,... | collective-permute-start | bytes 52232 | tf_op jit(solution)/shard_map/ppermute | solution.py:27
  32.3 1.9 %collective-permute-done.6 = f32[2,2176]{1,0:T(2,128)S(1)} collective-permute-done((f32[2,2176]{1,0:T(2,128)S(1)}, f32[2,2176]{1,0:T(2,128)S(1)}, u32[]{:S(2)}, u32[]{:S(2)}) %collective-permute-start.6) | collective-permute-done | bytes 17440 | tf_op jit(solution)/shard_map/ppermute | solution.py:27
  34.3 3.1 %collective-permute-start.7 = (f32[2,2176]{1,0:T(2,128)S(1)}, f32[2,2176]{1,0:T(2,128)S(1)}, u32[]{:S(2)}, u32[]{:S(2)}) collective-permute-start(f32[2,2176]{1,0:T(2,128)S(1)} %add.142), channel_id=1, source_target_pairs={{0,4},{1,5},{2,6},{3,7},{4,0},{5,1},{6,2},{7,3},{8,12},{9,13},{10,... | collective-permute-start | bytes 52232 | tf_op jit(solution)/shard_map/ppermute | solution.py:27
  37.3 1.7 %collective-permute-done.7 = f32[2,2176]{1,0:T(2,128)S(1)} collective-permute-done((f32[2,2176]{1,0:T(2,128)S(1)}, f32[2,2176]{1,0:T(2,128)S(1)}, u32[]{:S(2)}, u32[]{:S(2)}) %collective-permute-start.7) | collective-permute-done | bytes 17440 | tf_op jit(solution)/shard_map/ppermute | solution.py:27
  39.1 1.7 %fusion.7 = f32[1,256]{1,0:T(1,128)S(1)} fusion(f32[1,256,2048]{2,1,0:T(8,128)S(1)} %copy-done, f32[2,2176]{1,0:T(2,128)S(1)} %add.143), kind=kOutput, calls=%fused_computation.13 | convolution fusion | flops 6291456 | bytes 2106368 | tf_op jit(solution)/shard_map/dot_general | solution.py:134
  40.8 2.9 %collective-permute-start.8 = (f32[256]{0:T(256)S(1)}, f32[256]{0:T(256)S(1)}, u32[]{:S(2)}, u32[]{:S(2)}) collective-permute-start(f32[256]{0:T(256)S(1)} %bitcast.118), channel_id=1, source_target_pairs={{0,4},{1,5},{2,6},{3,7},{4,0},{5,1},{6,2},{7,3},{8,12},{9,13},{10,... | collective-permute-start | bytes 3080 | tf_op jit(solution)/shard_map/ppermute | solution.py:40
  43.8 1.6 %collective-permute-done.8 = f32[256]{0:T(256)S(1)} collective-permute-done((f32[256]{0:T(256)S(1)}, f32[256]{0:T(256)S(1)}, u32[]{:S(2)}, u32[]{:S(2)}) %collective-permute-start.8) | collective-permute-done | bytes 1056 | tf_op jit(solution)/shard_map/ppermute | solution.py:40
  45.3 1.7 %collective-permute-start.9 = (f32[512]{0:T(512)S(1)}, f32[512]{0:T(512)S(1)}, u32[]{:S(2)}, u32[]{:S(2)}) collective-permute-start(f32[512]{0:T(512)S(1)} %pad_maximum_fusion.10), channel_id=1, source_target_pairs={{0,2},{1,3},{2,0},{3,1},{4,6},{5,7},{6,4},{7,5},{8,10},{9,11},{10,... | collective-permute-start | bytes 6152 | tf_op jit(solution)/shard_map/ppermute | solution.py:40
  47.1 1.9 %collective-permute-done.9 = f32[512]{0:T(512)S(1)} collective-permute-done((f32[512]{0:T(512)S(1)}, f32[512]{0:T(512)S(1)}, u32[]{:S(2)}, u32[]{:S(2)}) %collective-permute-start.9) | collective-permute-done | bytes 2080 | tf_op jit(solution)/shard_map/ppermute | solution.py:40
  53.4 4.1 %fusion.4 = f32[1280,2]{0,1:T(2,128)S(1)} fusion(bf16[1,1280,2048]{2,1,0:T(8,128)(2,1)} %param.12, bf16[2048,1]{0,1:T(2,128)(2,1)S(1)} %stack.34, bf16[2048,1]{0,1:T(2,128)(2,1)S(1)} %bitcast.116), kind=kOutput, calls=%fused_computation.12 | convolution fusion | flops 10502144 | bytes 5261312 | tf_op jit(solution)/shard_map/dot_general | solution.py:137
  58.0 0.9 fusion.9
  58.9 0.9 fusion.11
  60.4 0.9 fusion.14
  61.2 1.6 %collective-permute-done.11 = f32[4,64,2,512]{3,1,2,0:T(8,128)S(1)} collective-permute-done((f32[4,64,2,512]{3,1,2,0:T(8,128)S(1)}, f32[4,64,2,512]{3,1,2,0:T(8,128)S(1)}, u32[]{:S(2)}, u32[]{:S(2)}) %collective-permute-start.11) | collective-permute-done | bytes 1048608 | tf_op jit(solution)/shard_map/ppermute | solution.py:66
  63.1 0.9 dynamic-slice_bitcast_fusion
  64.1 0.8 dynamic-slice_bitcast_fusion.1
  64.9 1.7 %collective-permute-start.12 = (f32[2,64,2,512]{3,1,2,0:T(8,128)}, f32[2,64,2,512]{3,1,2,0:T(8,128)}, u32[]{:S(2)}, u32[]{:S(2)}) collective-permute-start(f32[2,64,2,512]{3,1,2,0:T(8,128)} %dynamic-slice_bitcast_fusion.1), channel_id=1, source_target_pairs={{0,2},{1,3},{2,0},{3,1},{4,6},{5,7},{6,4},{7,5},{8,10},{9,11},{10,... | collective-permute-start | bytes 1572872 | tf_op jit(solution)/shard_map/ppermute | solution.py:66
  66.7 1.3 %bitcast_add_fusion.1 = f32[4,64,512]{2,1,0:T(8,128)S(1)} fusion(f32[4,64,512]{2,1,0:T(8,128)} %collective-permute-done.17, f32[4,2,64,512]{3,2,1,0:T(8,128)} %bitcast.111, s32[]{:T(128)S(6)} %select_n.160), kind=kLoop, calls=%fused_computation.38 | loop fusion | flops 131072 | bytes 1572868 | tf_op jit(solution)/shard_map/add | solution.py:66
  68.0 11.5 %collective-permute-done.12 = f32[2,64,2,512]{3,1,2,0:T(8,128)} collective-permute-done((f32[2,64,2,512]{3,1,2,0:T(8,128)}, f32[2,64,2,512]{3,1,2,0:T(8,128)}, u32[]{:S(2)}, u32[]{:S(2)}) %collective-permute-start.12) | collective-permute-done | bytes 524320 | tf_op jit(solution)/shard_map/ppermute | solution.py:66
  79.4 1.9 %bitcast_add_fusion.2 = f32[2,64,2,512]{3,1,2,0:T(8,128)} fusion(f32[2,64,2,512]{3,1,2,0:T(8,128)} %collective-permute-done.12, f32[2,2,64,2,512]{4,2,3,1,0:T(8,128)S(1)} %bitcast.98, s32[]{:T(128)S(6)} %select_n.162), kind=kLoop, calls=%fused_computation.39 | loop fusion | flops 131072 | bytes 1572868 | tf_op jit(solution)/shard_map/add | solution.py:66
  81.4 1.8 %collective-permute-start.18 = (f32[2,64,512]{2,1,0:T(8,128)S(1)}, f32[2,64,512]{2,1,0:T(8,128)S(1)}, u32[]{:S(2)}, u32[]{:S(2)}) collective-permute-start(f32[2,64,512]{2,1,0:T(8,128)S(1)} %dynamic-slice_bitcast_fusion.2), channel_id=1, source_target_pairs={{0,2},{1,3},{2,0},{3,1},{4,6},{5,7},{6,4},{7,5},{8,10},{9,11},{10,... | collective-permute-start | bytes 786440 | tf_op jit(solution)/shard_map/ppermute | solution.py:66
  83.2 1.0 constant_dynamic-slice_fusion.1
  84.1 3.0 %collective-permute-start.13 = (f32[1,64,2,512]{3,1,2,0:T(8,128)S(1)}, f32[1,64,2,512]{3,1,2,0:T(8,128)S(1)}, u32[]{:S(2)}, u32[]{:S(2)}) collective-permute-start(f32[1,64,2,512]{3,1,2,0:T(8,128)S(1)} %constant_dynamic-slice_fusion.1), channel_id=1, source_target_pairs={{0,4},{1,5},{2,6},{3,7},{4,0},{5,1},{6,2},{7,3},{8,12},{9,13},{10,... | collective-permute-start | bytes 786440 | tf_op jit(solution)/shard_map/ppermute | solution.py:66
  93.5 1.0 bitcast_add_fusion.3
  94.5 4.4 %collective-permute-done.13 = f32[1,64,2,512]{3,1,2,0:T(8,128)S(1)} collective-permute-done((f32[1,64,2,512]{3,1,2,0:T(8,128)S(1)}, f32[1,64,2,512]{3,1,2,0:T(8,128)S(1)}, u32[]{:S(2)}, u32[]{:S(2)}) %collective-permute-start.13) | collective-permute-done | bytes 262176 | tf_op jit(solution)/shard_map/ppermute | solution.py:66
  98.9 1.0 dynamic-slice_add_fusion
  100.0 1.5 %collective-permute-start.14 = (f32[64,512]{1,0:T(8,128)S(1)}, f32[64,512]{1,0:T(8,128)S(1)}, u32[]{:S(2)}, u32[]{:S(2)}) collective-permute-start(f32[64,512]{1,0:T(8,128)S(1)} %get-tuple-element.16), channel_id=1, source_target_pairs={{0,8},{8,16},{16,24},{24,0},{1,9},{9,17},{17,25},{25,1},{2,10},{10... | collective-permute-start | bytes 393224 | tf_op jit(solution)/shard_map/ppermute | solution.py:170
  101.6 1.5 %collective-permute-start.15 = (f32[64,512]{1,0:T(8,128)S(1)}, f32[64,512]{1,0:T(8,128)S(1)}, u32[]{:S(2)}, u32[]{:S(2)}) collective-permute-start(f32[64,512]{1,0:T(8,128)S(1)} %get-tuple-element.17), channel_id=1, source_target_pairs={{0,16},{8,24},{16,0},{24,8},{1,17},{9,25},{17,1},{25,9},{2,18},{10... | collective-permute-start | bytes 393224 | tf_op jit(solution)/shard_map/ppermute | solution.py:170
  103.1 1.4 %collective-permute-start.16 = (f32[64,512]{1,0:T(8,128)S(1)}, f32[64,512]{1,0:T(8,128)S(1)}, u32[]{:S(2)}, u32[]{:S(2)}) collective-permute-start(f32[64,512]{1,0:T(8,128)S(1)} %get-tuple-element.18), channel_id=1, source_target_pairs={{0,24},{8,0},{16,8},{24,16},{1,25},{9,1},{17,9},{25,17},{2,26},{10... | collective-permute-start | bytes 393224 | tf_op jit(solution)/shard_map/ppermute | solution.py:170
  104.5 1.7 %collective-permute-done.19 = f32[1,64,512]{2,1,0:T(8,128)S(1)} collective-permute-done((f32[1,64,512]{2,1,0:T(8,128)S(1)}, f32[1,64,512]{2,1,0:T(8,128)S(1)}, u32[]{:S(2)}, u32[]{:S(2)}) %collective-permute-start.19) | collective-permute-done | bytes 131104 | tf_op jit(solution)/shard_map/ppermute | solution.py:66
  107.4 0.7 collective-permute-done.16
  108.1 0.7 fusion.32
  (72 shorter events, 10.4 us)
Async XLA Ops:
  0.6 38.5 %copy-start = (f32[1,256,2048]{2,1,0:T(8,128)S(1)}, f32[1,256,2048]{2,1,0:T(8,128)}, u32[]{:S(2)}) copy-start(f32[1,256,2048]{2,1,0:T(8,128)} %param.18) | copy-start | bytes 6291460
  1.5 5.0 %collective-permute-start = (bf16[1,64,128]{2,0,1:T(2,128)(2,1)S(1)}, bf16[1,64,128]{2,0,1:T(2,128)(2,1)S(1)}, u32[]{:S(2)}, u32[]{:S(2)}) collective-permute-start(bf16[1,64,128]{2,0,1:T(2,128)(2,1)S(1)} %copy.33), channel_id=1, source_target_pairs={{0,16},{8,24},{16,0},{24,8},{1,17},{9,25},{17,1},{25,9},{2,18},{10... | collective-permute-start | bytes 49160 | tf_op jit(solution)/shard_map/ppermute | solution.py:40
  6.6 4.0 %collective-permute-start.1 = (bf16[2,64,128]{2,0,1:T(2,128)(2,1)S(1)}, bf16[2,64,128]{2,0,1:T(2,128)(2,1)S(1)}, u32[]{:S(2)}, u32[]{:S(2)}) collective-permute-start(bf16[2,64,128]{2,0,1:T(2,128)(2,1)S(1)} %pad_maximum_fusion.5), channel_id=1, source_target_pairs={{0,8},{8,0},{16,24},{24,16},{1,9},{9,1},{17,25},{25,17},{2,10},{10... | collective-permute-start | bytes 98312 | tf_op jit(solution)/shard_map/ppermute | solution.py:40
  10.8 5.2 %collective-permute-start.2 = (bf16[2,64,128]{2,0,1:T(2,128)(2,1)S(1)}, bf16[2,64,128]{2,0,1:T(2,128)(2,1)S(1)}, u32[]{:S(2)}, u32[]{:S(2)}) collective-permute-start(bf16[2,64,128]{2,0,1:T(2,128)(2,1)S(1)} %convolution_convert_fusion), channel_id=1, source_target_pairs={{0,4},{1,5},{2,6},{3,7},{4,0},{5,1},{6,2},{7,3},{8,12},{9,13},{10,... | collective-permute-start | bytes 98312 | tf_op jit(solution)/shard_map/ppermute | solution.py:40
  16.0 4.3 %collective-permute-start.3 = (bf16[2,128,128]{2,0,1:T(2,128)(2,1)S(1)}, bf16[2,128,128]{2,0,1:T(2,128)(2,1)S(1)}, u32[]{:S(2)}, u32[]{:S(2)}) collective-permute-start(bf16[2,128,128]{2,0,1:T(2,128)(2,1)S(1)} %pad_maximum_fusion.4), channel_id=1, source_target_pairs={{0,2},{1,3},{2,0},{3,1},{4,6},{5,7},{6,4},{7,5},{8,10},{9,11},{10,... | collective-permute-start | bytes 196616 | tf_op jit(solution)/shard_map/ppermute | solution.py:40
  20.6 1.5 %collective-permute-start.4 = (bf16[2,256,128]{2,0,1:T(2,128)(2,1)S(1)}, bf16[2,256,128]{2,0,1:T(2,128)(2,1)S(1)}, u32[]{:S(2)}, u32[]{:S(2)}) collective-permute-start(bf16[2,256,128]{2,0,1:T(2,128)(2,1)S(1)} %pad_maximum_fusion.1), channel_id=1, source_target_pairs={{0,1},{1,0},{2,3},{3,2},{4,5},{5,4},{6,7},{7,6},{8,9},{9,8},{10,11... | collective-permute-start | bytes 393224 | tf_op jit(solution)/shard_map/ppermute | solution.py:40
  23.2 3.5 %copy-start.5 = (f32[1,1280]{1,0:T(1,128)S(1)}, f32[1,1280]{1,0:T(1,128)}, u32[]{:S(2)}) copy-start(f32[1,1280]{1,0:T(1,128)} %param.17) | copy-start | bytes 15364
  23.2 3.6 %copy-start.1 = (bf16[1,1280,2048]{2,1,0:T(8,128)(2,1)S(1)}, bf16[1,1280,2048]{2,1,0:T(8,128)(2,1)}, u32[]{:S(2)}) copy-start(bf16[1,1280,2048]{2,1,0:T(8,128)(2,1)} %param.12) | copy-start | bytes 15728644
  29.0 1.4 %collective-permute-start.5 = (f32[2,2176]{1,0:T(2,128)S(1)}, f32[2,2176]{1,0:T(2,128)S(1)}, u32[]{:S(2)}, u32[]{:S(2)}) collective-permute-start(f32[2,2176]{1,0:T(2,128)S(1)} %pad_maximum_fusion.6), channel_id=1, source_target_pairs={{0,1},{1,0},{2,3},{3,2},{4,5},{5,4},{6,7},{7,6},{8,9},{9,8},{10,11... | collective-permute-start | bytes 52232 | tf_op jit(solution)/shard_map/ppermute | solution.py:27
  30.5 3.8 %collective-permute-start.6 = (f32[2,2176]{1,0:T(2,128)S(1)}, f32[2,2176]{1,0:T(2,128)S(1)}, u32[]{:S(2)}, u32[]{:S(2)}) collective-permute-start(f32[2,2176]{1,0:T(2,128)S(1)} %fusion.61), channel_id=1, source_target_pairs={{0,2},{1,3},{2,0},{3,1},{4,6},{5,7},{6,4},{7,5},{8,10},{9,11},{10,... | collective-permute-start | bytes 52232 | tf_op jit(solution)/shard_map/ppermute | solution.py:27
  34.3 4.8 %collective-permute-start.7 = (f32[2,2176]{1,0:T(2,128)S(1)}, f32[2,2176]{1,0:T(2,128)S(1)}, u32[]{:S(2)}, u32[]{:S(2)}) collective-permute-start(f32[2,2176]{1,0:T(2,128)S(1)} %add.142), channel_id=1, source_target_pairs={{0,4},{1,5},{2,6},{3,7},{4,0},{5,1},{6,2},{7,3},{8,12},{9,13},{10,... | collective-permute-start | bytes 52232 | tf_op jit(solution)/shard_map/ppermute | solution.py:27
  40.8 4.5 %collective-permute-start.8 = (f32[256]{0:T(256)S(1)}, f32[256]{0:T(256)S(1)}, u32[]{:S(2)}, u32[]{:S(2)}) collective-permute-start(f32[256]{0:T(256)S(1)} %bitcast.118), channel_id=1, source_target_pairs={{0,4},{1,5},{2,6},{3,7},{4,0},{5,1},{6,2},{7,3},{8,12},{9,13},{10,... | collective-permute-start | bytes 3080 | tf_op jit(solution)/shard_map/ppermute | solution.py:40
  45.3 3.6 %collective-permute-start.9 = (f32[512]{0:T(512)S(1)}, f32[512]{0:T(512)S(1)}, u32[]{:S(2)}, u32[]{:S(2)}) collective-permute-start(f32[512]{0:T(512)S(1)} %pad_maximum_fusion.10), channel_id=1, source_target_pairs={{0,2},{1,3},{2,0},{3,1},{4,6},{5,7},{6,4},{7,5},{8,10},{9,11},{10,... | collective-permute-start | bytes 6152 | tf_op jit(solution)/shard_map/ppermute | solution.py:40
  48.9 1.2 %collective-permute-start.10 = (f32[1024]{0:T(1024)S(1)}, f32[1024]{0:T(1024)S(1)}, u32[]{:S(2)}, u32[]{:S(2)}) collective-permute-start(f32[1024]{0:T(1024)S(1)} %pad_maximum_fusion.9), channel_id=1, source_target_pairs={{0,1},{1,0},{2,3},{3,2},{4,5},{5,4},{6,7},{7,6},{8,9},{9,8},{10,11... | collective-permute-start | bytes 12296 | tf_op jit(solution)/shard_map/ppermute | solution.py:40
  53.4 4.2 %copy-start.2 = (bf16[1,1280,1024]{2,1,0:T(8,128)(2,1)S(1)}, bf16[1,1280,1024]{2,1,0:T(8,128)(2,1)}, u32[]{:S(2)}) copy-start(bf16[1,1280,1024]{2,1,0:T(8,128)(2,1)} %param.11) | copy-start | bytes 7864324
  60.1 2.7 %collective-permute-start.11 = (f32[4,64,2,512]{3,1,2,0:T(8,128)S(1)}, f32[4,64,2,512]{3,1,2,0:T(8,128)S(1)}, u32[]{:S(2)}, u32[]{:S(2)}) collective-permute-start(f32[4,64,2,512]{3,1,2,0:T(8,128)S(1)} %bitcast.108), channel_id=1, source_target_pairs={{0,1},{1,0},{2,3},{3,2},{4,5},{5,4},{6,7},{7,6},{8,9},{9,8},{10,11... | collective-permute-start | bytes 3145736 | tf_op jit(solution)/shard_map/ppermute | solution.py:66
  61.2 1.8 %copy-start.4 = (f32[512,512]{1,0:T(8,128)}, f32[512,512]{1,0:T(8,128)S(1)}, u32[]{:S(2)}) copy-start(f32[512,512]{1,0:T(8,128)S(1)} %fusion.14) | copy-start | bytes 3145732
  63.9 2.7 %collective-permute-start.17 = (f32[4,64,512]{2,1,0:T(8,128)}, f32[4,64,512]{2,1,0:T(8,128)}, u32[]{:S(2)}, u32[]{:S(2)}) collective-permute-start(f32[4,64,512]{2,1,0:T(8,128)} %dynamic-slice_bitcast_fusion), channel_id=1, source_target_pairs={{0,1},{1,0},{2,3},{3,2},{4,5},{5,4},{6,7},{7,6},{8,9},{9,8},{10,11... | collective-permute-start | bytes 1572872 | tf_op jit(solution)/shard_map/ppermute | solution.py:66
  64.1 23.0 %copy-start.6 = (s32[1,2]{1,0:T(1,128)S(1)}, s32[1,2]{1,0:T(1,128)}, u32[]{:S(2)}) copy-start(s32[1,2]{1,0:T(1,128)} %param.15) | copy-start | bytes 28
  64.9 14.5 %collective-permute-start.12 = (f32[2,64,2,512]{3,1,2,0:T(8,128)}, f32[2,64,2,512]{3,1,2,0:T(8,128)}, u32[]{:S(2)}, u32[]{:S(2)}) collective-permute-start(f32[2,64,2,512]{3,1,2,0:T(8,128)} %dynamic-slice_bitcast_fusion.1), channel_id=1, source_target_pairs={{0,2},{1,3},{2,0},{3,1},{4,6},{5,7},{6,4},{7,5},{8,10},{9,11},{10,... | collective-permute-start | bytes 1572872 | tf_op jit(solution)/shard_map/ppermute | solution.py:66
  68.0 13.4 %copy-start.3 = (f32[4,64,512]{2,1,0:T(8,128)}, f32[4,64,512]{2,1,0:T(8,128)S(1)}, u32[]{:S(2)}) copy-start(f32[4,64,512]{2,1,0:T(8,128)S(1)} %bitcast_add_fusion.1) | copy-start | bytes 1572868
  81.4 12.2 %collective-permute-start.18 = (f32[2,64,512]{2,1,0:T(8,128)S(1)}, f32[2,64,512]{2,1,0:T(8,128)S(1)}, u32[]{:S(2)}, u32[]{:S(2)}) collective-permute-start(f32[2,64,512]{2,1,0:T(8,128)S(1)} %dynamic-slice_bitcast_fusion.2), channel_id=1, source_target_pairs={{0,2},{1,3},{2,0},{3,1},{4,6},{5,7},{6,4},{7,5},{8,10},{9,11},{10,... | collective-permute-start | bytes 786440 | tf_op jit(solution)/shard_map/ppermute | solution.py:66
  84.1 14.7 %collective-permute-start.13 = (f32[1,64,2,512]{3,1,2,0:T(8,128)S(1)}, f32[1,64,2,512]{3,1,2,0:T(8,128)S(1)}, u32[]{:S(2)}, u32[]{:S(2)}) collective-permute-start(f32[1,64,2,512]{3,1,2,0:T(8,128)S(1)} %constant_dynamic-slice_fusion.1), channel_id=1, source_target_pairs={{0,4},{1,5},{2,6},{3,7},{4,0},{5,1},{6,2},{7,3},{8,12},{9,13},{10,... | collective-permute-start | bytes 786440 | tf_op jit(solution)/shard_map/ppermute | solution.py:66
  99.9 6.4 %collective-permute-start.19 = (f32[1,64,512]{2,1,0:T(8,128)S(1)}, f32[1,64,512]{2,1,0:T(8,128)S(1)}, u32[]{:S(2)}, u32[]{:S(2)}) collective-permute-start(f32[1,64,512]{2,1,0:T(8,128)S(1)} %constant_dynamic-slice_fusion), channel_id=1, source_target_pairs={{0,4},{1,5},{2,6},{3,7},{4,0},{5,1},{6,2},{7,3},{8,12},{9,13},{10,... | collective-permute-start | bytes 393224 | tf_op jit(solution)/shard_map/ppermute | solution.py:66
  100.0 6.9 %collective-permute-start.14 = (f32[64,512]{1,0:T(8,128)S(1)}, f32[64,512]{1,0:T(8,128)S(1)}, u32[]{:S(2)}, u32[]{:S(2)}) collective-permute-start(f32[64,512]{1,0:T(8,128)S(1)} %get-tuple-element.16), channel_id=1, source_target_pairs={{0,8},{8,16},{16,24},{24,0},{1,9},{9,17},{17,25},{25,1},{2,10},{10... | collective-permute-start | bytes 393224 | tf_op jit(solution)/shard_map/ppermute | solution.py:170
  101.6 5.8 %collective-permute-start.15 = (f32[64,512]{1,0:T(8,128)S(1)}, f32[64,512]{1,0:T(8,128)S(1)}, u32[]{:S(2)}, u32[]{:S(2)}) collective-permute-start(f32[64,512]{1,0:T(8,128)S(1)} %get-tuple-element.17), channel_id=1, source_target_pairs={{0,16},{8,24},{16,0},{24,8},{1,17},{9,25},{17,1},{25,9},{2,18},{10... | collective-permute-start | bytes 393224 | tf_op jit(solution)/shard_map/ppermute | solution.py:170
  103.1 5.0 %collective-permute-start.16 = (f32[64,512]{1,0:T(8,128)S(1)}, f32[64,512]{1,0:T(8,128)S(1)}, u32[]{:S(2)}, u32[]{:S(2)}) collective-permute-start(f32[64,512]{1,0:T(8,128)S(1)} %get-tuple-element.18), channel_id=1, source_target_pairs={{0,24},{8,0},{16,8},{24,16},{1,25},{9,1},{17,9},{25,17},{2,26},{10... | collective-permute-start | bytes 393224 | tf_op jit(solution)/shard_map/ppermute | solution.py:170

commit v10 on v9

--- a/solution.py
+++ b/solution.py
@@ -66,22 +66,19 @@
     return keep + lax.ppermute(send, axis, [(i, i ^ (1 << bit)) for i in range(size)])
 
 
-def paired_scatter(lead, follow, axis):
+def chained_scatter(arrays, axis):
     size = lax.axis_size(axis)
     if size & (size - 1):
-        return (
-            lax.psum_scatter(lead, axis, scatter_dimension=0, tiled=True),
-            lax.psum_scatter(follow, axis, scatter_dimension=0, tiled=True),
-        )
-    lead = scatter_chunks(lead, axis)
-    follow = scatter_chunks(follow, axis)
+        return [lax.psum_scatter(a, axis, scatter_dimension=0, tiled=True) for a in arrays]
+    arrays = [scatter_chunks(a, axis) for a in arrays]
     bit = 0
     while (1 << bit) < size:
-        lead = scatter_step(lead, axis, bit)
-        follow, _ = lax.optimization_barrier((follow, lead))
-        follow = scatter_step(follow, axis, bit)
+        for index in range(len(arrays)):
+            if index:
+                arrays[index], _ = lax.optimization_barrier((arrays[index], arrays[index - 1]))
+            arrays[index] = scatter_step(arrays[index], axis, bit)
         bit += 1
-    return lead[0], follow[0]
+    return [a[0] for a in arrays]
 
 
 def shards(basis_values, aux_values, factors, frag_slot, dimer_pairs, counts, weights, metric_inv):
@@ -150,11 +147,9 @@
     first_first = contract(left_first, basis_rows[:, :frag_basis])
     first_second = contract(left_first, basis_rows[:, frag_basis:])
     second_second = contract(left_second, basis_rows[:, frag_basis:])
-    diagonal, own_cross = paired_scatter(
-        jnp.stack([first_first, second_second], axis=1), first_second, "grid"
+    own_first, own_second, own_cross = chained_scatter(
+        [first_first, second_second, first_second], "grid"
     )
-    own_first = diagonal[:, 0]
-    own_second = diagonal[:, 1]
     groups = lax.axis_size("dimer")
     me = lax.axis_index("dimer")
     zero = jnp.zeros((), jnp.float32)

time: 109 us -> 113 us (1.037)
  starting transfers between devices: 31.8 us -> 35.7 us
  other arithmetic: 14.3 us -> 12.2 us
  matrix products: 12.3 us -> 14 us
    ppermute x6 -> x9, starting transfers between devices: 6.94 us -> 11.6 us  [scatter_step(): lax.ppermute(send, axis, [(i, i ^ 1 << bit) for i in range(size)])]
    add x6 -> x8, other arithmetic: 6.05 us -> 2.26 us  [scatter_step(): keep + lax.ppermute(send, axis, [(i, i ^ 1 << bit) for i in range(size)])]
    ppermute x3, waiting for transfers between devices: 1.12 us -> 3.9 us  [shards(): lax.ppermute(sent, 'dimer', [(i, (i + shift) % groups) for i in range(gro...]
    convert_element_type x1, other arithmetic: 0.49 us -> 2.38 us  [shards(): weighted_basis = (basis_rows * potential[:, None]).astype(jnp.bfloat16)]
    dot_general x3, matrix products: 2.62 us -> 4.47 us  [contract(): lax.dot_general(left_side, right_side, numbers, preferred_element_type=jn...]
    ppermute x6 -> x9, waiting for transfers between devices: 19.8 us -> 18.2 us  [scatter_step(): lax.ppermute(send, axis, [(i, i ^ 1 << bit) for i in range(size)])]
    squeeze x5 -> x9, local copies, waits for them, and re-layouts: 2.71 us -> 1.03 us  [scatter_step(): send = lax.dynamic_index_in_dim(pairs, 1 - mine, axis=1, keepdims=False)]
  transfers between devices with their start and end apart: 20 -> 23, of which waited for: 17 -> 18; matrix products, arithmetic and copies ran while one was open for 9% -> 8% of each run, Pallas kernels for 0% -> 0%
where the time goes in v10:
time: 113 us; the launch traced here: 112 us
  waiting for transfers between devices  36.6 us (32%)
  starting transfers between devices  35.7 us (32%)
  matrix products  14 us (12%)
  other arithmetic  12.2 us (11%)
  between operations  8.81 us (8%)
  local copies, waits for them, and re-layouts  5.01 us (4%)
    ppermute x9, waiting for transfers between devices, scatter_step(): lax.ppermute(send, axis, [(i, i ^ 1 << bit) for i in range(size)])  18.2 us
    ppermute x8, starting transfers between devices, xor_gather(): other = lax.ppermute(value, axis, [(i, i ^ 1 << bit) for i in range(size)])  14.9 us
    ppermute x9, starting transfers between devices, scatter_step(): lax.ppermute(send, axis, [(i, i ^ 1 << bit) for i in range(size)])  11.6 us
    ppermute x8, waiting for transfers between devices, xor_gather(): other = lax.ppermute(value, axis, [(i, i ^ 1 << bit) for i in range(size)])  10.1 us
    ppermute x3, starting transfers between devices, xor_sum(): lax.ppermute(value, axis, [(i, i ^ step) for i in range(size)])  5.49 us
    ppermute x3, waiting for transfers between devices, xor_sum(): lax.ppermute(value, axis, [(i, i ^ step) for i in range(size)])  4.52 us
    dot_general x3, matrix products, contract(): lax.dot_general(left_side, right_side, numbers, preferred_element_type=jn...  4.47 us
    dot_general x1, matrix products, shards(): jnp.dot(aux_block, jnp.stack([coef_high, coef_low], axis=1), preferred_el...  3.94 us
  transfers between devices with their start and end apart: 23, of which 18 were waited for; matrix products, arithmetic and copies ran while one was open for 8% of the time, Pallas kernels for 0%

profile of v10, /device:TPU:0, one launch (start us, length us, event | category | flops | bytes accessed | tf_op | source)
XLA Modules:
  0.0 112.3 jit_solution(68246648823379747)
XLA Ops:
  0.6 0.9 copy.33
  1.5 3.1 %collective-permute-start = (bf16[1,64,128]{2,0,1:T(2,128)(2,1)S(1)}, bf16[1,64,128]{2,0,1:T(2,128)(2,1)S(1)}, u32[]{:S(2)}, u32[]{:S(2)}) collective-permute-start(bf16[1,64,128]{2,0,1:T(2,128)(2,1)S(1)} %copy.33), channel_id=1, source_target_pairs={{0,16},{8,24},{16,0},{24,8},{1,17},{9,25},{17,1},{25,9},{2,18},{10... | collective-permute-start | bytes 49160 | tf_op jit(solution)/shard_map/ppermute | solution.py:40
  5.3 1.2 %collective-permute-done = bf16[1,64,128]{2,0,1:T(2,128)(2,1)S(1)} collective-permute-done((bf16[1,64,128]{2,0,1:T(2,128)(2,1)S(1)}, bf16[1,64,128]{2,0,1:T(2,128)(2,1)S(1)}, u32[]{:S(2)}, u32[]{:S(2)}) %collective-permute-start) | collective-permute-done | bytes 16416 | tf_op jit(solution)/shard_map/ppermute | solution.py:40
  6.6 2.1 %collective-permute-start.1 = (bf16[2,64,128]{2,0,1:T(2,128)(2,1)S(1)}, bf16[2,64,128]{2,0,1:T(2,128)(2,1)S(1)}, u32[]{:S(2)}, u32[]{:S(2)}) collective-permute-start(bf16[2,64,128]{2,0,1:T(2,128)(2,1)S(1)} %pad_maximum_fusion.5), channel_id=1, source_target_pairs={{0,8},{8,0},{16,24},{24,16},{1,9},{9,1},{17,25},{25,17},{2,10},{10... | collective-permute-start | bytes 98312 | tf_op jit(solution)/shard_map/ppermute | solution.py:40
  8.6 0.9 fusion.49
  9.5 1.1 collective-permute-done.1
  10.8 3.2 %collective-permute-start.2 = (bf16[2,64,128]{2,0,1:T(2,128)(2,1)S(1)}, bf16[2,64,128]{2,0,1:T(2,128)(2,1)S(1)}, u32[]{:S(2)}, u32[]{:S(2)}) collective-permute-start(bf16[2,64,128]{2,0,1:T(2,128)(2,1)S(1)} %convolution_convert_fusion), channel_id=1, source_target_pairs={{0,4},{1,5},{2,6},{3,7},{4,0},{5,1},{6,2},{7,3},{8,12},{9,13},{10,... | collective-permute-start | bytes 98312 | tf_op jit(solution)/shard_map/ppermute | solution.py:40
  14.0 2.0 %collective-permute-done.2 = bf16[2,64,128]{2,0,1:T(2,128)(2,1)S(1)} collective-permute-done((bf16[2,64,128]{2,0,1:T(2,128)(2,1)S(1)}, bf16[2,64,128]{2,0,1:T(2,128)(2,1)S(1)}, u32[]{:S(2)}, u32[]{:S(2)}) %collective-permute-start.2) | collective-permute-done | bytes 32800 | tf_op jit(solution)/shard_map/ppermute | solution.py:40
  16.0 1.9 %collective-permute-start.3 = (bf16[2,128,128]{2,0,1:T(2,128)(2,1)S(1)}, bf16[2,128,128]{2,0,1:T(2,128)(2,1)S(1)}, u32[]{:S(2)}, u32[]{:S(2)}) collective-permute-start(bf16[2,128,128]{2,0,1:T(2,128)(2,1)S(1)} %pad_maximum_fusion.4), channel_id=1, source_target_pairs={{0,2},{1,3},{2,0},{3,1},{4,6},{5,7},{6,4},{7,5},{8,10},{9,11},{10,... | collective-permute-start | bytes 196616 | tf_op jit(solution)/shard_map/ppermute | solution.py:40
  18.6 1.8 %collective-permute-done.3 = bf16[2,128,128]{2,0,1:T(2,128)(2,1)S(1)} collective-permute-done((bf16[2,128,128]{2,0,1:T(2,128)(2,1)S(1)}, bf16[2,128,128]{2,0,1:T(2,128)(2,1)S(1)}, u32[]{:S(2)}, u32[]{:S(2)}) %collective-permute-start.3) | collective-permute-done | bytes 65568 | tf_op jit(solution)/shard_map/ppermute | solution.py:40
  21.3 0.7 reduce.2
  23.2 2.8 %fusion.13 = f32[1280]{0:T(1024)S(1)} fusion(bf16[512,128]{1,0:T(8,128)(2,1)S(1)} %bitcast.126, bf16[512,128]{1,0:T(8,128)(2,1)S(1)} %bitcast.125, bf16[1,1280,1024]{2,1,0:T(8,128)(2,1)} %param.11), kind=kOutput, calls=%fused_computation.15 | convolution fusion | flops 673839872 | bytes 2888704 | tf_op jit(solution)/shard_map/dot_general | solution.py:113
  26.0 0.7 multiply_reduce_fusion.1
  26.8 0.8 fusion.2
  27.6 1.4 %pad_maximum_fusion.11 = f32[2]{0:T(128)S(1)} fusion(f32[1]{0:T(128)} %bitcast.12, f32[1]{0:T(128)} %bitcast.11), kind=kLoop, calls=%fused_computation.106 | loop fusion | flops 2 | bytes 16 | tf_op jit(solution)/shard_map/stack | solution.py:121
  29.7 0.8 collective-permute-done.5
  30.5 1.9 %collective-permute-start.6 = (f32[2,2176]{1,0:T(2,128)S(1)}, f32[2,2176]{1,0:T(2,128)S(1)}, u32[]{:S(2)}, u32[]{:S(2)}) collective-permute-start(f32[2,2176]{1,0:T(2,128)S(1)} %fusion.59), channel_id=1, source_target_pairs={{0,2},{1,3},{2,0},{3,1},{4,6},{5,7},{6,4},{7,5},{8,10},{9,11},{10,... | collective-permute-start | bytes 52232 | tf_op jit(solution)/shard_map/ppermute | solution.py:27
  32.4 1.9 %collective-permute-done.6 = f32[2,2176]{1,0:T(2,128)S(1)} collective-permute-done((f32[2,2176]{1,0:T(2,128)S(1)}, f32[2,2176]{1,0:T(2,128)S(1)}, u32[]{:S(2)}, u32[]{:S(2)}) %collective-permute-start.6) | collective-permute-done | bytes 17440 | tf_op jit(solution)/shard_map/ppermute | solution.py:27
  34.4 3.1 %collective-permute-start.7 = (f32[2,2176]{1,0:T(2,128)S(1)}, f32[2,2176]{1,0:T(2,128)S(1)}, u32[]{:S(2)}, u32[]{:S(2)}) collective-permute-start(f32[2,2176]{1,0:T(2,128)S(1)} %add.154), channel_id=1, source_target_pairs={{0,4},{1,5},{2,6},{3,7},{4,0},{5,1},{6,2},{7,3},{8,12},{9,13},{10,... | collective-permute-start | bytes 52232 | tf_op jit(solution)/shard_map/ppermute | solution.py:27
  37.4 1.7 %collective-permute-done.7 = f32[2,2176]{1,0:T(2,128)S(1)} collective-permute-done((f32[2,2176]{1,0:T(2,128)S(1)}, f32[2,2176]{1,0:T(2,128)S(1)}, u32[]{:S(2)}, u32[]{:S(2)}) %collective-permute-start.7) | collective-permute-done | bytes 17440 | tf_op jit(solution)/shard_map/ppermute | solution.py:27
  39.2 1.7 %fusion.7 = f32[1,256]{1,0:T(1,128)S(1)} fusion(f32[1,256,2048]{2,1,0:T(8,128)S(1)} %copy-done, f32[2,2176]{1,0:T(2,128)S(1)} %add.155), kind=kOutput, calls=%fused_computation.9 | convolution fusion | flops 6291456 | bytes 2106368 | tf_op jit(solution)/shard_map/dot_general | solution.py:131
  40.9 2.9 %collective-permute-start.8 = (f32[256]{0:T(256)S(1)}, f32[256]{0:T(256)S(1)}, u32[]{:S(2)}, u32[]{:S(2)}) collective-permute-start(f32[256]{0:T(256)S(1)} %bitcast.131), channel_id=1, source_target_pairs={{0,4},{1,5},{2,6},{3,7},{4,0},{5,1},{6,2},{7,3},{8,12},{9,13},{10,... | collective-permute-start | bytes 3080 | tf_op jit(solution)/shard_map/ppermute | solution.py:40
  43.8 1.6 %collective-permute-done.8 = f32[256]{0:T(256)S(1)} collective-permute-done((f32[256]{0:T(256)S(1)}, f32[256]{0:T(256)S(1)}, u32[]{:S(2)}, u32[]{:S(2)}) %collective-permute-start.8) | collective-permute-done | bytes 1056 | tf_op jit(solution)/shard_map/ppermute | solution.py:40
  45.4 1.7 %collective-permute-start.9 = (f32[512]{0:T(512)S(1)}, f32[512]{0:T(512)S(1)}, u32[]{:S(2)}, u32[]{:S(2)}) collective-permute-start(f32[512]{0:T(512)S(1)} %pad_maximum_fusion.10), channel_id=1, source_target_pairs={{0,2},{1,3},{2,0},{3,1},{4,6},{5,7},{6,4},{7,5},{8,10},{9,11},{10,... | collective-permute-start | bytes 6152 | tf_op jit(solution)/shard_map/ppermute | solution.py:40
  47.1 1.9 %collective-permute-done.9 = f32[512]{0:T(512)S(1)} collective-permute-done((f32[512]{0:T(512)S(1)}, f32[512]{0:T(512)S(1)}, u32[]{:S(2)}, u32[]{:S(2)}) %collective-permute-start.9) | collective-permute-done | bytes 2080 | tf_op jit(solution)/shard_map/ppermute | solution.py:40
  51.5 3.9 %fusion.4 = f32[1280,2]{0,1:T(2,128)S(1)} fusion(bf16[1,1280,2048]{2,1,0:T(8,128)(2,1)} %param.12, bf16[2048,1]{0,1:T(2,128)(2,1)S(1)} %stack.25, bf16[2048,1]{0,1:T(2,128)(2,1)S(1)} %bitcast.129), kind=kOutput, calls=%fused_computation.8 | convolution fusion | flops 10502144 | bytes 5261312 | tf_op jit(solution)/shard_map/dot_general | solution.py:134
  57.5 2.4 %multiply_convert_fusion = bf16[1280,1024]{1,0:T(8,128)(2,1)S(1)} fusion(f32[1280]{0:T(1024)S(1)} %fusion.44, bf16[1,1280,1024]{2,1,0:T(8,128)(2,1)} %param.11), kind=kLoop, calls=%fused_computation.6 | loop fusion | flops 3932160 | bytes 5248000 | tf_op jit(solution)/shard_map/convert_element_type | solution.py:141
  60.0 0.9 fusion.11
  61.4 0.8 dynamic-slice_bitcast_fusion.2
  68.1 2.7 %fusion.9 = f32[512,512]{1,0:T(8,128)S(1)} fusion(bf16[1280,1024]{1,0:T(8,128)(2,1)} %copy-done.4, bf16[1280,1024]{1,0:T(8,128)(2,1)} %bitcast.109), kind=kOutput, calls=%fused_computation.11 | convolution fusion | flops 671088640 | bytes 3670016 | tf_op jit(solution)/shard_map/dot_general | solution.py:18
  70.9 1.3 %bitcast_add_fusion.2 = f32[4,64,512]{2,1,0:T(8,128)S(1)} fusion(f32[4,64,512]{2,1,0:T(8,128)} %collective-permute-done.11, f32[4,2,64,512]{3,2,1,0:T(8,128)S(1)} %bitcast.120, s32[]{:T(128)S(6)} %select_n.163), kind=kLoop, calls=%fused_computation.32 | loop fusion | flops 131072 | bytes 1572868 | tf_op jit(solution)/shard_map/add | solution.py:66
  72.2 1.8 %collective-permute-start.12 = (f32[2,64,512]{2,1,0:T(8,128)S(1)}, f32[2,64,512]{2,1,0:T(8,128)S(1)}, u32[]{:S(2)}, u32[]{:S(2)}) collective-permute-start(f32[2,64,512]{2,1,0:T(8,128)S(1)} %dynamic-slice_bitcast_fusion.5), channel_id=1, source_target_pairs={{0,2},{1,3},{2,0},{3,1},{4,6},{5,7},{6,4},{7,5},{8,10},{9,11},{10,... | collective-permute-start | bytes 786440 | tf_op jit(solution)/shard_map/ppermute | solution.py:66
  74.2 0.9 fusion.14
  75.0 5.8 %collective-permute-done.12 = f32[2,64,512]{2,1,0:T(8,128)S(1)} collective-permute-done((f32[2,64,512]{2,1,0:T(8,128)S(1)}, f32[2,64,512]{2,1,0:T(8,128)S(1)}, u32[]{:S(2)}, u32[]{:S(2)}) %collective-permute-start.12) | collective-permute-done | bytes 262176 | tf_op jit(solution)/shard_map/ppermute | solution.py:66
  80.9 3.0 %collective-permute-start.13 = (f32[1,64,512]{2,1,0:T(8,128)S(1)}, f32[1,64,512]{2,1,0:T(8,128)S(1)}, u32[]{:S(2)}, u32[]{:S(2)}) collective-permute-start(f32[1,64,512]{2,1,0:T(8,128)S(1)} %constant_dynamic-slice_fusion.2), channel_id=1, source_target_pairs={{0,4},{1,5},{2,6},{3,7},{4,0},{5,1},{6,2},{7,3},{8,12},{9,13},{10,... | collective-permute-start | bytes 393224 | tf_op jit(solution)/shard_map/ppermute | solution.py:66
  84.0 1.8 %collective-permute-start.15 = (f32[2,64,512]{2,1,0:T(8,128)S(1)}, f32[2,64,512]{2,1,0:T(8,128)S(1)}, u32[]{:S(2)}, u32[]{:S(2)}) collective-permute-start(f32[2,64,512]{2,1,0:T(8,128)S(1)} %dynamic-slice_bitcast_fusion.4), channel_id=1, source_target_pairs={{0,2},{1,3},{2,0},{3,1},{4,6},{5,7},{6,4},{7,5},{8,10},{9,11},{10,... | collective-permute-start | bytes 786440 | tf_op jit(solution)/shard_map/ppermute | solution.py:66
  85.9 4.0 %collective-permute-done.13 = f32[1,64,512]{2,1,0:T(8,128)S(1)} collective-permute-done((f32[1,64,512]{2,1,0:T(8,128)S(1)}, f32[1,64,512]{2,1,0:T(8,128)S(1)}, u32[]{:S(2)}, u32[]{:S(2)}) %collective-permute-start.13) | collective-permute-done | bytes 131104 | tf_op jit(solution)/shard_map/ppermute | solution.py:66
  90.0 3.1 %collective-permute-done.15 = f32[2,64,512]{2,1,0:T(8,128)S(1)} collective-permute-done((f32[2,64,512]{2,1,0:T(8,128)S(1)}, f32[2,64,512]{2,1,0:T(8,128)S(1)}, u32[]{:S(2)}, u32[]{:S(2)}) %collective-permute-start.15) | collective-permute-done | bytes 262176 | tf_op jit(solution)/shard_map/ppermute | solution.py:66
  93.1 1.4 %collective-permute-start.16 = (f32[1,64,512]{2,1,0:T(8,128)S(1)}, f32[1,64,512]{2,1,0:T(8,128)S(1)}, u32[]{:S(2)}, u32[]{:S(2)}) collective-permute-start(f32[1,64,512]{2,1,0:T(8,128)S(1)} %constant_dynamic-slice_fusion.1), channel_id=1, source_target_pairs={{0,4},{1,5},{2,6},{3,7},{4,0},{5,1},{6,2},{7,3},{8,12},{9,13},{10,... | collective-permute-start | bytes 393224 | tf_op jit(solution)/shard_map/ppermute | solution.py:66
  94.7 2.0 %collective-permute-start.21 = (f32[2,64,512]{2,1,0:T(8,128)S(1)}, f32[2,64,512]{2,1,0:T(8,128)S(1)}, u32[]{:S(2)}, u32[]{:S(2)}) collective-permute-start(f32[2,64,512]{2,1,0:T(8,128)S(1)} %dynamic-slice_bitcast_fusion.3), channel_id=1, source_target_pairs={{0,2},{1,3},{2,0},{3,1},{4,6},{5,7},{6,4},{7,5},{8,10},{9,11},{10,... | collective-permute-start | bytes 786440 | tf_op jit(solution)/shard_map/ppermute | solution.py:66
  96.6 3.8 %collective-permute-done.16 = f32[1,64,512]{2,1,0:T(8,128)S(1)} collective-permute-done((f32[1,64,512]{2,1,0:T(8,128)S(1)}, f32[1,64,512]{2,1,0:T(8,128)S(1)}, u32[]{:S(2)}, u32[]{:S(2)}) %collective-permute-start.16) | collective-permute-done | bytes 131104 | tf_op jit(solution)/shard_map/ppermute | solution.py:66
  100.5 2.6 %collective-permute-start.19 = (f32[64,512]{1,0:T(8,128)S(1)}, f32[64,512]{1,0:T(8,128)S(1)}, u32[]{:S(2)}, u32[]{:S(2)}) collective-permute-start(f32[64,512]{1,0:T(8,128)S(1)} %get-tuple-element.23), channel_id=1, source_target_pairs={{0,24},{8,0},{16,8},{24,16},{1,25},{9,1},{17,9},{25,17},{2,26},{10... | collective-permute-start | bytes 393224 | tf_op jit(solution)/shard_map/ppermute | solution.py:165
  104.3 1.3 %collective-permute-start.22 = (f32[1,64,512]{2,1,0:T(8,128)S(1)}, f32[1,64,512]{2,1,0:T(8,128)S(1)}, u32[]{:S(2)}, u32[]{:S(2)}) collective-permute-start(f32[1,64,512]{2,1,0:T(8,128)S(1)} %constant_dynamic-slice_fusion), channel_id=1, source_target_pairs={{0,4},{1,5},{2,6},{3,7},{4,0},{5,1},{6,2},{7,3},{8,12},{9,13},{10,... | collective-permute-start | bytes 393224 | tf_op jit(solution)/shard_map/ppermute | solution.py:66
  105.6 0.9 collective-permute-done.19
  106.6 1.6 %collective-permute-done.18 = f32[64,512]{1,0:T(8,128)S(1)} collective-permute-done((f32[64,512]{1,0:T(8,128)S(1)}, f32[64,512]{1,0:T(8,128)S(1)}, u32[]{:S(2)}, u32[]{:S(2)}) %collective-permute-start.18) | collective-permute-done | bytes 131104 | tf_op jit(solution)/shard_map/ppermute | solution.py:165
  108.1 1.4 %collective-permute-done.17 = f32[64,512]{1,0:T(8,128)S(1)} collective-permute-done((f32[64,512]{1,0:T(8,128)S(1)}, f32[64,512]{1,0:T(8,128)S(1)}, u32[]{:S(2)}, u32[]{:S(2)}) %collective-permute-start.17) | collective-permute-done | bytes 131104 | tf_op jit(solution)/shard_map/ppermute | solution.py:165
  109.5 0.7 fusion.30
  110.2 1.4 %collective-permute-done.22 = f32[1,64,512]{2,1,0:T(8,128)S(1)} collective-permute-done((f32[1,64,512]{2,1,0:T(8,128)S(1)}, f32[1,64,512]{2,1,0:T(8,128)S(1)}, u32[]{:S(2)}, u32[]{:S(2)}) %collective-permute-start.22) | collective-permute-done | bytes 131104 | tf_op jit(solution)/shard_map/ppermute | solution.py:66
  (85 shorter events, 10.3 us)
Async XLA Ops:
  0.6 38.5 %copy-start = (f32[1,256,2048]{2,1,0:T(8,128)S(1)}, f32[1,256,2048]{2,1,0:T(8,128)}, u32[]{:S(2)}) copy-start(f32[1,256,2048]{2,1,0:T(8,128)} %param.18) | copy-start | bytes 6291460
  1.5 5.0 %collective-permute-start = (bf16[1,64,128]{2,0,1:T(2,128)(2,1)S(1)}, bf16[1,64,128]{2,0,1:T(2,128)(2,1)S(1)}, u32[]{:S(2)}, u32[]{:S(2)}) collective-permute-start(bf16[1,64,128]{2,0,1:T(2,128)(2,1)S(1)} %copy.33), channel_id=1, source_target_pairs={{0,16},{8,24},{16,0},{24,8},{1,17},{9,25},{17,1},{25,9},{2,18},{10... | collective-permute-start | bytes 49160 | tf_op jit(solution)/shard_map/ppermute | solution.py:40
  6.6 4.0 %collective-permute-start.1 = (bf16[2,64,128]{2,0,1:T(2,128)(2,1)S(1)}, bf16[2,64,128]{2,0,1:T(2,128)(2,1)S(1)}, u32[]{:S(2)}, u32[]{:S(2)}) collective-permute-start(bf16[2,64,128]{2,0,1:T(2,128)(2,1)S(1)} %pad_maximum_fusion.5), channel_id=1, source_target_pairs={{0,8},{8,0},{16,24},{24,16},{1,9},{9,1},{17,25},{25,17},{2,10},{10... | collective-permute-start | bytes 98312 | tf_op jit(solution)/shard_map/ppermute | solution.py:40
  10.8 5.2 %collective-permute-start.2 = (bf16[2,64,128]{2,0,1:T(2,128)(2,1)S(1)}, bf16[2,64,128]{2,0,1:T(2,128)(2,1)S(1)}, u32[]{:S(2)}, u32[]{:S(2)}) collective-permute-start(bf16[2,64,128]{2,0,1:T(2,128)(2,1)S(1)} %convolution_convert_fusion), channel_id=1, source_target_pairs={{0,4},{1,5},{2,6},{3,7},{4,0},{5,1},{6,2},{7,3},{8,12},{9,13},{10,... | collective-permute-start | bytes 98312 | tf_op jit(solution)/shard_map/ppermute | solution.py:40
  16.0 4.3 %collective-permute-start.3 = (bf16[2,128,128]{2,0,1:T(2,128)(2,1)S(1)}, bf16[2,128,128]{2,0,1:T(2,128)(2,1)S(1)}, u32[]{:S(2)}, u32[]{:S(2)}) collective-permute-start(bf16[2,128,128]{2,0,1:T(2,128)(2,1)S(1)} %pad_maximum_fusion.4), channel_id=1, source_target_pairs={{0,2},{1,3},{2,0},{3,1},{4,6},{5,7},{6,4},{7,5},{8,10},{9,11},{10,... | collective-permute-start | bytes 196616 | tf_op jit(solution)/shard_map/ppermute | solution.py:40
  20.6 1.5 %collective-permute-start.4 = (bf16[2,256,128]{2,0,1:T(2,128)(2,1)S(1)}, bf16[2,256,128]{2,0,1:T(2,128)(2,1)S(1)}, u32[]{:S(2)}, u32[]{:S(2)}) collective-permute-start(bf16[2,256,128]{2,0,1:T(2,128)(2,1)S(1)} %pad_maximum_fusion.1), channel_id=1, source_target_pairs={{0,1},{1,0},{2,3},{3,2},{4,5},{5,4},{6,7},{7,6},{8,9},{9,8},{10,11... | collective-permute-start | bytes 393224 | tf_op jit(solution)/shard_map/ppermute | solution.py:40
  23.2 3.5 %copy-start.6 = (f32[1,1280]{1,0:T(1,128)S(1)}, f32[1,1280]{1,0:T(1,128)}, u32[]{:S(2)}) copy-start(f32[1,1280]{1,0:T(1,128)} %param.17) | copy-start | bytes 15364
  23.2 3.6 %copy-start.1 = (bf16[1,1280,2048]{2,1,0:T(8,128)(2,1)S(1)}, bf16[1,1280,2048]{2,1,0:T(8,128)(2,1)}, u32[]{:S(2)}) copy-start(bf16[1,1280,2048]{2,1,0:T(8,128)(2,1)} %param.12) | copy-start | bytes 15728644
  29.1 1.4 %collective-permute-start.5 = (f32[2,2176]{1,0:T(2,128)S(1)}, f32[2,2176]{1,0:T(2,128)S(1)}, u32[]{:S(2)}, u32[]{:S(2)}) collective-permute-start(f32[2,2176]{1,0:T(2,128)S(1)} %pad_maximum_fusion.6), channel_id=1, source_target_pairs={{0,1},{1,0},{2,3},{3,2},{4,5},{5,4},{6,7},{7,6},{8,9},{9,8},{10,11... | collective-permute-start | bytes 52232 | tf_op jit(solution)/shard_map/ppermute | solution.py:27
  30.5 3.8 %collective-permute-start.6 = (f32[2,2176]{1,0:T(2,128)S(1)}, f32[2,2176]{1,0:T(2,128)S(1)}, u32[]{:S(2)}, u32[]{:S(2)}) collective-permute-start(f32[2,2176]{1,0:T(2,128)S(1)} %fusion.59), channel_id=1, source_target_pairs={{0,2},{1,3},{2,0},{3,1},{4,6},{5,7},{6,4},{7,5},{8,10},{9,11},{10,... | collective-permute-start | bytes 52232 | tf_op jit(solution)/shard_map/ppermute | solution.py:27
  34.4 4.8 %collective-permute-start.7 = (f32[2,2176]{1,0:T(2,128)S(1)}, f32[2,2176]{1,0:T(2,128)S(1)}, u32[]{:S(2)}, u32[]{:S(2)}) collective-permute-start(f32[2,2176]{1,0:T(2,128)S(1)} %add.154), channel_id=1, source_target_pairs={{0,4},{1,5},{2,6},{3,7},{4,0},{5,1},{6,2},{7,3},{8,12},{9,13},{10,... | collective-permute-start | bytes 52232 | tf_op jit(solution)/shard_map/ppermute | solution.py:27
  40.9 4.5 %collective-permute-start.8 = (f32[256]{0:T(256)S(1)}, f32[256]{0:T(256)S(1)}, u32[]{:S(2)}, u32[]{:S(2)}) collective-permute-start(f32[256]{0:T(256)S(1)} %bitcast.131), channel_id=1, source_target_pairs={{0,4},{1,5},{2,6},{3,7},{4,0},{5,1},{6,2},{7,3},{8,12},{9,13},{10,... | collective-permute-start | bytes 3080 | tf_op jit(solution)/shard_map/ppermute | solution.py:40
  45.4 3.6 %collective-permute-start.9 = (f32[512]{0:T(512)S(1)}, f32[512]{0:T(512)S(1)}, u32[]{:S(2)}, u32[]{:S(2)}) collective-permute-start(f32[512]{0:T(512)S(1)} %pad_maximum_fusion.10), channel_id=1, source_target_pairs={{0,2},{1,3},{2,0},{3,1},{4,6},{5,7},{6,4},{7,5},{8,10},{9,11},{10,... | collective-permute-start | bytes 6152 | tf_op jit(solution)/shard_map/ppermute | solution.py:40
  49.0 1.2 %collective-permute-start.10 = (f32[1024]{0:T(1024)S(1)}, f32[1024]{0:T(1024)S(1)}, u32[]{:S(2)}, u32[]{:S(2)}) collective-permute-start(f32[1024]{0:T(1024)S(1)} %pad_maximum_fusion.9), channel_id=1, source_target_pairs={{0,1},{1,0},{2,3},{3,2},{4,5},{5,4},{6,7},{7,6},{8,9},{9,8},{10,11... | collective-permute-start | bytes 12296 | tf_op jit(solution)/shard_map/ppermute | solution.py:40
  57.5 2.5 %copy-start.2 = (bf16[1,1280,1024]{2,1,0:T(8,128)(2,1)S(1)}, bf16[1,1280,1024]{2,1,0:T(8,128)(2,1)}, u32[]{:S(2)}) copy-start(bf16[1,1280,1024]{2,1,0:T(8,128)(2,1)} %param.11) | copy-start | bytes 7864324
  59.9 1.5 %copy-start.4 = (bf16[1280,1024]{1,0:T(8,128)(2,1)}, bf16[1280,1024]{1,0:T(8,128)(2,1)S(1)}, u32[]{:S(2)}) copy-start(bf16[1280,1024]{1,0:T(8,128)(2,1)S(1)} %multiply_convert_fusion) | copy-start | bytes 7864324
  60.0 2.4 %copy-start.7 = (s32[1,2]{1,0:T(1,128)S(1)}, s32[1,2]{1,0:T(1,128)}, u32[]{:S(2)}) copy-start(s32[1,2]{1,0:T(1,128)} %param.15) | copy-start | bytes 28
  62.2 8.7 %collective-permute-start.11 = (f32[4,64,512]{2,1,0:T(8,128)}, f32[4,64,512]{2,1,0:T(8,128)}, u32[]{:S(2)}, u32[]{:S(2)}) collective-permute-start(f32[4,64,512]{2,1,0:T(8,128)} %dynamic-slice_bitcast_fusion.2), channel_id=1, source_target_pairs={{0,1},{1,0},{2,3},{3,2},{4,5},{5,4},{6,7},{7,6},{8,9},{9,8},{10,11... | collective-permute-start | bytes 1572872 | tf_op jit(solution)/shard_map/ppermute | solution.py:66
  68.1 6.0 %copy-start.5 = (bf16[1280,1024]{1,0:T(8,128)(2,1)S(1)}, bf16[1280,1024]{1,0:T(8,128)(2,1)}, u32[]{:S(2)}) copy-start(bf16[1280,1024]{1,0:T(8,128)(2,1)} %copy-done.4) | copy-start | bytes 7864324
  70.9 3.3 %copy-start.3 = (bf16[1,1280,1024]{2,1,0:T(8,128)(2,1)S(1)}, bf16[1,1280,1024]{2,1,0:T(8,128)(2,1)}, u32[]{:S(2)}) copy-start(bf16[1,1280,1024]{2,1,0:T(8,128)(2,1)} %param.11) | copy-start | bytes 7864324
  72.2 8.6 %collective-permute-start.12 = (f32[2,64,512]{2,1,0:T(8,128)S(1)}, f32[2,64,512]{2,1,0:T(8,128)S(1)}, u32[]{:S(2)}, u32[]{:S(2)}) collective-permute-start(f32[2,64,512]{2,1,0:T(8,128)S(1)} %dynamic-slice_bitcast_fusion.5), channel_id=1, source_target_pairs={{0,2},{1,3},{2,0},{3,1},{4,6},{5,7},{6,4},{7,5},{8,10},{9,11},{10,... | collective-permute-start | bytes 786440 | tf_op jit(solution)/shard_map/ppermute | solution.py:66
  74.0 9.8 %collective-permute-start.14 = (f32[4,64,512]{2,1,0:T(8,128)S(1)}, f32[4,64,512]{2,1,0:T(8,128)S(1)}, u32[]{:S(2)}, u32[]{:S(2)}) collective-permute-start(f32[4,64,512]{2,1,0:T(8,128)S(1)} %dynamic-slice_bitcast_fusion.1), channel_id=1, source_target_pairs={{0,1},{1,0},{2,3},{3,2},{4,5},{5,4},{6,7},{7,6},{8,9},{9,8},{10,11... | collective-permute-start | bytes 1572872 | tf_op jit(solution)/shard_map/ppermute | solution.py:66
  80.9 9.0 %collective-permute-start.13 = (f32[1,64,512]{2,1,0:T(8,128)S(1)}, f32[1,64,512]{2,1,0:T(8,128)S(1)}, u32[]{:S(2)}, u32[]{:S(2)}) collective-permute-start(f32[1,64,512]{2,1,0:T(8,128)S(1)} %constant_dynamic-slice_fusion.2), channel_id=1, source_target_pairs={{0,4},{1,5},{2,6},{3,7},{4,0},{5,1},{6,2},{7,3},{8,12},{9,13},{10,... | collective-permute-start | bytes 393224 | tf_op jit(solution)/shard_map/ppermute | solution.py:66
  84.0 9.0 %collective-permute-start.15 = (f32[2,64,512]{2,1,0:T(8,128)S(1)}, f32[2,64,512]{2,1,0:T(8,128)S(1)}, u32[]{:S(2)}, u32[]{:S(2)}) collective-permute-start(f32[2,64,512]{2,1,0:T(8,128)S(1)} %dynamic-slice_bitcast_fusion.4), channel_id=1, source_target_pairs={{0,2},{1,3},{2,0},{3,1},{4,6},{5,7},{6,4},{7,5},{8,10},{9,11},{10,... | collective-permute-start | bytes 786440 | tf_op jit(solution)/shard_map/ppermute | solution.py:66
  85.8 8.7 %collective-permute-start.20 = (f32[4,64,512]{2,1,0:T(8,128)S(1)}, f32[4,64,512]{2,1,0:T(8,128)S(1)}, u32[]{:S(2)}, u32[]{:S(2)}) collective-permute-start(f32[4,64,512]{2,1,0:T(8,128)S(1)} %dynamic-slice_bitcast_fusion), channel_id=1, source_target_pairs={{0,1},{1,0},{2,3},{3,2},{4,5},{5,4},{6,7},{7,6},{8,9},{9,8},{10,11... | collective-permute-start | bytes 1572872 | tf_op jit(solution)/shard_map/ppermute | solution.py:66
  93.1 7.4 %collective-permute-start.16 = (f32[1,64,512]{2,1,0:T(8,128)S(1)}, f32[1,64,512]{2,1,0:T(8,128)S(1)}, u32[]{:S(2)}, u32[]{:S(2)}) collective-permute-start(f32[1,64,512]{2,1,0:T(8,128)S(1)} %constant_dynamic-slice_fusion.1), channel_id=1, source_target_pairs={{0,4},{1,5},{2,6},{3,7},{4,0},{5,1},{6,2},{7,3},{8,12},{9,13},{10,... | collective-permute-start | bytes 393224 | tf_op jit(solution)/shard_map/ppermute | solution.py:66
  94.7 9.5 %collective-permute-start.21 = (f32[2,64,512]{2,1,0:T(8,128)S(1)}, f32[2,64,512]{2,1,0:T(8,128)S(1)}, u32[]{:S(2)}, u32[]{:S(2)}) collective-permute-start(f32[2,64,512]{2,1,0:T(8,128)S(1)} %dynamic-slice_bitcast_fusion.3), channel_id=1, source_target_pairs={{0,2},{1,3},{2,0},{3,1},{4,6},{5,7},{6,4},{7,5},{8,10},{9,11},{10,... | collective-permute-start | bytes 786440 | tf_op jit(solution)/shard_map/ppermute | solution.py:66
  100.5 6.0 %collective-permute-start.19 = (f32[64,512]{1,0:T(8,128)S(1)}, f32[64,512]{1,0:T(8,128)S(1)}, u32[]{:S(2)}, u32[]{:S(2)}) collective-permute-start(f32[64,512]{1,0:T(8,128)S(1)} %get-tuple-element.23), channel_id=1, source_target_pairs={{0,24},{8,0},{16,8},{24,16},{1,25},{9,1},{17,9},{25,17},{2,26},{10... | collective-permute-start | bytes 393224 | tf_op jit(solution)/shard_map/ppermute | solution.py:165
  103.1 5.0 %collective-permute-start.18 = (f32[64,512]{1,0:T(8,128)S(1)}, f32[64,512]{1,0:T(8,128)S(1)}, u32[]{:S(2)}, u32[]{:S(2)}) collective-permute-start(f32[64,512]{1,0:T(8,128)S(1)} %get-tuple-element.22), channel_id=1, source_target_pairs={{0,16},{8,24},{16,0},{24,8},{1,17},{9,25},{17,1},{25,9},{2,18},{10... | collective-permute-start | bytes 393224 | tf_op jit(solution)/shard_map/ppermute | solution.py:165
  103.6 5.9 %collective-permute-start.17 = (f32[64,512]{1,0:T(8,128)S(1)}, f32[64,512]{1,0:T(8,128)S(1)}, u32[]{:S(2)}, u32[]{:S(2)}) collective-permute-start(f32[64,512]{1,0:T(8,128)S(1)} %get-tuple-element.16), channel_id=1, source_target_pairs={{0,8},{8,16},{16,24},{24,0},{1,9},{9,17},{17,25},{25,1},{2,10},{10... | collective-permute-start | bytes 393224 | tf_op jit(solution)/shard_map/ppermute | solution.py:165
  104.3 7.3 %collective-permute-start.22 = (f32[1,64,512]{2,1,0:T(8,128)S(1)}, f32[1,64,512]{2,1,0:T(8,128)S(1)}, u32[]{:S(2)}, u32[]{:S(2)}) collective-permute-start(f32[1,64,512]{2,1,0:T(8,128)S(1)} %constant_dynamic-slice_fusion), channel_id=1, source_target_pairs={{0,4},{1,5},{2,6},{3,7},{4,0},{5,1},{6,2},{7,3},{8,12},{9,13},{10,... | collective-permute-start | bytes 393224 | tf_op jit(solution)/shard_map/ppermute | solution.py:66

commit v11 on v9

--- a/solution.py
+++ b/solution.py
@@ -1,6 +1,7 @@
 import jax
 import jax.numpy as jnp
 from jax import lax
+from jax.experimental import pallas as pl
 from jax.sharding import PartitionSpec as P
 
 exchange_coeff = 0.9847450218426964
@@ -84,6 +85,31 @@
     return lead[0], follow[0]
 
 
+def coulomb_kernel(aux_ref, coef_ref, out_ref):
+    out_ref[...] = jnp.dot(aux_ref[...], coef_ref[...], preferred_element_type=jnp.float32)
+
+
+def coulomb_columns(aux_block, coef_columns):
+    points, naux = aux_block.shape
+    width = coef_columns.shape[1]
+    tile = 256 if points % 256 == 0 else points
+    return pl.pallas_call(
+        coulomb_kernel,
+        grid=(points // tile,),
+        in_specs=[
+            pl.BlockSpec((tile, naux), lambda i: (i, 0)),
+            pl.BlockSpec((naux, width), lambda i: (0, 0)),
+        ],
+        out_specs=pl.BlockSpec((tile, width), lambda i: (i, 0)),
+        out_shape=jax.ShapeDtypeStruct((points, width), jnp.float32),
+        cost_estimate=pl.CostEstimate(
+            flops=2 * points * naux * width,
+            bytes_accessed=points * naux * 2 + naux * width * 2 + points * width * 4,
+            transcendentals=0,
+        ),
+    )(aux_block, coef_columns)
+
+
 def shards(basis_values, aux_values, factors, frag_slot, dimer_pairs, counts, weights, metric_inv):
     highest = lax.Precision.HIGHEST
     basis_rows = basis_values[0]
@@ -134,9 +160,13 @@
     coef_rows = jnp.dot(metric_inv[0], fitted, precision=highest)
     coefficients = in_order(*xor_gather(coef_rows, "grid", 0), 0)
     coef_high, coef_low = split_rows(coefficients)
-    coulomb_parts = jnp.dot(
-        aux_block, jnp.stack([coef_high, coef_low], axis=1), preferred_element_type=jnp.float32
-    )
+    first_two = lax.broadcasted_iota(jnp.int32, (naux, 128), 1)
+    coef_columns = jnp.where(
+        first_two == 0,
+        coef_high[:, None],
+        jnp.where(first_two == 1, coef_low[:, None], jnp.zeros((), jnp.bfloat16)),
+    )
+    coulomb_parts = coulomb_columns(aux_block, coef_columns)
     coulomb = coulomb_parts[:, 0] + coulomb_parts[:, 1]
     potential_total = jnp.dot(coefficients, weight_projection, precision=highest) + exchange_total
     average = potential_total / weight_sum

time: 109 us -> 116 us (1.064)
  Pallas kernels: 0 us -> 5.92 us
  other arithmetic: 14.3 us -> 19.4 us
  matrix products: 12.3 us -> 8.17 us
    pallas_call x0 -> x1, Pallas kernels: none -> 5.92 us  [coulomb_columns(): pl.pallas_call(coulomb_kernel, grid=(points // tile,), in_specs=[pl.Block...]
    dot_general x1 -> x0, matrix products: 4.09 us -> none  [shards(): jnp.dot(aux_block, jnp.stack([coef_high, coef_low], axis=1), preferred_el...]
    convert_element_type x1, other arithmetic: 0.49 us -> 2.38 us  [shards(): weighted_basis = (basis_rows * potential[:, None]).astype(jnp.bfloat16)]
    mul x1, other arithmetic: 0.04 us -> 1.92 us  [shards(): potential = live_weight * (coulomb + exchange - average)]
    select_n x0 -> x1, other arithmetic: none -> 1.42 us  [shards(): jnp.where(first_two == 0, coef_high[:, None], jnp.where(first_two == 1, c...]
where the time goes in v11:
time: 116 us
  waiting for transfers between devices  35.3 us (30%)
  starting transfers between devices  31.8 us (27%)
  other arithmetic  19.4 us (17%)
  between operations  8.66 us (7%)
  matrix products  8.17 us (7%)
  local copies, waits for them, and re-layouts  6.47 us (6%)
  Pallas kernels  5.92 us (5%)
    ppermute x6, waiting for transfers between devices, scatter_step(): lax.ppermute(send, axis, [(i, i ^ 1 << bit) for i in range(size)])  19.8 us
    ppermute x8, starting transfers between devices, xor_gather(): other = lax.ppermute(value, axis, [(i, i ^ 1 << bit) for i in range(size)])  14.9 us
    ppermute x8, waiting for transfers between devices, xor_gather(): other = lax.ppermute(value, axis, [(i, i ^ 1 << bit) for i in range(size)])  9.85 us
    ppermute x6, starting transfers between devices, scatter_step(): lax.ppermute(send, axis, [(i, i ^ 1 << bit) for i in range(size)])  6.95 us
    add x6, other arithmetic, scatter_step(): keep + lax.ppermute(send, axis, [(i, i ^ 1 << bit) for i in range(size)])  6.05 us
    pallas_call x1, Pallas kernels, coulomb_columns(): pl.pallas_call(coulomb_kernel, grid=(points // tile,), in_specs=[pl.Block...  5.92 us
    ppermute x3, starting transfers between devices, xor_sum(): lax.ppermute(value, axis, [(i, i ^ step) for i in range(size)])  5.49 us
    ppermute x3, waiting for transfers between devices, xor_sum(): lax.ppermute(value, axis, [(i, i ^ step) for i in range(size)])  4.52 us
  transfers between devices with their start and end apart: 20, of which 17 were waited for; matrix products, arithmetic and copies ran while one was open for 9% of the time, Pallas kernels for 0%

profile of v11, /device:TPU:0, one launch (start us, length us, event | category | flops | bytes accessed | tf_op | source)
XLA Modules:
  0.0 115.7 jit_solution(13306091835933343075)
XLA Ops:
  0.6 0.9 copy.38
  1.5 3.1 %collective-permute-start = (bf16[1,64,128]{2,0,1:T(2,128)(2,1)S(1)}, bf16[1,64,128]{2,0,1:T(2,128)(2,1)S(1)}, u32[]{:S(2)}, u32[]{:S(2)}) collective-permute-start(bf16[1,64,128]{2,0,1:T(2,128)(2,1)S(1)} %copy.38), channel_id=1, source_target_pairs={{0,16},{8,24},{16,0},{24,8},{1,17},{9,25},{17,1},{25,9},{2,18},{10... | collective-permute-start | bytes 49160 | tf_op jit(solution)/shard_map/ppermute | solution.py:41
  5.3 1.2 %collective-permute-done = bf16[1,64,128]{2,0,1:T(2,128)(2,1)S(1)} collective-permute-done((bf16[1,64,128]{2,0,1:T(2,128)(2,1)S(1)}, bf16[1,64,128]{2,0,1:T(2,128)(2,1)S(1)}, u32[]{:S(2)}, u32[]{:S(2)}) %collective-permute-start) | collective-permute-done | bytes 16416 | tf_op jit(solution)/shard_map/ppermute | solution.py:41
  6.6 2.1 %collective-permute-start.1 = (bf16[2,64,128]{2,0,1:T(2,128)(2,1)S(1)}, bf16[2,64,128]{2,0,1:T(2,128)(2,1)S(1)}, u32[]{:S(2)}, u32[]{:S(2)}) collective-permute-start(bf16[2,64,128]{2,0,1:T(2,128)(2,1)S(1)} %pad_maximum_fusion.5), channel_id=1, source_target_pairs={{0,8},{8,0},{16,24},{24,16},{1,9},{9,1},{17,25},{25,17},{2,10},{10... | collective-permute-start | bytes 98312 | tf_op jit(solution)/shard_map/ppermute | solution.py:41
  8.6 0.9 fusion.42
  9.5 1.1 collective-permute-done.1
  10.8 3.2 %collective-permute-start.2 = (bf16[2,64,128]{2,0,1:T(2,128)(2,1)S(1)}, bf16[2,64,128]{2,0,1:T(2,128)(2,1)S(1)}, u32[]{:S(2)}, u32[]{:S(2)}) collective-permute-start(bf16[2,64,128]{2,0,1:T(2,128)(2,1)S(1)} %convolution_convert_fusion), channel_id=1, source_target_pairs={{0,4},{1,5},{2,6},{3,7},{4,0},{5,1},{6,2},{7,3},{8,12},{9,13},{10,... | collective-permute-start | bytes 98312 | tf_op jit(solution)/shard_map/ppermute | solution.py:41
  14.0 2.0 %collective-permute-done.2 = bf16[2,64,128]{2,0,1:T(2,128)(2,1)S(1)} collective-permute-done((bf16[2,64,128]{2,0,1:T(2,128)(2,1)S(1)}, bf16[2,64,128]{2,0,1:T(2,128)(2,1)S(1)}, u32[]{:S(2)}, u32[]{:S(2)}) %collective-permute-start.2) | collective-permute-done | bytes 32800 | tf_op jit(solution)/shard_map/ppermute | solution.py:41
  16.0 1.9 %collective-permute-start.3 = (bf16[2,128,128]{2,0,1:T(2,128)(2,1)S(1)}, bf16[2,128,128]{2,0,1:T(2,128)(2,1)S(1)}, u32[]{:S(2)}, u32[]{:S(2)}) collective-permute-start(bf16[2,128,128]{2,0,1:T(2,128)(2,1)S(1)} %pad_maximum_fusion.4), channel_id=1, source_target_pairs={{0,2},{1,3},{2,0},{3,1},{4,6},{5,7},{6,4},{7,5},{8,10},{9,11},{10,... | collective-permute-start | bytes 196616 | tf_op jit(solution)/shard_map/ppermute | solution.py:41
  18.6 1.8 %collective-permute-done.3 = bf16[2,128,128]{2,0,1:T(2,128)(2,1)S(1)} collective-permute-done((bf16[2,128,128]{2,0,1:T(2,128)(2,1)S(1)}, bf16[2,128,128]{2,0,1:T(2,128)(2,1)S(1)}, u32[]{:S(2)}, u32[]{:S(2)}) %collective-permute-start.3) | collective-permute-done | bytes 65568 | tf_op jit(solution)/shard_map/ppermute | solution.py:41
  21.3 0.7 reduce.2
  23.2 2.8 %fusion.6 = f32[1280]{0:T(1024)S(1)} fusion(bf16[512,128]{1,0:T(8,128)(2,1)S(1)} %bitcast.100, bf16[512,128]{1,0:T(8,128)(2,1)S(1)} %bitcast.99, bf16[1,1280,1024]{2,1,0:T(8,128)(2,1)} %param.11), kind=kOutput, calls=%fused_computation.14 | convolution fusion | flops 673839872 | bytes 2888704 | tf_op jit(solution)/shard_map/dot_general | solution.py:142
  26.8 0.8 fusion.33
  27.6 1.4 %pad_maximum_fusion.11 = f32[2]{0:T(128)S(1)} fusion(f32[1]{0:T(128)} %bitcast.12, f32[1]{0:T(128)} %bitcast.11), kind=kLoop, calls=%fused_computation.99 | loop fusion | flops 2 | bytes 16 | tf_op jit(solution)/shard_map/stack | solution.py:150
  29.6 0.8 collective-permute-done.5
  30.4 1.9 %collective-permute-start.6 = (f32[2,2176]{1,0:T(2,128)S(1)}, f32[2,2176]{1,0:T(2,128)S(1)}, u32[]{:S(2)}, u32[]{:S(2)}) collective-permute-start(f32[2,2176]{1,0:T(2,128)S(1)} %fusion.52), channel_id=1, source_target_pairs={{0,2},{1,3},{2,0},{3,1},{4,6},{5,7},{6,4},{7,5},{8,10},{9,11},{10,... | collective-permute-start | bytes 52232 | tf_op jit(solution)/shard_map/ppermute | solution.py:28
  32.3 1.9 %collective-permute-done.6 = f32[2,2176]{1,0:T(2,128)S(1)} collective-permute-done((f32[2,2176]{1,0:T(2,128)S(1)}, f32[2,2176]{1,0:T(2,128)S(1)}, u32[]{:S(2)}, u32[]{:S(2)}) %collective-permute-start.6) | collective-permute-done | bytes 17440 | tf_op jit(solution)/shard_map/ppermute | solution.py:28
  34.3 3.1 %collective-permute-start.7 = (f32[2,2176]{1,0:T(2,128)S(1)}, f32[2,2176]{1,0:T(2,128)S(1)}, u32[]{:S(2)}, u32[]{:S(2)}) collective-permute-start(f32[2,2176]{1,0:T(2,128)S(1)} %add.142), channel_id=1, source_target_pairs={{0,4},{1,5},{2,6},{3,7},{4,0},{5,1},{6,2},{7,3},{8,12},{9,13},{10,... | collective-permute-start | bytes 52232 | tf_op jit(solution)/shard_map/ppermute | solution.py:28
  37.3 1.7 %collective-permute-done.7 = f32[2,2176]{1,0:T(2,128)S(1)} collective-permute-done((f32[2,2176]{1,0:T(2,128)S(1)}, f32[2,2176]{1,0:T(2,128)S(1)}, u32[]{:S(2)}, u32[]{:S(2)}) %collective-permute-start.7) | collective-permute-done | bytes 17440 | tf_op jit(solution)/shard_map/ppermute | solution.py:28
  39.1 1.7 %fusion = f32[1,256]{1,0:T(1,128)S(1)} fusion(f32[1,256,2048]{2,1,0:T(8,128)S(1)} %copy-done, f32[2,2176]{1,0:T(2,128)S(1)} %add.143), kind=kOutput, calls=%fused_computation.8 | convolution fusion | flops 6291456 | bytes 2106368 | tf_op jit(solution)/shard_map/dot_general | solution.py:160
  40.8 2.9 %collective-permute-start.8 = (f32[256]{0:T(256)S(1)}, f32[256]{0:T(256)S(1)}, u32[]{:S(2)}, u32[]{:S(2)}) collective-permute-start(f32[256]{0:T(256)S(1)} %bitcast.105), channel_id=1, source_target_pairs={{0,4},{1,5},{2,6},{3,7},{4,0},{5,1},{6,2},{7,3},{8,12},{9,13},{10,... | collective-permute-start | bytes 3080 | tf_op jit(solution)/shard_map/ppermute | solution.py:41
  43.7 1.6 %collective-permute-done.8 = f32[256]{0:T(256)S(1)} collective-permute-done((f32[256]{0:T(256)S(1)}, f32[256]{0:T(256)S(1)}, u32[]{:S(2)}, u32[]{:S(2)}) %collective-permute-start.8) | collective-permute-done | bytes 1056 | tf_op jit(solution)/shard_map/ppermute | solution.py:41
  45.3 1.7 %collective-permute-start.9 = (f32[512]{0:T(512)S(1)}, f32[512]{0:T(512)S(1)}, u32[]{:S(2)}, u32[]{:S(2)}) collective-permute-start(f32[512]{0:T(512)S(1)} %pad_maximum_fusion.10), channel_id=1, source_target_pairs={{0,2},{1,3},{2,0},{3,1},{4,6},{5,7},{6,4},{7,5},{8,10},{9,11},{10,... | collective-permute-start | bytes 6152 | tf_op jit(solution)/shard_map/ppermute | solution.py:41
  47.3 1.6 %collective-permute-done.9 = f32[512]{0:T(512)S(1)} collective-permute-done((f32[512]{0:T(512)S(1)}, f32[512]{0:T(512)S(1)}, u32[]{:S(2)}, u32[]{:S(2)}) %collective-permute-start.9) | collective-permute-done | bytes 2080 | tf_op jit(solution)/shard_map/ppermute | solution.py:41
  53.2 1.4 %select_select_fusion.coef_ref = bf16[2048,128]{1,0:T(8,128)(2,1)} fusion(pred[128]{0:T(512)(128)(4,1)S(1)} %get-tuple-element.29, pred[128]{0:T(512)(128)(4,1)S(1)} %get-tuple-element.30, bf16[2048]{0:T(1024)(128)(2,1)S(1)} %get-tuple-element.24, bf16[2048]{0:T(1024)(128)(2,1)S(1)} %convert_element_type.37), kind=kLoop, calls=%fused_computation.43 | loop fusion | flops 524288 | bytes 532736 | tf_op jit(solution)/shard_map/jit(_where)/select_n | solution.py:164
  54.6 5.9 %shard_map.122 = f32[1280,128]{1,0:T(8,128)} custom-call(bf16[1280,2048]{1,0:T(8,128)(2,1)} %bitcast.83, bf16[2048,128]{1,0:T(8,128)(2,1)} %select_select_fusion.coef_ref), custom_call_target="tpu_custom_call" | custom-call | flops 671088640 | bytes 6422528 | tf_op jit(solution)/shard_map/pallas_call | solution.py:96
  60.5 1.9 %fusion.19 = f32[1280]{0:T(1024)S(1)} fusion(f32[1280,128]{1,0:T(8,128)} %shard_map.122, f32[1280]{0:T(1024)S(1)} %get-tuple-element.25, f32[1280,1]{1,0:T(8,128)S(1)} %copy.35, f32[]{:T(128)S(6)} %div.14, s32[]{:T(128)} %bitcast.80), kind=kLoop, calls=%fused_computation.33 | loop fusion | flops 7680 | bytes 25608 | tf_op jit(solution)/shard_map/mul | solution.py:173
  62.5 2.4 %multiply_convert_fusion = bf16[1280,1024]{1,0:T(8,128)(2,1)S(1)} fusion(f32[1280]{0:T(1024)S(1)} %fusion.19, bf16[1,1280,1024]{2,1,0:T(8,128)(2,1)} %param.11), kind=kLoop, calls=%fused_computation.2 | loop fusion | flops 3932160 | bytes 5248000 | tf_op jit(solution)/shard_map/convert_element_type | solution.py:174
  65.0 0.9 fusion.2
  65.9 0.9 fusion.4
  67.3 0.9 fusion.7
  68.2 1.6 %collective-permute-done.11 = f32[4,64,2,512]{3,1,2,0:T(8,128)S(1)} collective-permute-done((f32[4,64,2,512]{3,1,2,0:T(8,128)S(1)}, f32[4,64,2,512]{3,1,2,0:T(8,128)S(1)}, u32[]{:S(2)}, u32[]{:S(2)}) %collective-permute-start.11) | collective-permute-done | bytes 1048608 | tf_op jit(solution)/shard_map/ppermute | solution.py:67
  70.0 0.9 dynamic-slice_bitcast_fusion
  71.0 0.9 dynamic-slice_bitcast_fusion.1
  71.9 1.7 %collective-permute-start.12 = (f32[2,64,2,512]{3,1,2,0:T(8,128)}, f32[2,64,2,512]{3,1,2,0:T(8,128)}, u32[]{:S(2)}, u32[]{:S(2)}) collective-permute-start(f32[2,64,2,512]{3,1,2,0:T(8,128)} %dynamic-slice_bitcast_fusion.1), channel_id=1, source_target_pairs={{0,2},{1,3},{2,0},{3,1},{4,6},{5,7},{6,4},{7,5},{8,10},{9,11},{10,... | collective-permute-start | bytes 1572872 | tf_op jit(solution)/shard_map/ppermute | solution.py:67
  73.6 1.3 %bitcast_add_fusion.1 = f32[4,64,512]{2,1,0:T(8,128)S(1)} fusion(f32[4,64,512]{2,1,0:T(8,128)} %collective-permute-done.17, f32[4,2,64,512]{3,2,1,0:T(8,128)} %bitcast.98, s32[]{:T(128)S(6)} %select_n.166), kind=kLoop, calls=%fused_computation.39 | loop fusion | flops 131072 | bytes 1572868 | tf_op jit(solution)/shard_map/add | solution.py:67
  74.9 11.5 %collective-permute-done.12 = f32[2,64,2,512]{3,1,2,0:T(8,128)} collective-permute-done((f32[2,64,2,512]{3,1,2,0:T(8,128)}, f32[2,64,2,512]{3,1,2,0:T(8,128)}, u32[]{:S(2)}, u32[]{:S(2)}) %collective-permute-start.12) | collective-permute-done | bytes 524320 | tf_op jit(solution)/shard_map/ppermute | solution.py:67
  86.4 1.9 %bitcast_add_fusion.2 = f32[2,64,2,512]{3,1,2,0:T(8,128)} fusion(f32[2,64,2,512]{3,1,2,0:T(8,128)} %collective-permute-done.12, f32[2,2,64,2,512]{4,2,3,1,0:T(8,128)S(1)} %bitcast.85, s32[]{:T(128)S(6)} %select_n.168), kind=kLoop, calls=%fused_computation.40 | loop fusion | flops 131072 | bytes 1572868 | tf_op jit(solution)/shard_map/add | solution.py:67
  88.3 1.8 %collective-permute-start.18 = (f32[2,64,512]{2,1,0:T(8,128)S(1)}, f32[2,64,512]{2,1,0:T(8,128)S(1)}, u32[]{:S(2)}, u32[]{:S(2)}) collective-permute-start(f32[2,64,512]{2,1,0:T(8,128)S(1)} %dynamic-slice_bitcast_fusion.2), channel_id=1, source_target_pairs={{0,2},{1,3},{2,0},{3,1},{4,6},{5,7},{6,4},{7,5},{8,10},{9,11},{10,... | collective-permute-start | bytes 786440 | tf_op jit(solution)/shard_map/ppermute | solution.py:67
  90.1 1.0 constant_dynamic-slice_fusion.1
  91.1 3.0 %collective-permute-start.13 = (f32[1,64,2,512]{3,1,2,0:T(8,128)S(1)}, f32[1,64,2,512]{3,1,2,0:T(8,128)S(1)}, u32[]{:S(2)}, u32[]{:S(2)}) collective-permute-start(f32[1,64,2,512]{3,1,2,0:T(8,128)S(1)} %constant_dynamic-slice_fusion.1), channel_id=1, source_target_pairs={{0,4},{1,5},{2,6},{3,7},{4,0},{5,1},{6,2},{7,3},{8,12},{9,13},{10,... | collective-permute-start | bytes 786440 | tf_op jit(solution)/shard_map/ppermute | solution.py:67
  100.5 1.0 bitcast_add_fusion.3
  101.5 4.4 %collective-permute-done.13 = f32[1,64,2,512]{3,1,2,0:T(8,128)S(1)} collective-permute-done((f32[1,64,2,512]{3,1,2,0:T(8,128)S(1)}, f32[1,64,2,512]{3,1,2,0:T(8,128)S(1)}, u32[]{:S(2)}, u32[]{:S(2)}) %collective-permute-start.13) | collective-permute-done | bytes 262176 | tf_op jit(solution)/shard_map/ppermute | solution.py:67
  105.8 1.0 dynamic-slice_add_fusion
  107.0 1.5 %collective-permute-start.14 = (f32[64,512]{1,0:T(8,128)S(1)}, f32[64,512]{1,0:T(8,128)S(1)}, u32[]{:S(2)}, u32[]{:S(2)}) collective-permute-start(f32[64,512]{1,0:T(8,128)S(1)} %get-tuple-element.16), channel_id=1, source_target_pairs={{0,8},{8,16},{16,24},{24,0},{1,9},{9,17},{17,25},{25,1},{2,10},{10... | collective-permute-start | bytes 393224 | tf_op jit(solution)/shard_map/ppermute | solution.py:200
  108.5 1.5 %collective-permute-start.15 = (f32[64,512]{1,0:T(8,128)S(1)}, f32[64,512]{1,0:T(8,128)S(1)}, u32[]{:S(2)}, u32[]{:S(2)}) collective-permute-start(f32[64,512]{1,0:T(8,128)S(1)} %get-tuple-element.17), channel_id=1, source_target_pairs={{0,16},{8,24},{16,0},{24,8},{1,17},{9,25},{17,1},{25,9},{2,18},{10... | collective-permute-start | bytes 393224 | tf_op jit(solution)/shard_map/ppermute | solution.py:200
  110.0 1.4 %collective-permute-start.16 = (f32[64,512]{1,0:T(8,128)S(1)}, f32[64,512]{1,0:T(8,128)S(1)}, u32[]{:S(2)}, u32[]{:S(2)}) collective-permute-start(f32[64,512]{1,0:T(8,128)S(1)} %get-tuple-element.18), channel_id=1, source_target_pairs={{0,24},{8,0},{16,8},{24,16},{1,25},{9,1},{17,9},{25,17},{2,26},{10... | collective-permute-start | bytes 393224 | tf_op jit(solution)/shard_map/ppermute | solution.py:200
  111.5 1.7 %collective-permute-done.19 = f32[1,64,512]{2,1,0:T(8,128)S(1)} collective-permute-done((f32[1,64,512]{2,1,0:T(8,128)S(1)}, f32[1,64,512]{2,1,0:T(8,128)S(1)}, u32[]{:S(2)}, u32[]{:S(2)}) %collective-permute-start.19) | collective-permute-done | bytes 131104 | tf_op jit(solution)/shard_map/ppermute | solution.py:67
  (71 shorter events, 12.2 us)
Async XLA Ops:
  0.6 38.4 %copy-start = (f32[1,256,2048]{2,1,0:T(8,128)S(1)}, f32[1,256,2048]{2,1,0:T(8,128)}, u32[]{:S(2)}) copy-start(f32[1,256,2048]{2,1,0:T(8,128)} %param.18) | copy-start | bytes 6291460
  1.5 5.0 %collective-permute-start = (bf16[1,64,128]{2,0,1:T(2,128)(2,1)S(1)}, bf16[1,64,128]{2,0,1:T(2,128)(2,1)S(1)}, u32[]{:S(2)}, u32[]{:S(2)}) collective-permute-start(bf16[1,64,128]{2,0,1:T(2,128)(2,1)S(1)} %copy.38), channel_id=1, source_target_pairs={{0,16},{8,24},{16,0},{24,8},{1,17},{9,25},{17,1},{25,9},{2,18},{10... | collective-permute-start | bytes 49160 | tf_op jit(solution)/shard_map/ppermute | solution.py:41
  6.6 4.0 %collective-permute-start.1 = (bf16[2,64,128]{2,0,1:T(2,128)(2,1)S(1)}, bf16[2,64,128]{2,0,1:T(2,128)(2,1)S(1)}, u32[]{:S(2)}, u32[]{:S(2)}) collective-permute-start(bf16[2,64,128]{2,0,1:T(2,128)(2,1)S(1)} %pad_maximum_fusion.5), channel_id=1, source_target_pairs={{0,8},{8,0},{16,24},{24,16},{1,9},{9,1},{17,25},{25,17},{2,10},{10... | collective-permute-start | bytes 98312 | tf_op jit(solution)/shard_map/ppermute | solution.py:41
  10.8 5.2 %collective-permute-start.2 = (bf16[2,64,128]{2,0,1:T(2,128)(2,1)S(1)}, bf16[2,64,128]{2,0,1:T(2,128)(2,1)S(1)}, u32[]{:S(2)}, u32[]{:S(2)}) collective-permute-start(bf16[2,64,128]{2,0,1:T(2,128)(2,1)S(1)} %convolution_convert_fusion), channel_id=1, source_target_pairs={{0,4},{1,5},{2,6},{3,7},{4,0},{5,1},{6,2},{7,3},{8,12},{9,13},{10,... | collective-permute-start | bytes 98312 | tf_op jit(solution)/shard_map/ppermute | solution.py:41
  16.0 4.3 %collective-permute-start.3 = (bf16[2,128,128]{2,0,1:T(2,128)(2,1)S(1)}, bf16[2,128,128]{2,0,1:T(2,128)(2,1)S(1)}, u32[]{:S(2)}, u32[]{:S(2)}) collective-permute-start(bf16[2,128,128]{2,0,1:T(2,128)(2,1)S(1)} %pad_maximum_fusion.4), channel_id=1, source_target_pairs={{0,2},{1,3},{2,0},{3,1},{4,6},{5,7},{6,4},{7,5},{8,10},{9,11},{10,... | collective-permute-start | bytes 196616 | tf_op jit(solution)/shard_map/ppermute | solution.py:41
  20.6 1.5 %collective-permute-start.4 = (bf16[2,256,128]{2,0,1:T(2,128)(2,1)S(1)}, bf16[2,256,128]{2,0,1:T(2,128)(2,1)S(1)}, u32[]{:S(2)}, u32[]{:S(2)}) collective-permute-start(bf16[2,256,128]{2,0,1:T(2,128)(2,1)S(1)} %pad_maximum_fusion.1), channel_id=1, source_target_pairs={{0,1},{1,0},{2,3},{3,2},{4,5},{5,4},{6,7},{7,6},{8,9},{9,8},{10,11... | collective-permute-start | bytes 393224 | tf_op jit(solution)/shard_map/ppermute | solution.py:41
  23.2 3.5 %copy-start.5 = (f32[1,1280]{1,0:T(1,128)S(1)}, f32[1,1280]{1,0:T(1,128)}, u32[]{:S(2)}) copy-start(f32[1,1280]{1,0:T(1,128)} %param.17) | copy-start | bytes 15364
  23.2 3.5 %copy-start.1 = (bf16[1,1280,2048]{2,1,0:T(8,128)(2,1)S(1)}, bf16[1,1280,2048]{2,1,0:T(8,128)(2,1)}, u32[]{:S(2)}) copy-start(bf16[1,1280,2048]{2,1,0:T(8,128)(2,1)} %param.12) | copy-start | bytes 15728644
  29.0 1.4 %collective-permute-start.5 = (f32[2,2176]{1,0:T(2,128)S(1)}, f32[2,2176]{1,0:T(2,128)S(1)}, u32[]{:S(2)}, u32[]{:S(2)}) collective-permute-start(f32[2,2176]{1,0:T(2,128)S(1)} %pad_maximum_fusion.6), channel_id=1, source_target_pairs={{0,1},{1,0},{2,3},{3,2},{4,5},{5,4},{6,7},{7,6},{8,9},{9,8},{10,11... | collective-permute-start | bytes 52232 | tf_op jit(solution)/shard_map/ppermute | solution.py:28
  30.4 3.8 %collective-permute-start.6 = (f32[2,2176]{1,0:T(2,128)S(1)}, f32[2,2176]{1,0:T(2,128)S(1)}, u32[]{:S(2)}, u32[]{:S(2)}) collective-permute-start(f32[2,2176]{1,0:T(2,128)S(1)} %fusion.52), channel_id=1, source_target_pairs={{0,2},{1,3},{2,0},{3,1},{4,6},{5,7},{6,4},{7,5},{8,10},{9,11},{10,... | collective-permute-start | bytes 52232 | tf_op jit(solution)/shard_map/ppermute | solution.py:28
  34.3 4.8 %collective-permute-start.7 = (f32[2,2176]{1,0:T(2,128)S(1)}, f32[2,2176]{1,0:T(2,128)S(1)}, u32[]{:S(2)}, u32[]{:S(2)}) collective-permute-start(f32[2,2176]{1,0:T(2,128)S(1)} %add.142), channel_id=1, source_target_pairs={{0,4},{1,5},{2,6},{3,7},{4,0},{5,1},{6,2},{7,3},{8,12},{9,13},{10,... | collective-permute-start | bytes 52232 | tf_op jit(solution)/shard_map/ppermute | solution.py:28
  40.8 4.5 %collective-permute-start.8 = (f32[256]{0:T(256)S(1)}, f32[256]{0:T(256)S(1)}, u32[]{:S(2)}, u32[]{:S(2)}) collective-permute-start(f32[256]{0:T(256)S(1)} %bitcast.105), channel_id=1, source_target_pairs={{0,4},{1,5},{2,6},{3,7},{4,0},{5,1},{6,2},{7,3},{8,12},{9,13},{10,... | collective-permute-start | bytes 3080 | tf_op jit(solution)/shard_map/ppermute | solution.py:41
  45.3 3.6 %collective-permute-start.9 = (f32[512]{0:T(512)S(1)}, f32[512]{0:T(512)S(1)}, u32[]{:S(2)}, u32[]{:S(2)}) collective-permute-start(f32[512]{0:T(512)S(1)} %pad_maximum_fusion.10), channel_id=1, source_target_pairs={{0,2},{1,3},{2,0},{3,1},{4,6},{5,7},{6,4},{7,5},{8,10},{9,11},{10,... | collective-permute-start | bytes 6152 | tf_op jit(solution)/shard_map/ppermute | solution.py:41
  48.9 1.2 %collective-permute-start.10 = (f32[1024]{0:T(1024)S(1)}, f32[1024]{0:T(1024)S(1)}, u32[]{:S(2)}, u32[]{:S(2)}) collective-permute-start(f32[1024]{0:T(1024)S(1)} %pad_maximum_fusion.9), channel_id=1, source_target_pairs={{0,1},{1,0},{2,3},{3,2},{4,5},{5,4},{6,7},{7,6},{8,9},{9,8},{10,11... | collective-permute-start | bytes 12296 | tf_op jit(solution)/shard_map/ppermute | solution.py:41
  62.5 2.5 %copy-start.2 = (bf16[1,1280,1024]{2,1,0:T(8,128)(2,1)S(1)}, bf16[1,1280,1024]{2,1,0:T(8,128)(2,1)}, u32[]{:S(2)}) copy-start(bf16[1,1280,1024]{2,1,0:T(8,128)(2,1)} %param.11) | copy-start | bytes 7864324
  67.1 2.7 %collective-permute-start.11 = (f32[4,64,2,512]{3,1,2,0:T(8,128)S(1)}, f32[4,64,2,512]{3,1,2,0:T(8,128)S(1)}, u32[]{:S(2)}, u32[]{:S(2)}) collective-permute-start(f32[4,64,2,512]{3,1,2,0:T(8,128)S(1)} %bitcast.95), channel_id=1, source_target_pairs={{0,1},{1,0},{2,3},{3,2},{4,5},{5,4},{6,7},{7,6},{8,9},{9,8},{10,11... | collective-permute-start | bytes 3145736 | tf_op jit(solution)/shard_map/ppermute | solution.py:67
  68.2 1.8 %copy-start.4 = (f32[512,512]{1,0:T(8,128)}, f32[512,512]{1,0:T(8,128)S(1)}, u32[]{:S(2)}) copy-start(f32[512,512]{1,0:T(8,128)S(1)} %fusion.7) | copy-start | bytes 3145732
  70.9 2.8 %collective-permute-start.17 = (f32[4,64,512]{2,1,0:T(8,128)}, f32[4,64,512]{2,1,0:T(8,128)}, u32[]{:S(2)}, u32[]{:S(2)}) collective-permute-start(f32[4,64,512]{2,1,0:T(8,128)} %dynamic-slice_bitcast_fusion), channel_id=1, source_target_pairs={{0,1},{1,0},{2,3},{3,2},{4,5},{5,4},{6,7},{7,6},{8,9},{9,8},{10,11... | collective-permute-start | bytes 1572872 | tf_op jit(solution)/shard_map/ppermute | solution.py:67
  71.0 23.0 %copy-start.6 = (s32[1,2]{1,0:T(1,128)S(1)}, s32[1,2]{1,0:T(1,128)}, u32[]{:S(2)}) copy-start(s32[1,2]{1,0:T(1,128)} %param.15) | copy-start | bytes 28
  71.9 14.5 %collective-permute-start.12 = (f32[2,64,2,512]{3,1,2,0:T(8,128)}, f32[2,64,2,512]{3,1,2,0:T(8,128)}, u32[]{:S(2)}, u32[]{:S(2)}) collective-permute-start(f32[2,64,2,512]{3,1,2,0:T(8,128)} %dynamic-slice_bitcast_fusion.1), channel_id=1, source_target_pairs={{0,2},{1,3},{2,0},{3,1},{4,6},{5,7},{6,4},{7,5},{8,10},{9,11},{10,... | collective-permute-start | bytes 1572872 | tf_op jit(solution)/shard_map/ppermute | solution.py:67
  74.9 13.4 %copy-start.3 = (f32[4,64,512]{2,1,0:T(8,128)}, f32[4,64,512]{2,1,0:T(8,128)S(1)}, u32[]{:S(2)}) copy-start(f32[4,64,512]{2,1,0:T(8,128)S(1)} %bitcast_add_fusion.1) | copy-start | bytes 1572868
  88.3 12.1 %collective-permute-start.18 = (f32[2,64,512]{2,1,0:T(8,128)S(1)}, f32[2,64,512]{2,1,0:T(8,128)S(1)}, u32[]{:S(2)}, u32[]{:S(2)}) collective-permute-start(f32[2,64,512]{2,1,0:T(8,128)S(1)} %dynamic-slice_bitcast_fusion.2), channel_id=1, source_target_pairs={{0,2},{1,3},{2,0},{3,1},{4,6},{5,7},{6,4},{7,5},{8,10},{9,11},{10,... | collective-permute-start | bytes 786440 | tf_op jit(solution)/shard_map/ppermute | solution.py:67
  91.1 14.7 %collective-permute-start.13 = (f32[1,64,2,512]{3,1,2,0:T(8,128)S(1)}, f32[1,64,2,512]{3,1,2,0:T(8,128)S(1)}, u32[]{:S(2)}, u32[]{:S(2)}) collective-permute-start(f32[1,64,2,512]{3,1,2,0:T(8,128)S(1)} %constant_dynamic-slice_fusion.1), channel_id=1, source_target_pairs={{0,4},{1,5},{2,6},{3,7},{4,0},{5,1},{6,2},{7,3},{8,12},{9,13},{10,... | collective-permute-start | bytes 786440 | tf_op jit(solution)/shard_map/ppermute | solution.py:67
  106.8 6.4 %collective-permute-start.19 = (f32[1,64,512]{2,1,0:T(8,128)S(1)}, f32[1,64,512]{2,1,0:T(8,128)S(1)}, u32[]{:S(2)}, u32[]{:S(2)}) collective-permute-start(f32[1,64,512]{2,1,0:T(8,128)S(1)} %constant_dynamic-slice_fusion), channel_id=1, source_target_pairs={{0,4},{1,5},{2,6},{3,7},{4,0},{5,1},{6,2},{7,3},{8,12},{9,13},{10,... | collective-permute-start | bytes 393224 | tf_op jit(solution)/shard_map/ppermute | solution.py:67
  107.0 6.9 %collective-permute-start.14 = (f32[64,512]{1,0:T(8,128)S(1)}, f32[64,512]{1,0:T(8,128)S(1)}, u32[]{:S(2)}, u32[]{:S(2)}) collective-permute-start(f32[64,512]{1,0:T(8,128)S(1)} %get-tuple-element.16), channel_id=1, source_target_pairs={{0,8},{8,16},{16,24},{24,0},{1,9},{9,17},{17,25},{25,1},{2,10},{10... | collective-permute-start | bytes 393224 | tf_op jit(solution)/shard_map/ppermute | solution.py:200
  108.5 5.8 %collective-permute-start.15 = (f32[64,512]{1,0:T(8,128)S(1)}, f32[64,512]{1,0:T(8,128)S(1)}, u32[]{:S(2)}, u32[]{:S(2)}) collective-permute-start(f32[64,512]{1,0:T(8,128)S(1)} %get-tuple-element.17), channel_id=1, source_target_pairs={{0,16},{8,24},{16,0},{24,8},{1,17},{9,25},{17,1},{25,9},{2,18},{10... | collective-permute-start | bytes 393224 | tf_op jit(solution)/shard_map/ppermute | solution.py:200
  110.0 5.0 %collective-permute-start.16 = (f32[64,512]{1,0:T(8,128)S(1)}, f32[64,512]{1,0:T(8,128)S(1)}, u32[]{:S(2)}, u32[]{:S(2)}) collective-permute-start(f32[64,512]{1,0:T(8,128)S(1)} %get-tuple-element.18), channel_id=1, source_target_pairs={{0,24},{8,0},{16,8},{24,16},{1,25},{9,1},{17,9},{25,17},{2,26},{10... | collective-permute-start | bytes 393224 | tf_op jit(solution)/shard_map/ppermute | solution.py:200

commit v12 on v9

--- a/solution.py
+++ b/solution.py
@@ -94,7 +94,8 @@
     live_count = counts[0, 0]
     position = lax.iota(jnp.int32, points)
     live_weight = jnp.where(position < live_count, weights[0], jnp.zeros((), jnp.float32))
-    gathered, slot_held, _ = xor_gather(factors, "dimer", 0)
+    gathered, slot_held, _ = xor_gather(factors[0], "dimer", 0)
+    gathered = gathered.reshape((slot_held.shape[0],) + factors.shape[1:])
     frag_ids = lax.iota(jnp.int32, frag_slot.shape[0])
     wanted = jnp.sum(
         jnp.where(frag_ids[None, :] == dimer_pairs[0][:, None], frag_slot[None, :], 0), axis=1

time: 109 us -> 110 us (level)
  other arithmetic: 14.3 us -> 15.6 us
    concatenate x7 -> x8, other arithmetic: 0.75 us -> 2.11 us  [xor_gather(): value = jnp.concatenate([value, other], axis=dim)]
where the time goes in v12:
time: 110 us; the launch traced here: 109 us
  waiting for transfers between devices  35.6 us (32%)
  starting transfers between devices  31.8 us (29%)
  other arithmetic  15.6 us (14%)
  matrix products  12.3 us (11%)
  between operations  8.74 us (8%)
  local copies, waits for them, and re-layouts  5.24 us (5%)
    ppermute x6, waiting for transfers between devices, scatter_step(): lax.ppermute(send, axis, [(i, i ^ 1 << bit) for i in range(size)])  19.8 us
    ppermute x8, starting transfers between devices, xor_gather(): other = lax.ppermute(value, axis, [(i, i ^ 1 << bit) for i in range(size)])  14.8 us
    ppermute x8, waiting for transfers between devices, xor_gather(): other = lax.ppermute(value, axis, [(i, i ^ 1 << bit) for i in range(size)])  10.1 us
    ppermute x6, starting transfers between devices, scatter_step(): lax.ppermute(send, axis, [(i, i ^ 1 << bit) for i in range(size)])  6.95 us
    add x6, other arithmetic, scatter_step(): keep + lax.ppermute(send, axis, [(i, i ^ 1 << bit) for i in range(size)])  6.05 us
    ppermute x3, starting transfers between devices, xor_sum(): lax.ppermute(value, axis, [(i, i ^ step) for i in range(size)])  5.48 us
    ppermute x3, waiting for transfers between devices, xor_sum(): lax.ppermute(value, axis, [(i, i ^ step) for i in range(size)])  4.52 us
    ppermute x3, starting transfers between devices, shards(): lax.ppermute(sent, 'dimer', [(i, (i + shift) % groups) for i in range(gro...  4.51 us
  transfers between devices with their start and end apart: 20, of which 17 were waited for; matrix products, arithmetic and copies ran while one was open for 9% of the time, Pallas kernels for 0%

profile of v12, /device:TPU:0, one launch (start us, length us, event | category | flops | bytes accessed | tf_op | source)
XLA Modules:
  0.0 109.2 jit_solution(13963308794349690978)
XLA Ops:
  0.6 3.1 %collective-permute-start = (bf16[64,128]{1,0:T(8,128)(2,1)}, bf16[64,128]{1,0:T(8,128)(2,1)S(1)}, u32[]{:S(2)}, u32[]{:S(2)}) collective-permute-start(bf16[64,128]{1,0:T(8,128)(2,1)} %bitcast.119), channel_id=1, source_target_pairs={{0,16},{8,24},{16,0},{24,8},{1,17},{9,25},{17,1},{25,9},{2,18},{10... | collective-permute-start | bytes 49160 | tf_op jit(solution)/shard_map/ppermute | solution.py:40
  4.4 1.3 %collective-permute-done = bf16[64,128]{1,0:T(8,128)(2,1)S(1)} collective-permute-done((bf16[64,128]{1,0:T(8,128)(2,1)}, bf16[64,128]{1,0:T(8,128)(2,1)S(1)}, u32[]{:S(2)}, u32[]{:S(2)}) %collective-permute-start) | collective-permute-done | bytes 16416 | tf_op jit(solution)/shard_map/ppermute | solution.py:40
  5.6 0.7 pad_maximum_fusion.4
  6.4 2.0 %collective-permute-start.1 = (bf16[128,128]{1,0:T(8,128)(2,1)S(1)}, bf16[128,128]{1,0:T(8,128)(2,1)S(1)}, u32[]{:S(2)}, u32[]{:S(2)}) collective-permute-start(bf16[128,128]{1,0:T(8,128)(2,1)S(1)} %pad_maximum_fusion.4), channel_id=1, source_target_pairs={{0,8},{8,0},{16,24},{24,16},{1,9},{9,1},{17,25},{25,17},{2,10},{10... | collective-permute-start | bytes 98312 | tf_op jit(solution)/shard_map/ppermute | solution.py:40
  8.3 0.9 fusion.49
  9.2 1.1 collective-permute-done.1
  10.3 0.7 pad_maximum_fusion.2
  11.2 3.2 %collective-permute-start.2 = (bf16[2,64,128]{2,0,1:T(2,128)(2,1)S(1)}, bf16[2,64,128]{2,0,1:T(2,128)(2,1)S(1)}, u32[]{:S(2)}, u32[]{:S(2)}) collective-permute-start(bf16[2,64,128]{2,0,1:T(2,128)(2,1)S(1)} %convolution_convert_fusion), channel_id=1, source_target_pairs={{0,4},{1,5},{2,6},{3,7},{4,0},{5,1},{6,2},{7,3},{8,12},{9,13},{10,... | collective-permute-start | bytes 98312 | tf_op jit(solution)/shard_map/ppermute | solution.py:40
  14.4 2.0 %collective-permute-done.2 = bf16[2,64,128]{2,0,1:T(2,128)(2,1)S(1)} collective-permute-done((bf16[2,64,128]{2,0,1:T(2,128)(2,1)S(1)}, bf16[2,64,128]{2,0,1:T(2,128)(2,1)S(1)}, u32[]{:S(2)}, u32[]{:S(2)}) %collective-permute-start.2) | collective-permute-done | bytes 32800 | tf_op jit(solution)/shard_map/ppermute | solution.py:40
  16.5 1.9 %collective-permute-start.3 = (bf16[2,128,128]{2,0,1:T(2,128)(2,1)S(1)}, bf16[2,128,128]{2,0,1:T(2,128)(2,1)S(1)}, u32[]{:S(2)}, u32[]{:S(2)}) collective-permute-start(bf16[2,128,128]{2,0,1:T(2,128)(2,1)S(1)} %pad_maximum_fusion.3), channel_id=1, source_target_pairs={{0,2},{1,3},{2,0},{3,1},{4,6},{5,7},{6,4},{7,5},{8,10},{9,11},{10,... | collective-permute-start | bytes 196616 | tf_op jit(solution)/shard_map/ppermute | solution.py:40
  19.0 1.8 %collective-permute-done.3 = bf16[2,128,128]{2,0,1:T(2,128)(2,1)S(1)} collective-permute-done((bf16[2,128,128]{2,0,1:T(2,128)(2,1)S(1)}, bf16[2,128,128]{2,0,1:T(2,128)(2,1)S(1)}, u32[]{:S(2)}, u32[]{:S(2)}) %collective-permute-start.3) | collective-permute-done | bytes 65568 | tf_op jit(solution)/shard_map/ppermute | solution.py:40
  21.7 0.7 reduce.2
  23.6 2.8 %fusion.13 = f32[1280]{0:T(1024)S(1)} fusion(bf16[512,128]{1,0:T(8,128)(2,1)S(1)} %bitcast.115, bf16[512,128]{1,0:T(8,128)(2,1)S(1)} %bitcast.114, bf16[1,1280,1024]{2,1,0:T(8,128)(2,1)} %param.11), kind=kOutput, calls=%fused_computation.19 | convolution fusion | flops 673839872 | bytes 2888704 | tf_op jit(solution)/shard_map/dot_general | solution.py:117
  27.2 0.8 fusion.2
  28.0 1.3 %pad_maximum_fusion.10 = f32[2]{0:T(128)S(1)} fusion(f32[1]{0:T(128)} %bitcast.14, f32[1]{0:T(128)} %bitcast.13), kind=kLoop, calls=%fused_computation.104 | loop fusion | flops 2 | bytes 16 | tf_op jit(solution)/shard_map/stack | solution.py:125
  30.0 0.8 collective-permute-done.5
  30.9 1.9 %collective-permute-start.6 = (f32[2,2176]{1,0:T(2,128)S(1)}, f32[2,2176]{1,0:T(2,128)S(1)}, u32[]{:S(2)}, u32[]{:S(2)}) collective-permute-start(f32[2,2176]{1,0:T(2,128)S(1)} %fusion.58), channel_id=1, source_target_pairs={{0,2},{1,3},{2,0},{3,1},{4,6},{5,7},{6,4},{7,5},{8,10},{9,11},{10,... | collective-permute-start | bytes 52232 | tf_op jit(solution)/shard_map/ppermute | solution.py:27
  32.8 1.9 %collective-permute-done.6 = f32[2,2176]{1,0:T(2,128)S(1)} collective-permute-done((f32[2,2176]{1,0:T(2,128)S(1)}, f32[2,2176]{1,0:T(2,128)S(1)}, u32[]{:S(2)}, u32[]{:S(2)}) %collective-permute-start.6) | collective-permute-done | bytes 17440 | tf_op jit(solution)/shard_map/ppermute | solution.py:27
  34.7 3.1 %collective-permute-start.7 = (f32[2,2176]{1,0:T(2,128)S(1)}, f32[2,2176]{1,0:T(2,128)S(1)}, u32[]{:S(2)}, u32[]{:S(2)}) collective-permute-start(f32[2,2176]{1,0:T(2,128)S(1)} %add.142), channel_id=1, source_target_pairs={{0,4},{1,5},{2,6},{3,7},{4,0},{5,1},{6,2},{7,3},{8,12},{9,13},{10,... | collective-permute-start | bytes 52232 | tf_op jit(solution)/shard_map/ppermute | solution.py:27
  37.8 1.7 %collective-permute-done.7 = f32[2,2176]{1,0:T(2,128)S(1)} collective-permute-done((f32[2,2176]{1,0:T(2,128)S(1)}, f32[2,2176]{1,0:T(2,128)S(1)}, u32[]{:S(2)}, u32[]{:S(2)}) %collective-permute-start.7) | collective-permute-done | bytes 17440 | tf_op jit(solution)/shard_map/ppermute | solution.py:27
  39.5 1.7 %fusion.7 = f32[1,256]{1,0:T(1,128)S(1)} fusion(f32[1,256,2048]{2,1,0:T(8,128)S(1)} %copy-done, f32[2,2176]{1,0:T(2,128)S(1)} %add.143), kind=kOutput, calls=%fused_computation.13 | convolution fusion | flops 6291456 | bytes 2106368 | tf_op jit(solution)/shard_map/dot_general | solution.py:135
  41.3 2.9 %collective-permute-start.8 = (f32[256]{0:T(256)S(1)}, f32[256]{0:T(256)S(1)}, u32[]{:S(2)}, u32[]{:S(2)}) collective-permute-start(f32[256]{0:T(256)S(1)} %bitcast.124), channel_id=1, source_target_pairs={{0,4},{1,5},{2,6},{3,7},{4,0},{5,1},{6,2},{7,3},{8,12},{9,13},{10,... | collective-permute-start | bytes 3080 | tf_op jit(solution)/shard_map/ppermute | solution.py:40
  44.2 1.6 %collective-permute-done.8 = f32[256]{0:T(256)S(1)} collective-permute-done((f32[256]{0:T(256)S(1)}, f32[256]{0:T(256)S(1)}, u32[]{:S(2)}, u32[]{:S(2)}) %collective-permute-start.8) | collective-permute-done | bytes 1056 | tf_op jit(solution)/shard_map/ppermute | solution.py:40
  45.8 1.7 %collective-permute-start.9 = (f32[512]{0:T(512)S(1)}, f32[512]{0:T(512)S(1)}, u32[]{:S(2)}, u32[]{:S(2)}) collective-permute-start(f32[512]{0:T(512)S(1)} %pad_maximum_fusion.9), channel_id=1, source_target_pairs={{0,2},{1,3},{2,0},{3,1},{4,6},{5,7},{6,4},{7,5},{8,10},{9,11},{10,... | collective-permute-start | bytes 6152 | tf_op jit(solution)/shard_map/ppermute | solution.py:40
  47.5 1.9 %collective-permute-done.9 = f32[512]{0:T(512)S(1)} collective-permute-done((f32[512]{0:T(512)S(1)}, f32[512]{0:T(512)S(1)}, u32[]{:S(2)}, u32[]{:S(2)}) %collective-permute-start.9) | collective-permute-done | bytes 2080 | tf_op jit(solution)/shard_map/ppermute | solution.py:40
  53.8 4.1 %fusion.4 = f32[1280,2]{0,1:T(2,128)S(1)} fusion(bf16[1,1280,2048]{2,1,0:T(8,128)(2,1)} %param.12, bf16[2048,1]{0,1:T(2,128)(2,1)S(1)} %stack.34, bf16[2048,1]{0,1:T(2,128)(2,1)S(1)} %bitcast.122), kind=kOutput, calls=%fused_computation.12 | convolution fusion | flops 10502144 | bytes 5261312 | tf_op jit(solution)/shard_map/dot_general | solution.py:138
  58.5 0.9 fusion.9
  59.4 0.9 fusion.11
  60.8 0.9 fusion.14
  61.7 1.6 %collective-permute-done.11 = f32[4,64,2,512]{3,1,2,0:T(8,128)S(1)} collective-permute-done((f32[4,64,2,512]{3,1,2,0:T(8,128)S(1)}, f32[4,64,2,512]{3,1,2,0:T(8,128)S(1)}, u32[]{:S(2)}, u32[]{:S(2)}) %collective-permute-start.11) | collective-permute-done | bytes 1048608 | tf_op jit(solution)/shard_map/ppermute | solution.py:66
  63.5 0.9 dynamic-slice_bitcast_fusion
  64.5 0.8 dynamic-slice_bitcast_fusion.1
  65.4 1.7 %collective-permute-start.12 = (f32[2,64,2,512]{3,1,2,0:T(8,128)}, f32[2,64,2,512]{3,1,2,0:T(8,128)}, u32[]{:S(2)}, u32[]{:S(2)}) collective-permute-start(f32[2,64,2,512]{3,1,2,0:T(8,128)} %dynamic-slice_bitcast_fusion.1), channel_id=1, source_target_pairs={{0,2},{1,3},{2,0},{3,1},{4,6},{5,7},{6,4},{7,5},{8,10},{9,11},{10,... | collective-permute-start | bytes 1572872 | tf_op jit(solution)/shard_map/ppermute | solution.py:66
  67.1 1.3 %bitcast_add_fusion.1 = f32[4,64,512]{2,1,0:T(8,128)S(1)} fusion(f32[4,64,512]{2,1,0:T(8,128)} %collective-permute-done.17, f32[4,2,64,512]{3,2,1,0:T(8,128)} %bitcast.113, s32[]{:T(128)S(6)} %select_n.160), kind=kLoop, calls=%fused_computation.38 | loop fusion | flops 131072 | bytes 1572868 | tf_op jit(solution)/shard_map/add | solution.py:66
  68.4 11.5 %collective-permute-done.12 = f32[2,64,2,512]{3,1,2,0:T(8,128)} collective-permute-done((f32[2,64,2,512]{3,1,2,0:T(8,128)}, f32[2,64,2,512]{3,1,2,0:T(8,128)}, u32[]{:S(2)}, u32[]{:S(2)}) %collective-permute-start.12) | collective-permute-done | bytes 524320 | tf_op jit(solution)/shard_map/ppermute | solution.py:66
  79.9 1.9 %bitcast_add_fusion.2 = f32[2,64,2,512]{3,1,2,0:T(8,128)} fusion(f32[2,64,2,512]{3,1,2,0:T(8,128)} %collective-permute-done.12, f32[2,2,64,2,512]{4,2,3,1,0:T(8,128)S(1)} %bitcast.100, s32[]{:T(128)S(6)} %select_n.162), kind=kLoop, calls=%fused_computation.39 | loop fusion | flops 131072 | bytes 1572868 | tf_op jit(solution)/shard_map/add | solution.py:66
  81.8 1.8 %collective-permute-start.18 = (f32[2,64,512]{2,1,0:T(8,128)S(1)}, f32[2,64,512]{2,1,0:T(8,128)S(1)}, u32[]{:S(2)}, u32[]{:S(2)}) collective-permute-start(f32[2,64,512]{2,1,0:T(8,128)S(1)} %dynamic-slice_bitcast_fusion.2), channel_id=1, source_target_pairs={{0,2},{1,3},{2,0},{3,1},{4,6},{5,7},{6,4},{7,5},{8,10},{9,11},{10,... | collective-permute-start | bytes 786440 | tf_op jit(solution)/shard_map/ppermute | solution.py:66
  83.6 1.0 constant_dynamic-slice_fusion.1
  84.6 3.0 %collective-permute-start.13 = (f32[1,64,2,512]{3,1,2,0:T(8,128)S(1)}, f32[1,64,2,512]{3,1,2,0:T(8,128)S(1)}, u32[]{:S(2)}, u32[]{:S(2)}) collective-permute-start(f32[1,64,2,512]{3,1,2,0:T(8,128)S(1)} %constant_dynamic-slice_fusion.1), channel_id=1, source_target_pairs={{0,4},{1,5},{2,6},{3,7},{4,0},{5,1},{6,2},{7,3},{8,12},{9,13},{10,... | collective-permute-start | bytes 786440 | tf_op jit(solution)/shard_map/ppermute | solution.py:66
  94.0 1.0 bitcast_add_fusion.3
  95.0 4.3 %collective-permute-done.13 = f32[1,64,2,512]{3,1,2,0:T(8,128)S(1)} collective-permute-done((f32[1,64,2,512]{3,1,2,0:T(8,128)S(1)}, f32[1,64,2,512]{3,1,2,0:T(8,128)S(1)}, u32[]{:S(2)}, u32[]{:S(2)}) %collective-permute-start.13) | collective-permute-done | bytes 262176 | tf_op jit(solution)/shard_map/ppermute | solution.py:66
  99.3 1.0 dynamic-slice_add_fusion
  100.5 1.5 %collective-permute-start.14 = (f32[64,512]{1,0:T(8,128)S(1)}, f32[64,512]{1,0:T(8,128)S(1)}, u32[]{:S(2)}, u32[]{:S(2)}) collective-permute-start(f32[64,512]{1,0:T(8,128)S(1)} %get-tuple-element.16), channel_id=1, source_target_pairs={{0,8},{8,16},{16,24},{24,0},{1,9},{9,17},{17,25},{25,1},{2,10},{10... | collective-permute-start | bytes 393224 | tf_op jit(solution)/shard_map/ppermute | solution.py:171
  102.0 1.5 %collective-permute-start.15 = (f32[64,512]{1,0:T(8,128)S(1)}, f32[64,512]{1,0:T(8,128)S(1)}, u32[]{:S(2)}, u32[]{:S(2)}) collective-permute-start(f32[64,512]{1,0:T(8,128)S(1)} %get-tuple-element.17), channel_id=1, source_target_pairs={{0,16},{8,24},{16,0},{24,8},{1,17},{9,25},{17,1},{25,9},{2,18},{10... | collective-permute-start | bytes 393224 | tf_op jit(solution)/shard_map/ppermute | solution.py:171
  103.5 1.5 %collective-permute-start.16 = (f32[64,512]{1,0:T(8,128)S(1)}, f32[64,512]{1,0:T(8,128)S(1)}, u32[]{:S(2)}, u32[]{:S(2)}) collective-permute-start(f32[64,512]{1,0:T(8,128)S(1)} %get-tuple-element.18), channel_id=1, source_target_pairs={{0,24},{8,0},{16,8},{24,16},{1,25},{9,1},{17,9},{25,17},{2,26},{10... | collective-permute-start | bytes 393224 | tf_op jit(solution)/shard_map/ppermute | solution.py:171
  105.0 1.7 %collective-permute-done.19 = f32[1,64,512]{2,1,0:T(8,128)S(1)} collective-permute-done((f32[1,64,512]{2,1,0:T(8,128)S(1)}, f32[1,64,512]{2,1,0:T(8,128)S(1)}, u32[]{:S(2)}, u32[]{:S(2)}) %collective-permute-start.19) | collective-permute-done | bytes 131104 | tf_op jit(solution)/shard_map/ppermute | solution.py:66
  107.8 0.7 collective-permute-done.16
  108.5 0.7 fusion.32
  (72 shorter events, 11.0 us)
Async XLA Ops:
  0.6 38.9 %copy-start = (f32[1,256,2048]{2,1,0:T(8,128)S(1)}, f32[1,256,2048]{2,1,0:T(8,128)}, u32[]{:S(2)}) copy-start(f32[1,256,2048]{2,1,0:T(8,128)} %param.18) | copy-start | bytes 6291460
  0.6 5.0 %collective-permute-start = (bf16[64,128]{1,0:T(8,128)(2,1)}, bf16[64,128]{1,0:T(8,128)(2,1)S(1)}, u32[]{:S(2)}, u32[]{:S(2)}) collective-permute-start(bf16[64,128]{1,0:T(8,128)(2,1)} %bitcast.119), channel_id=1, source_target_pairs={{0,16},{8,24},{16,0},{24,8},{1,17},{9,25},{17,1},{25,9},{2,18},{10... | collective-permute-start | bytes 49160 | tf_op jit(solution)/shard_map/ppermute | solution.py:40
  6.4 3.9 %collective-permute-start.1 = (bf16[128,128]{1,0:T(8,128)(2,1)S(1)}, bf16[128,128]{1,0:T(8,128)(2,1)S(1)}, u32[]{:S(2)}, u32[]{:S(2)}) collective-permute-start(bf16[128,128]{1,0:T(8,128)(2,1)S(1)} %pad_maximum_fusion.4), channel_id=1, source_target_pairs={{0,8},{8,0},{16,24},{24,16},{1,9},{9,1},{17,25},{25,17},{2,10},{10... | collective-permute-start | bytes 98312 | tf_op jit(solution)/shard_map/ppermute | solution.py:40
  11.2 5.2 %collective-permute-start.2 = (bf16[2,64,128]{2,0,1:T(2,128)(2,1)S(1)}, bf16[2,64,128]{2,0,1:T(2,128)(2,1)S(1)}, u32[]{:S(2)}, u32[]{:S(2)}) collective-permute-start(bf16[2,64,128]{2,0,1:T(2,128)(2,1)S(1)} %convolution_convert_fusion), channel_id=1, source_target_pairs={{0,4},{1,5},{2,6},{3,7},{4,0},{5,1},{6,2},{7,3},{8,12},{9,13},{10,... | collective-permute-start | bytes 98312 | tf_op jit(solution)/shard_map/ppermute | solution.py:40
  16.5 4.3 %collective-permute-start.3 = (bf16[2,128,128]{2,0,1:T(2,128)(2,1)S(1)}, bf16[2,128,128]{2,0,1:T(2,128)(2,1)S(1)}, u32[]{:S(2)}, u32[]{:S(2)}) collective-permute-start(bf16[2,128,128]{2,0,1:T(2,128)(2,1)S(1)} %pad_maximum_fusion.3), channel_id=1, source_target_pairs={{0,2},{1,3},{2,0},{3,1},{4,6},{5,7},{6,4},{7,5},{8,10},{9,11},{10,... | collective-permute-start | bytes 196616 | tf_op jit(solution)/shard_map/ppermute | solution.py:40
  21.0 1.5 %collective-permute-start.4 = (bf16[2,256,128]{2,0,1:T(2,128)(2,1)S(1)}, bf16[2,256,128]{2,0,1:T(2,128)(2,1)S(1)}, u32[]{:S(2)}, u32[]{:S(2)}) collective-permute-start(bf16[2,256,128]{2,0,1:T(2,128)(2,1)S(1)} %pad_maximum_fusion.1), channel_id=1, source_target_pairs={{0,1},{1,0},{2,3},{3,2},{4,5},{5,4},{6,7},{7,6},{8,9},{9,8},{10,11... | collective-permute-start | bytes 393224 | tf_op jit(solution)/shard_map/ppermute | solution.py:40
  23.6 3.5 %copy-start.5 = (f32[1,1280]{1,0:T(1,128)S(1)}, f32[1,1280]{1,0:T(1,128)}, u32[]{:S(2)}) copy-start(f32[1,1280]{1,0:T(1,128)} %param.17) | copy-start | bytes 15364
  23.6 3.6 %copy-start.1 = (bf16[1,1280,2048]{2,1,0:T(8,128)(2,1)S(1)}, bf16[1,1280,2048]{2,1,0:T(8,128)(2,1)}, u32[]{:S(2)}) copy-start(bf16[1,1280,2048]{2,1,0:T(8,128)(2,1)} %param.12) | copy-start | bytes 15728644
  29.5 1.4 %collective-permute-start.5 = (f32[2,2176]{1,0:T(2,128)S(1)}, f32[2,2176]{1,0:T(2,128)S(1)}, u32[]{:S(2)}, u32[]{:S(2)}) collective-permute-start(f32[2,2176]{1,0:T(2,128)S(1)} %pad_maximum_fusion.5), channel_id=1, source_target_pairs={{0,1},{1,0},{2,3},{3,2},{4,5},{5,4},{6,7},{7,6},{8,9},{9,8},{10,11... | collective-permute-start | bytes 52232 | tf_op jit(solution)/shard_map/ppermute | solution.py:27
  30.9 3.8 %collective-permute-start.6 = (f32[2,2176]{1,0:T(2,128)S(1)}, f32[2,2176]{1,0:T(2,128)S(1)}, u32[]{:S(2)}, u32[]{:S(2)}) collective-permute-start(f32[2,2176]{1,0:T(2,128)S(1)} %fusion.58), channel_id=1, source_target_pairs={{0,2},{1,3},{2,0},{3,1},{4,6},{5,7},{6,4},{7,5},{8,10},{9,11},{10,... | collective-permute-start | bytes 52232 | tf_op jit(solution)/shard_map/ppermute | solution.py:27
  34.7 4.8 %collective-permute-start.7 = (f32[2,2176]{1,0:T(2,128)S(1)}, f32[2,2176]{1,0:T(2,128)S(1)}, u32[]{:S(2)}, u32[]{:S(2)}) collective-permute-start(f32[2,2176]{1,0:T(2,128)S(1)} %add.142), channel_id=1, source_target_pairs={{0,4},{1,5},{2,6},{3,7},{4,0},{5,1},{6,2},{7,3},{8,12},{9,13},{10,... | collective-permute-start | bytes 52232 | tf_op jit(solution)/shard_map/ppermute | solution.py:27
  41.3 4.5 %collective-permute-start.8 = (f32[256]{0:T(256)S(1)}, f32[256]{0:T(256)S(1)}, u32[]{:S(2)}, u32[]{:S(2)}) collective-permute-start(f32[256]{0:T(256)S(1)} %bitcast.124), channel_id=1, source_target_pairs={{0,4},{1,5},{2,6},{3,7},{4,0},{5,1},{6,2},{7,3},{8,12},{9,13},{10,... | collective-permute-start | bytes 3080 | tf_op jit(solution)/shard_map/ppermute | solution.py:40
  45.8 3.6 %collective-permute-start.9 = (f32[512]{0:T(512)S(1)}, f32[512]{0:T(512)S(1)}, u32[]{:S(2)}, u32[]{:S(2)}) collective-permute-start(f32[512]{0:T(512)S(1)} %pad_maximum_fusion.9), channel_id=1, source_target_pairs={{0,2},{1,3},{2,0},{3,1},{4,6},{5,7},{6,4},{7,5},{8,10},{9,11},{10,... | collective-permute-start | bytes 6152 | tf_op jit(solution)/shard_map/ppermute | solution.py:40
  49.3 1.2 %collective-permute-start.10 = (f32[1024]{0:T(1024)S(1)}, f32[1024]{0:T(1024)S(1)}, u32[]{:S(2)}, u32[]{:S(2)}) collective-permute-start(f32[1024]{0:T(1024)S(1)} %pad_maximum_fusion.8), channel_id=1, source_target_pairs={{0,1},{1,0},{2,3},{3,2},{4,5},{5,4},{6,7},{7,6},{8,9},{9,8},{10,11... | collective-permute-start | bytes 12296 | tf_op jit(solution)/shard_map/ppermute | solution.py:40
  53.8 4.2 %copy-start.2 = (bf16[1,1280,1024]{2,1,0:T(8,128)(2,1)S(1)}, bf16[1,1280,1024]{2,1,0:T(8,128)(2,1)}, u32[]{:S(2)}) copy-start(bf16[1,1280,1024]{2,1,0:T(8,128)(2,1)} %param.11) | copy-start | bytes 7864324
  60.6 2.7 %collective-permute-start.11 = (f32[4,64,2,512]{3,1,2,0:T(8,128)S(1)}, f32[4,64,2,512]{3,1,2,0:T(8,128)S(1)}, u32[]{:S(2)}, u32[]{:S(2)}) collective-permute-start(f32[4,64,2,512]{3,1,2,0:T(8,128)S(1)} %bitcast.110), channel_id=1, source_target_pairs={{0,1},{1,0},{2,3},{3,2},{4,5},{5,4},{6,7},{7,6},{8,9},{9,8},{10,11... | collective-permute-start | bytes 3145736 | tf_op jit(solution)/shard_map/ppermute | solution.py:66
  61.7 1.8 %copy-start.4 = (f32[512,512]{1,0:T(8,128)}, f32[512,512]{1,0:T(8,128)S(1)}, u32[]{:S(2)}) copy-start(f32[512,512]{1,0:T(8,128)S(1)} %fusion.14) | copy-start | bytes 3145732
  64.4 2.8 %collective-permute-start.17 = (f32[4,64,512]{2,1,0:T(8,128)}, f32[4,64,512]{2,1,0:T(8,128)}, u32[]{:S(2)}, u32[]{:S(2)}) collective-permute-start(f32[4,64,512]{2,1,0:T(8,128)} %dynamic-slice_bitcast_fusion), channel_id=1, source_target_pairs={{0,1},{1,0},{2,3},{3,2},{4,5},{5,4},{6,7},{7,6},{8,9},{9,8},{10,11... | collective-permute-start | bytes 1572872 | tf_op jit(solution)/shard_map/ppermute | solution.py:66
  64.5 23.0 %copy-start.6 = (s32[1,2]{1,0:T(1,128)S(1)}, s32[1,2]{1,0:T(1,128)}, u32[]{:S(2)}) copy-start(s32[1,2]{1,0:T(1,128)} %param.15) | copy-start | bytes 28
  65.4 14.5 %collective-permute-start.12 = (f32[2,64,2,512]{3,1,2,0:T(8,128)}, f32[2,64,2,512]{3,1,2,0:T(8,128)}, u32[]{:S(2)}, u32[]{:S(2)}) collective-permute-start(f32[2,64,2,512]{3,1,2,0:T(8,128)} %dynamic-slice_bitcast_fusion.1), channel_id=1, source_target_pairs={{0,2},{1,3},{2,0},{3,1},{4,6},{5,7},{6,4},{7,5},{8,10},{9,11},{10,... | collective-permute-start | bytes 1572872 | tf_op jit(solution)/shard_map/ppermute | solution.py:66
  68.4 13.4 %copy-start.3 = (f32[4,64,512]{2,1,0:T(8,128)}, f32[4,64,512]{2,1,0:T(8,128)S(1)}, u32[]{:S(2)}) copy-start(f32[4,64,512]{2,1,0:T(8,128)S(1)} %bitcast_add_fusion.1) | copy-start | bytes 1572868
  81.8 12.2 %collective-permute-start.18 = (f32[2,64,512]{2,1,0:T(8,128)S(1)}, f32[2,64,512]{2,1,0:T(8,128)S(1)}, u32[]{:S(2)}, u32[]{:S(2)}) collective-permute-start(f32[2,64,512]{2,1,0:T(8,128)S(1)} %dynamic-slice_bitcast_fusion.2), channel_id=1, source_target_pairs={{0,2},{1,3},{2,0},{3,1},{4,6},{5,7},{6,4},{7,5},{8,10},{9,11},{10,... | collective-permute-start | bytes 786440 | tf_op jit(solution)/shard_map/ppermute | solution.py:66
  84.6 14.7 %collective-permute-start.13 = (f32[1,64,2,512]{3,1,2,0:T(8,128)S(1)}, f32[1,64,2,512]{3,1,2,0:T(8,128)S(1)}, u32[]{:S(2)}, u32[]{:S(2)}) collective-permute-start(f32[1,64,2,512]{3,1,2,0:T(8,128)S(1)} %constant_dynamic-slice_fusion.1), channel_id=1, source_target_pairs={{0,4},{1,5},{2,6},{3,7},{4,0},{5,1},{6,2},{7,3},{8,12},{9,13},{10,... | collective-permute-start | bytes 786440 | tf_op jit(solution)/shard_map/ppermute | solution.py:66
  100.3 6.4 %collective-permute-start.19 = (f32[1,64,512]{2,1,0:T(8,128)S(1)}, f32[1,64,512]{2,1,0:T(8,128)S(1)}, u32[]{:S(2)}, u32[]{:S(2)}) collective-permute-start(f32[1,64,512]{2,1,0:T(8,128)S(1)} %constant_dynamic-slice_fusion), channel_id=1, source_target_pairs={{0,4},{1,5},{2,6},{3,7},{4,0},{5,1},{6,2},{7,3},{8,12},{9,13},{10,... | collective-permute-start | bytes 393224 | tf_op jit(solution)/shard_map/ppermute | solution.py:66
  100.5 6.9 %collective-permute-start.14 = (f32[64,512]{1,0:T(8,128)S(1)}, f32[64,512]{1,0:T(8,128)S(1)}, u32[]{:S(2)}, u32[]{:S(2)}) collective-permute-start(f32[64,512]{1,0:T(8,128)S(1)} %get-tuple-element.16), channel_id=1, source_target_pairs={{0,8},{8,16},{16,24},{24,0},{1,9},{9,17},{17,25},{25,1},{2,10},{10... | collective-permute-start | bytes 393224 | tf_op jit(solution)/shard_map/ppermute | solution.py:171
  102.0 5.8 %collective-permute-start.15 = (f32[64,512]{1,0:T(8,128)S(1)}, f32[64,512]{1,0:T(8,128)S(1)}, u32[]{:S(2)}, u32[]{:S(2)}) collective-permute-start(f32[64,512]{1,0:T(8,128)S(1)} %get-tuple-element.17), channel_id=1, source_target_pairs={{0,16},{8,24},{16,0},{24,8},{1,17},{9,25},{17,1},{25,9},{2,18},{10... | collective-permute-start | bytes 393224 | tf_op jit(solution)/shard_map/ppermute | solution.py:171
  103.5 5.0 %collective-permute-start.16 = (f32[64,512]{1,0:T(8,128)S(1)}, f32[64,512]{1,0:T(8,128)S(1)}, u32[]{:S(2)}, u32[]{:S(2)}) collective-permute-start(f32[64,512]{1,0:T(8,128)S(1)} %get-tuple-element.18), channel_id=1, source_target_pairs={{0,24},{8,0},{16,8},{24,16},{1,25},{9,1},{17,9},{25,17},{2,26},{10... | collective-permute-start | bytes 393224 | tf_op jit(solution)/shard_map/ppermute | solution.py:171

commit v13 on v9

--- a/solution.py
+++ b/solution.py
@@ -129,8 +129,8 @@
     totals = xor_sum(payload, "grid")
     fitted = totals[0, :naux]
     weight_projection = totals[1, :naux]
-    exchange_total = totals[0, naux]
-    weight_sum = totals[1, naux]
+    exchange_total = totals[0, naux : naux + 1]
+    weight_sum = totals[1, naux : naux + 1]
     coef_rows = jnp.dot(metric_inv[0], fitted, precision=highest)
     coefficients = in_order(*xor_gather(coef_rows, "grid", 0), 0)
     coef_high, coef_low = split_rows(coefficients)
@@ -138,9 +138,10 @@
         aux_block, jnp.stack([coef_high, coef_low], axis=1), preferred_element_type=jnp.float32
     )
     coulomb = coulomb_parts[:, 0] + coulomb_parts[:, 1]
-    potential_total = jnp.dot(coefficients, weight_projection, precision=highest) + exchange_total
-    average = potential_total / weight_sum
-    potential = live_weight * (coulomb + exchange - average)
+    coulomb_total = jnp.sum(coefficients * weight_projection, axis=0, keepdims=True)
+    potential = live_weight * (
+        coulomb + exchange - coulomb_total / weight_sum - exchange_total / weight_sum
+    )
     weighted_basis = (basis_rows * potential[:, None]).astype(jnp.bfloat16)
     half_rows = frag_basis // lax.axis_size("grid")
     left_first = lax.slice_in_dim(weighted_basis, 0, half_rows * lax.axis_size("grid"), axis=1)

time: 109 us -> 110 us (level)
  transfers between devices with their start and end apart: 20 -> 20, of which waited for: 17 -> 16; matrix products, arithmetic and copies ran while one was open for 9% -> 9% of each run, Pallas kernels for 0% -> 0%
where the time goes in v13:
time: 110 us; the launch traced here: 109 us
  waiting for transfers between devices  34.6 us (31%)
  starting transfers between devices  32.4 us (29%)
  other arithmetic  14.3 us (13%)
  matrix products  12.3 us (11%)
  between operations  9.45 us (9%)
  local copies, waits for them, and re-layouts  6.13 us (6%)
    ppermute x6, waiting for transfers between devices, scatter_step(): lax.ppermute(send, axis, [(i, i ^ 1 << bit) for i in range(size)])  19.2 us
    ppermute x8, starting transfers between devices, xor_gather(): other = lax.ppermute(value, axis, [(i, i ^ 1 << bit) for i in range(size)])  14.9 us
    ppermute x8, waiting for transfers between devices, xor_gather(): other = lax.ppermute(value, axis, [(i, i ^ 1 << bit) for i in range(size)])  9.52 us
    ppermute x6, starting transfers between devices, scatter_step(): lax.ppermute(send, axis, [(i, i ^ 1 << bit) for i in range(size)])  7.49 us
    add x6, other arithmetic, scatter_step(): keep + lax.ppermute(send, axis, [(i, i ^ 1 << bit) for i in range(size)])  6.05 us
    ppermute x3, starting transfers between devices, xor_sum(): lax.ppermute(value, axis, [(i, i ^ step) for i in range(size)])  5.49 us
    ppermute x3, waiting for transfers between devices, xor_sum(): lax.ppermute(value, axis, [(i, i ^ step) for i in range(size)])  4.52 us
    ppermute x3, starting transfers between devices, shards(): lax.ppermute(sent, 'dimer', [(i, (i + shift) % groups) for i in range(gro...  4.49 us
  transfers between devices with their start and end apart: 20, of which 16 were waited for; matrix products, arithmetic and copies ran while one was open for 9% of the time, Pallas kernels for 0%

profile of v13, /device:TPU:0, one launch (start us, length us, event | category | flops | bytes accessed | tf_op | source)
XLA Modules:
  0.0 109.0 jit_solution(2034614285568974964)
XLA Ops:
  0.6 0.9 copy.33
  1.5 3.1 %collective-permute-start = (bf16[1,64,128]{2,0,1:T(2,128)(2,1)S(1)}, bf16[1,64,128]{2,0,1:T(2,128)(2,1)S(1)}, u32[]{:S(2)}, u32[]{:S(2)}) collective-permute-start(bf16[1,64,128]{2,0,1:T(2,128)(2,1)S(1)} %copy.33), channel_id=1, source_target_pairs={{0,16},{8,24},{16,0},{24,8},{1,17},{9,25},{17,1},{25,9},{2,18},{10... | collective-permute-start | bytes 49160 | tf_op jit(solution)/shard_map/ppermute | solution.py:40
  5.3 1.2 %collective-permute-done = bf16[1,64,128]{2,0,1:T(2,128)(2,1)S(1)} collective-permute-done((bf16[1,64,128]{2,0,1:T(2,128)(2,1)S(1)}, bf16[1,64,128]{2,0,1:T(2,128)(2,1)S(1)}, u32[]{:S(2)}, u32[]{:S(2)}) %collective-permute-start) | collective-permute-done | bytes 16416 | tf_op jit(solution)/shard_map/ppermute | solution.py:40
  6.6 2.1 %collective-permute-start.1 = (bf16[2,64,128]{2,0,1:T(2,128)(2,1)S(1)}, bf16[2,64,128]{2,0,1:T(2,128)(2,1)S(1)}, u32[]{:S(2)}, u32[]{:S(2)}) collective-permute-start(bf16[2,64,128]{2,0,1:T(2,128)(2,1)S(1)} %pad_maximum_fusion.5), channel_id=1, source_target_pairs={{0,8},{8,0},{16,24},{24,16},{1,9},{9,1},{17,25},{25,17},{2,10},{10... | collective-permute-start | bytes 98312 | tf_op jit(solution)/shard_map/ppermute | solution.py:40
  8.6 0.9 fusion.51
  9.5 1.1 collective-permute-done.1
  10.8 3.2 %collective-permute-start.2 = (bf16[2,64,128]{2,0,1:T(2,128)(2,1)S(1)}, bf16[2,64,128]{2,0,1:T(2,128)(2,1)S(1)}, u32[]{:S(2)}, u32[]{:S(2)}) collective-permute-start(bf16[2,64,128]{2,0,1:T(2,128)(2,1)S(1)} %convolution_convert_fusion), channel_id=1, source_target_pairs={{0,4},{1,5},{2,6},{3,7},{4,0},{5,1},{6,2},{7,3},{8,12},{9,13},{10,... | collective-permute-start | bytes 98312 | tf_op jit(solution)/shard_map/ppermute | solution.py:40
  14.0 2.0 %collective-permute-done.2 = bf16[2,64,128]{2,0,1:T(2,128)(2,1)S(1)} collective-permute-done((bf16[2,64,128]{2,0,1:T(2,128)(2,1)S(1)}, bf16[2,64,128]{2,0,1:T(2,128)(2,1)S(1)}, u32[]{:S(2)}, u32[]{:S(2)}) %collective-permute-start.2) | collective-permute-done | bytes 32800 | tf_op jit(solution)/shard_map/ppermute | solution.py:40
  16.0 1.9 %collective-permute-start.3 = (bf16[2,128,128]{2,0,1:T(2,128)(2,1)S(1)}, bf16[2,128,128]{2,0,1:T(2,128)(2,1)S(1)}, u32[]{:S(2)}, u32[]{:S(2)}) collective-permute-start(bf16[2,128,128]{2,0,1:T(2,128)(2,1)S(1)} %pad_maximum_fusion.4), channel_id=1, source_target_pairs={{0,2},{1,3},{2,0},{3,1},{4,6},{5,7},{6,4},{7,5},{8,10},{9,11},{10,... | collective-permute-start | bytes 196616 | tf_op jit(solution)/shard_map/ppermute | solution.py:40
  18.6 1.8 %collective-permute-done.3 = bf16[2,128,128]{2,0,1:T(2,128)(2,1)S(1)} collective-permute-done((bf16[2,128,128]{2,0,1:T(2,128)(2,1)S(1)}, bf16[2,128,128]{2,0,1:T(2,128)(2,1)S(1)}, u32[]{:S(2)}, u32[]{:S(2)}) %collective-permute-start.3) | collective-permute-done | bytes 65568 | tf_op jit(solution)/shard_map/ppermute | solution.py:40
  21.3 0.7 reduce.1
  23.2 2.8 %fusion.13 = f32[1280]{0:T(1024)S(1)} fusion(bf16[512,128]{1,0:T(8,128)(2,1)S(1)} %bitcast.116, bf16[512,128]{1,0:T(8,128)(2,1)S(1)} %bitcast.115, bf16[1,1280,1024]{2,1,0:T(8,128)(2,1)} %param.11), kind=kOutput, calls=%fused_computation.19 | convolution fusion | flops 673839872 | bytes 2888704 | tf_op jit(solution)/shard_map/dot_general | solution.py:116
  26.0 0.7 multiply_reduce_fusion.1
  26.8 0.8 fusion.2
  27.6 1.3 %pad_maximum_fusion.11 = f32[2]{0:T(128)S(1)} fusion(f32[1]{0:T(128)} %bitcast.12, f32[1]{0:T(128)} %bitcast.11), kind=kLoop, calls=%fused_computation.106 | loop fusion | flops 2 | bytes 16 | tf_op jit(solution)/shard_map/stack | solution.py:124
  29.6 0.8 collective-permute-done.5
  30.5 1.9 %collective-permute-start.6 = (f32[2,2176]{1,0:T(2,128)S(1)}, f32[2,2176]{1,0:T(2,128)S(1)}, u32[]{:S(2)}, u32[]{:S(2)}) collective-permute-start(f32[2,2176]{1,0:T(2,128)S(1)} %fusion.61), channel_id=1, source_target_pairs={{0,2},{1,3},{2,0},{3,1},{4,6},{5,7},{6,4},{7,5},{8,10},{9,11},{10,... | collective-permute-start | bytes 52232 | tf_op jit(solution)/shard_map/ppermute | solution.py:27
  32.3 1.9 %collective-permute-done.6 = f32[2,2176]{1,0:T(2,128)S(1)} collective-permute-done((f32[2,2176]{1,0:T(2,128)S(1)}, f32[2,2176]{1,0:T(2,128)S(1)}, u32[]{:S(2)}, u32[]{:S(2)}) %collective-permute-start.6) | collective-permute-done | bytes 17440 | tf_op jit(solution)/shard_map/ppermute | solution.py:27
  34.3 3.1 %collective-permute-start.7 = (f32[2,2176]{1,0:T(2,128)S(1)}, f32[2,2176]{1,0:T(2,128)S(1)}, u32[]{:S(2)}, u32[]{:S(2)}) collective-permute-start(f32[2,2176]{1,0:T(2,128)S(1)} %add.139), channel_id=1, source_target_pairs={{0,4},{1,5},{2,6},{3,7},{4,0},{5,1},{6,2},{7,3},{8,12},{9,13},{10,... | collective-permute-start | bytes 52232 | tf_op jit(solution)/shard_map/ppermute | solution.py:27
  37.3 1.7 %collective-permute-done.7 = f32[2,2176]{1,0:T(2,128)S(1)} collective-permute-done((f32[2,2176]{1,0:T(2,128)S(1)}, f32[2,2176]{1,0:T(2,128)S(1)}, u32[]{:S(2)}, u32[]{:S(2)}) %collective-permute-start.7) | collective-permute-done | bytes 17440 | tf_op jit(solution)/shard_map/ppermute | solution.py:27
  39.1 1.7 %fusion.7 = f32[1,256]{1,0:T(1,128)S(1)} fusion(f32[1,256,2048]{2,1,0:T(8,128)S(1)} %copy-done, f32[2,2176]{1,0:T(2,128)S(1)} %add.140), kind=kOutput, calls=%fused_computation.13 | convolution fusion | flops 6291456 | bytes 2106368 | tf_op jit(solution)/shard_map/dot_general | solution.py:134
  40.8 2.9 %collective-permute-start.8 = (f32[256]{0:T(256)S(1)}, f32[256]{0:T(256)S(1)}, u32[]{:S(2)}, u32[]{:S(2)}) collective-permute-start(f32[256]{0:T(256)S(1)} %bitcast.121), channel_id=1, source_target_pairs={{0,4},{1,5},{2,6},{3,7},{4,0},{5,1},{6,2},{7,3},{8,12},{9,13},{10,... | collective-permute-start | bytes 3080 | tf_op jit(solution)/shard_map/ppermute | solution.py:40
  43.8 1.6 %collective-permute-done.8 = f32[256]{0:T(256)S(1)} collective-permute-done((f32[256]{0:T(256)S(1)}, f32[256]{0:T(256)S(1)}, u32[]{:S(2)}, u32[]{:S(2)}) %collective-permute-start.8) | collective-permute-done | bytes 1056 | tf_op jit(solution)/shard_map/ppermute | solution.py:40
  45.3 1.7 %collective-permute-start.9 = (f32[512]{0:T(512)S(1)}, f32[512]{0:T(512)S(1)}, u32[]{:S(2)}, u32[]{:S(2)}) collective-permute-start(f32[512]{0:T(512)S(1)} %pad_maximum_fusion.10), channel_id=1, source_target_pairs={{0,2},{1,3},{2,0},{3,1},{4,6},{5,7},{6,4},{7,5},{8,10},{9,11},{10,... | collective-permute-start | bytes 6152 | tf_op jit(solution)/shard_map/ppermute | solution.py:40
  47.1 1.9 %collective-permute-done.9 = f32[512]{0:T(512)S(1)} collective-permute-done((f32[512]{0:T(512)S(1)}, f32[512]{0:T(512)S(1)}, u32[]{:S(2)}, u32[]{:S(2)}) %collective-permute-start.9) | collective-permute-done | bytes 2080 | tf_op jit(solution)/shard_map/ppermute | solution.py:40
  53.5 4.1 %fusion.4 = f32[1280,2]{0,1:T(2,128)S(1)} fusion(bf16[1,1280,2048]{2,1,0:T(8,128)(2,1)} %param.12, bf16[2048,1]{0,1:T(2,128)(2,1)S(1)} %stack.34, bf16[2048,1]{0,1:T(2,128)(2,1)S(1)} %bitcast.119), kind=kOutput, calls=%fused_computation.12 | convolution fusion | flops 10502144 | bytes 5261312 | tf_op jit(solution)/shard_map/dot_general | solution.py:137
  58.2 0.9 fusion.9
  59.1 0.9 fusion.11
  60.8 0.9 fusion.14
  61.7 1.4 %collective-permute-done.11 = f32[4,64,2,512]{3,1,2,0:T(8,128)S(1)} collective-permute-done((f32[4,64,2,512]{3,1,2,0:T(8,128)S(1)}, f32[4,64,2,512]{3,1,2,0:T(8,128)S(1)}, u32[]{:S(2)}, u32[]{:S(2)}) %collective-permute-start.11) | collective-permute-done | bytes 1048608 | tf_op jit(solution)/shard_map/ppermute | solution.py:66
  63.3 0.9 dynamic-slice_bitcast_fusion
  64.6 0.8 dynamic-slice_bitcast_fusion.1
  65.4 1.7 %collective-permute-start.12 = (f32[2,64,2,512]{3,1,2,0:T(8,128)}, f32[2,64,2,512]{3,1,2,0:T(8,128)}, u32[]{:S(2)}, u32[]{:S(2)}) collective-permute-start(f32[2,64,2,512]{3,1,2,0:T(8,128)} %dynamic-slice_bitcast_fusion.1), channel_id=1, source_target_pairs={{0,2},{1,3},{2,0},{3,1},{4,6},{5,7},{6,4},{7,5},{8,10},{9,11},{10,... | collective-permute-start | bytes 1572872 | tf_op jit(solution)/shard_map/ppermute | solution.py:66
  67.2 1.3 %bitcast_add_fusion.1 = f32[4,64,512]{2,1,0:T(8,128)S(1)} fusion(f32[4,64,512]{2,1,0:T(8,128)} %collective-permute-done.17, f32[4,2,64,512]{3,2,1,0:T(8,128)} %bitcast.114, s32[]{:T(128)S(6)} %select_n.153), kind=kLoop, calls=%fused_computation.38 | loop fusion | flops 131072 | bytes 1572868 | tf_op jit(solution)/shard_map/add | solution.py:66
  68.5 11.3 %collective-permute-done.12 = f32[2,64,2,512]{3,1,2,0:T(8,128)} collective-permute-done((f32[2,64,2,512]{3,1,2,0:T(8,128)}, f32[2,64,2,512]{3,1,2,0:T(8,128)}, u32[]{:S(2)}, u32[]{:S(2)}) %collective-permute-start.12) | collective-permute-done | bytes 524320 | tf_op jit(solution)/shard_map/ppermute | solution.py:66
  79.7 1.9 %bitcast_add_fusion.2 = f32[2,64,2,512]{3,1,2,0:T(8,128)} fusion(f32[2,64,2,512]{3,1,2,0:T(8,128)} %collective-permute-done.12, f32[2,2,64,2,512]{4,2,3,1,0:T(8,128)S(1)} %bitcast.101, s32[]{:T(128)S(6)} %select_n.155), kind=kLoop, calls=%fused_computation.39 | loop fusion | flops 131072 | bytes 1572868 | tf_op jit(solution)/shard_map/add | solution.py:66
  81.7 1.8 %collective-permute-start.18 = (f32[2,64,512]{2,1,0:T(8,128)S(1)}, f32[2,64,512]{2,1,0:T(8,128)S(1)}, u32[]{:S(2)}, u32[]{:S(2)}) collective-permute-start(f32[2,64,512]{2,1,0:T(8,128)S(1)} %dynamic-slice_bitcast_fusion.2), channel_id=1, source_target_pairs={{0,2},{1,3},{2,0},{3,1},{4,6},{5,7},{6,4},{7,5},{8,10},{9,11},{10,... | collective-permute-start | bytes 786440 | tf_op jit(solution)/shard_map/ppermute | solution.py:66
  83.4 1.0 constant_dynamic-slice_fusion.1
  84.4 3.0 %collective-permute-start.13 = (f32[1,64,2,512]{3,1,2,0:T(8,128)S(1)}, f32[1,64,2,512]{3,1,2,0:T(8,128)S(1)}, u32[]{:S(2)}, u32[]{:S(2)}) collective-permute-start(f32[1,64,2,512]{3,1,2,0:T(8,128)S(1)} %constant_dynamic-slice_fusion.1), channel_id=1, source_target_pairs={{0,4},{1,5},{2,6},{3,7},{4,0},{5,1},{6,2},{7,3},{8,12},{9,13},{10,... | collective-permute-start | bytes 786440 | tf_op jit(solution)/shard_map/ppermute | solution.py:66
  93.6 1.0 bitcast_add_fusion.3
  94.6 4.6 %collective-permute-done.13 = f32[1,64,2,512]{3,1,2,0:T(8,128)S(1)} collective-permute-done((f32[1,64,2,512]{3,1,2,0:T(8,128)S(1)}, f32[1,64,2,512]{3,1,2,0:T(8,128)S(1)}, u32[]{:S(2)}, u32[]{:S(2)}) %collective-permute-start.13) | collective-permute-done | bytes 262176 | tf_op jit(solution)/shard_map/ppermute | solution.py:66
  99.2 1.0 dynamic-slice_add_fusion
  100.3 1.5 %collective-permute-start.14 = (f32[64,512]{1,0:T(8,128)S(1)}, f32[64,512]{1,0:T(8,128)S(1)}, u32[]{:S(2)}, u32[]{:S(2)}) collective-permute-start(f32[64,512]{1,0:T(8,128)S(1)} %get-tuple-element.16), channel_id=1, source_target_pairs={{0,8},{8,16},{16,24},{24,0},{1,9},{9,17},{17,25},{25,1},{2,10},{10... | collective-permute-start | bytes 393224 | tf_op jit(solution)/shard_map/ppermute | solution.py:171
  101.8 1.5 %collective-permute-start.15 = (f32[64,512]{1,0:T(8,128)S(1)}, f32[64,512]{1,0:T(8,128)S(1)}, u32[]{:S(2)}, u32[]{:S(2)}) collective-permute-start(f32[64,512]{1,0:T(8,128)S(1)} %get-tuple-element.17), channel_id=1, source_target_pairs={{0,16},{8,24},{16,0},{24,8},{1,17},{9,25},{17,1},{25,9},{2,18},{10... | collective-permute-start | bytes 393224 | tf_op jit(solution)/shard_map/ppermute | solution.py:171
  103.4 1.4 %collective-permute-start.16 = (f32[64,512]{1,0:T(8,128)S(1)}, f32[64,512]{1,0:T(8,128)S(1)}, u32[]{:S(2)}, u32[]{:S(2)}) collective-permute-start(f32[64,512]{1,0:T(8,128)S(1)} %get-tuple-element.18), channel_id=1, source_target_pairs={{0,24},{8,0},{16,8},{24,16},{1,25},{9,1},{17,9},{25,17},{2,26},{10... | collective-permute-start | bytes 393224 | tf_op jit(solution)/shard_map/ppermute | solution.py:171
  104.8 1.5 %collective-permute-done.19 = f32[1,64,512]{2,1,0:T(8,128)S(1)} collective-permute-done((f32[1,64,512]{2,1,0:T(8,128)S(1)}, f32[1,64,512]{2,1,0:T(8,128)S(1)}, u32[]{:S(2)}, u32[]{:S(2)}) %collective-permute-start.19) | collective-permute-done | bytes 131104 | tf_op jit(solution)/shard_map/ppermute | solution.py:66
  107.6 0.7 collective-permute-done.16
  108.3 0.7 fusion.32
  (72 shorter events, 10.3 us)
Async XLA Ops:
  0.6 38.5 %copy-start = (f32[1,256,2048]{2,1,0:T(8,128)S(1)}, f32[1,256,2048]{2,1,0:T(8,128)}, u32[]{:S(2)}) copy-start(f32[1,256,2048]{2,1,0:T(8,128)} %param.18) | copy-start | bytes 6291460
  1.5 5.0 %collective-permute-start = (bf16[1,64,128]{2,0,1:T(2,128)(2,1)S(1)}, bf16[1,64,128]{2,0,1:T(2,128)(2,1)S(1)}, u32[]{:S(2)}, u32[]{:S(2)}) collective-permute-start(bf16[1,64,128]{2,0,1:T(2,128)(2,1)S(1)} %copy.33), channel_id=1, source_target_pairs={{0,16},{8,24},{16,0},{24,8},{1,17},{9,25},{17,1},{25,9},{2,18},{10... | collective-permute-start | bytes 49160 | tf_op jit(solution)/shard_map/ppermute | solution.py:40
  6.6 4.0 %collective-permute-start.1 = (bf16[2,64,128]{2,0,1:T(2,128)(2,1)S(1)}, bf16[2,64,128]{2,0,1:T(2,128)(2,1)S(1)}, u32[]{:S(2)}, u32[]{:S(2)}) collective-permute-start(bf16[2,64,128]{2,0,1:T(2,128)(2,1)S(1)} %pad_maximum_fusion.5), channel_id=1, source_target_pairs={{0,8},{8,0},{16,24},{24,16},{1,9},{9,1},{17,25},{25,17},{2,10},{10... | collective-permute-start | bytes 98312 | tf_op jit(solution)/shard_map/ppermute | solution.py:40
  10.8 5.2 %collective-permute-start.2 = (bf16[2,64,128]{2,0,1:T(2,128)(2,1)S(1)}, bf16[2,64,128]{2,0,1:T(2,128)(2,1)S(1)}, u32[]{:S(2)}, u32[]{:S(2)}) collective-permute-start(bf16[2,64,128]{2,0,1:T(2,128)(2,1)S(1)} %convolution_convert_fusion), channel_id=1, source_target_pairs={{0,4},{1,5},{2,6},{3,7},{4,0},{5,1},{6,2},{7,3},{8,12},{9,13},{10,... | collective-permute-start | bytes 98312 | tf_op jit(solution)/shard_map/ppermute | solution.py:40
  16.0 4.3 %collective-permute-start.3 = (bf16[2,128,128]{2,0,1:T(2,128)(2,1)S(1)}, bf16[2,128,128]{2,0,1:T(2,128)(2,1)S(1)}, u32[]{:S(2)}, u32[]{:S(2)}) collective-permute-start(bf16[2,128,128]{2,0,1:T(2,128)(2,1)S(1)} %pad_maximum_fusion.4), channel_id=1, source_target_pairs={{0,2},{1,3},{2,0},{3,1},{4,6},{5,7},{6,4},{7,5},{8,10},{9,11},{10,... | collective-permute-start | bytes 196616 | tf_op jit(solution)/shard_map/ppermute | solution.py:40
  20.6 1.5 %collective-permute-start.4 = (bf16[2,256,128]{2,0,1:T(2,128)(2,1)S(1)}, bf16[2,256,128]{2,0,1:T(2,128)(2,1)S(1)}, u32[]{:S(2)}, u32[]{:S(2)}) collective-permute-start(bf16[2,256,128]{2,0,1:T(2,128)(2,1)S(1)} %pad_maximum_fusion.1), channel_id=1, source_target_pairs={{0,1},{1,0},{2,3},{3,2},{4,5},{5,4},{6,7},{7,6},{8,9},{9,8},{10,11... | collective-permute-start | bytes 393224 | tf_op jit(solution)/shard_map/ppermute | solution.py:40
  23.2 3.5 %copy-start.5 = (f32[1,1280]{1,0:T(1,128)S(1)}, f32[1,1280]{1,0:T(1,128)}, u32[]{:S(2)}) copy-start(f32[1,1280]{1,0:T(1,128)} %param.17) | copy-start | bytes 15364
  23.2 3.6 %copy-start.1 = (bf16[1,1280,2048]{2,1,0:T(8,128)(2,1)S(1)}, bf16[1,1280,2048]{2,1,0:T(8,128)(2,1)}, u32[]{:S(2)}) copy-start(bf16[1,1280,2048]{2,1,0:T(8,128)(2,1)} %param.12) | copy-start | bytes 15728644
  29.0 1.4 %collective-permute-start.5 = (f32[2,2176]{1,0:T(2,128)S(1)}, f32[2,2176]{1,0:T(2,128)S(1)}, u32[]{:S(2)}, u32[]{:S(2)}) collective-permute-start(f32[2,2176]{1,0:T(2,128)S(1)} %pad_maximum_fusion.6), channel_id=1, source_target_pairs={{0,1},{1,0},{2,3},{3,2},{4,5},{5,4},{6,7},{7,6},{8,9},{9,8},{10,11... | collective-permute-start | bytes 52232 | tf_op jit(solution)/shard_map/ppermute | solution.py:27
  30.5 3.8 %collective-permute-start.6 = (f32[2,2176]{1,0:T(2,128)S(1)}, f32[2,2176]{1,0:T(2,128)S(1)}, u32[]{:S(2)}, u32[]{:S(2)}) collective-permute-start(f32[2,2176]{1,0:T(2,128)S(1)} %fusion.61), channel_id=1, source_target_pairs={{0,2},{1,3},{2,0},{3,1},{4,6},{5,7},{6,4},{7,5},{8,10},{9,11},{10,... | collective-permute-start | bytes 52232 | tf_op jit(solution)/shard_map/ppermute | solution.py:27
  34.3 4.8 %collective-permute-start.7 = (f32[2,2176]{1,0:T(2,128)S(1)}, f32[2,2176]{1,0:T(2,128)S(1)}, u32[]{:S(2)}, u32[]{:S(2)}) collective-permute-start(f32[2,2176]{1,0:T(2,128)S(1)} %add.139), channel_id=1, source_target_pairs={{0,4},{1,5},{2,6},{3,7},{4,0},{5,1},{6,2},{7,3},{8,12},{9,13},{10,... | collective-permute-start | bytes 52232 | tf_op jit(solution)/shard_map/ppermute | solution.py:27
  40.8 4.5 %collective-permute-start.8 = (f32[256]{0:T(256)S(1)}, f32[256]{0:T(256)S(1)}, u32[]{:S(2)}, u32[]{:S(2)}) collective-permute-start(f32[256]{0:T(256)S(1)} %bitcast.121), channel_id=1, source_target_pairs={{0,4},{1,5},{2,6},{3,7},{4,0},{5,1},{6,2},{7,3},{8,12},{9,13},{10,... | collective-permute-start | bytes 3080 | tf_op jit(solution)/shard_map/ppermute | solution.py:40
  45.3 3.6 %collective-permute-start.9 = (f32[512]{0:T(512)S(1)}, f32[512]{0:T(512)S(1)}, u32[]{:S(2)}, u32[]{:S(2)}) collective-permute-start(f32[512]{0:T(512)S(1)} %pad_maximum_fusion.10), channel_id=1, source_target_pairs={{0,2},{1,3},{2,0},{3,1},{4,6},{5,7},{6,4},{7,5},{8,10},{9,11},{10,... | collective-permute-start | bytes 6152 | tf_op jit(solution)/shard_map/ppermute | solution.py:40
  48.9 1.9 %collective-permute-start.10 = (f32[1024]{0:T(1024)S(1)}, f32[1024]{0:T(1024)S(1)}, u32[]{:S(2)}, u32[]{:S(2)}) collective-permute-start(f32[1024]{0:T(1024)S(1)} %pad_maximum_fusion.9), channel_id=1, source_target_pairs={{0,1},{1,0},{2,3},{3,2},{4,5},{5,4},{6,7},{7,6},{8,9},{9,8},{10,11... | collective-permute-start | bytes 12296 | tf_op jit(solution)/shard_map/ppermute | solution.py:40
  53.5 4.2 %copy-start.2 = (bf16[1,1280,1024]{2,1,0:T(8,128)(2,1)S(1)}, bf16[1,1280,1024]{2,1,0:T(8,128)(2,1)}, u32[]{:S(2)}) copy-start(bf16[1,1280,1024]{2,1,0:T(8,128)(2,1)} %param.11) | copy-start | bytes 7864324
  60.3 2.9 %collective-permute-start.11 = (f32[4,64,2,512]{3,1,2,0:T(8,128)S(1)}, f32[4,64,2,512]{3,1,2,0:T(8,128)S(1)}, u32[]{:S(2)}, u32[]{:S(2)}) collective-permute-start(f32[4,64,2,512]{3,1,2,0:T(8,128)S(1)} %bitcast.111), channel_id=1, source_target_pairs={{0,1},{1,0},{2,3},{3,2},{4,5},{5,4},{6,7},{7,6},{8,9},{9,8},{10,11... | collective-permute-start | bytes 3145736 | tf_op jit(solution)/shard_map/ppermute | solution.py:66
  61.7 1.6 %copy-start.4 = (f32[512,512]{1,0:T(8,128)}, f32[512,512]{1,0:T(8,128)S(1)}, u32[]{:S(2)}) copy-start(f32[512,512]{1,0:T(8,128)S(1)} %fusion.14) | copy-start | bytes 3145732
  64.2 3.0 %collective-permute-start.17 = (f32[4,64,512]{2,1,0:T(8,128)}, f32[4,64,512]{2,1,0:T(8,128)}, u32[]{:S(2)}, u32[]{:S(2)}) collective-permute-start(f32[4,64,512]{2,1,0:T(8,128)} %dynamic-slice_bitcast_fusion), channel_id=1, source_target_pairs={{0,1},{1,0},{2,3},{3,2},{4,5},{5,4},{6,7},{7,6},{8,9},{9,8},{10,11... | collective-permute-start | bytes 1572872 | tf_op jit(solution)/shard_map/ppermute | solution.py:66
  64.6 22.8 %copy-start.6 = (s32[1,2]{1,0:T(1,128)S(1)}, s32[1,2]{1,0:T(1,128)}, u32[]{:S(2)}) copy-start(s32[1,2]{1,0:T(1,128)} %param.15) | copy-start | bytes 28
  65.4 14.3 %collective-permute-start.12 = (f32[2,64,2,512]{3,1,2,0:T(8,128)}, f32[2,64,2,512]{3,1,2,0:T(8,128)}, u32[]{:S(2)}, u32[]{:S(2)}) collective-permute-start(f32[2,64,2,512]{3,1,2,0:T(8,128)} %dynamic-slice_bitcast_fusion.1), channel_id=1, source_target_pairs={{0,2},{1,3},{2,0},{3,1},{4,6},{5,7},{6,4},{7,5},{8,10},{9,11},{10,... | collective-permute-start | bytes 1572872 | tf_op jit(solution)/shard_map/ppermute | solution.py:66
  68.4 13.2 %copy-start.3 = (f32[4,64,512]{2,1,0:T(8,128)}, f32[4,64,512]{2,1,0:T(8,128)S(1)}, u32[]{:S(2)}) copy-start(f32[4,64,512]{2,1,0:T(8,128)S(1)} %bitcast_add_fusion.1) | copy-start | bytes 1572868
  81.7 12.0 %collective-permute-start.18 = (f32[2,64,512]{2,1,0:T(8,128)S(1)}, f32[2,64,512]{2,1,0:T(8,128)S(1)}, u32[]{:S(2)}, u32[]{:S(2)}) collective-permute-start(f32[2,64,512]{2,1,0:T(8,128)S(1)} %dynamic-slice_bitcast_fusion.2), channel_id=1, source_target_pairs={{0,2},{1,3},{2,0},{3,1},{4,6},{5,7},{6,4},{7,5},{8,10},{9,11},{10,... | collective-permute-start | bytes 786440 | tf_op jit(solution)/shard_map/ppermute | solution.py:66
  84.4 14.7 %collective-permute-start.13 = (f32[1,64,2,512]{3,1,2,0:T(8,128)S(1)}, f32[1,64,2,512]{3,1,2,0:T(8,128)S(1)}, u32[]{:S(2)}, u32[]{:S(2)}) collective-permute-start(f32[1,64,2,512]{3,1,2,0:T(8,128)S(1)} %constant_dynamic-slice_fusion.1), channel_id=1, source_target_pairs={{0,4},{1,5},{2,6},{3,7},{4,0},{5,1},{6,2},{7,3},{8,12},{9,13},{10,... | collective-permute-start | bytes 786440 | tf_op jit(solution)/shard_map/ppermute | solution.py:66
  100.2 6.2 %collective-permute-start.19 = (f32[1,64,512]{2,1,0:T(8,128)S(1)}, f32[1,64,512]{2,1,0:T(8,128)S(1)}, u32[]{:S(2)}, u32[]{:S(2)}) collective-permute-start(f32[1,64,512]{2,1,0:T(8,128)S(1)} %constant_dynamic-slice_fusion), channel_id=1, source_target_pairs={{0,4},{1,5},{2,6},{3,7},{4,0},{5,1},{6,2},{7,3},{8,12},{9,13},{10,... | collective-permute-start | bytes 393224 | tf_op jit(solution)/shard_map/ppermute | solution.py:66
  100.3 6.7 %collective-permute-start.14 = (f32[64,512]{1,0:T(8,128)S(1)}, f32[64,512]{1,0:T(8,128)S(1)}, u32[]{:S(2)}, u32[]{:S(2)}) collective-permute-start(f32[64,512]{1,0:T(8,128)S(1)} %get-tuple-element.16), channel_id=1, source_target_pairs={{0,8},{8,16},{16,24},{24,0},{1,9},{9,17},{17,25},{25,1},{2,10},{10... | collective-permute-start | bytes 393224 | tf_op jit(solution)/shard_map/ppermute | solution.py:171
  101.8 5.8 %collective-permute-start.15 = (f32[64,512]{1,0:T(8,128)S(1)}, f32[64,512]{1,0:T(8,128)S(1)}, u32[]{:S(2)}, u32[]{:S(2)}) collective-permute-start(f32[64,512]{1,0:T(8,128)S(1)} %get-tuple-element.17), channel_id=1, source_target_pairs={{0,16},{8,24},{16,0},{24,8},{1,17},{9,25},{17,1},{25,9},{2,18},{10... | collective-permute-start | bytes 393224 | tf_op jit(solution)/shard_map/ppermute | solution.py:171
  103.4 5.0 %collective-permute-start.16 = (f32[64,512]{1,0:T(8,128)S(1)}, f32[64,512]{1,0:T(8,128)S(1)}, u32[]{:S(2)}, u32[]{:S(2)}) collective-permute-start(f32[64,512]{1,0:T(8,128)S(1)} %get-tuple-element.18), channel_id=1, source_target_pairs={{0,24},{8,0},{16,8},{24,16},{1,25},{9,1},{17,9},{25,17},{2,26},{10... | collective-permute-start | bytes 393224 | tf_op jit(solution)/shard_map/ppermute | solution.py:171

commit v14 on v9

--- a/solution.py
+++ b/solution.py
@@ -131,7 +131,7 @@
     weight_projection = totals[1, :naux]
     exchange_total = totals[0, naux]
     weight_sum = totals[1, naux]
-    coef_rows = jnp.dot(metric_inv[0], fitted, precision=highest)
+    coef_rows = jnp.sum(metric_inv[0] * fitted[None, :], axis=1)
     coefficients = in_order(*xor_gather(coef_rows, "grid", 0), 0)
     coef_high, coef_low = split_rows(coefficients)
     coulomb_parts = jnp.dot(
@@ -165,11 +165,13 @@
         )
 
     frag_fock = piece(me)
+    paired = groups & (groups - 1) == 0
     for shift in range(1, groups):
-        sent = piece(lax.rem(me + shift, groups))
-        frag_fock = frag_fock + lax.ppermute(
-            sent, "dimer", [(i, (i + shift) % groups) for i in range(groups)]
-        )
+        if paired:
+            dest, pairs = jnp.bitwise_xor(me, shift), [(i, i ^ shift) for i in range(groups)]
+        else:
+            dest, pairs = lax.rem(me + shift, groups), [(i, (i + shift) % groups) for i in range(groups)]
+        frag_fock = frag_fock + lax.ppermute(piece(dest), "dimer", pairs)
     return (frag_fock[None], own_cross[None])
 
 

time: 109 us -> 102 us (0.936)
  matrix products: 12.3 us -> 8.5 us
  other arithmetic: 14.3 us -> 10.6 us
  waiting for transfers between devices: 35.6 us -> 38.1 us
  local copies, waits for them, and re-layouts: 6.13 us -> 4.37 us
    add x6, other arithmetic: 6.05 us -> 2.16 us  [scatter_step(): keep + lax.ppermute(send, axis, [(i, i ^ 1 << bit) for i in range(size)])]
    squeeze x5, local copies, waits for them, and re-layouts: 2.71 us -> 0.14 us  [scatter_step(): send = lax.dynamic_index_in_dim(pairs, 1 - mine, axis=1, keepdims=False)]
    ppermute x6, waiting for transfers between devices: 19.8 us -> 21.8 us  [scatter_step(): lax.ppermute(send, axis, [(i, i ^ 1 << bit) for i in range(size)])]
    dot_general x1, matrix products: 2.8 us -> 0.91 us  [shards(): jnp.dot(basis_rows, block_factors, preferred_element_type=jnp.float32)]
    dot_general x1 -> x0, matrix products: 1.72 us -> none  [shards(): coef_rows = jnp.dot(metric_inv[0], fitted, precision=highest)]
  transfers between devices with their start and end apart: 20 -> 20, of which waited for: 17 -> 16; matrix products, arithmetic and copies ran while one was open for 9% -> 7% of each run, Pallas kernels for 0% -> 0%
where the time goes in v14:
time: 102 us; the launch traced here: 101 us
  waiting for transfers between devices  38.1 us (37%)
  starting transfers between devices  31 us (30%)
  other arithmetic  10.6 us (10%)
  between operations  8.69 us (9%)
  matrix products  8.5 us (8%)
  local copies, waits for them, and re-layouts  4.37 us (4%)
    ppermute x6, waiting for transfers between devices, scatter_step(): lax.ppermute(send, axis, [(i, i ^ 1 << bit) for i in range(size)])  21.8 us
    ppermute x8, starting transfers between devices, xor_gather(): other = lax.ppermute(value, axis, [(i, i ^ 1 << bit) for i in range(size)])  14.9 us
    ppermute x8, waiting for transfers between devices, xor_gather(): other = lax.ppermute(value, axis, [(i, i ^ 1 << bit) for i in range(size)])  10.1 us
    ppermute x6, starting transfers between devices, scatter_step(): lax.ppermute(send, axis, [(i, i ^ 1 << bit) for i in range(size)])  7.08 us
    ppermute x3, starting transfers between devices, xor_sum(): lax.ppermute(value, axis, [(i, i ^ step) for i in range(size)])  5.49 us
    ppermute x3, waiting for transfers between devices, xor_sum(): lax.ppermute(value, axis, [(i, i ^ step) for i in range(size)])  4.52 us
    dot_general x1, matrix products, shards(): jnp.dot(aux_block, jnp.stack([coef_high, coef_low], axis=1), preferred_el...  3.94 us
    ppermute x3, starting transfers between devices, shards(): frag_fock = frag_fock + lax.ppermute(piece(dest), 'dimer', pairs)  3.55 us
  transfers between devices with their start and end apart: 20, of which 16 were waited for; matrix products, arithmetic and copies ran while one was open for 7% of the time, Pallas kernels for 0%

profile of v14, /device:TPU:0, one launch (start us, length us, event | category | flops | bytes accessed | tf_op | source)
XLA Modules:
  0.0 101.3 jit_solution(4546360484127202932)
XLA Ops:
  0.6 0.9 copy.33
  1.5 3.1 %collective-permute-start = (bf16[1,64,128]{2,0,1:T(2,128)(2,1)S(1)}, bf16[1,64,128]{2,0,1:T(2,128)(2,1)S(1)}, u32[]{:S(2)}, u32[]{:S(2)}) collective-permute-start(bf16[1,64,128]{2,0,1:T(2,128)(2,1)S(1)} %copy.33), channel_id=1, source_target_pairs={{0,16},{8,24},{16,0},{24,8},{1,17},{9,25},{17,1},{25,9},{2,18},{10... | collective-permute-start | bytes 49160 | tf_op jit(solution)/shard_map/ppermute | solution.py:40
  4.6 0.7 broadcast_xor_fusion
  5.3 1.2 %collective-permute-done = bf16[1,64,128]{2,0,1:T(2,128)(2,1)S(1)} collective-permute-done((bf16[1,64,128]{2,0,1:T(2,128)(2,1)S(1)}, bf16[1,64,128]{2,0,1:T(2,128)(2,1)S(1)}, u32[]{:S(2)}, u32[]{:S(2)}) %collective-permute-start) | collective-permute-done | bytes 16416 | tf_op jit(solution)/shard_map/ppermute | solution.py:40
  6.6 2.1 %collective-permute-start.1 = (bf16[2,64,128]{2,0,1:T(2,128)(2,1)S(1)}, bf16[2,64,128]{2,0,1:T(2,128)(2,1)S(1)}, u32[]{:S(2)}, u32[]{:S(2)}) collective-permute-start(bf16[2,64,128]{2,0,1:T(2,128)(2,1)S(1)} %pad_maximum_fusion.5), channel_id=1, source_target_pairs={{0,8},{8,0},{16,24},{24,16},{1,9},{9,1},{17,25},{25,17},{2,10},{10... | collective-permute-start | bytes 98312 | tf_op jit(solution)/shard_map/ppermute | solution.py:40
  8.6 0.9 fusion.50
  9.5 1.1 %collective-permute-done.1 = bf16[2,64,128]{2,0,1:T(2,128)(2,1)S(1)} collective-permute-done((bf16[2,64,128]{2,0,1:T(2,128)(2,1)S(1)}, bf16[2,64,128]{2,0,1:T(2,128)(2,1)S(1)}, u32[]{:S(2)}, u32[]{:S(2)}) %collective-permute-start.1) | collective-permute-done | bytes 32800 | tf_op jit(solution)/shard_map/ppermute | solution.py:40
  10.8 3.2 %collective-permute-start.2 = (bf16[2,64,128]{2,0,1:T(2,128)(2,1)S(1)}, bf16[2,64,128]{2,0,1:T(2,128)(2,1)S(1)}, u32[]{:S(2)}, u32[]{:S(2)}) collective-permute-start(bf16[2,64,128]{2,0,1:T(2,128)(2,1)S(1)} %convolution_convert_fusion), channel_id=1, source_target_pairs={{0,4},{1,5},{2,6},{3,7},{4,0},{5,1},{6,2},{7,3},{8,12},{9,13},{10,... | collective-permute-start | bytes 98312 | tf_op jit(solution)/shard_map/ppermute | solution.py:40
  13.9 2.0 %collective-permute-done.2 = bf16[2,64,128]{2,0,1:T(2,128)(2,1)S(1)} collective-permute-done((bf16[2,64,128]{2,0,1:T(2,128)(2,1)S(1)}, bf16[2,64,128]{2,0,1:T(2,128)(2,1)S(1)}, u32[]{:S(2)}, u32[]{:S(2)}) %collective-permute-start.2) | collective-permute-done | bytes 32800 | tf_op jit(solution)/shard_map/ppermute | solution.py:40
  16.0 1.9 %collective-permute-start.3 = (bf16[2,128,128]{2,0,1:T(2,128)(2,1)S(1)}, bf16[2,128,128]{2,0,1:T(2,128)(2,1)S(1)}, u32[]{:S(2)}, u32[]{:S(2)}) collective-permute-start(bf16[2,128,128]{2,0,1:T(2,128)(2,1)S(1)} %pad_maximum_fusion.4), channel_id=1, source_target_pairs={{0,2},{1,3},{2,0},{3,1},{4,6},{5,7},{6,4},{7,5},{8,10},{9,11},{10,... | collective-permute-start | bytes 196616 | tf_op jit(solution)/shard_map/ppermute | solution.py:40
  17.9 0.7 compare_and_fusion
  18.6 1.8 %collective-permute-done.3 = bf16[2,128,128]{2,0,1:T(2,128)(2,1)S(1)} collective-permute-done((bf16[2,128,128]{2,0,1:T(2,128)(2,1)S(1)}, bf16[2,128,128]{2,0,1:T(2,128)(2,1)S(1)}, u32[]{:S(2)}, u32[]{:S(2)}) %collective-permute-start.3) | collective-permute-done | bytes 65568 | tf_op jit(solution)/shard_map/ppermute | solution.py:40
  21.3 0.7 reduce.2
  22.5 0.6 gather_fusion
  23.2 0.9 fusion.12
  24.1 0.7 multiply_reduce_fusion.1
  24.9 0.8 copy-done
  25.7 0.8 fusion.2
  26.5 1.4 %pad_maximum_fusion.11 = f32[2]{0:T(128)S(1)} fusion(f32[1]{0:T(128)} %bitcast.13, f32[1]{0:T(128)} %bitcast.12), kind=kLoop, calls=%fused_computation.105 | loop fusion | flops 2 | bytes 16 | tf_op jit(solution)/shard_map/stack | solution.py:124
  28.5 0.8 collective-permute-done.5
  29.4 1.9 %collective-permute-start.6 = (f32[2,2176]{1,0:T(2,128)S(1)}, f32[2,2176]{1,0:T(2,128)S(1)}, u32[]{:S(2)}, u32[]{:S(2)}) collective-permute-start(f32[2,2176]{1,0:T(2,128)S(1)} %fusion.60), channel_id=1, source_target_pairs={{0,2},{1,3},{2,0},{3,1},{4,6},{5,7},{6,4},{7,5},{8,10},{9,11},{10,... | collective-permute-start | bytes 52232 | tf_op jit(solution)/shard_map/ppermute | solution.py:27
  31.3 1.9 %collective-permute-done.6 = f32[2,2176]{1,0:T(2,128)S(1)} collective-permute-done((f32[2,2176]{1,0:T(2,128)S(1)}, f32[2,2176]{1,0:T(2,128)S(1)}, u32[]{:S(2)}, u32[]{:S(2)}) %collective-permute-start.6) | collective-permute-done | bytes 17440 | tf_op jit(solution)/shard_map/ppermute | solution.py:27
  33.2 3.1 %collective-permute-start.7 = (f32[2,2176]{1,0:T(2,128)S(1)}, f32[2,2176]{1,0:T(2,128)S(1)}, u32[]{:S(2)}, u32[]{:S(2)}) collective-permute-start(f32[2,2176]{1,0:T(2,128)S(1)} %add.133), channel_id=1, source_target_pairs={{0,4},{1,5},{2,6},{3,7},{4,0},{5,1},{6,2},{7,3},{8,12},{9,13},{10,... | collective-permute-start | bytes 52232 | tf_op jit(solution)/shard_map/ppermute | solution.py:27
  36.3 1.7 %collective-permute-done.7 = f32[2,2176]{1,0:T(2,128)S(1)} collective-permute-done((f32[2,2176]{1,0:T(2,128)S(1)}, f32[2,2176]{1,0:T(2,128)S(1)}, u32[]{:S(2)}, u32[]{:S(2)}) %collective-permute-start.7) | collective-permute-done | bytes 17440 | tf_op jit(solution)/shard_map/ppermute | solution.py:27
  38.3 3.0 %collective-permute-start.8 = (f32[256]{0:T(256)S(1)}, f32[256]{0:T(256)S(1)}, u32[]{:S(2)}, u32[]{:S(2)}) collective-permute-start(f32[256]{0:T(256)S(1)} %fusion.7), channel_id=1, source_target_pairs={{0,4},{1,5},{2,6},{3,7},{4,0},{5,1},{6,2},{7,3},{8,12},{9,13},{10,... | collective-permute-start | bytes 3080 | tf_op jit(solution)/shard_map/ppermute | solution.py:40
  41.2 1.6 %collective-permute-done.8 = f32[256]{0:T(256)S(1)} collective-permute-done((f32[256]{0:T(256)S(1)}, f32[256]{0:T(256)S(1)}, u32[]{:S(2)}, u32[]{:S(2)}) %collective-permute-start.8) | collective-permute-done | bytes 1056 | tf_op jit(solution)/shard_map/ppermute | solution.py:40
  42.8 1.7 %collective-permute-start.9 = (f32[512]{0:T(512)S(1)}, f32[512]{0:T(512)S(1)}, u32[]{:S(2)}, u32[]{:S(2)}) collective-permute-start(f32[512]{0:T(512)S(1)} %pad_maximum_fusion.10), channel_id=1, source_target_pairs={{0,2},{1,3},{2,0},{3,1},{4,6},{5,7},{6,4},{7,5},{8,10},{9,11},{10,... | collective-permute-start | bytes 6152 | tf_op jit(solution)/shard_map/ppermute | solution.py:40
  44.5 1.9 %collective-permute-done.9 = f32[512]{0:T(512)S(1)} collective-permute-done((f32[512]{0:T(512)S(1)}, f32[512]{0:T(512)S(1)}, u32[]{:S(2)}, u32[]{:S(2)}) %collective-permute-start.9) | collective-permute-done | bytes 2080 | tf_op jit(solution)/shard_map/ppermute | solution.py:40
  47.0 0.6 collective-permute-done.10
  48.3 0.6 multiply_reduce_fusion
  50.8 3.9 %fusion.4 = f32[1280,2]{0,1:T(2,128)S(1)} fusion(bf16[1,1280,2048]{2,1,0:T(8,128)(2,1)} %param.12, bf16[2048,1]{0,1:T(2,128)(2,1)S(1)} %stack.34, bf16[2048,1]{0,1:T(2,128)(2,1)S(1)} %bitcast.113), kind=kOutput, calls=%fused_computation.12 | convolution fusion | flops 10502144 | bytes 5261312 | tf_op jit(solution)/shard_map/dot_general | solution.py:137
  55.3 0.9 fusion.8
  56.2 0.9 fusion.10
  57.6 0.9 fusion.13
  58.5 1.6 %collective-permute-done.11 = f32[4,64,2,512]{3,1,2,0:T(8,128)S(1)} collective-permute-done((f32[4,64,2,512]{3,1,2,0:T(8,128)S(1)}, f32[4,64,2,512]{3,1,2,0:T(8,128)S(1)}, u32[]{:S(2)}, u32[]{:S(2)}) %collective-permute-start.11) | collective-permute-done | bytes 1048608 | tf_op jit(solution)/shard_map/ppermute | solution.py:66
  60.7 1.8 %collective-permute-start.12 = (f32[2,64,2,512]{3,1,2,0:T(8,128)S(1)}, f32[2,64,2,512]{3,1,2,0:T(8,128)S(1)}, u32[]{:S(2)}, u32[]{:S(2)}) collective-permute-start(f32[2,64,2,512]{3,1,2,0:T(8,128)S(1)} %dynamic-slice_bitcast_fusion.1), channel_id=1, source_target_pairs={{0,2},{1,3},{2,0},{3,1},{4,6},{5,7},{6,4},{7,5},{8,10},{9,11},{10,... | collective-permute-start | bytes 1572872 | tf_op jit(solution)/shard_map/ppermute | solution.py:66
  62.5 1.1 %bitcast_add_fusion.1 = f32[4,64,512]{2,1,0:T(8,128)S(1)} fusion(f32[4,64,512]{2,1,0:T(8,128)S(1)} %collective-permute-done.17, f32[4,2,64,512]{3,2,1,0:T(8,128)} %bitcast.108, s32[]{:T(128)S(6)} %select_n.160), kind=kLoop, calls=%fused_computation.38 | loop fusion | flops 131072 | bytes 1572868 | tf_op jit(solution)/shard_map/add | solution.py:66
  63.6 11.3 %collective-permute-done.12 = f32[2,64,2,512]{3,1,2,0:T(8,128)S(1)} collective-permute-done((f32[2,64,2,512]{3,1,2,0:T(8,128)S(1)}, f32[2,64,2,512]{3,1,2,0:T(8,128)S(1)}, u32[]{:S(2)}, u32[]{:S(2)}) %collective-permute-start.12) | collective-permute-done | bytes 524320 | tf_op jit(solution)/shard_map/ppermute | solution.py:66
  75.0 1.8 %collective-permute-start.18 = (f32[2,64,512]{2,1,0:T(8,128)S(1)}, f32[2,64,512]{2,1,0:T(8,128)S(1)}, u32[]{:S(2)}, u32[]{:S(2)}) collective-permute-start(f32[2,64,512]{2,1,0:T(8,128)S(1)} %dynamic-slice_bitcast_fusion.2), channel_id=1, source_target_pairs={{0,2},{1,3},{2,0},{3,1},{4,6},{5,7},{6,4},{7,5},{8,10},{9,11},{10,... | collective-permute-start | bytes 786440 | tf_op jit(solution)/shard_map/ppermute | solution.py:66
  76.8 2.9 %collective-permute-start.13 = (f32[1,64,2,512]{3,1,2,0:T(8,128)S(1)}, f32[1,64,2,512]{3,1,2,0:T(8,128)S(1)}, u32[]{:S(2)}, u32[]{:S(2)}) collective-permute-start(f32[1,64,2,512]{3,1,2,0:T(8,128)S(1)} %constant_dynamic-slice_fusion.1), channel_id=1, source_target_pairs={{0,4},{1,5},{2,6},{3,7},{4,0},{5,1},{6,2},{7,3},{8,12},{9,13},{10,... | collective-permute-start | bytes 786440 | tf_op jit(solution)/shard_map/ppermute | solution.py:66
  85.6 2.6 %collective-permute-done.18 = f32[2,64,512]{2,1,0:T(8,128)S(1)} collective-permute-done((f32[2,64,512]{2,1,0:T(8,128)S(1)}, f32[2,64,512]{2,1,0:T(8,128)S(1)}, u32[]{:S(2)}, u32[]{:S(2)}) %collective-permute-start.18) | collective-permute-done | bytes 262176 | tf_op jit(solution)/shard_map/ppermute | solution.py:66
  88.2 3.2 %collective-permute-done.13 = f32[1,64,2,512]{3,1,2,0:T(8,128)S(1)} collective-permute-done((f32[1,64,2,512]{3,1,2,0:T(8,128)S(1)}, f32[1,64,2,512]{3,1,2,0:T(8,128)S(1)}, u32[]{:S(2)}, u32[]{:S(2)}) %collective-permute-start.13) | collective-permute-done | bytes 262176 | tf_op jit(solution)/shard_map/ppermute | solution.py:66
  91.6 1.6 %collective-permute-start.14 = (f32[64,512]{1,0:T(8,128)S(1)}, f32[64,512]{1,0:T(8,128)S(1)}, u32[]{:S(2)}, u32[]{:S(2)}) collective-permute-start(f32[64,512]{1,0:T(8,128)S(1)} %get-tuple-element.16), channel_id=1, source_target_pairs={{0,8},{8,0},{16,24},{24,16},{1,9},{9,1},{17,25},{25,17},{2,10},{10... | collective-permute-start | bytes 393224 | tf_op jit(solution)/shard_map/ppermute | solution.py:174
  93.2 1.5 %collective-permute-start.15 = (f32[64,512]{1,0:T(8,128)S(1)}, f32[64,512]{1,0:T(8,128)S(1)}, u32[]{:S(2)}, u32[]{:S(2)}) collective-permute-start(f32[64,512]{1,0:T(8,128)S(1)} %get-tuple-element.17), channel_id=1, source_target_pairs={{0,16},{8,24},{16,0},{24,8},{1,17},{9,25},{17,1},{25,9},{2,18},{10... | collective-permute-start | bytes 393224 | tf_op jit(solution)/shard_map/ppermute | solution.py:174
  95.2 3.1 %collective-permute-done.19 = f32[1,64,512]{2,1,0:T(8,128)S(1)} collective-permute-done((f32[1,64,512]{2,1,0:T(8,128)S(1)}, f32[1,64,512]{2,1,0:T(8,128)S(1)}, u32[]{:S(2)}, u32[]{:S(2)}) %collective-permute-start.19) | collective-permute-done | bytes 131104 | tf_op jit(solution)/shard_map/ppermute | solution.py:66
  98.3 0.7 dynamic-slice_add_fusion.1
  98.9 1.6 %collective-permute-done.16 = f32[64,512]{1,0:T(8,128)S(1)} collective-permute-done((f32[64,512]{1,0:T(8,128)S(1)}, f32[64,512]{1,0:T(8,128)S(1)}, u32[]{:S(2)}, u32[]{:S(2)}) %collective-permute-start.16) | collective-permute-done | bytes 131104 | tf_op jit(solution)/shard_map/ppermute | solution.py:174
  100.6 0.7 fusion.31
  (70 shorter events, 6.5 us)
Async XLA Ops:
  0.6 22.6 %copy-start.1 = (bf16[1,1280,1024]{2,1,0:T(8,128)(2,1)S(1)}, bf16[1,1280,1024]{2,1,0:T(8,128)(2,1)}, u32[]{:S(2)}) copy-start(bf16[1,1280,1024]{2,1,0:T(8,128)(2,1)} %param.11) | copy-start | bytes 7864324
  1.5 5.0 %collective-permute-start = (bf16[1,64,128]{2,0,1:T(2,128)(2,1)S(1)}, bf16[1,64,128]{2,0,1:T(2,128)(2,1)S(1)}, u32[]{:S(2)}, u32[]{:S(2)}) collective-permute-start(bf16[1,64,128]{2,0,1:T(2,128)(2,1)S(1)} %copy.33), channel_id=1, source_target_pairs={{0,16},{8,24},{16,0},{24,8},{1,17},{9,25},{17,1},{25,9},{2,18},{10... | collective-permute-start | bytes 49160 | tf_op jit(solution)/shard_map/ppermute | solution.py:40
  6.6 4.0 %collective-permute-start.1 = (bf16[2,64,128]{2,0,1:T(2,128)(2,1)S(1)}, bf16[2,64,128]{2,0,1:T(2,128)(2,1)S(1)}, u32[]{:S(2)}, u32[]{:S(2)}) collective-permute-start(bf16[2,64,128]{2,0,1:T(2,128)(2,1)S(1)} %pad_maximum_fusion.5), channel_id=1, source_target_pairs={{0,8},{8,0},{16,24},{24,16},{1,9},{9,1},{17,25},{25,17},{2,10},{10... | collective-permute-start | bytes 98312 | tf_op jit(solution)/shard_map/ppermute | solution.py:40
  10.8 5.2 %collective-permute-start.2 = (bf16[2,64,128]{2,0,1:T(2,128)(2,1)S(1)}, bf16[2,64,128]{2,0,1:T(2,128)(2,1)S(1)}, u32[]{:S(2)}, u32[]{:S(2)}) collective-permute-start(bf16[2,64,128]{2,0,1:T(2,128)(2,1)S(1)} %convolution_convert_fusion), channel_id=1, source_target_pairs={{0,4},{1,5},{2,6},{3,7},{4,0},{5,1},{6,2},{7,3},{8,12},{9,13},{10,... | collective-permute-start | bytes 98312 | tf_op jit(solution)/shard_map/ppermute | solution.py:40
  16.0 4.3 %collective-permute-start.3 = (bf16[2,128,128]{2,0,1:T(2,128)(2,1)S(1)}, bf16[2,128,128]{2,0,1:T(2,128)(2,1)S(1)}, u32[]{:S(2)}, u32[]{:S(2)}) collective-permute-start(bf16[2,128,128]{2,0,1:T(2,128)(2,1)S(1)} %pad_maximum_fusion.4), channel_id=1, source_target_pairs={{0,2},{1,3},{2,0},{3,1},{4,6},{5,7},{6,4},{7,5},{8,10},{9,11},{10,... | collective-permute-start | bytes 196616 | tf_op jit(solution)/shard_map/ppermute | solution.py:40
  20.6 1.5 %collective-permute-start.4 = (bf16[2,256,128]{2,0,1:T(2,128)(2,1)S(1)}, bf16[2,256,128]{2,0,1:T(2,128)(2,1)S(1)}, u32[]{:S(2)}, u32[]{:S(2)}) collective-permute-start(bf16[2,256,128]{2,0,1:T(2,128)(2,1)S(1)} %pad_maximum_fusion.1), channel_id=1, source_target_pairs={{0,1},{1,0},{2,3},{3,2},{4,5},{5,4},{6,7},{7,6},{8,9},{9,8},{10,11... | collective-permute-start | bytes 393224 | tf_op jit(solution)/shard_map/ppermute | solution.py:40
  23.2 1.6 %copy-start.4 = (f32[1,1280]{1,0:T(1,128)S(1)}, f32[1,1280]{1,0:T(1,128)}, u32[]{:S(2)}) copy-start(f32[1,1280]{1,0:T(1,128)} %param.17) | copy-start | bytes 15364
  23.2 2.5 %copy-start = (bf16[1,1280,2048]{2,1,0:T(8,128)(2,1)S(1)}, bf16[1,1280,2048]{2,1,0:T(8,128)(2,1)}, u32[]{:S(2)}) copy-start(bf16[1,1280,2048]{2,1,0:T(8,128)(2,1)} %param.12) | copy-start | bytes 15728644
  25.7 12.3 %copy-start.2 = (f32[1,256,2048]{2,1,0:T(8,128)S(1)}, f32[1,256,2048]{2,1,0:T(8,128)}, u32[]{:S(2)}) copy-start(f32[1,256,2048]{2,1,0:T(8,128)} %param.18) | copy-start | bytes 6291460
  28.0 1.4 %collective-permute-start.5 = (f32[2,2176]{1,0:T(2,128)S(1)}, f32[2,2176]{1,0:T(2,128)S(1)}, u32[]{:S(2)}, u32[]{:S(2)}) collective-permute-start(f32[2,2176]{1,0:T(2,128)S(1)} %pad_maximum_fusion.6), channel_id=1, source_target_pairs={{0,1},{1,0},{2,3},{3,2},{4,5},{5,4},{6,7},{7,6},{8,9},{9,8},{10,11... | collective-permute-start | bytes 52232 | tf_op jit(solution)/shard_map/ppermute | solution.py:27
  29.4 3.8 %collective-permute-start.6 = (f32[2,2176]{1,0:T(2,128)S(1)}, f32[2,2176]{1,0:T(2,128)S(1)}, u32[]{:S(2)}, u32[]{:S(2)}) collective-permute-start(f32[2,2176]{1,0:T(2,128)S(1)} %fusion.60), channel_id=1, source_target_pairs={{0,2},{1,3},{2,0},{3,1},{4,6},{5,7},{6,4},{7,5},{8,10},{9,11},{10,... | collective-permute-start | bytes 52232 | tf_op jit(solution)/shard_map/ppermute | solution.py:27
  33.2 4.8 %collective-permute-start.7 = (f32[2,2176]{1,0:T(2,128)S(1)}, f32[2,2176]{1,0:T(2,128)S(1)}, u32[]{:S(2)}, u32[]{:S(2)}) collective-permute-start(f32[2,2176]{1,0:T(2,128)S(1)} %add.133), channel_id=1, source_target_pairs={{0,4},{1,5},{2,6},{3,7},{4,0},{5,1},{6,2},{7,3},{8,12},{9,13},{10,... | collective-permute-start | bytes 52232 | tf_op jit(solution)/shard_map/ppermute | solution.py:27
  38.3 4.5 %collective-permute-start.8 = (f32[256]{0:T(256)S(1)}, f32[256]{0:T(256)S(1)}, u32[]{:S(2)}, u32[]{:S(2)}) collective-permute-start(f32[256]{0:T(256)S(1)} %fusion.7), channel_id=1, source_target_pairs={{0,4},{1,5},{2,6},{3,7},{4,0},{5,1},{6,2},{7,3},{8,12},{9,13},{10,... | collective-permute-start | bytes 3080 | tf_op jit(solution)/shard_map/ppermute | solution.py:40
  42.8 3.6 %collective-permute-start.9 = (f32[512]{0:T(512)S(1)}, f32[512]{0:T(512)S(1)}, u32[]{:S(2)}, u32[]{:S(2)}) collective-permute-start(f32[512]{0:T(512)S(1)} %pad_maximum_fusion.10), channel_id=1, source_target_pairs={{0,2},{1,3},{2,0},{3,1},{4,6},{5,7},{6,4},{7,5},{8,10},{9,11},{10,... | collective-permute-start | bytes 6152 | tf_op jit(solution)/shard_map/ppermute | solution.py:40
  46.4 1.2 %collective-permute-start.10 = (f32[1024]{0:T(1024)S(1)}, f32[1024]{0:T(1024)S(1)}, u32[]{:S(2)}, u32[]{:S(2)}) collective-permute-start(f32[1024]{0:T(1024)S(1)} %pad_maximum_fusion.9), channel_id=1, source_target_pairs={{0,1},{1,0},{2,3},{3,2},{4,5},{5,4},{6,7},{7,6},{8,9},{9,8},{10,11... | collective-permute-start | bytes 12296 | tf_op jit(solution)/shard_map/ppermute | solution.py:40
  57.4 2.7 %collective-permute-start.11 = (f32[4,64,2,512]{3,1,2,0:T(8,128)S(1)}, f32[4,64,2,512]{3,1,2,0:T(8,128)S(1)}, u32[]{:S(2)}, u32[]{:S(2)}) collective-permute-start(f32[4,64,2,512]{3,1,2,0:T(8,128)S(1)} %bitcast.105), channel_id=1, source_target_pairs={{0,1},{1,0},{2,3},{3,2},{4,5},{5,4},{6,7},{7,6},{8,9},{9,8},{10,11... | collective-permute-start | bytes 3145736 | tf_op jit(solution)/shard_map/ppermute | solution.py:66
  58.5 1.8 %copy-start.3 = (f32[512,512]{1,0:T(8,128)}, f32[512,512]{1,0:T(8,128)S(1)}, u32[]{:S(2)}) copy-start(f32[512,512]{1,0:T(8,128)S(1)} %fusion.13) | copy-start | bytes 3145732
  60.4 2.1 %collective-permute-start.17 = (f32[4,64,512]{2,1,0:T(8,128)S(1)}, f32[4,64,512]{2,1,0:T(8,128)S(1)}, u32[]{:S(2)}, u32[]{:S(2)}) collective-permute-start(f32[4,64,512]{2,1,0:T(8,128)S(1)} %dynamic-slice_bitcast_fusion), channel_id=1, source_target_pairs={{0,1},{1,0},{2,3},{3,2},{4,5},{5,4},{6,7},{7,6},{8,9},{9,8},{10,11... | collective-permute-start | bytes 1572872 | tf_op jit(solution)/shard_map/ppermute | solution.py:66
  60.6 19.2 %copy-start.5 = (s32[1,2]{1,0:T(1,128)S(1)}, s32[1,2]{1,0:T(1,128)}, u32[]{:S(2)}) copy-start(s32[1,2]{1,0:T(1,128)} %param.15) | copy-start | bytes 28
  60.7 14.2 %collective-permute-start.12 = (f32[2,64,2,512]{3,1,2,0:T(8,128)S(1)}, f32[2,64,2,512]{3,1,2,0:T(8,128)S(1)}, u32[]{:S(2)}, u32[]{:S(2)}) collective-permute-start(f32[2,64,2,512]{3,1,2,0:T(8,128)S(1)} %dynamic-slice_bitcast_fusion.1), channel_id=1, source_target_pairs={{0,2},{1,3},{2,0},{3,1},{4,6},{5,7},{6,4},{7,5},{8,10},{9,11},{10,... | collective-permute-start | bytes 1572872 | tf_op jit(solution)/shard_map/ppermute | solution.py:66
  75.0 13.1 %collective-permute-start.18 = (f32[2,64,512]{2,1,0:T(8,128)S(1)}, f32[2,64,512]{2,1,0:T(8,128)S(1)}, u32[]{:S(2)}, u32[]{:S(2)}) collective-permute-start(f32[2,64,512]{2,1,0:T(8,128)S(1)} %dynamic-slice_bitcast_fusion.2), channel_id=1, source_target_pairs={{0,2},{1,3},{2,0},{3,1},{4,6},{5,7},{6,4},{7,5},{8,10},{9,11},{10,... | collective-permute-start | bytes 786440 | tf_op jit(solution)/shard_map/ppermute | solution.py:66
  76.8 14.6 %collective-permute-start.13 = (f32[1,64,2,512]{3,1,2,0:T(8,128)S(1)}, f32[1,64,2,512]{3,1,2,0:T(8,128)S(1)}, u32[]{:S(2)}, u32[]{:S(2)}) collective-permute-start(f32[1,64,2,512]{3,1,2,0:T(8,128)S(1)} %constant_dynamic-slice_fusion.1), channel_id=1, source_target_pairs={{0,4},{1,5},{2,6},{3,7},{4,0},{5,1},{6,2},{7,3},{8,12},{9,13},{10,... | collective-permute-start | bytes 786440 | tf_op jit(solution)/shard_map/ppermute | solution.py:66
  91.5 6.8 %collective-permute-start.19 = (f32[1,64,512]{2,1,0:T(8,128)S(1)}, f32[1,64,512]{2,1,0:T(8,128)S(1)}, u32[]{:S(2)}, u32[]{:S(2)}) collective-permute-start(f32[1,64,512]{2,1,0:T(8,128)S(1)} %constant_dynamic-slice_fusion), channel_id=1, source_target_pairs={{0,4},{1,5},{2,6},{3,7},{4,0},{5,1},{6,2},{7,3},{8,12},{9,13},{10,... | collective-permute-start | bytes 393224 | tf_op jit(solution)/shard_map/ppermute | solution.py:66
  91.6 7.3 %collective-permute-start.14 = (f32[64,512]{1,0:T(8,128)S(1)}, f32[64,512]{1,0:T(8,128)S(1)}, u32[]{:S(2)}, u32[]{:S(2)}) collective-permute-start(f32[64,512]{1,0:T(8,128)S(1)} %get-tuple-element.16), channel_id=1, source_target_pairs={{0,8},{8,0},{16,24},{24,16},{1,9},{9,1},{17,25},{25,17},{2,10},{10... | collective-permute-start | bytes 393224 | tf_op jit(solution)/shard_map/ppermute | solution.py:174
  93.2 5.7 %collective-permute-start.15 = (f32[64,512]{1,0:T(8,128)S(1)}, f32[64,512]{1,0:T(8,128)S(1)}, u32[]{:S(2)}, u32[]{:S(2)}) collective-permute-start(f32[64,512]{1,0:T(8,128)S(1)} %get-tuple-element.17), channel_id=1, source_target_pairs={{0,16},{8,24},{16,0},{24,8},{1,17},{9,25},{17,1},{25,9},{2,18},{10... | collective-permute-start | bytes 393224 | tf_op jit(solution)/shard_map/ppermute | solution.py:174
  94.7 5.9 %collective-permute-start.16 = (f32[64,512]{1,0:T(8,128)S(1)}, f32[64,512]{1,0:T(8,128)S(1)}, u32[]{:S(2)}, u32[]{:S(2)}) collective-permute-start(f32[64,512]{1,0:T(8,128)S(1)} %get-tuple-element.18), channel_id=1, source_target_pairs={{0,24},{8,16},{16,8},{24,0},{1,25},{9,17},{17,9},{25,1},{2,26},{10... | collective-permute-start | bytes 393224 | tf_op jit(solution)/shard_map/ppermute | solution.py:174

commit v15 on v14

--- a/solution.py
+++ b/solution.py
@@ -133,11 +133,7 @@
     weight_sum = totals[1, naux]
     coef_rows = jnp.sum(metric_inv[0] * fitted[None, :], axis=1)
     coefficients = in_order(*xor_gather(coef_rows, "grid", 0), 0)
-    coef_high, coef_low = split_rows(coefficients)
-    coulomb_parts = jnp.dot(
-        aux_block, jnp.stack([coef_high, coef_low], axis=1), preferred_element_type=jnp.float32
-    )
-    coulomb = coulomb_parts[:, 0] + coulomb_parts[:, 1]
+    coulomb = jnp.sum(aux_block.astype(jnp.float32) * coefficients[None, :], axis=1)
     potential_total = jnp.dot(coefficients, weight_projection, precision=highest) + exchange_total
     average = potential_total / weight_sum
     potential = live_weight * (coulomb + exchange - average)

time: 102 us -> 101 us (level)
  matrix products: 8.5 us -> 4.56 us
  other arithmetic: 10.6 us -> 14.1 us
    dot_general x1 -> x0, matrix products: 3.94 us -> none  [shards(): jnp.dot(aux_block, jnp.stack([coef_high, coef_low], axis=1), preferred_el...]
    reduce_sum x0 -> x1, other arithmetic: none -> 3.59 us  [shards(): jnp.sum(aux_block.astype(jnp.float32) * coefficients[None, :], axis=1)]
where the time goes in v15:
time: 101 us
  waiting for transfers between devices  38 us (38%)
  starting transfers between devices  31 us (31%)
  other arithmetic  14.1 us (14%)
  between operations  8.74 us (9%)
  matrix products  4.56 us (5%)
  local copies, waits for them, and re-layouts  4.35 us (4%)
    ppermute x6, waiting for transfers between devices, scatter_step(): lax.ppermute(send, axis, [(i, i ^ 1 << bit) for i in range(size)])  21.9 us
    ppermute x8, starting transfers between devices, xor_gather(): other = lax.ppermute(value, axis, [(i, i ^ 1 << bit) for i in range(size)])  14.9 us
    ppermute x8, waiting for transfers between devices, xor_gather(): other = lax.ppermute(value, axis, [(i, i ^ 1 << bit) for i in range(size)])  10.1 us
    ppermute x6, starting transfers between devices, scatter_step(): lax.ppermute(send, axis, [(i, i ^ 1 << bit) for i in range(size)])  7.06 us
    ppermute x3, starting transfers between devices, xor_sum(): lax.ppermute(value, axis, [(i, i ^ step) for i in range(size)])  5.49 us
    ppermute x3, waiting for transfers between devices, xor_sum(): lax.ppermute(value, axis, [(i, i ^ step) for i in range(size)])  4.52 us
    reduce_sum x1, other arithmetic, shards(): jnp.sum(aux_block.astype(jnp.float32) * coefficients[None, :], axis=1)  3.59 us
    ppermute x3, starting transfers between devices, shards(): frag_fock = frag_fock + lax.ppermute(piece(dest), 'dimer', pairs)  3.55 us
  transfers between devices with their start and end apart: 20, of which 16 were waited for; matrix products, arithmetic and copies ran while one was open for 7% of the time, Pallas kernels for 0%

profile of v15, /device:TPU:0, one launch (start us, length us, event | category | flops | bytes accessed | tf_op | source)
XLA Modules:
  0.0 100.8 jit_solution(1591705660939666765)
XLA Ops:
  0.6 0.9 copy.33
  1.5 3.1 %collective-permute-start = (bf16[1,64,128]{2,0,1:T(2,128)(2,1)S(1)}, bf16[1,64,128]{2,0,1:T(2,128)(2,1)S(1)}, u32[]{:S(2)}, u32[]{:S(2)}) collective-permute-start(bf16[1,64,128]{2,0,1:T(2,128)(2,1)S(1)} %copy.33), channel_id=1, source_target_pairs={{0,16},{8,24},{16,0},{24,8},{1,17},{9,25},{17,1},{25,9},{2,18},{10... | collective-permute-start | bytes 49160 | tf_op jit(solution)/shard_map/ppermute | solution.py:40
  4.6 0.7 broadcast_xor_fusion
  5.3 1.2 %collective-permute-done = bf16[1,64,128]{2,0,1:T(2,128)(2,1)S(1)} collective-permute-done((bf16[1,64,128]{2,0,1:T(2,128)(2,1)S(1)}, bf16[1,64,128]{2,0,1:T(2,128)(2,1)S(1)}, u32[]{:S(2)}, u32[]{:S(2)}) %collective-permute-start) | collective-permute-done | bytes 16416 | tf_op jit(solution)/shard_map/ppermute | solution.py:40
  6.6 2.1 %collective-permute-start.1 = (bf16[2,64,128]{2,0,1:T(2,128)(2,1)S(1)}, bf16[2,64,128]{2,0,1:T(2,128)(2,1)S(1)}, u32[]{:S(2)}, u32[]{:S(2)}) collective-permute-start(bf16[2,64,128]{2,0,1:T(2,128)(2,1)S(1)} %pad_maximum_fusion.5), channel_id=1, source_target_pairs={{0,8},{8,0},{16,24},{24,16},{1,9},{9,1},{17,25},{25,17},{2,10},{10... | collective-permute-start | bytes 98312 | tf_op jit(solution)/shard_map/ppermute | solution.py:40
  8.6 0.9 fusion.38
  9.5 1.1 %collective-permute-done.1 = bf16[2,64,128]{2,0,1:T(2,128)(2,1)S(1)} collective-permute-done((bf16[2,64,128]{2,0,1:T(2,128)(2,1)S(1)}, bf16[2,64,128]{2,0,1:T(2,128)(2,1)S(1)}, u32[]{:S(2)}, u32[]{:S(2)}) %collective-permute-start.1) | collective-permute-done | bytes 32800 | tf_op jit(solution)/shard_map/ppermute | solution.py:40
  10.8 3.2 %collective-permute-start.2 = (bf16[2,64,128]{2,0,1:T(2,128)(2,1)S(1)}, bf16[2,64,128]{2,0,1:T(2,128)(2,1)S(1)}, u32[]{:S(2)}, u32[]{:S(2)}) collective-permute-start(bf16[2,64,128]{2,0,1:T(2,128)(2,1)S(1)} %convolution_convert_fusion), channel_id=1, source_target_pairs={{0,4},{1,5},{2,6},{3,7},{4,0},{5,1},{6,2},{7,3},{8,12},{9,13},{10,... | collective-permute-start | bytes 98312 | tf_op jit(solution)/shard_map/ppermute | solution.py:40
  13.9 2.0 %collective-permute-done.2 = bf16[2,64,128]{2,0,1:T(2,128)(2,1)S(1)} collective-permute-done((bf16[2,64,128]{2,0,1:T(2,128)(2,1)S(1)}, bf16[2,64,128]{2,0,1:T(2,128)(2,1)S(1)}, u32[]{:S(2)}, u32[]{:S(2)}) %collective-permute-start.2) | collective-permute-done | bytes 32800 | tf_op jit(solution)/shard_map/ppermute | solution.py:40
  16.0 1.9 %collective-permute-start.3 = (bf16[2,128,128]{2,0,1:T(2,128)(2,1)S(1)}, bf16[2,128,128]{2,0,1:T(2,128)(2,1)S(1)}, u32[]{:S(2)}, u32[]{:S(2)}) collective-permute-start(bf16[2,128,128]{2,0,1:T(2,128)(2,1)S(1)} %pad_maximum_fusion.4), channel_id=1, source_target_pairs={{0,2},{1,3},{2,0},{3,1},{4,6},{5,7},{6,4},{7,5},{8,10},{9,11},{10,... | collective-permute-start | bytes 196616 | tf_op jit(solution)/shard_map/ppermute | solution.py:40
  17.9 0.7 compare_and_fusion
  18.6 1.8 %collective-permute-done.3 = bf16[2,128,128]{2,0,1:T(2,128)(2,1)S(1)} collective-permute-done((bf16[2,128,128]{2,0,1:T(2,128)(2,1)S(1)}, bf16[2,128,128]{2,0,1:T(2,128)(2,1)S(1)}, u32[]{:S(2)}, u32[]{:S(2)}) %collective-permute-start.3) | collective-permute-done | bytes 65568 | tf_op jit(solution)/shard_map/ppermute | solution.py:40
  21.3 0.7 reduce.2
  22.5 0.6 gather_fusion
  23.2 0.9 fusion.7
  24.1 0.7 multiply_reduce_fusion.2
  24.9 0.8 copy-done
  25.7 0.8 fusion
  26.5 1.3 %pad_maximum_fusion.11 = f32[2]{0:T(128)S(1)} fusion(f32[1]{0:T(128)} %bitcast.12, f32[1]{0:T(128)} %bitcast.11), kind=kLoop, calls=%fused_computation.93 | loop fusion | flops 2 | bytes 16 | tf_op jit(solution)/shard_map/stack | solution.py:124
  28.5 0.8 collective-permute-done.5
  29.4 1.9 %collective-permute-start.6 = (f32[2,2176]{1,0:T(2,128)S(1)}, f32[2,2176]{1,0:T(2,128)S(1)}, u32[]{:S(2)}, u32[]{:S(2)}) collective-permute-start(f32[2,2176]{1,0:T(2,128)S(1)} %fusion.47), channel_id=1, source_target_pairs={{0,2},{1,3},{2,0},{3,1},{4,6},{5,7},{6,4},{7,5},{8,10},{9,11},{10,... | collective-permute-start | bytes 52232 | tf_op jit(solution)/shard_map/ppermute | solution.py:27
  31.2 1.9 %collective-permute-done.6 = f32[2,2176]{1,0:T(2,128)S(1)} collective-permute-done((f32[2,2176]{1,0:T(2,128)S(1)}, f32[2,2176]{1,0:T(2,128)S(1)}, u32[]{:S(2)}, u32[]{:S(2)}) %collective-permute-start.6) | collective-permute-done | bytes 17440 | tf_op jit(solution)/shard_map/ppermute | solution.py:27
  33.2 3.1 %collective-permute-start.7 = (f32[2,2176]{1,0:T(2,128)S(1)}, f32[2,2176]{1,0:T(2,128)S(1)}, u32[]{:S(2)}, u32[]{:S(2)}) collective-permute-start(f32[2,2176]{1,0:T(2,128)S(1)} %add.132), channel_id=1, source_target_pairs={{0,4},{1,5},{2,6},{3,7},{4,0},{5,1},{6,2},{7,3},{8,12},{9,13},{10,... | collective-permute-start | bytes 52232 | tf_op jit(solution)/shard_map/ppermute | solution.py:27
  36.3 1.7 %collective-permute-done.7 = f32[2,2176]{1,0:T(2,128)S(1)} collective-permute-done((f32[2,2176]{1,0:T(2,128)S(1)}, f32[2,2176]{1,0:T(2,128)S(1)}, u32[]{:S(2)}, u32[]{:S(2)}) %collective-permute-start.7) | collective-permute-done | bytes 17440 | tf_op jit(solution)/shard_map/ppermute | solution.py:27
  38.3 3.0 %collective-permute-start.8 = (f32[256]{0:T(256)S(1)}, f32[256]{0:T(256)S(1)}, u32[]{:S(2)}, u32[]{:S(2)}) collective-permute-start(f32[256]{0:T(256)S(1)} %fusion.2), channel_id=1, source_target_pairs={{0,4},{1,5},{2,6},{3,7},{4,0},{5,1},{6,2},{7,3},{8,12},{9,13},{10,... | collective-permute-start | bytes 3080 | tf_op jit(solution)/shard_map/ppermute | solution.py:40
  41.2 1.6 %collective-permute-done.8 = f32[256]{0:T(256)S(1)} collective-permute-done((f32[256]{0:T(256)S(1)}, f32[256]{0:T(256)S(1)}, u32[]{:S(2)}, u32[]{:S(2)}) %collective-permute-start.8) | collective-permute-done | bytes 1056 | tf_op jit(solution)/shard_map/ppermute | solution.py:40
  42.8 1.7 %collective-permute-start.9 = (f32[512]{0:T(512)S(1)}, f32[512]{0:T(512)S(1)}, u32[]{:S(2)}, u32[]{:S(2)}) collective-permute-start(f32[512]{0:T(512)S(1)} %pad_maximum_fusion.10), channel_id=1, source_target_pairs={{0,2},{1,3},{2,0},{3,1},{4,6},{5,7},{6,4},{7,5},{8,10},{9,11},{10,... | collective-permute-start | bytes 6152 | tf_op jit(solution)/shard_map/ppermute | solution.py:40
  44.5 1.9 %collective-permute-done.9 = f32[512]{0:T(512)S(1)} collective-permute-done((f32[512]{0:T(512)S(1)}, f32[512]{0:T(512)S(1)}, u32[]{:S(2)}, u32[]{:S(2)}) %collective-permute-start.9) | collective-permute-done | bytes 2080 | tf_op jit(solution)/shard_map/ppermute | solution.py:40
  46.4 0.6 fusion.49
  48.2 3.6 %multiply_reduce_fusion = f32[1280]{0:T(1024)S(1)} fusion(bf16[1,1280,2048]{2,1,0:T(8,128)(2,1)} %param.12, f32[2048]{0:T(1024)S(1)} %bitcast.97), kind=kLoop, calls=%fused_computation.2 | loop fusion | flops 7863040 | bytes 5256192 | tf_op jit(solution)/shard_map/reduce_sum | solution.py:136
  51.8 0.6 multiply_reduce_fusion.1
  54.9 0.9 fusion.3
  55.8 0.9 fusion.5
  57.2 0.9 fusion.8
  58.1 1.6 %collective-permute-done.11 = f32[4,64,2,512]{3,1,2,0:T(8,128)S(1)} collective-permute-done((f32[4,64,2,512]{3,1,2,0:T(8,128)S(1)}, f32[4,64,2,512]{3,1,2,0:T(8,128)S(1)}, u32[]{:S(2)}, u32[]{:S(2)}) %collective-permute-start.11) | collective-permute-done | bytes 1048608 | tf_op jit(solution)/shard_map/ppermute | solution.py:66
  60.2 1.8 %collective-permute-start.12 = (f32[2,64,2,512]{3,1,2,0:T(8,128)S(1)}, f32[2,64,2,512]{3,1,2,0:T(8,128)S(1)}, u32[]{:S(2)}, u32[]{:S(2)}) collective-permute-start(f32[2,64,2,512]{3,1,2,0:T(8,128)S(1)} %dynamic-slice_bitcast_fusion.1), channel_id=1, source_target_pairs={{0,2},{1,3},{2,0},{3,1},{4,6},{5,7},{6,4},{7,5},{8,10},{9,11},{10,... | collective-permute-start | bytes 1572872 | tf_op jit(solution)/shard_map/ppermute | solution.py:66
  62.0 1.1 %bitcast_add_fusion.1 = f32[4,64,512]{2,1,0:T(8,128)S(1)} fusion(f32[4,64,512]{2,1,0:T(8,128)S(1)} %collective-permute-done.17, f32[4,2,64,512]{3,2,1,0:T(8,128)} %bitcast.94, s32[]{:T(128)S(6)} %select_n.150), kind=kLoop, calls=%fused_computation.36 | loop fusion | flops 131072 | bytes 1572868 | tf_op jit(solution)/shard_map/add | solution.py:66
  63.2 11.3 %collective-permute-done.12 = f32[2,64,2,512]{3,1,2,0:T(8,128)S(1)} collective-permute-done((f32[2,64,2,512]{3,1,2,0:T(8,128)S(1)}, f32[2,64,2,512]{3,1,2,0:T(8,128)S(1)}, u32[]{:S(2)}, u32[]{:S(2)}) %collective-permute-start.12) | collective-permute-done | bytes 524320 | tf_op jit(solution)/shard_map/ppermute | solution.py:66
  74.6 1.8 %collective-permute-start.18 = (f32[2,64,512]{2,1,0:T(8,128)S(1)}, f32[2,64,512]{2,1,0:T(8,128)S(1)}, u32[]{:S(2)}, u32[]{:S(2)}) collective-permute-start(f32[2,64,512]{2,1,0:T(8,128)S(1)} %dynamic-slice_bitcast_fusion.2), channel_id=1, source_target_pairs={{0,2},{1,3},{2,0},{3,1},{4,6},{5,7},{6,4},{7,5},{8,10},{9,11},{10,... | collective-permute-start | bytes 786440 | tf_op jit(solution)/shard_map/ppermute | solution.py:66
  76.4 3.0 %collective-permute-start.13 = (f32[1,64,2,512]{3,1,2,0:T(8,128)S(1)}, f32[1,64,2,512]{3,1,2,0:T(8,128)S(1)}, u32[]{:S(2)}, u32[]{:S(2)}) collective-permute-start(f32[1,64,2,512]{3,1,2,0:T(8,128)S(1)} %constant_dynamic-slice_fusion.1), channel_id=1, source_target_pairs={{0,4},{1,5},{2,6},{3,7},{4,0},{5,1},{6,2},{7,3},{8,12},{9,13},{10,... | collective-permute-start | bytes 786440 | tf_op jit(solution)/shard_map/ppermute | solution.py:66
  85.1 2.6 %collective-permute-done.18 = f32[2,64,512]{2,1,0:T(8,128)S(1)} collective-permute-done((f32[2,64,512]{2,1,0:T(8,128)S(1)}, f32[2,64,512]{2,1,0:T(8,128)S(1)}, u32[]{:S(2)}, u32[]{:S(2)}) %collective-permute-start.18) | collective-permute-done | bytes 262176 | tf_op jit(solution)/shard_map/ppermute | solution.py:66
  87.8 3.2 %collective-permute-done.13 = f32[1,64,2,512]{3,1,2,0:T(8,128)S(1)} collective-permute-done((f32[1,64,2,512]{3,1,2,0:T(8,128)S(1)}, f32[1,64,2,512]{3,1,2,0:T(8,128)S(1)}, u32[]{:S(2)}, u32[]{:S(2)}) %collective-permute-start.13) | collective-permute-done | bytes 262176 | tf_op jit(solution)/shard_map/ppermute | solution.py:66
  91.2 1.6 %collective-permute-start.14 = (f32[64,512]{1,0:T(8,128)S(1)}, f32[64,512]{1,0:T(8,128)S(1)}, u32[]{:S(2)}, u32[]{:S(2)}) collective-permute-start(f32[64,512]{1,0:T(8,128)S(1)} %get-tuple-element.16), channel_id=1, source_target_pairs={{0,8},{8,0},{16,24},{24,16},{1,9},{9,1},{17,25},{25,17},{2,10},{10... | collective-permute-start | bytes 393224 | tf_op jit(solution)/shard_map/ppermute | solution.py:170
  92.8 1.5 %collective-permute-start.15 = (f32[64,512]{1,0:T(8,128)S(1)}, f32[64,512]{1,0:T(8,128)S(1)}, u32[]{:S(2)}, u32[]{:S(2)}) collective-permute-start(f32[64,512]{1,0:T(8,128)S(1)} %get-tuple-element.17), channel_id=1, source_target_pairs={{0,16},{8,24},{16,0},{24,8},{1,17},{9,25},{17,1},{25,9},{2,18},{10... | collective-permute-start | bytes 393224 | tf_op jit(solution)/shard_map/ppermute | solution.py:170
  94.7 3.1 %collective-permute-done.19 = f32[1,64,512]{2,1,0:T(8,128)S(1)} collective-permute-done((f32[1,64,512]{2,1,0:T(8,128)S(1)}, f32[1,64,512]{2,1,0:T(8,128)S(1)}, u32[]{:S(2)}, u32[]{:S(2)}) %collective-permute-start.19) | collective-permute-done | bytes 131104 | tf_op jit(solution)/shard_map/ppermute | solution.py:66
  97.9 0.7 dynamic-slice_add_fusion.1
  98.5 1.6 %collective-permute-done.16 = f32[64,512]{1,0:T(8,128)S(1)} collective-permute-done((f32[64,512]{1,0:T(8,128)S(1)}, f32[64,512]{1,0:T(8,128)S(1)}, u32[]{:S(2)}, u32[]{:S(2)}) %collective-permute-start.16) | collective-permute-done | bytes 131104 | tf_op jit(solution)/shard_map/ppermute | solution.py:170
  100.1 0.7 fusion.26
  (66 shorter events, 6.4 us)
Async XLA Ops:
  0.6 22.6 %copy-start.1 = (bf16[1,1280,1024]{2,1,0:T(8,128)(2,1)S(1)}, bf16[1,1280,1024]{2,1,0:T(8,128)(2,1)}, u32[]{:S(2)}) copy-start(bf16[1,1280,1024]{2,1,0:T(8,128)(2,1)} %param.11) | copy-start | bytes 7864324
  1.5 5.0 %collective-permute-start = (bf16[1,64,128]{2,0,1:T(2,128)(2,1)S(1)}, bf16[1,64,128]{2,0,1:T(2,128)(2,1)S(1)}, u32[]{:S(2)}, u32[]{:S(2)}) collective-permute-start(bf16[1,64,128]{2,0,1:T(2,128)(2,1)S(1)} %copy.33), channel_id=1, source_target_pairs={{0,16},{8,24},{16,0},{24,8},{1,17},{9,25},{17,1},{25,9},{2,18},{10... | collective-permute-start | bytes 49160 | tf_op jit(solution)/shard_map/ppermute | solution.py:40
  6.6 4.0 %collective-permute-start.1 = (bf16[2,64,128]{2,0,1:T(2,128)(2,1)S(1)}, bf16[2,64,128]{2,0,1:T(2,128)(2,1)S(1)}, u32[]{:S(2)}, u32[]{:S(2)}) collective-permute-start(bf16[2,64,128]{2,0,1:T(2,128)(2,1)S(1)} %pad_maximum_fusion.5), channel_id=1, source_target_pairs={{0,8},{8,0},{16,24},{24,16},{1,9},{9,1},{17,25},{25,17},{2,10},{10... | collective-permute-start | bytes 98312 | tf_op jit(solution)/shard_map/ppermute | solution.py:40
  10.8 5.2 %collective-permute-start.2 = (bf16[2,64,128]{2,0,1:T(2,128)(2,1)S(1)}, bf16[2,64,128]{2,0,1:T(2,128)(2,1)S(1)}, u32[]{:S(2)}, u32[]{:S(2)}) collective-permute-start(bf16[2,64,128]{2,0,1:T(2,128)(2,1)S(1)} %convolution_convert_fusion), channel_id=1, source_target_pairs={{0,4},{1,5},{2,6},{3,7},{4,0},{5,1},{6,2},{7,3},{8,12},{9,13},{10,... | collective-permute-start | bytes 98312 | tf_op jit(solution)/shard_map/ppermute | solution.py:40
  16.0 4.3 %collective-permute-start.3 = (bf16[2,128,128]{2,0,1:T(2,128)(2,1)S(1)}, bf16[2,128,128]{2,0,1:T(2,128)(2,1)S(1)}, u32[]{:S(2)}, u32[]{:S(2)}) collective-permute-start(bf16[2,128,128]{2,0,1:T(2,128)(2,1)S(1)} %pad_maximum_fusion.4), channel_id=1, source_target_pairs={{0,2},{1,3},{2,0},{3,1},{4,6},{5,7},{6,4},{7,5},{8,10},{9,11},{10,... | collective-permute-start | bytes 196616 | tf_op jit(solution)/shard_map/ppermute | solution.py:40
  20.6 1.5 %collective-permute-start.4 = (bf16[2,256,128]{2,0,1:T(2,128)(2,1)S(1)}, bf16[2,256,128]{2,0,1:T(2,128)(2,1)S(1)}, u32[]{:S(2)}, u32[]{:S(2)}) collective-permute-start(bf16[2,256,128]{2,0,1:T(2,128)(2,1)S(1)} %pad_maximum_fusion.1), channel_id=1, source_target_pairs={{0,1},{1,0},{2,3},{3,2},{4,5},{5,4},{6,7},{7,6},{8,9},{9,8},{10,11... | collective-permute-start | bytes 393224 | tf_op jit(solution)/shard_map/ppermute | solution.py:40
  23.2 1.6 %copy-start.4 = (f32[1,1280]{1,0:T(1,128)S(1)}, f32[1,1280]{1,0:T(1,128)}, u32[]{:S(2)}) copy-start(f32[1,1280]{1,0:T(1,128)} %param.17) | copy-start | bytes 15364
  23.2 2.5 %copy-start = (bf16[1,1280,2048]{2,1,0:T(8,128)(2,1)S(1)}, bf16[1,1280,2048]{2,1,0:T(8,128)(2,1)}, u32[]{:S(2)}) copy-start(bf16[1,1280,2048]{2,1,0:T(8,128)(2,1)} %param.12) | copy-start | bytes 15728644
  25.7 12.3 %copy-start.2 = (f32[1,256,2048]{2,1,0:T(8,128)S(1)}, f32[1,256,2048]{2,1,0:T(8,128)}, u32[]{:S(2)}) copy-start(f32[1,256,2048]{2,1,0:T(8,128)} %param.18) | copy-start | bytes 6291460
  27.9 1.4 %collective-permute-start.5 = (f32[2,2176]{1,0:T(2,128)S(1)}, f32[2,2176]{1,0:T(2,128)S(1)}, u32[]{:S(2)}, u32[]{:S(2)}) collective-permute-start(f32[2,2176]{1,0:T(2,128)S(1)} %pad_maximum_fusion.6), channel_id=1, source_target_pairs={{0,1},{1,0},{2,3},{3,2},{4,5},{5,4},{6,7},{7,6},{8,9},{9,8},{10,11... | collective-permute-start | bytes 52232 | tf_op jit(solution)/shard_map/ppermute | solution.py:27
  29.4 3.8 %collective-permute-start.6 = (f32[2,2176]{1,0:T(2,128)S(1)}, f32[2,2176]{1,0:T(2,128)S(1)}, u32[]{:S(2)}, u32[]{:S(2)}) collective-permute-start(f32[2,2176]{1,0:T(2,128)S(1)} %fusion.47), channel_id=1, source_target_pairs={{0,2},{1,3},{2,0},{3,1},{4,6},{5,7},{6,4},{7,5},{8,10},{9,11},{10,... | collective-permute-start | bytes 52232 | tf_op jit(solution)/shard_map/ppermute | solution.py:27
  33.2 4.8 %collective-permute-start.7 = (f32[2,2176]{1,0:T(2,128)S(1)}, f32[2,2176]{1,0:T(2,128)S(1)}, u32[]{:S(2)}, u32[]{:S(2)}) collective-permute-start(f32[2,2176]{1,0:T(2,128)S(1)} %add.132), channel_id=1, source_target_pairs={{0,4},{1,5},{2,6},{3,7},{4,0},{5,1},{6,2},{7,3},{8,12},{9,13},{10,... | collective-permute-start | bytes 52232 | tf_op jit(solution)/shard_map/ppermute | solution.py:27
  38.3 4.5 %collective-permute-start.8 = (f32[256]{0:T(256)S(1)}, f32[256]{0:T(256)S(1)}, u32[]{:S(2)}, u32[]{:S(2)}) collective-permute-start(f32[256]{0:T(256)S(1)} %fusion.2), channel_id=1, source_target_pairs={{0,4},{1,5},{2,6},{3,7},{4,0},{5,1},{6,2},{7,3},{8,12},{9,13},{10,... | collective-permute-start | bytes 3080 | tf_op jit(solution)/shard_map/ppermute | solution.py:40
  42.8 3.6 %collective-permute-start.9 = (f32[512]{0:T(512)S(1)}, f32[512]{0:T(512)S(1)}, u32[]{:S(2)}, u32[]{:S(2)}) collective-permute-start(f32[512]{0:T(512)S(1)} %pad_maximum_fusion.10), channel_id=1, source_target_pairs={{0,2},{1,3},{2,0},{3,1},{4,6},{5,7},{6,4},{7,5},{8,10},{9,11},{10,... | collective-permute-start | bytes 6152 | tf_op jit(solution)/shard_map/ppermute | solution.py:40
  46.4 1.2 %collective-permute-start.10 = (f32[1024]{0:T(1024)S(1)}, f32[1024]{0:T(1024)S(1)}, u32[]{:S(2)}, u32[]{:S(2)}) collective-permute-start(f32[1024]{0:T(1024)S(1)} %pad_maximum_fusion.9), channel_id=1, source_target_pairs={{0,1},{1,0},{2,3},{3,2},{4,5},{5,4},{6,7},{7,6},{8,9},{9,8},{10,11... | collective-permute-start | bytes 12296 | tf_op jit(solution)/shard_map/ppermute | solution.py:40
  57.0 2.7 %collective-permute-start.11 = (f32[4,64,2,512]{3,1,2,0:T(8,128)S(1)}, f32[4,64,2,512]{3,1,2,0:T(8,128)S(1)}, u32[]{:S(2)}, u32[]{:S(2)}) collective-permute-start(f32[4,64,2,512]{3,1,2,0:T(8,128)S(1)} %bitcast.91), channel_id=1, source_target_pairs={{0,1},{1,0},{2,3},{3,2},{4,5},{5,4},{6,7},{7,6},{8,9},{9,8},{10,11... | collective-permute-start | bytes 3145736 | tf_op jit(solution)/shard_map/ppermute | solution.py:66
  58.1 1.8 %copy-start.3 = (f32[512,512]{1,0:T(8,128)}, f32[512,512]{1,0:T(8,128)S(1)}, u32[]{:S(2)}) copy-start(f32[512,512]{1,0:T(8,128)S(1)} %fusion.8) | copy-start | bytes 3145732
  60.0 2.1 %collective-permute-start.17 = (f32[4,64,512]{2,1,0:T(8,128)S(1)}, f32[4,64,512]{2,1,0:T(8,128)S(1)}, u32[]{:S(2)}, u32[]{:S(2)}) collective-permute-start(f32[4,64,512]{2,1,0:T(8,128)S(1)} %dynamic-slice_bitcast_fusion), channel_id=1, source_target_pairs={{0,1},{1,0},{2,3},{3,2},{4,5},{5,4},{6,7},{7,6},{8,9},{9,8},{10,11... | collective-permute-start | bytes 1572872 | tf_op jit(solution)/shard_map/ppermute | solution.py:66
  60.2 19.2 %copy-start.5 = (s32[1,2]{1,0:T(1,128)S(1)}, s32[1,2]{1,0:T(1,128)}, u32[]{:S(2)}) copy-start(s32[1,2]{1,0:T(1,128)} %param.15) | copy-start | bytes 28
  60.2 14.2 %collective-permute-start.12 = (f32[2,64,2,512]{3,1,2,0:T(8,128)S(1)}, f32[2,64,2,512]{3,1,2,0:T(8,128)S(1)}, u32[]{:S(2)}, u32[]{:S(2)}) collective-permute-start(f32[2,64,2,512]{3,1,2,0:T(8,128)S(1)} %dynamic-slice_bitcast_fusion.1), channel_id=1, source_target_pairs={{0,2},{1,3},{2,0},{3,1},{4,6},{5,7},{6,4},{7,5},{8,10},{9,11},{10,... | collective-permute-start | bytes 1572872 | tf_op jit(solution)/shard_map/ppermute | solution.py:66
  74.6 13.1 %collective-permute-start.18 = (f32[2,64,512]{2,1,0:T(8,128)S(1)}, f32[2,64,512]{2,1,0:T(8,128)S(1)}, u32[]{:S(2)}, u32[]{:S(2)}) collective-permute-start(f32[2,64,512]{2,1,0:T(8,128)S(1)} %dynamic-slice_bitcast_fusion.2), channel_id=1, source_target_pairs={{0,2},{1,3},{2,0},{3,1},{4,6},{5,7},{6,4},{7,5},{8,10},{9,11},{10,... | collective-permute-start | bytes 786440 | tf_op jit(solution)/shard_map/ppermute | solution.py:66
  76.4 14.5 %collective-permute-start.13 = (f32[1,64,2,512]{3,1,2,0:T(8,128)S(1)}, f32[1,64,2,512]{3,1,2,0:T(8,128)S(1)}, u32[]{:S(2)}, u32[]{:S(2)}) collective-permute-start(f32[1,64,2,512]{3,1,2,0:T(8,128)S(1)} %constant_dynamic-slice_fusion.1), channel_id=1, source_target_pairs={{0,4},{1,5},{2,6},{3,7},{4,0},{5,1},{6,2},{7,3},{8,12},{9,13},{10,... | collective-permute-start | bytes 786440 | tf_op jit(solution)/shard_map/ppermute | solution.py:66
  91.0 6.8 %collective-permute-start.19 = (f32[1,64,512]{2,1,0:T(8,128)S(1)}, f32[1,64,512]{2,1,0:T(8,128)S(1)}, u32[]{:S(2)}, u32[]{:S(2)}) collective-permute-start(f32[1,64,512]{2,1,0:T(8,128)S(1)} %constant_dynamic-slice_fusion), channel_id=1, source_target_pairs={{0,4},{1,5},{2,6},{3,7},{4,0},{5,1},{6,2},{7,3},{8,12},{9,13},{10,... | collective-permute-start | bytes 393224 | tf_op jit(solution)/shard_map/ppermute | solution.py:66
  91.2 7.4 %collective-permute-start.14 = (f32[64,512]{1,0:T(8,128)S(1)}, f32[64,512]{1,0:T(8,128)S(1)}, u32[]{:S(2)}, u32[]{:S(2)}) collective-permute-start(f32[64,512]{1,0:T(8,128)S(1)} %get-tuple-element.16), channel_id=1, source_target_pairs={{0,8},{8,0},{16,24},{24,16},{1,9},{9,1},{17,25},{25,17},{2,10},{10... | collective-permute-start | bytes 393224 | tf_op jit(solution)/shard_map/ppermute | solution.py:170
  92.8 5.8 %collective-permute-start.15 = (f32[64,512]{1,0:T(8,128)S(1)}, f32[64,512]{1,0:T(8,128)S(1)}, u32[]{:S(2)}, u32[]{:S(2)}) collective-permute-start(f32[64,512]{1,0:T(8,128)S(1)} %get-tuple-element.17), channel_id=1, source_target_pairs={{0,16},{8,24},{16,0},{24,8},{1,17},{9,25},{17,1},{25,9},{2,18},{10... | collective-permute-start | bytes 393224 | tf_op jit(solution)/shard_map/ppermute | solution.py:170
  94.3 5.9 %collective-permute-start.16 = (f32[64,512]{1,0:T(8,128)S(1)}, f32[64,512]{1,0:T(8,128)S(1)}, u32[]{:S(2)}, u32[]{:S(2)}) collective-permute-start(f32[64,512]{1,0:T(8,128)S(1)} %get-tuple-element.18), channel_id=1, source_target_pairs={{0,24},{8,16},{16,8},{24,0},{1,25},{9,17},{17,9},{25,1},{2,26},{10... | collective-permute-start | bytes 393224 | tf_op jit(solution)/shard_map/ppermute | solution.py:170

commit v16 on v15

--- a/solution.py
+++ b/solution.py
@@ -99,10 +99,17 @@
     wanted = jnp.sum(
         jnp.where(frag_ids[None, :] == dimer_pairs[0][:, None], frag_slot[None, :], 0), axis=1
     )
-    selector = (slot_held[None, :] == wanted[:, None]).astype(jnp.bfloat16)
-    chosen = jnp.einsum(
-        "as,srk->ark", selector, gathered, preferred_element_type=jnp.float32
-    ).astype(jnp.bfloat16)
+    chosen = jnp.stack(
+        [
+            jnp.sum(
+                jnp.where(
+                    (slot_held == wanted[a])[:, None, None], gathered, jnp.zeros((), gathered.dtype)
+                ),
+                axis=0,
+            )
+            for a in range(2)
+        ]
+    )
     dimer_factors = in_order(*xor_gather(chosen, "grid", 1), 1)
     nocc = dimer_factors.shape[2]
     empty = jnp.zeros((frag_basis, nocc), jnp.bfloat16)
@@ -134,7 +141,7 @@
     coef_rows = jnp.sum(metric_inv[0] * fitted[None, :], axis=1)
     coefficients = in_order(*xor_gather(coef_rows, "grid", 0), 0)
     coulomb = jnp.sum(aux_block.astype(jnp.float32) * coefficients[None, :], axis=1)
-    potential_total = jnp.dot(coefficients, weight_projection, precision=highest) + exchange_total
+    potential_total = jnp.sum(coefficients * weight_projection) + exchange_total
     average = potential_total / weight_sum
     potential = live_weight * (coulomb + exchange - average)
     weighted_basis = (basis_rows * potential[:, None]).astype(jnp.bfloat16)

time: 101 us -> 101 us (level)
  starting transfers between devices: 31 us -> 28.8 us
  other arithmetic: 14.1 us -> 15.6 us
    eq x0 -> x1, other arithmetic: none -> 1.95 us  [shards(): slot_held == wanted[a]]
    ppermute x8, starting transfers between devices: 14.9 us -> 13.3 us  [xor_gather(): other = lax.ppermute(value, axis, [(i, i ^ 1 << bit) for i in range(size)])]
  transfers between devices with their start and end apart: 20 -> 20, of which waited for: 16 -> 16; matrix products, arithmetic and copies ran while one was open for 7% -> 9% of each run, Pallas kernels for 0% -> 0%
where the time goes in v16:
time: 101 us
  waiting for transfers between devices  38.5 us (38%)
  starting transfers between devices  28.8 us (29%)
  other arithmetic  15.6 us (15%)
  between operations  8.8 us (9%)
  local copies, waits for them, and re-layouts  4.73 us (5%)
  matrix products  4.33 us (4%)
    ppermute x6, waiting for transfers between devices, scatter_step(): lax.ppermute(send, axis, [(i, i ^ 1 << bit) for i in range(size)])  22 us
    ppermute x8, starting transfers between devices, xor_gather(): other = lax.ppermute(value, axis, [(i, i ^ 1 << bit) for i in range(size)])  13.3 us
    ppermute x8, waiting for transfers between devices, xor_gather(): other = lax.ppermute(value, axis, [(i, i ^ 1 << bit) for i in range(size)])  10.9 us
    ppermute x6, starting transfers between devices, scatter_step(): lax.ppermute(send, axis, [(i, i ^ 1 << bit) for i in range(size)])  6.83 us
    ppermute x3, starting transfers between devices, xor_sum(): lax.ppermute(value, axis, [(i, i ^ step) for i in range(size)])  5.09 us
    ppermute x3, waiting for transfers between devices, xor_sum(): lax.ppermute(value, axis, [(i, i ^ step) for i in range(size)])  4.84 us
    reduce_sum x1, other arithmetic, shards(): jnp.sum(aux_block.astype(jnp.float32) * coefficients[None, :], axis=1)  3.59 us
    ppermute x3, starting transfers between devices, shards(): frag_fock = frag_fock + lax.ppermute(piece(dest), 'dimer', pairs)  3.55 us
  transfers between devices with their start and end apart: 20, of which 16 were waited for; matrix products, arithmetic and copies ran while one was open for 9% of the time, Pallas kernels for 0%

profile of v16, /device:TPU:0, one launch (start us, length us, event | category | flops | bytes accessed | tf_op | source)
XLA Modules:
  0.0 100.7 jit_solution(10190922123710753703)
XLA Ops:
  0.6 3.1 %collective-permute-start = (bf16[1,64,128]{2,1,0:T(8,128)(2,1)}, bf16[1,64,128]{2,1,0:T(8,128)(2,1)S(1)}, u32[]{:S(2)}, u32[]{:S(2)}) collective-permute-start(bf16[1,64,128]{2,1,0:T(8,128)(2,1)} %param.13), channel_id=1, source_target_pairs={{0,16},{8,24},{16,0},{24,8},{1,17},{9,25},{17,1},{25,9},{2,18},{10... | collective-permute-start | bytes 49160 | tf_op jit(solution)/shard_map/ppermute | solution.py:40
  3.7 0.9 fusion.33
  5.1 2.0 %xor_compare_fusion = (pred[4]{0:T(512)(128)(4,1)S(1)}, pred[4]{0:T(512)(128)(4,1)S(1)}) fusion(s32[4]{0:T(128)} %constant.100.clone, s32[]{:T(128)} %bitcast.8, s32[]{:T(128)S(6)} %axis_index.15, s32[]{:T(128)} %bitcast.6), kind=kLoop, calls=%fused_computation.92 | loop fusion | flops 12 | bytes 36 | tf_op jit(solution)/shard_map/eq | solution.py:106
  7.1 0.7 constant_dynamic-update-slice_fusion.2
  7.8 0.7 pad_maximum_fusion.3
  8.5 1.5 %collective-permute-start.1 = (bf16[2,64,128]{2,1,0:T(8,128)(2,1)S(1)}, bf16[2,64,128]{2,1,0:T(8,128)(2,1)S(1)}, u32[]{:S(2)}, u32[]{:S(2)}) collective-permute-start(bf16[2,64,128]{2,1,0:T(8,128)(2,1)S(1)} %pad_maximum_fusion.3), channel_id=1, source_target_pairs={{0,8},{8,0},{16,24},{24,16},{1,9},{9,1},{17,25},{25,17},{2,10},{10... | collective-permute-start | bytes 98312 | tf_op jit(solution)/shard_map/ppermute | solution.py:40
  10.0 2.4 %collective-permute-done.1 = bf16[2,64,128]{2,1,0:T(8,128)(2,1)S(1)} collective-permute-done((bf16[2,64,128]{2,1,0:T(8,128)(2,1)S(1)}, bf16[2,64,128]{2,1,0:T(8,128)(2,1)S(1)}, u32[]{:S(2)}, u32[]{:S(2)}) %collective-permute-start.1) | collective-permute-done | bytes 32800 | tf_op jit(solution)/shard_map/ppermute | solution.py:40
  12.6 2.7 %collective-permute-start.2 = (bf16[2,64,128]{2,1,0:T(8,128)(2,1)S(1)}, bf16[2,64,128]{2,1,0:T(8,128)(2,1)S(1)}, u32[]{:S(2)}, u32[]{:S(2)}) collective-permute-start(bf16[2,64,128]{2,1,0:T(8,128)(2,1)S(1)} %pad_maximum_fusion.4), channel_id=1, source_target_pairs={{0,4},{1,5},{2,6},{3,7},{4,0},{5,1},{6,2},{7,3},{8,12},{9,13},{10,... | collective-permute-start | bytes 98312 | tf_op jit(solution)/shard_map/ppermute | solution.py:40
  15.2 2.2 %collective-permute-done.2 = bf16[2,64,128]{2,1,0:T(8,128)(2,1)S(1)} collective-permute-done((bf16[2,64,128]{2,1,0:T(8,128)(2,1)S(1)}, bf16[2,64,128]{2,1,0:T(8,128)(2,1)S(1)}, u32[]{:S(2)}, u32[]{:S(2)}) %collective-permute-start.2) | collective-permute-done | bytes 32800 | tf_op jit(solution)/shard_map/ppermute | solution.py:40
  17.5 1.6 %collective-permute-start.3 = (bf16[2,128,128]{2,1,0:T(8,128)(2,1)S(1)}, bf16[2,128,128]{2,1,0:T(8,128)(2,1)S(1)}, u32[]{:S(2)}, u32[]{:S(2)}) collective-permute-start(bf16[2,128,128]{2,1,0:T(8,128)(2,1)S(1)} %pad_maximum_fusion.2), channel_id=1, source_target_pairs={{0,2},{1,3},{2,0},{3,1},{4,6},{5,7},{6,4},{7,5},{8,10},{9,11},{10,... | collective-permute-start | bytes 196616 | tf_op jit(solution)/shard_map/ppermute | solution.py:40
  19.0 0.7 compare_and_fusion
  19.7 2.0 %collective-permute-done.3 = bf16[2,128,128]{2,1,0:T(8,128)(2,1)S(1)} collective-permute-done((bf16[2,128,128]{2,1,0:T(8,128)(2,1)S(1)}, bf16[2,128,128]{2,1,0:T(8,128)(2,1)S(1)}, u32[]{:S(2)}, u32[]{:S(2)}) %collective-permute-start.3) | collective-permute-done | bytes 65568 | tf_op jit(solution)/shard_map/ppermute | solution.py:40
  22.5 0.7 reduce.3
  23.3 0.6 gather_fusion
  24.0 0.9 fusion.7
  24.9 0.7 multiply_reduce_fusion.2
  25.7 0.8 copy-done
  26.5 0.8 fusion
  27.3 1.4 %pad_maximum_fusion.10 = f32[2]{0:T(128)S(1)} fusion(f32[1]{0:T(128)} %bitcast.15, f32[1]{0:T(128)} %bitcast.14), kind=kLoop, calls=%fused_computation.94 | loop fusion | flops 2 | bytes 16 | tf_op jit(solution)/shard_map/stack | solution.py:131
  29.4 0.8 collective-permute-done.5
  30.2 1.6 %collective-permute-start.6 = (f32[2,2176]{1,0:T(2,128)S(1)}, f32[2,2176]{1,0:T(2,128)S(1)}, u32[]{:S(2)}, u32[]{:S(2)}) collective-permute-start(f32[2,2176]{1,0:T(2,128)S(1)} %fusion.39), channel_id=1, source_target_pairs={{0,2},{1,3},{2,0},{3,1},{4,6},{5,7},{6,4},{7,5},{8,10},{9,11},{10,... | collective-permute-start | bytes 52232 | tf_op jit(solution)/shard_map/ppermute | solution.py:27
  31.9 2.2 %collective-permute-done.6 = f32[2,2176]{1,0:T(2,128)S(1)} collective-permute-done((f32[2,2176]{1,0:T(2,128)S(1)}, f32[2,2176]{1,0:T(2,128)S(1)}, u32[]{:S(2)}, u32[]{:S(2)}) %collective-permute-start.6) | collective-permute-done | bytes 17440 | tf_op jit(solution)/shard_map/ppermute | solution.py:27
  34.1 2.9 %collective-permute-start.7 = (f32[2,2176]{1,0:T(2,128)S(1)}, f32[2,2176]{1,0:T(2,128)S(1)}, u32[]{:S(2)}, u32[]{:S(2)}) collective-permute-start(f32[2,2176]{1,0:T(2,128)S(1)} %add.132), channel_id=1, source_target_pairs={{0,4},{1,5},{2,6},{3,7},{4,0},{5,1},{6,2},{7,3},{8,12},{9,13},{10,... | collective-permute-start | bytes 52232 | tf_op jit(solution)/shard_map/ppermute | solution.py:27
  37.0 1.8 %collective-permute-done.7 = f32[2,2176]{1,0:T(2,128)S(1)} collective-permute-done((f32[2,2176]{1,0:T(2,128)S(1)}, f32[2,2176]{1,0:T(2,128)S(1)}, u32[]{:S(2)}, u32[]{:S(2)}) %collective-permute-start.7) | collective-permute-done | bytes 17440 | tf_op jit(solution)/shard_map/ppermute | solution.py:27
  39.0 2.9 %collective-permute-start.8 = (f32[256]{0:T(256)S(1)}, f32[256]{0:T(256)S(1)}, u32[]{:S(2)}, u32[]{:S(2)}) collective-permute-start(f32[256]{0:T(256)S(1)} %fusion.2), channel_id=1, source_target_pairs={{0,4},{1,5},{2,6},{3,7},{4,0},{5,1},{6,2},{7,3},{8,12},{9,13},{10,... | collective-permute-start | bytes 3080 | tf_op jit(solution)/shard_map/ppermute | solution.py:40
  41.9 1.6 %collective-permute-done.8 = f32[256]{0:T(256)S(1)} collective-permute-done((f32[256]{0:T(256)S(1)}, f32[256]{0:T(256)S(1)}, u32[]{:S(2)}, u32[]{:S(2)}) %collective-permute-start.8) | collective-permute-done | bytes 1056 | tf_op jit(solution)/shard_map/ppermute | solution.py:40
  43.6 1.6 %collective-permute-start.9 = (f32[512]{0:T(512)S(1)}, f32[512]{0:T(512)S(1)}, u32[]{:S(2)}, u32[]{:S(2)}) collective-permute-start(f32[512]{0:T(512)S(1)} %pad_maximum_fusion.9), channel_id=1, source_target_pairs={{0,2},{1,3},{2,0},{3,1},{4,6},{5,7},{6,4},{7,5},{8,10},{9,11},{10,... | collective-permute-start | bytes 6152 | tf_op jit(solution)/shard_map/ppermute | solution.py:40
  45.2 2.0 %collective-permute-done.9 = f32[512]{0:T(512)S(1)} collective-permute-done((f32[512]{0:T(512)S(1)}, f32[512]{0:T(512)S(1)}, u32[]{:S(2)}, u32[]{:S(2)}) %collective-permute-start.9) | collective-permute-done | bytes 2080 | tf_op jit(solution)/shard_map/ppermute | solution.py:40
  49.0 3.6 %multiply_reduce_fusion = f32[1280]{0:T(1024)S(1)} fusion(bf16[1,1280,2048]{2,1,0:T(8,128)(2,1)} %param.12, f32[2048]{0:T(1024)S(1)} %bitcast.106), kind=kLoop, calls=%fused_computation.2 | loop fusion | flops 7863040 | bytes 5256192 | tf_op jit(solution)/shard_map/reduce_sum | solution.py:143
  52.6 0.6 multiply_reduce_fusion.1
  55.7 0.9 fusion.3
  56.6 0.9 fusion.5
  58.0 0.9 fusion.8
  58.9 1.6 %collective-permute-done.11 = f32[4,64,2,512]{3,1,2,0:T(8,128)S(1)} collective-permute-done((f32[4,64,2,512]{3,1,2,0:T(8,128)S(1)}, f32[4,64,2,512]{3,1,2,0:T(8,128)S(1)}, u32[]{:S(2)}, u32[]{:S(2)}) %collective-permute-start.11) | collective-permute-done | bytes 1048608 | tf_op jit(solution)/shard_map/ppermute | solution.py:66
  61.1 1.6 %collective-permute-start.12 = (f32[2,64,2,512]{3,1,2,0:T(8,128)S(1)}, f32[2,64,2,512]{3,1,2,0:T(8,128)S(1)}, u32[]{:S(2)}, u32[]{:S(2)}) collective-permute-start(f32[2,64,2,512]{3,1,2,0:T(8,128)S(1)} %dynamic-slice_bitcast_fusion.1), channel_id=1, source_target_pairs={{0,2},{1,3},{2,0},{3,1},{4,6},{5,7},{6,4},{7,5},{8,10},{9,11},{10,... | collective-permute-start | bytes 1572872 | tf_op jit(solution)/shard_map/ppermute | solution.py:66
  62.8 1.1 %bitcast_add_fusion.1 = f32[4,64,512]{2,1,0:T(8,128)S(1)} fusion(f32[4,64,512]{2,1,0:T(8,128)S(1)} %collective-permute-done.17, f32[4,2,64,512]{3,2,1,0:T(8,128)} %bitcast.95, s32[]{:T(128)S(6)} %select_n.152), kind=kLoop, calls=%fused_computation.35 | loop fusion | flops 131072 | bytes 1572868 | tf_op jit(solution)/shard_map/add | solution.py:66
  63.9 11.4 %collective-permute-done.12 = f32[2,64,2,512]{3,1,2,0:T(8,128)S(1)} collective-permute-done((f32[2,64,2,512]{3,1,2,0:T(8,128)S(1)}, f32[2,64,2,512]{3,1,2,0:T(8,128)S(1)}, u32[]{:S(2)}, u32[]{:S(2)}) %collective-permute-start.12) | collective-permute-done | bytes 524320 | tf_op jit(solution)/shard_map/ppermute | solution.py:66
  75.4 1.6 %collective-permute-start.18 = (f32[2,64,512]{2,1,0:T(8,128)S(1)}, f32[2,64,512]{2,1,0:T(8,128)S(1)}, u32[]{:S(2)}, u32[]{:S(2)}) collective-permute-start(f32[2,64,512]{2,1,0:T(8,128)S(1)} %dynamic-slice_bitcast_fusion.2), channel_id=1, source_target_pairs={{0,2},{1,3},{2,0},{3,1},{4,6},{5,7},{6,4},{7,5},{8,10},{9,11},{10,... | collective-permute-start | bytes 786440 | tf_op jit(solution)/shard_map/ppermute | solution.py:66
  77.1 3.0 %collective-permute-start.13 = (f32[1,64,2,512]{3,1,2,0:T(8,128)S(1)}, f32[1,64,2,512]{3,1,2,0:T(8,128)S(1)}, u32[]{:S(2)}, u32[]{:S(2)}) collective-permute-start(f32[1,64,2,512]{3,1,2,0:T(8,128)S(1)} %constant_dynamic-slice_fusion.1), channel_id=1, source_target_pairs={{0,4},{1,5},{2,6},{3,7},{4,0},{5,1},{6,2},{7,3},{8,12},{9,13},{10,... | collective-permute-start | bytes 786440 | tf_op jit(solution)/shard_map/ppermute | solution.py:66
  85.9 2.7 %collective-permute-done.18 = f32[2,64,512]{2,1,0:T(8,128)S(1)} collective-permute-done((f32[2,64,512]{2,1,0:T(8,128)S(1)}, f32[2,64,512]{2,1,0:T(8,128)S(1)}, u32[]{:S(2)}, u32[]{:S(2)}) %collective-permute-start.18) | collective-permute-done | bytes 262176 | tf_op jit(solution)/shard_map/ppermute | solution.py:66
  88.6 3.1 %collective-permute-done.13 = f32[1,64,2,512]{3,1,2,0:T(8,128)S(1)} collective-permute-done((f32[1,64,2,512]{3,1,2,0:T(8,128)S(1)}, f32[1,64,2,512]{3,1,2,0:T(8,128)S(1)}, u32[]{:S(2)}, u32[]{:S(2)}) %collective-permute-start.13) | collective-permute-done | bytes 262176 | tf_op jit(solution)/shard_map/ppermute | solution.py:66
  91.9 1.5 %collective-permute-start.14 = (f32[64,512]{1,0:T(8,128)S(1)}, f32[64,512]{1,0:T(8,128)S(1)}, u32[]{:S(2)}, u32[]{:S(2)}) collective-permute-start(f32[64,512]{1,0:T(8,128)S(1)} %get-tuple-element.18), channel_id=1, source_target_pairs={{0,8},{8,0},{16,24},{24,16},{1,9},{9,1},{17,25},{25,17},{2,10},{10... | collective-permute-start | bytes 393224 | tf_op jit(solution)/shard_map/ppermute | solution.py:177
  93.5 0.7 collective-permute-start.15
  94.2 1.3 %collective-permute-start.16 = (f32[64,512]{1,0:T(8,128)S(1)}, f32[64,512]{1,0:T(8,128)S(1)}, u32[]{:S(2)}, u32[]{:S(2)}) collective-permute-start(f32[64,512]{1,0:T(8,128)S(1)} %get-tuple-element.20), channel_id=1, source_target_pairs={{0,24},{8,16},{16,8},{24,0},{1,25},{9,17},{17,9},{25,1},{2,26},{10... | collective-permute-start | bytes 393224 | tf_op jit(solution)/shard_map/ppermute | solution.py:177
  95.5 3.2 %collective-permute-done.19 = f32[1,64,512]{2,1,0:T(8,128)S(1)} collective-permute-done((f32[1,64,512]{2,1,0:T(8,128)S(1)}, f32[1,64,512]{2,1,0:T(8,128)S(1)}, u32[]{:S(2)}, u32[]{:S(2)}) %collective-permute-start.19) | collective-permute-done | bytes 131104 | tf_op jit(solution)/shard_map/ppermute | solution.py:66
  98.6 0.7 dynamic-slice_add_fusion.1
  99.3 0.7 collective-permute-done.16
  100.0 0.7 fusion.26
  (69 shorter events, 6.4 us)
Async XLA Ops:
  0.6 23.4 %copy-start.1 = (bf16[1,1280,1024]{2,1,0:T(8,128)(2,1)S(1)}, bf16[1,1280,1024]{2,1,0:T(8,128)(2,1)}, u32[]{:S(2)}) copy-start(bf16[1,1280,1024]{2,1,0:T(8,128)(2,1)} %param.11) | copy-start | bytes 7864324
  0.6 7.2 %collective-permute-start = (bf16[1,64,128]{2,1,0:T(8,128)(2,1)}, bf16[1,64,128]{2,1,0:T(8,128)(2,1)S(1)}, u32[]{:S(2)}, u32[]{:S(2)}) collective-permute-start(bf16[1,64,128]{2,1,0:T(8,128)(2,1)} %param.13), channel_id=1, source_target_pairs={{0,16},{8,24},{16,0},{24,8},{1,17},{9,25},{17,1},{25,9},{2,18},{10... | collective-permute-start | bytes 49160 | tf_op jit(solution)/shard_map/ppermute | solution.py:40
  8.5 3.9 %collective-permute-start.1 = (bf16[2,64,128]{2,1,0:T(8,128)(2,1)S(1)}, bf16[2,64,128]{2,1,0:T(8,128)(2,1)S(1)}, u32[]{:S(2)}, u32[]{:S(2)}) collective-permute-start(bf16[2,64,128]{2,1,0:T(8,128)(2,1)S(1)} %pad_maximum_fusion.3), channel_id=1, source_target_pairs={{0,8},{8,0},{16,24},{24,16},{1,9},{9,1},{17,25},{25,17},{2,10},{10... | collective-permute-start | bytes 98312 | tf_op jit(solution)/shard_map/ppermute | solution.py:40
  12.6 4.9 %collective-permute-start.2 = (bf16[2,64,128]{2,1,0:T(8,128)(2,1)S(1)}, bf16[2,64,128]{2,1,0:T(8,128)(2,1)S(1)}, u32[]{:S(2)}, u32[]{:S(2)}) collective-permute-start(bf16[2,64,128]{2,1,0:T(8,128)(2,1)S(1)} %pad_maximum_fusion.4), channel_id=1, source_target_pairs={{0,4},{1,5},{2,6},{3,7},{4,0},{5,1},{6,2},{7,3},{8,12},{9,13},{10,... | collective-permute-start | bytes 98312 | tf_op jit(solution)/shard_map/ppermute | solution.py:40
  17.5 4.3 %collective-permute-start.3 = (bf16[2,128,128]{2,1,0:T(8,128)(2,1)S(1)}, bf16[2,128,128]{2,1,0:T(8,128)(2,1)S(1)}, u32[]{:S(2)}, u32[]{:S(2)}) collective-permute-start(bf16[2,128,128]{2,1,0:T(8,128)(2,1)S(1)} %pad_maximum_fusion.2), channel_id=1, source_target_pairs={{0,2},{1,3},{2,0},{3,1},{4,6},{5,7},{6,4},{7,5},{8,10},{9,11},{10,... | collective-permute-start | bytes 196616 | tf_op jit(solution)/shard_map/ppermute | solution.py:40
  21.7 1.5 %collective-permute-start.4 = (bf16[2,256,128]{2,1,0:T(8,128)(2,1)S(1)}, bf16[2,256,128]{2,1,0:T(8,128)(2,1)S(1)}, u32[]{:S(2)}, u32[]{:S(2)}) collective-permute-start(bf16[2,256,128]{2,1,0:T(8,128)(2,1)S(1)} %pad_maximum_fusion.1), channel_id=1, source_target_pairs={{0,1},{1,0},{2,3},{3,2},{4,5},{5,4},{6,7},{7,6},{8,9},{9,8},{10,11... | collective-permute-start | bytes 393224 | tf_op jit(solution)/shard_map/ppermute | solution.py:40
  24.0 1.6 %copy-start.4 = (f32[1,1280]{1,0:T(1,128)S(1)}, f32[1,1280]{1,0:T(1,128)}, u32[]{:S(2)}) copy-start(f32[1,1280]{1,0:T(1,128)} %param.17) | copy-start | bytes 15364
  24.0 2.5 %copy-start = (bf16[1,1280,2048]{2,1,0:T(8,128)(2,1)S(1)}, bf16[1,1280,2048]{2,1,0:T(8,128)(2,1)}, u32[]{:S(2)}) copy-start(bf16[1,1280,2048]{2,1,0:T(8,128)(2,1)} %param.12) | copy-start | bytes 15728644
  26.5 12.3 %copy-start.2 = (f32[1,256,2048]{2,1,0:T(8,128)S(1)}, f32[1,256,2048]{2,1,0:T(8,128)}, u32[]{:S(2)}) copy-start(f32[1,256,2048]{2,1,0:T(8,128)} %param.18) | copy-start | bytes 6291460
  28.8 1.4 %collective-permute-start.5 = (f32[2,2176]{1,0:T(2,128)S(1)}, f32[2,2176]{1,0:T(2,128)S(1)}, u32[]{:S(2)}, u32[]{:S(2)}) collective-permute-start(f32[2,2176]{1,0:T(2,128)S(1)} %pad_maximum_fusion.5), channel_id=1, source_target_pairs={{0,1},{1,0},{2,3},{3,2},{4,5},{5,4},{6,7},{7,6},{8,9},{9,8},{10,11... | collective-permute-start | bytes 52232 | tf_op jit(solution)/shard_map/ppermute | solution.py:27
  30.2 3.8 %collective-permute-start.6 = (f32[2,2176]{1,0:T(2,128)S(1)}, f32[2,2176]{1,0:T(2,128)S(1)}, u32[]{:S(2)}, u32[]{:S(2)}) collective-permute-start(f32[2,2176]{1,0:T(2,128)S(1)} %fusion.39), channel_id=1, source_target_pairs={{0,2},{1,3},{2,0},{3,1},{4,6},{5,7},{6,4},{7,5},{8,10},{9,11},{10,... | collective-permute-start | bytes 52232 | tf_op jit(solution)/shard_map/ppermute | solution.py:27
  34.1 4.7 %collective-permute-start.7 = (f32[2,2176]{1,0:T(2,128)S(1)}, f32[2,2176]{1,0:T(2,128)S(1)}, u32[]{:S(2)}, u32[]{:S(2)}) collective-permute-start(f32[2,2176]{1,0:T(2,128)S(1)} %add.132), channel_id=1, source_target_pairs={{0,4},{1,5},{2,6},{3,7},{4,0},{5,1},{6,2},{7,3},{8,12},{9,13},{10,... | collective-permute-start | bytes 52232 | tf_op jit(solution)/shard_map/ppermute | solution.py:27
  39.0 4.5 %collective-permute-start.8 = (f32[256]{0:T(256)S(1)}, f32[256]{0:T(256)S(1)}, u32[]{:S(2)}, u32[]{:S(2)}) collective-permute-start(f32[256]{0:T(256)S(1)} %fusion.2), channel_id=1, source_target_pairs={{0,4},{1,5},{2,6},{3,7},{4,0},{5,1},{6,2},{7,3},{8,12},{9,13},{10,... | collective-permute-start | bytes 3080 | tf_op jit(solution)/shard_map/ppermute | solution.py:40
  43.6 3.6 %collective-permute-start.9 = (f32[512]{0:T(512)S(1)}, f32[512]{0:T(512)S(1)}, u32[]{:S(2)}, u32[]{:S(2)}) collective-permute-start(f32[512]{0:T(512)S(1)} %pad_maximum_fusion.9), channel_id=1, source_target_pairs={{0,2},{1,3},{2,0},{3,1},{4,6},{5,7},{6,4},{7,5},{8,10},{9,11},{10,... | collective-permute-start | bytes 6152 | tf_op jit(solution)/shard_map/ppermute | solution.py:40
  47.2 1.2 %collective-permute-start.10 = (f32[1024]{0:T(1024)S(1)}, f32[1024]{0:T(1024)S(1)}, u32[]{:S(2)}, u32[]{:S(2)}) collective-permute-start(f32[1024]{0:T(1024)S(1)} %pad_maximum_fusion.8), channel_id=1, source_target_pairs={{0,1},{1,0},{2,3},{3,2},{4,5},{5,4},{6,7},{7,6},{8,9},{9,8},{10,11... | collective-permute-start | bytes 12296 | tf_op jit(solution)/shard_map/ppermute | solution.py:40
  57.8 2.7 %collective-permute-start.11 = (f32[4,64,2,512]{3,1,2,0:T(8,128)S(1)}, f32[4,64,2,512]{3,1,2,0:T(8,128)S(1)}, u32[]{:S(2)}, u32[]{:S(2)}) collective-permute-start(f32[4,64,2,512]{3,1,2,0:T(8,128)S(1)} %bitcast.93), channel_id=1, source_target_pairs={{0,1},{1,0},{2,3},{3,2},{4,5},{5,4},{6,7},{7,6},{8,9},{9,8},{10,11... | collective-permute-start | bytes 3145736 | tf_op jit(solution)/shard_map/ppermute | solution.py:66
  58.9 1.8 %copy-start.3 = (f32[512,512]{1,0:T(8,128)}, f32[512,512]{1,0:T(8,128)S(1)}, u32[]{:S(2)}) copy-start(f32[512,512]{1,0:T(8,128)S(1)} %fusion.8) | copy-start | bytes 3145732
  60.8 2.0 %collective-permute-start.17 = (f32[4,64,512]{2,1,0:T(8,128)S(1)}, f32[4,64,512]{2,1,0:T(8,128)S(1)}, u32[]{:S(2)}, u32[]{:S(2)}) collective-permute-start(f32[4,64,512]{2,1,0:T(8,128)S(1)} %dynamic-slice_bitcast_fusion), channel_id=1, source_target_pairs={{0,1},{1,0},{2,3},{3,2},{4,5},{5,4},{6,7},{7,6},{8,9},{9,8},{10,11... | collective-permute-start | bytes 1572872 | tf_op jit(solution)/shard_map/ppermute | solution.py:66
  61.0 19.1 %copy-start.5 = (s32[1,2]{1,0:T(1,128)S(1)}, s32[1,2]{1,0:T(1,128)}, u32[]{:S(2)}) copy-start(s32[1,2]{1,0:T(1,128)} %param.15) | copy-start | bytes 28
  61.1 14.2 %collective-permute-start.12 = (f32[2,64,2,512]{3,1,2,0:T(8,128)S(1)}, f32[2,64,2,512]{3,1,2,0:T(8,128)S(1)}, u32[]{:S(2)}, u32[]{:S(2)}) collective-permute-start(f32[2,64,2,512]{3,1,2,0:T(8,128)S(1)} %dynamic-slice_bitcast_fusion.1), channel_id=1, source_target_pairs={{0,2},{1,3},{2,0},{3,1},{4,6},{5,7},{6,4},{7,5},{8,10},{9,11},{10,... | collective-permute-start | bytes 1572872 | tf_op jit(solution)/shard_map/ppermute | solution.py:66
  75.4 13.1 %collective-permute-start.18 = (f32[2,64,512]{2,1,0:T(8,128)S(1)}, f32[2,64,512]{2,1,0:T(8,128)S(1)}, u32[]{:S(2)}, u32[]{:S(2)}) collective-permute-start(f32[2,64,512]{2,1,0:T(8,128)S(1)} %dynamic-slice_bitcast_fusion.2), channel_id=1, source_target_pairs={{0,2},{1,3},{2,0},{3,1},{4,6},{5,7},{6,4},{7,5},{8,10},{9,11},{10,... | collective-permute-start | bytes 786440 | tf_op jit(solution)/shard_map/ppermute | solution.py:66
  77.1 14.6 %collective-permute-start.13 = (f32[1,64,2,512]{3,1,2,0:T(8,128)S(1)}, f32[1,64,2,512]{3,1,2,0:T(8,128)S(1)}, u32[]{:S(2)}, u32[]{:S(2)}) collective-permute-start(f32[1,64,2,512]{3,1,2,0:T(8,128)S(1)} %constant_dynamic-slice_fusion.1), channel_id=1, source_target_pairs={{0,4},{1,5},{2,6},{3,7},{4,0},{5,1},{6,2},{7,3},{8,12},{9,13},{10,... | collective-permute-start | bytes 786440 | tf_op jit(solution)/shard_map/ppermute | solution.py:66
  91.8 6.9 %collective-permute-start.19 = (f32[1,64,512]{2,1,0:T(8,128)S(1)}, f32[1,64,512]{2,1,0:T(8,128)S(1)}, u32[]{:S(2)}, u32[]{:S(2)}) collective-permute-start(f32[1,64,512]{2,1,0:T(8,128)S(1)} %constant_dynamic-slice_fusion), channel_id=1, source_target_pairs={{0,4},{1,5},{2,6},{3,7},{4,0},{5,1},{6,2},{7,3},{8,12},{9,13},{10,... | collective-permute-start | bytes 393224 | tf_op jit(solution)/shard_map/ppermute | solution.py:66
  91.9 7.4 %collective-permute-start.14 = (f32[64,512]{1,0:T(8,128)S(1)}, f32[64,512]{1,0:T(8,128)S(1)}, u32[]{:S(2)}, u32[]{:S(2)}) collective-permute-start(f32[64,512]{1,0:T(8,128)S(1)} %get-tuple-element.18), channel_id=1, source_target_pairs={{0,8},{8,0},{16,24},{24,16},{1,9},{9,1},{17,25},{25,17},{2,10},{10... | collective-permute-start | bytes 393224 | tf_op jit(solution)/shard_map/ppermute | solution.py:177
  93.5 5.8 %collective-permute-start.15 = (f32[64,512]{1,0:T(8,128)S(1)}, f32[64,512]{1,0:T(8,128)S(1)}, u32[]{:S(2)}, u32[]{:S(2)}) collective-permute-start(f32[64,512]{1,0:T(8,128)S(1)} %get-tuple-element.19), channel_id=1, source_target_pairs={{0,16},{8,24},{16,0},{24,8},{1,17},{9,25},{17,1},{25,9},{2,18},{10... | collective-permute-start | bytes 393224 | tf_op jit(solution)/shard_map/ppermute | solution.py:177
  94.2 5.9 %collective-permute-start.16 = (f32[64,512]{1,0:T(8,128)S(1)}, f32[64,512]{1,0:T(8,128)S(1)}, u32[]{:S(2)}, u32[]{:S(2)}) collective-permute-start(f32[64,512]{1,0:T(8,128)S(1)} %get-tuple-element.20), channel_id=1, source_target_pairs={{0,24},{8,16},{16,8},{24,0},{1,25},{9,17},{17,9},{25,1},{2,26},{10... | collective-permute-start | bytes 393224 | tf_op jit(solution)/shard_map/ppermute | solution.py:177

commit v17 on v15

--- a/solution.py
+++ b/solution.py
@@ -129,14 +129,15 @@
     totals = xor_sum(payload, "grid")
     fitted = totals[0, :naux]
     weight_projection = totals[1, :naux]
-    exchange_total = totals[0, naux]
-    weight_sum = totals[1, naux]
+    exchange_total = totals[0, naux : naux + 1]
+    weight_sum = totals[1, naux : naux + 1]
     coef_rows = jnp.sum(metric_inv[0] * fitted[None, :], axis=1)
     coefficients = in_order(*xor_gather(coef_rows, "grid", 0), 0)
     coulomb = jnp.sum(aux_block.astype(jnp.float32) * coefficients[None, :], axis=1)
-    potential_total = jnp.dot(coefficients, weight_projection, precision=highest) + exchange_total
-    average = potential_total / weight_sum
-    potential = live_weight * (coulomb + exchange - average)
+    coulomb_total = jnp.sum(coefficients * weight_projection, axis=0, keepdims=True)
+    potential = live_weight * (
+        coulomb + exchange - coulomb_total / weight_sum - exchange_total / weight_sum
+    )
     weighted_basis = (basis_rows * potential[:, None]).astype(jnp.bfloat16)
     half_rows = frag_basis // lax.axis_size("grid")
     left_first = lax.slice_in_dim(weighted_basis, 0, half_rows * lax.axis_size("grid"), axis=1)

time: 101 us -> 101 us (level)
  waiting for transfers between devices: 38 us -> 36.9 us
  transfers between devices with their start and end apart: 20 -> 20, of which waited for: 16 -> 15; matrix products, arithmetic and copies ran while one was open for 7% -> 7% of each run, Pallas kernels for 0% -> 0%
where the time goes in v17:
time: 101 us
  waiting for transfers between devices  36.9 us (37%)
  starting transfers between devices  31.6 us (31%)
  other arithmetic  14.1 us (14%)
  between operations  9.47 us (9%)
  matrix products  4.56 us (5%)
  local copies, waits for them, and re-layouts  4.3 us (4%)
    ppermute x6, waiting for transfers between devices, scatter_step(): lax.ppermute(send, axis, [(i, i ^ 1 << bit) for i in range(size)])  21.2 us
    ppermute x8, starting transfers between devices, xor_gather(): other = lax.ppermute(value, axis, [(i, i ^ 1 << bit) for i in range(size)])  14.9 us
    ppermute x8, waiting for transfers between devices, xor_gather(): other = lax.ppermute(value, axis, [(i, i ^ 1 << bit) for i in range(size)])  9.51 us
    ppermute x6, starting transfers between devices, scatter_step(): lax.ppermute(send, axis, [(i, i ^ 1 << bit) for i in range(size)])  7.62 us
    ppermute x3, starting transfers between devices, xor_sum(): lax.ppermute(value, axis, [(i, i ^ step) for i in range(size)])  5.49 us
    ppermute x3, waiting for transfers between devices, xor_sum(): lax.ppermute(value, axis, [(i, i ^ step) for i in range(size)])  4.52 us
    reduce_sum x1, other arithmetic, shards(): jnp.sum(aux_block.astype(jnp.float32) * coefficients[None, :], axis=1)  3.59 us
    ppermute x3, starting transfers between devices, shards(): frag_fock = frag_fock + lax.ppermute(piece(dest), 'dimer', pairs)  3.55 us
  transfers between devices with their start and end apart: 20, of which 15 were waited for; matrix products, arithmetic and copies ran while one was open for 7% of the time, Pallas kernels for 0%

profile of v17, /device:TPU:0, one launch (start us, length us, event | category | flops | bytes accessed | tf_op | source)
XLA Modules:
  0.0 100.9 jit_solution(6963101152734010240)
XLA Ops:
  0.6 0.9 copy.33
  1.5 3.1 %collective-permute-start = (bf16[1,64,128]{2,0,1:T(2,128)(2,1)S(1)}, bf16[1,64,128]{2,0,1:T(2,128)(2,1)S(1)}, u32[]{:S(2)}, u32[]{:S(2)}) collective-permute-start(bf16[1,64,128]{2,0,1:T(2,128)(2,1)S(1)} %copy.33), channel_id=1, source_target_pairs={{0,16},{8,24},{16,0},{24,8},{1,17},{9,25},{17,1},{25,9},{2,18},{10... | collective-permute-start | bytes 49160 | tf_op jit(solution)/shard_map/ppermute | solution.py:40
  4.6 0.7 broadcast_xor_fusion
  5.3 1.2 %collective-permute-done = bf16[1,64,128]{2,0,1:T(2,128)(2,1)S(1)} collective-permute-done((bf16[1,64,128]{2,0,1:T(2,128)(2,1)S(1)}, bf16[1,64,128]{2,0,1:T(2,128)(2,1)S(1)}, u32[]{:S(2)}, u32[]{:S(2)}) %collective-permute-start) | collective-permute-done | bytes 16416 | tf_op jit(solution)/shard_map/ppermute | solution.py:40
  6.6 2.1 %collective-permute-start.1 = (bf16[2,64,128]{2,0,1:T(2,128)(2,1)S(1)}, bf16[2,64,128]{2,0,1:T(2,128)(2,1)S(1)}, u32[]{:S(2)}, u32[]{:S(2)}) collective-permute-start(bf16[2,64,128]{2,0,1:T(2,128)(2,1)S(1)} %pad_maximum_fusion.5), channel_id=1, source_target_pairs={{0,8},{8,0},{16,24},{24,16},{1,9},{9,1},{17,25},{25,17},{2,10},{10... | collective-permute-start | bytes 98312 | tf_op jit(solution)/shard_map/ppermute | solution.py:40
  8.6 0.9 fusion.38
  9.5 1.1 %collective-permute-done.1 = bf16[2,64,128]{2,0,1:T(2,128)(2,1)S(1)} collective-permute-done((bf16[2,64,128]{2,0,1:T(2,128)(2,1)S(1)}, bf16[2,64,128]{2,0,1:T(2,128)(2,1)S(1)}, u32[]{:S(2)}, u32[]{:S(2)}) %collective-permute-start.1) | collective-permute-done | bytes 32800 | tf_op jit(solution)/shard_map/ppermute | solution.py:40
  10.8 3.2 %collective-permute-start.2 = (bf16[2,64,128]{2,0,1:T(2,128)(2,1)S(1)}, bf16[2,64,128]{2,0,1:T(2,128)(2,1)S(1)}, u32[]{:S(2)}, u32[]{:S(2)}) collective-permute-start(bf16[2,64,128]{2,0,1:T(2,128)(2,1)S(1)} %convolution_convert_fusion), channel_id=1, source_target_pairs={{0,4},{1,5},{2,6},{3,7},{4,0},{5,1},{6,2},{7,3},{8,12},{9,13},{10,... | collective-permute-start | bytes 98312 | tf_op jit(solution)/shard_map/ppermute | solution.py:40
  13.9 2.0 %collective-permute-done.2 = bf16[2,64,128]{2,0,1:T(2,128)(2,1)S(1)} collective-permute-done((bf16[2,64,128]{2,0,1:T(2,128)(2,1)S(1)}, bf16[2,64,128]{2,0,1:T(2,128)(2,1)S(1)}, u32[]{:S(2)}, u32[]{:S(2)}) %collective-permute-start.2) | collective-permute-done | bytes 32800 | tf_op jit(solution)/shard_map/ppermute | solution.py:40
  16.0 1.9 %collective-permute-start.3 = (bf16[2,128,128]{2,0,1:T(2,128)(2,1)S(1)}, bf16[2,128,128]{2,0,1:T(2,128)(2,1)S(1)}, u32[]{:S(2)}, u32[]{:S(2)}) collective-permute-start(bf16[2,128,128]{2,0,1:T(2,128)(2,1)S(1)} %pad_maximum_fusion.4), channel_id=1, source_target_pairs={{0,2},{1,3},{2,0},{3,1},{4,6},{5,7},{6,4},{7,5},{8,10},{9,11},{10,... | collective-permute-start | bytes 196616 | tf_op jit(solution)/shard_map/ppermute | solution.py:40
  17.9 0.7 compare_and_fusion
  18.6 1.8 %collective-permute-done.3 = bf16[2,128,128]{2,0,1:T(2,128)(2,1)S(1)} collective-permute-done((bf16[2,128,128]{2,0,1:T(2,128)(2,1)S(1)}, bf16[2,128,128]{2,0,1:T(2,128)(2,1)S(1)}, u32[]{:S(2)}, u32[]{:S(2)}) %collective-permute-start.3) | collective-permute-done | bytes 65568 | tf_op jit(solution)/shard_map/ppermute | solution.py:40
  21.3 0.7 reduce.1
  22.5 0.6 gather_fusion
  23.2 0.9 fusion.7
  24.1 0.7 multiply_reduce_fusion.2
  24.9 0.8 copy-done
  25.7 0.8 fusion
  26.5 1.3 %pad_maximum_fusion.11 = f32[2]{0:T(128)S(1)} fusion(f32[1]{0:T(128)} %bitcast.12, f32[1]{0:T(128)} %bitcast.11), kind=kLoop, calls=%fused_computation.93 | loop fusion | flops 2 | bytes 16 | tf_op jit(solution)/shard_map/stack | solution.py:124
  28.5 0.8 collective-permute-done.5
  29.4 1.9 %collective-permute-start.6 = (f32[2,2176]{1,0:T(2,128)S(1)}, f32[2,2176]{1,0:T(2,128)S(1)}, u32[]{:S(2)}, u32[]{:S(2)}) collective-permute-start(f32[2,2176]{1,0:T(2,128)S(1)} %fusion.47), channel_id=1, source_target_pairs={{0,2},{1,3},{2,0},{3,1},{4,6},{5,7},{6,4},{7,5},{8,10},{9,11},{10,... | collective-permute-start | bytes 52232 | tf_op jit(solution)/shard_map/ppermute | solution.py:27
  31.2 1.9 %collective-permute-done.6 = f32[2,2176]{1,0:T(2,128)S(1)} collective-permute-done((f32[2,2176]{1,0:T(2,128)S(1)}, f32[2,2176]{1,0:T(2,128)S(1)}, u32[]{:S(2)}, u32[]{:S(2)}) %collective-permute-start.6) | collective-permute-done | bytes 17440 | tf_op jit(solution)/shard_map/ppermute | solution.py:27
  33.2 3.1 %collective-permute-start.7 = (f32[2,2176]{1,0:T(2,128)S(1)}, f32[2,2176]{1,0:T(2,128)S(1)}, u32[]{:S(2)}, u32[]{:S(2)}) collective-permute-start(f32[2,2176]{1,0:T(2,128)S(1)} %add.129), channel_id=1, source_target_pairs={{0,4},{1,5},{2,6},{3,7},{4,0},{5,1},{6,2},{7,3},{8,12},{9,13},{10,... | collective-permute-start | bytes 52232 | tf_op jit(solution)/shard_map/ppermute | solution.py:27
  36.3 1.7 %collective-permute-done.7 = f32[2,2176]{1,0:T(2,128)S(1)} collective-permute-done((f32[2,2176]{1,0:T(2,128)S(1)}, f32[2,2176]{1,0:T(2,128)S(1)}, u32[]{:S(2)}, u32[]{:S(2)}) %collective-permute-start.7) | collective-permute-done | bytes 17440 | tf_op jit(solution)/shard_map/ppermute | solution.py:27
  38.3 3.0 %collective-permute-start.8 = (f32[256]{0:T(256)S(1)}, f32[256]{0:T(256)S(1)}, u32[]{:S(2)}, u32[]{:S(2)}) collective-permute-start(f32[256]{0:T(256)S(1)} %fusion.2), channel_id=1, source_target_pairs={{0,4},{1,5},{2,6},{3,7},{4,0},{5,1},{6,2},{7,3},{8,12},{9,13},{10,... | collective-permute-start | bytes 3080 | tf_op jit(solution)/shard_map/ppermute | solution.py:40
  41.2 1.6 %collective-permute-done.8 = f32[256]{0:T(256)S(1)} collective-permute-done((f32[256]{0:T(256)S(1)}, f32[256]{0:T(256)S(1)}, u32[]{:S(2)}, u32[]{:S(2)}) %collective-permute-start.8) | collective-permute-done | bytes 1056 | tf_op jit(solution)/shard_map/ppermute | solution.py:40
  42.8 1.7 %collective-permute-start.9 = (f32[512]{0:T(512)S(1)}, f32[512]{0:T(512)S(1)}, u32[]{:S(2)}, u32[]{:S(2)}) collective-permute-start(f32[512]{0:T(512)S(1)} %pad_maximum_fusion.10), channel_id=1, source_target_pairs={{0,2},{1,3},{2,0},{3,1},{4,6},{5,7},{6,4},{7,5},{8,10},{9,11},{10,... | collective-permute-start | bytes 6152 | tf_op jit(solution)/shard_map/ppermute | solution.py:40
  44.5 1.9 %collective-permute-done.9 = f32[512]{0:T(512)S(1)} collective-permute-done((f32[512]{0:T(512)S(1)}, f32[512]{0:T(512)S(1)}, u32[]{:S(2)}, u32[]{:S(2)}) %collective-permute-start.9) | collective-permute-done | bytes 2080 | tf_op jit(solution)/shard_map/ppermute | solution.py:40
  49.0 3.6 %multiply_reduce_fusion = f32[1280]{0:T(1024)S(1)} fusion(bf16[1,1280,2048]{2,1,0:T(8,128)(2,1)} %param.12, f32[2048]{0:T(1024)S(1)} %bitcast.100), kind=kLoop, calls=%fused_computation.2 | loop fusion | flops 7863040 | bytes 5256192 | tf_op jit(solution)/shard_map/reduce_sum | solution.py:136
  52.5 0.6 multiply_reduce_fusion.1
  55.0 0.9 fusion.3
  55.9 0.9 fusion.5
  57.7 0.9 fusion.8
  58.6 1.4 %collective-permute-done.11 = f32[4,64,2,512]{3,1,2,0:T(8,128)S(1)} collective-permute-done((f32[4,64,2,512]{3,1,2,0:T(8,128)S(1)}, f32[4,64,2,512]{3,1,2,0:T(8,128)S(1)}, u32[]{:S(2)}, u32[]{:S(2)}) %collective-permute-start.11) | collective-permute-done | bytes 1048608 | tf_op jit(solution)/shard_map/ppermute | solution.py:66
  60.7 1.8 %collective-permute-start.12 = (f32[2,64,2,512]{3,1,2,0:T(8,128)S(1)}, f32[2,64,2,512]{3,1,2,0:T(8,128)S(1)}, u32[]{:S(2)}, u32[]{:S(2)}) collective-permute-start(f32[2,64,2,512]{3,1,2,0:T(8,128)S(1)} %dynamic-slice_bitcast_fusion.1), channel_id=1, source_target_pairs={{0,2},{1,3},{2,0},{3,1},{4,6},{5,7},{6,4},{7,5},{8,10},{9,11},{10,... | collective-permute-start | bytes 1572872 | tf_op jit(solution)/shard_map/ppermute | solution.py:66
  62.5 1.1 %bitcast_add_fusion.1 = f32[4,64,512]{2,1,0:T(8,128)S(1)} fusion(f32[4,64,512]{2,1,0:T(8,128)S(1)} %collective-permute-done.17, f32[4,2,64,512]{3,2,1,0:T(8,128)} %bitcast.97, s32[]{:T(128)S(6)} %select_n.143), kind=kLoop, calls=%fused_computation.36 | loop fusion | flops 131072 | bytes 1572868 | tf_op jit(solution)/shard_map/add | solution.py:66
  63.6 11.1 %collective-permute-done.12 = f32[2,64,2,512]{3,1,2,0:T(8,128)S(1)} collective-permute-done((f32[2,64,2,512]{3,1,2,0:T(8,128)S(1)}, f32[2,64,2,512]{3,1,2,0:T(8,128)S(1)}, u32[]{:S(2)}, u32[]{:S(2)}) %collective-permute-start.12) | collective-permute-done | bytes 524320 | tf_op jit(solution)/shard_map/ppermute | solution.py:66
  74.9 1.8 %collective-permute-start.18 = (f32[2,64,512]{2,1,0:T(8,128)S(1)}, f32[2,64,512]{2,1,0:T(8,128)S(1)}, u32[]{:S(2)}, u32[]{:S(2)}) collective-permute-start(f32[2,64,512]{2,1,0:T(8,128)S(1)} %dynamic-slice_bitcast_fusion.2), channel_id=1, source_target_pairs={{0,2},{1,3},{2,0},{3,1},{4,6},{5,7},{6,4},{7,5},{8,10},{9,11},{10,... | collective-permute-start | bytes 786440 | tf_op jit(solution)/shard_map/ppermute | solution.py:66
  76.7 2.9 %collective-permute-start.13 = (f32[1,64,2,512]{3,1,2,0:T(8,128)S(1)}, f32[1,64,2,512]{3,1,2,0:T(8,128)S(1)}, u32[]{:S(2)}, u32[]{:S(2)}) collective-permute-start(f32[1,64,2,512]{3,1,2,0:T(8,128)S(1)} %constant_dynamic-slice_fusion.1), channel_id=1, source_target_pairs={{0,4},{1,5},{2,6},{3,7},{4,0},{5,1},{6,2},{7,3},{8,12},{9,13},{10,... | collective-permute-start | bytes 786440 | tf_op jit(solution)/shard_map/ppermute | solution.py:66
  79.6 0.6 fusion.51
  85.4 2.4 %collective-permute-done.18 = f32[2,64,512]{2,1,0:T(8,128)S(1)} collective-permute-done((f32[2,64,512]{2,1,0:T(8,128)S(1)}, f32[2,64,512]{2,1,0:T(8,128)S(1)}, u32[]{:S(2)}, u32[]{:S(2)}) %collective-permute-start.18) | collective-permute-done | bytes 262176 | tf_op jit(solution)/shard_map/ppermute | solution.py:66
  87.8 3.2 %collective-permute-done.13 = f32[1,64,2,512]{3,1,2,0:T(8,128)S(1)} collective-permute-done((f32[1,64,2,512]{3,1,2,0:T(8,128)S(1)}, f32[1,64,2,512]{3,1,2,0:T(8,128)S(1)}, u32[]{:S(2)}, u32[]{:S(2)}) %collective-permute-start.13) | collective-permute-done | bytes 262176 | tf_op jit(solution)/shard_map/ppermute | solution.py:66
  91.3 1.6 %collective-permute-start.14 = (f32[64,512]{1,0:T(8,128)S(1)}, f32[64,512]{1,0:T(8,128)S(1)}, u32[]{:S(2)}, u32[]{:S(2)}) collective-permute-start(f32[64,512]{1,0:T(8,128)S(1)} %get-tuple-element.16), channel_id=1, source_target_pairs={{0,8},{8,0},{16,24},{24,16},{1,9},{9,1},{17,25},{25,17},{2,10},{10... | collective-permute-start | bytes 393224 | tf_op jit(solution)/shard_map/ppermute | solution.py:171
  92.8 1.5 %collective-permute-start.15 = (f32[64,512]{1,0:T(8,128)S(1)}, f32[64,512]{1,0:T(8,128)S(1)}, u32[]{:S(2)}, u32[]{:S(2)}) collective-permute-start(f32[64,512]{1,0:T(8,128)S(1)} %get-tuple-element.17), channel_id=1, source_target_pairs={{0,16},{8,24},{16,0},{24,8},{1,17},{9,25},{17,1},{25,9},{2,18},{10... | collective-permute-start | bytes 393224 | tf_op jit(solution)/shard_map/ppermute | solution.py:171
  94.8 3.1 %collective-permute-done.19 = f32[1,64,512]{2,1,0:T(8,128)S(1)} collective-permute-done((f32[1,64,512]{2,1,0:T(8,128)S(1)}, f32[1,64,512]{2,1,0:T(8,128)S(1)}, u32[]{:S(2)}, u32[]{:S(2)}) %collective-permute-start.19) | collective-permute-done | bytes 131104 | tf_op jit(solution)/shard_map/ppermute | solution.py:66
  97.9 0.7 dynamic-slice_add_fusion.1
  98.6 1.6 %collective-permute-done.16 = f32[64,512]{1,0:T(8,128)S(1)} collective-permute-done((f32[64,512]{1,0:T(8,128)S(1)}, f32[64,512]{1,0:T(8,128)S(1)}, u32[]{:S(2)}, u32[]{:S(2)}) %collective-permute-start.16) | collective-permute-done | bytes 131104 | tf_op jit(solution)/shard_map/ppermute | solution.py:171
  100.2 0.7 fusion.26
  (66 shorter events, 6.4 us)
Async XLA Ops:
  0.6 22.6 %copy-start.1 = (bf16[1,1280,1024]{2,1,0:T(8,128)(2,1)S(1)}, bf16[1,1280,1024]{2,1,0:T(8,128)(2,1)}, u32[]{:S(2)}) copy-start(bf16[1,1280,1024]{2,1,0:T(8,128)(2,1)} %param.11) | copy-start | bytes 7864324
  1.5 5.0 %collective-permute-start = (bf16[1,64,128]{2,0,1:T(2,128)(2,1)S(1)}, bf16[1,64,128]{2,0,1:T(2,128)(2,1)S(1)}, u32[]{:S(2)}, u32[]{:S(2)}) collective-permute-start(bf16[1,64,128]{2,0,1:T(2,128)(2,1)S(1)} %copy.33), channel_id=1, source_target_pairs={{0,16},{8,24},{16,0},{24,8},{1,17},{9,25},{17,1},{25,9},{2,18},{10... | collective-permute-start | bytes 49160 | tf_op jit(solution)/shard_map/ppermute | solution.py:40
  6.6 4.0 %collective-permute-start.1 = (bf16[2,64,128]{2,0,1:T(2,128)(2,1)S(1)}, bf16[2,64,128]{2,0,1:T(2,128)(2,1)S(1)}, u32[]{:S(2)}, u32[]{:S(2)}) collective-permute-start(bf16[2,64,128]{2,0,1:T(2,128)(2,1)S(1)} %pad_maximum_fusion.5), channel_id=1, source_target_pairs={{0,8},{8,0},{16,24},{24,16},{1,9},{9,1},{17,25},{25,17},{2,10},{10... | collective-permute-start | bytes 98312 | tf_op jit(solution)/shard_map/ppermute | solution.py:40
  10.8 5.2 %collective-permute-start.2 = (bf16[2,64,128]{2,0,1:T(2,128)(2,1)S(1)}, bf16[2,64,128]{2,0,1:T(2,128)(2,1)S(1)}, u32[]{:S(2)}, u32[]{:S(2)}) collective-permute-start(bf16[2,64,128]{2,0,1:T(2,128)(2,1)S(1)} %convolution_convert_fusion), channel_id=1, source_target_pairs={{0,4},{1,5},{2,6},{3,7},{4,0},{5,1},{6,2},{7,3},{8,12},{9,13},{10,... | collective-permute-start | bytes 98312 | tf_op jit(solution)/shard_map/ppermute | solution.py:40
  16.0 4.3 %collective-permute-start.3 = (bf16[2,128,128]{2,0,1:T(2,128)(2,1)S(1)}, bf16[2,128,128]{2,0,1:T(2,128)(2,1)S(1)}, u32[]{:S(2)}, u32[]{:S(2)}) collective-permute-start(bf16[2,128,128]{2,0,1:T(2,128)(2,1)S(1)} %pad_maximum_fusion.4), channel_id=1, source_target_pairs={{0,2},{1,3},{2,0},{3,1},{4,6},{5,7},{6,4},{7,5},{8,10},{9,11},{10,... | collective-permute-start | bytes 196616 | tf_op jit(solution)/shard_map/ppermute | solution.py:40
  20.6 1.5 %collective-permute-start.4 = (bf16[2,256,128]{2,0,1:T(2,128)(2,1)S(1)}, bf16[2,256,128]{2,0,1:T(2,128)(2,1)S(1)}, u32[]{:S(2)}, u32[]{:S(2)}) collective-permute-start(bf16[2,256,128]{2,0,1:T(2,128)(2,1)S(1)} %pad_maximum_fusion.1), channel_id=1, source_target_pairs={{0,1},{1,0},{2,3},{3,2},{4,5},{5,4},{6,7},{7,6},{8,9},{9,8},{10,11... | collective-permute-start | bytes 393224 | tf_op jit(solution)/shard_map/ppermute | solution.py:40
  23.2 1.6 %copy-start.4 = (f32[1,1280]{1,0:T(1,128)S(1)}, f32[1,1280]{1,0:T(1,128)}, u32[]{:S(2)}) copy-start(f32[1,1280]{1,0:T(1,128)} %param.17) | copy-start | bytes 15364
  23.2 2.5 %copy-start = (bf16[1,1280,2048]{2,1,0:T(8,128)(2,1)S(1)}, bf16[1,1280,2048]{2,1,0:T(8,128)(2,1)}, u32[]{:S(2)}) copy-start(bf16[1,1280,2048]{2,1,0:T(8,128)(2,1)} %param.12) | copy-start | bytes 15728644
  25.7 12.3 %copy-start.2 = (f32[1,256,2048]{2,1,0:T(8,128)S(1)}, f32[1,256,2048]{2,1,0:T(8,128)}, u32[]{:S(2)}) copy-start(f32[1,256,2048]{2,1,0:T(8,128)} %param.18) | copy-start | bytes 6291460
  27.9 1.4 %collective-permute-start.5 = (f32[2,2176]{1,0:T(2,128)S(1)}, f32[2,2176]{1,0:T(2,128)S(1)}, u32[]{:S(2)}, u32[]{:S(2)}) collective-permute-start(f32[2,2176]{1,0:T(2,128)S(1)} %pad_maximum_fusion.6), channel_id=1, source_target_pairs={{0,1},{1,0},{2,3},{3,2},{4,5},{5,4},{6,7},{7,6},{8,9},{9,8},{10,11... | collective-permute-start | bytes 52232 | tf_op jit(solution)/shard_map/ppermute | solution.py:27
  29.4 3.8 %collective-permute-start.6 = (f32[2,2176]{1,0:T(2,128)S(1)}, f32[2,2176]{1,0:T(2,128)S(1)}, u32[]{:S(2)}, u32[]{:S(2)}) collective-permute-start(f32[2,2176]{1,0:T(2,128)S(1)} %fusion.47), channel_id=1, source_target_pairs={{0,2},{1,3},{2,0},{3,1},{4,6},{5,7},{6,4},{7,5},{8,10},{9,11},{10,... | collective-permute-start | bytes 52232 | tf_op jit(solution)/shard_map/ppermute | solution.py:27
  33.2 4.8 %collective-permute-start.7 = (f32[2,2176]{1,0:T(2,128)S(1)}, f32[2,2176]{1,0:T(2,128)S(1)}, u32[]{:S(2)}, u32[]{:S(2)}) collective-permute-start(f32[2,2176]{1,0:T(2,128)S(1)} %add.129), channel_id=1, source_target_pairs={{0,4},{1,5},{2,6},{3,7},{4,0},{5,1},{6,2},{7,3},{8,12},{9,13},{10,... | collective-permute-start | bytes 52232 | tf_op jit(solution)/shard_map/ppermute | solution.py:27
  38.3 4.5 %collective-permute-start.8 = (f32[256]{0:T(256)S(1)}, f32[256]{0:T(256)S(1)}, u32[]{:S(2)}, u32[]{:S(2)}) collective-permute-start(f32[256]{0:T(256)S(1)} %fusion.2), channel_id=1, source_target_pairs={{0,4},{1,5},{2,6},{3,7},{4,0},{5,1},{6,2},{7,3},{8,12},{9,13},{10,... | collective-permute-start | bytes 3080 | tf_op jit(solution)/shard_map/ppermute | solution.py:40
  42.8 3.6 %collective-permute-start.9 = (f32[512]{0:T(512)S(1)}, f32[512]{0:T(512)S(1)}, u32[]{:S(2)}, u32[]{:S(2)}) collective-permute-start(f32[512]{0:T(512)S(1)} %pad_maximum_fusion.10), channel_id=1, source_target_pairs={{0,2},{1,3},{2,0},{3,1},{4,6},{5,7},{6,4},{7,5},{8,10},{9,11},{10,... | collective-permute-start | bytes 6152 | tf_op jit(solution)/shard_map/ppermute | solution.py:40
  46.4 1.9 %collective-permute-start.10 = (f32[1024]{0:T(1024)S(1)}, f32[1024]{0:T(1024)S(1)}, u32[]{:S(2)}, u32[]{:S(2)}) collective-permute-start(f32[1024]{0:T(1024)S(1)} %pad_maximum_fusion.9), channel_id=1, source_target_pairs={{0,1},{1,0},{2,3},{3,2},{4,5},{5,4},{6,7},{7,6},{8,9},{9,8},{10,11... | collective-permute-start | bytes 12296 | tf_op jit(solution)/shard_map/ppermute | solution.py:40
  57.1 2.9 %collective-permute-start.11 = (f32[4,64,2,512]{3,1,2,0:T(8,128)S(1)}, f32[4,64,2,512]{3,1,2,0:T(8,128)S(1)}, u32[]{:S(2)}, u32[]{:S(2)}) collective-permute-start(f32[4,64,2,512]{3,1,2,0:T(8,128)S(1)} %bitcast.94), channel_id=1, source_target_pairs={{0,1},{1,0},{2,3},{3,2},{4,5},{5,4},{6,7},{7,6},{8,9},{9,8},{10,11... | collective-permute-start | bytes 3145736 | tf_op jit(solution)/shard_map/ppermute | solution.py:66
  58.6 1.6 %copy-start.3 = (f32[512,512]{1,0:T(8,128)}, f32[512,512]{1,0:T(8,128)S(1)}, u32[]{:S(2)}) copy-start(f32[512,512]{1,0:T(8,128)S(1)} %fusion.8) | copy-start | bytes 3145732
  60.2 2.3 %collective-permute-start.17 = (f32[4,64,512]{2,1,0:T(8,128)S(1)}, f32[4,64,512]{2,1,0:T(8,128)S(1)}, u32[]{:S(2)}, u32[]{:S(2)}) collective-permute-start(f32[4,64,512]{2,1,0:T(8,128)S(1)} %dynamic-slice_bitcast_fusion), channel_id=1, source_target_pairs={{0,1},{1,0},{2,3},{3,2},{4,5},{5,4},{6,7},{7,6},{8,9},{9,8},{10,11... | collective-permute-start | bytes 1572872 | tf_op jit(solution)/shard_map/ppermute | solution.py:66
  60.7 19.0 %copy-start.5 = (s32[1,2]{1,0:T(1,128)S(1)}, s32[1,2]{1,0:T(1,128)}, u32[]{:S(2)}) copy-start(s32[1,2]{1,0:T(1,128)} %param.15) | copy-start | bytes 28
  60.7 14.0 %collective-permute-start.12 = (f32[2,64,2,512]{3,1,2,0:T(8,128)S(1)}, f32[2,64,2,512]{3,1,2,0:T(8,128)S(1)}, u32[]{:S(2)}, u32[]{:S(2)}) collective-permute-start(f32[2,64,2,512]{3,1,2,0:T(8,128)S(1)} %dynamic-slice_bitcast_fusion.1), channel_id=1, source_target_pairs={{0,2},{1,3},{2,0},{3,1},{4,6},{5,7},{6,4},{7,5},{8,10},{9,11},{10,... | collective-permute-start | bytes 1572872 | tf_op jit(solution)/shard_map/ppermute | solution.py:66
  74.9 12.9 %collective-permute-start.18 = (f32[2,64,512]{2,1,0:T(8,128)S(1)}, f32[2,64,512]{2,1,0:T(8,128)S(1)}, u32[]{:S(2)}, u32[]{:S(2)}) collective-permute-start(f32[2,64,512]{2,1,0:T(8,128)S(1)} %dynamic-slice_bitcast_fusion.2), channel_id=1, source_target_pairs={{0,2},{1,3},{2,0},{3,1},{4,6},{5,7},{6,4},{7,5},{8,10},{9,11},{10,... | collective-permute-start | bytes 786440 | tf_op jit(solution)/shard_map/ppermute | solution.py:66
  76.7 14.4 %collective-permute-start.13 = (f32[1,64,2,512]{3,1,2,0:T(8,128)S(1)}, f32[1,64,2,512]{3,1,2,0:T(8,128)S(1)}, u32[]{:S(2)}, u32[]{:S(2)}) collective-permute-start(f32[1,64,2,512]{3,1,2,0:T(8,128)S(1)} %constant_dynamic-slice_fusion.1), channel_id=1, source_target_pairs={{0,4},{1,5},{2,6},{3,7},{4,0},{5,1},{6,2},{7,3},{8,12},{9,13},{10,... | collective-permute-start | bytes 786440 | tf_op jit(solution)/shard_map/ppermute | solution.py:66
  91.1 6.8 %collective-permute-start.19 = (f32[1,64,512]{2,1,0:T(8,128)S(1)}, f32[1,64,512]{2,1,0:T(8,128)S(1)}, u32[]{:S(2)}, u32[]{:S(2)}) collective-permute-start(f32[1,64,512]{2,1,0:T(8,128)S(1)} %constant_dynamic-slice_fusion), channel_id=1, source_target_pairs={{0,4},{1,5},{2,6},{3,7},{4,0},{5,1},{6,2},{7,3},{8,12},{9,13},{10,... | collective-permute-start | bytes 393224 | tf_op jit(solution)/shard_map/ppermute | solution.py:66
  91.3 7.3 %collective-permute-start.14 = (f32[64,512]{1,0:T(8,128)S(1)}, f32[64,512]{1,0:T(8,128)S(1)}, u32[]{:S(2)}, u32[]{:S(2)}) collective-permute-start(f32[64,512]{1,0:T(8,128)S(1)} %get-tuple-element.16), channel_id=1, source_target_pairs={{0,8},{8,0},{16,24},{24,16},{1,9},{9,1},{17,25},{25,17},{2,10},{10... | collective-permute-start | bytes 393224 | tf_op jit(solution)/shard_map/ppermute | solution.py:171
  92.8 5.8 %collective-permute-start.15 = (f32[64,512]{1,0:T(8,128)S(1)}, f32[64,512]{1,0:T(8,128)S(1)}, u32[]{:S(2)}, u32[]{:S(2)}) collective-permute-start(f32[64,512]{1,0:T(8,128)S(1)} %get-tuple-element.17), channel_id=1, source_target_pairs={{0,16},{8,24},{16,0},{24,8},{1,17},{9,25},{17,1},{25,9},{2,18},{10... | collective-permute-start | bytes 393224 | tf_op jit(solution)/shard_map/ppermute | solution.py:171
  94.3 5.9 %collective-permute-start.16 = (f32[64,512]{1,0:T(8,128)S(1)}, f32[64,512]{1,0:T(8,128)S(1)}, u32[]{:S(2)}, u32[]{:S(2)}) collective-permute-start(f32[64,512]{1,0:T(8,128)S(1)} %get-tuple-element.18), channel_id=1, source_target_pairs={{0,24},{8,16},{16,8},{24,0},{1,25},{9,17},{17,9},{25,1},{2,26},{10... | collective-permute-start | bytes 393224 | tf_op jit(solution)/shard_map/ppermute | solution.py:171

commit v18 on v15

--- a/solution.py
+++ b/solution.py
@@ -121,7 +121,8 @@
     projections = jnp.dot(
         jnp.concatenate([high_rows, low_rows]), aux_block, preferred_element_type=jnp.float32
     )
-    sums_part = jnp.stack([jnp.sum(live_weight * exchange), jnp.sum(live_weight)])
+    weight_total = lax.optimization_barrier(jnp.sum(live_weight))
+    sums_part = jnp.stack([jnp.sum(live_weight * exchange), weight_total])
     first_lane = lax.broadcasted_iota(jnp.int32, (2, 128), 1) == 0
     payload = jnp.concatenate(
         [projections[:2] + projections[2:], jnp.where(first_lane, sums_part[:, None], 0.0)], axis=1

time: 101 us -> 101 us (level)
  no operation moved by 1% of the time
where the time goes in v18:
time: 101 us
  waiting for transfers between devices  38 us (38%)
  starting transfers between devices  31 us (31%)
  other arithmetic  14.1 us (14%)
  between operations  8.74 us (9%)
  matrix products  4.56 us (5%)
  local copies, waits for them, and re-layouts  4.35 us (4%)
    ppermute x6, waiting for transfers between devices, scatter_step(): lax.ppermute(send, axis, [(i, i ^ 1 << bit) for i in range(size)])  21.9 us
    ppermute x8, starting transfers between devices, xor_gather(): other = lax.ppermute(value, axis, [(i, i ^ 1 << bit) for i in range(size)])  14.9 us
    ppermute x8, waiting for transfers between devices, xor_gather(): other = lax.ppermute(value, axis, [(i, i ^ 1 << bit) for i in range(size)])  10.1 us
    ppermute x6, starting transfers between devices, scatter_step(): lax.ppermute(send, axis, [(i, i ^ 1 << bit) for i in range(size)])  7.06 us
    ppermute x3, starting transfers between devices, xor_sum(): lax.ppermute(value, axis, [(i, i ^ step) for i in range(size)])  5.49 us
    ppermute x3, waiting for transfers between devices, xor_sum(): lax.ppermute(value, axis, [(i, i ^ step) for i in range(size)])  4.52 us
    reduce_sum x1, other arithmetic, shards(): jnp.sum(aux_block.astype(jnp.float32) * coefficients[None, :], axis=1)  3.59 us
    ppermute x3, starting transfers between devices, shards(): frag_fock = frag_fock + lax.ppermute(piece(dest), 'dimer', pairs)  3.55 us
  transfers between devices with their start and end apart: 20, of which 16 were waited for; matrix products, arithmetic and copies ran while one was open for 7% of the time, Pallas kernels for 0%

profile of v18, /device:TPU:0, one launch (start us, length us, event | category | flops | bytes accessed | tf_op | source)
XLA Modules:
  0.0 100.8 jit_solution(1591705660939666765)
XLA Ops:
  0.6 0.9 copy.33
  1.5 3.1 %collective-permute-start = (bf16[1,64,128]{2,0,1:T(2,128)(2,1)S(1)}, bf16[1,64,128]{2,0,1:T(2,128)(2,1)S(1)}, u32[]{:S(2)}, u32[]{:S(2)}) collective-permute-start(bf16[1,64,128]{2,0,1:T(2,128)(2,1)S(1)} %copy.33), channel_id=1, source_target_pairs={{0,16},{8,24},{16,0},{24,8},{1,17},{9,25},{17,1},{25,9},{2,18},{10... | collective-permute-start | bytes 49160 | tf_op jit(solution)/shard_map/ppermute | solution.py:40
  4.6 0.7 broadcast_xor_fusion
  5.3 1.2 %collective-permute-done = bf16[1,64,128]{2,0,1:T(2,128)(2,1)S(1)} collective-permute-done((bf16[1,64,128]{2,0,1:T(2,128)(2,1)S(1)}, bf16[1,64,128]{2,0,1:T(2,128)(2,1)S(1)}, u32[]{:S(2)}, u32[]{:S(2)}) %collective-permute-start) | collective-permute-done | bytes 16416 | tf_op jit(solution)/shard_map/ppermute | solution.py:40
  6.6 2.1 %collective-permute-start.1 = (bf16[2,64,128]{2,0,1:T(2,128)(2,1)S(1)}, bf16[2,64,128]{2,0,1:T(2,128)(2,1)S(1)}, u32[]{:S(2)}, u32[]{:S(2)}) collective-permute-start(bf16[2,64,128]{2,0,1:T(2,128)(2,1)S(1)} %pad_maximum_fusion.5), channel_id=1, source_target_pairs={{0,8},{8,0},{16,24},{24,16},{1,9},{9,1},{17,25},{25,17},{2,10},{10... | collective-permute-start | bytes 98312 | tf_op jit(solution)/shard_map/ppermute | solution.py:40
  8.6 0.9 fusion.38
  9.5 1.1 %collective-permute-done.1 = bf16[2,64,128]{2,0,1:T(2,128)(2,1)S(1)} collective-permute-done((bf16[2,64,128]{2,0,1:T(2,128)(2,1)S(1)}, bf16[2,64,128]{2,0,1:T(2,128)(2,1)S(1)}, u32[]{:S(2)}, u32[]{:S(2)}) %collective-permute-start.1) | collective-permute-done | bytes 32800 | tf_op jit(solution)/shard_map/ppermute | solution.py:40
  10.8 3.2 %collective-permute-start.2 = (bf16[2,64,128]{2,0,1:T(2,128)(2,1)S(1)}, bf16[2,64,128]{2,0,1:T(2,128)(2,1)S(1)}, u32[]{:S(2)}, u32[]{:S(2)}) collective-permute-start(bf16[2,64,128]{2,0,1:T(2,128)(2,1)S(1)} %convolution_convert_fusion), channel_id=1, source_target_pairs={{0,4},{1,5},{2,6},{3,7},{4,0},{5,1},{6,2},{7,3},{8,12},{9,13},{10,... | collective-permute-start | bytes 98312 | tf_op jit(solution)/shard_map/ppermute | solution.py:40
  13.9 2.0 %collective-permute-done.2 = bf16[2,64,128]{2,0,1:T(2,128)(2,1)S(1)} collective-permute-done((bf16[2,64,128]{2,0,1:T(2,128)(2,1)S(1)}, bf16[2,64,128]{2,0,1:T(2,128)(2,1)S(1)}, u32[]{:S(2)}, u32[]{:S(2)}) %collective-permute-start.2) | collective-permute-done | bytes 32800 | tf_op jit(solution)/shard_map/ppermute | solution.py:40
  16.0 1.9 %collective-permute-start.3 = (bf16[2,128,128]{2,0,1:T(2,128)(2,1)S(1)}, bf16[2,128,128]{2,0,1:T(2,128)(2,1)S(1)}, u32[]{:S(2)}, u32[]{:S(2)}) collective-permute-start(bf16[2,128,128]{2,0,1:T(2,128)(2,1)S(1)} %pad_maximum_fusion.4), channel_id=1, source_target_pairs={{0,2},{1,3},{2,0},{3,1},{4,6},{5,7},{6,4},{7,5},{8,10},{9,11},{10,... | collective-permute-start | bytes 196616 | tf_op jit(solution)/shard_map/ppermute | solution.py:40
  17.9 0.7 compare_and_fusion
  18.6 1.8 %collective-permute-done.3 = bf16[2,128,128]{2,0,1:T(2,128)(2,1)S(1)} collective-permute-done((bf16[2,128,128]{2,0,1:T(2,128)(2,1)S(1)}, bf16[2,128,128]{2,0,1:T(2,128)(2,1)S(1)}, u32[]{:S(2)}, u32[]{:S(2)}) %collective-permute-start.3) | collective-permute-done | bytes 65568 | tf_op jit(solution)/shard_map/ppermute | solution.py:40
  21.3 0.7 reduce.2
  22.5 0.6 gather_fusion
  23.2 0.9 fusion.7
  24.1 0.7 multiply_reduce_fusion.2
  24.9 0.8 copy-done
  25.7 0.8 fusion
  26.5 1.3 %pad_maximum_fusion.11 = f32[2]{0:T(128)S(1)} fusion(f32[1]{0:T(128)} %bitcast.12, f32[1]{0:T(128)} %bitcast.11), kind=kLoop, calls=%fused_computation.93 | loop fusion | flops 2 | bytes 16 | tf_op jit(solution)/shard_map/stack | solution.py:125
  28.5 0.8 collective-permute-done.5
  29.4 1.9 %collective-permute-start.6 = (f32[2,2176]{1,0:T(2,128)S(1)}, f32[2,2176]{1,0:T(2,128)S(1)}, u32[]{:S(2)}, u32[]{:S(2)}) collective-permute-start(f32[2,2176]{1,0:T(2,128)S(1)} %fusion.47), channel_id=1, source_target_pairs={{0,2},{1,3},{2,0},{3,1},{4,6},{5,7},{6,4},{7,5},{8,10},{9,11},{10,... | collective-permute-start | bytes 52232 | tf_op jit(solution)/shard_map/ppermute | solution.py:27
  31.2 1.9 %collective-permute-done.6 = f32[2,2176]{1,0:T(2,128)S(1)} collective-permute-done((f32[2,2176]{1,0:T(2,128)S(1)}, f32[2,2176]{1,0:T(2,128)S(1)}, u32[]{:S(2)}, u32[]{:S(2)}) %collective-permute-start.6) | collective-permute-done | bytes 17440 | tf_op jit(solution)/shard_map/ppermute | solution.py:27
  33.2 3.1 %collective-permute-start.7 = (f32[2,2176]{1,0:T(2,128)S(1)}, f32[2,2176]{1,0:T(2,128)S(1)}, u32[]{:S(2)}, u32[]{:S(2)}) collective-permute-start(f32[2,2176]{1,0:T(2,128)S(1)} %add.132), channel_id=1, source_target_pairs={{0,4},{1,5},{2,6},{3,7},{4,0},{5,1},{6,2},{7,3},{8,12},{9,13},{10,... | collective-permute-start | bytes 52232 | tf_op jit(solution)/shard_map/ppermute | solution.py:27
  36.3 1.7 %collective-permute-done.7 = f32[2,2176]{1,0:T(2,128)S(1)} collective-permute-done((f32[2,2176]{1,0:T(2,128)S(1)}, f32[2,2176]{1,0:T(2,128)S(1)}, u32[]{:S(2)}, u32[]{:S(2)}) %collective-permute-start.7) | collective-permute-done | bytes 17440 | tf_op jit(solution)/shard_map/ppermute | solution.py:27
  38.3 3.0 %collective-permute-start.8 = (f32[256]{0:T(256)S(1)}, f32[256]{0:T(256)S(1)}, u32[]{:S(2)}, u32[]{:S(2)}) collective-permute-start(f32[256]{0:T(256)S(1)} %fusion.2), channel_id=1, source_target_pairs={{0,4},{1,5},{2,6},{3,7},{4,0},{5,1},{6,2},{7,3},{8,12},{9,13},{10,... | collective-permute-start | bytes 3080 | tf_op jit(solution)/shard_map/ppermute | solution.py:40
  41.2 1.6 %collective-permute-done.8 = f32[256]{0:T(256)S(1)} collective-permute-done((f32[256]{0:T(256)S(1)}, f32[256]{0:T(256)S(1)}, u32[]{:S(2)}, u32[]{:S(2)}) %collective-permute-start.8) | collective-permute-done | bytes 1056 | tf_op jit(solution)/shard_map/ppermute | solution.py:40
  42.8 1.7 %collective-permute-start.9 = (f32[512]{0:T(512)S(1)}, f32[512]{0:T(512)S(1)}, u32[]{:S(2)}, u32[]{:S(2)}) collective-permute-start(f32[512]{0:T(512)S(1)} %pad_maximum_fusion.10), channel_id=1, source_target_pairs={{0,2},{1,3},{2,0},{3,1},{4,6},{5,7},{6,4},{7,5},{8,10},{9,11},{10,... | collective-permute-start | bytes 6152 | tf_op jit(solution)/shard_map/ppermute | solution.py:40
  44.5 1.9 %collective-permute-done.9 = f32[512]{0:T(512)S(1)} collective-permute-done((f32[512]{0:T(512)S(1)}, f32[512]{0:T(512)S(1)}, u32[]{:S(2)}, u32[]{:S(2)}) %collective-permute-start.9) | collective-permute-done | bytes 2080 | tf_op jit(solution)/shard_map/ppermute | solution.py:40
  46.4 0.6 fusion.49
  48.2 3.6 %multiply_reduce_fusion = f32[1280]{0:T(1024)S(1)} fusion(bf16[1,1280,2048]{2,1,0:T(8,128)(2,1)} %param.12, f32[2048]{0:T(1024)S(1)} %bitcast.97), kind=kLoop, calls=%fused_computation.2 | loop fusion | flops 7863040 | bytes 5256192 | tf_op jit(solution)/shard_map/reduce_sum | solution.py:137
  51.8 0.6 multiply_reduce_fusion.1
  54.9 0.9 fusion.3
  55.8 0.9 fusion.5
  57.2 0.9 fusion.8
  58.1 1.6 %collective-permute-done.11 = f32[4,64,2,512]{3,1,2,0:T(8,128)S(1)} collective-permute-done((f32[4,64,2,512]{3,1,2,0:T(8,128)S(1)}, f32[4,64,2,512]{3,1,2,0:T(8,128)S(1)}, u32[]{:S(2)}, u32[]{:S(2)}) %collective-permute-start.11) | collective-permute-done | bytes 1048608 | tf_op jit(solution)/shard_map/ppermute | solution.py:66
  60.2 1.8 %collective-permute-start.12 = (f32[2,64,2,512]{3,1,2,0:T(8,128)S(1)}, f32[2,64,2,512]{3,1,2,0:T(8,128)S(1)}, u32[]{:S(2)}, u32[]{:S(2)}) collective-permute-start(f32[2,64,2,512]{3,1,2,0:T(8,128)S(1)} %dynamic-slice_bitcast_fusion.1), channel_id=1, source_target_pairs={{0,2},{1,3},{2,0},{3,1},{4,6},{5,7},{6,4},{7,5},{8,10},{9,11},{10,... | collective-permute-start | bytes 1572872 | tf_op jit(solution)/shard_map/ppermute | solution.py:66
  62.0 1.1 %bitcast_add_fusion.1 = f32[4,64,512]{2,1,0:T(8,128)S(1)} fusion(f32[4,64,512]{2,1,0:T(8,128)S(1)} %collective-permute-done.17, f32[4,2,64,512]{3,2,1,0:T(8,128)} %bitcast.94, s32[]{:T(128)S(6)} %select_n.150), kind=kLoop, calls=%fused_computation.36 | loop fusion | flops 131072 | bytes 1572868 | tf_op jit(solution)/shard_map/add | solution.py:66
  63.2 11.3 %collective-permute-done.12 = f32[2,64,2,512]{3,1,2,0:T(8,128)S(1)} collective-permute-done((f32[2,64,2,512]{3,1,2,0:T(8,128)S(1)}, f32[2,64,2,512]{3,1,2,0:T(8,128)S(1)}, u32[]{:S(2)}, u32[]{:S(2)}) %collective-permute-start.12) | collective-permute-done | bytes 524320 | tf_op jit(solution)/shard_map/ppermute | solution.py:66
  74.6 1.8 %collective-permute-start.18 = (f32[2,64,512]{2,1,0:T(8,128)S(1)}, f32[2,64,512]{2,1,0:T(8,128)S(1)}, u32[]{:S(2)}, u32[]{:S(2)}) collective-permute-start(f32[2,64,512]{2,1,0:T(8,128)S(1)} %dynamic-slice_bitcast_fusion.2), channel_id=1, source_target_pairs={{0,2},{1,3},{2,0},{3,1},{4,6},{5,7},{6,4},{7,5},{8,10},{9,11},{10,... | collective-permute-start | bytes 786440 | tf_op jit(solution)/shard_map/ppermute | solution.py:66
  76.4 3.0 %collective-permute-start.13 = (f32[1,64,2,512]{3,1,2,0:T(8,128)S(1)}, f32[1,64,2,512]{3,1,2,0:T(8,128)S(1)}, u32[]{:S(2)}, u32[]{:S(2)}) collective-permute-start(f32[1,64,2,512]{3,1,2,0:T(8,128)S(1)} %constant_dynamic-slice_fusion.1), channel_id=1, source_target_pairs={{0,4},{1,5},{2,6},{3,7},{4,0},{5,1},{6,2},{7,3},{8,12},{9,13},{10,... | collective-permute-start | bytes 786440 | tf_op jit(solution)/shard_map/ppermute | solution.py:66
  85.1 2.6 %collective-permute-done.18 = f32[2,64,512]{2,1,0:T(8,128)S(1)} collective-permute-done((f32[2,64,512]{2,1,0:T(8,128)S(1)}, f32[2,64,512]{2,1,0:T(8,128)S(1)}, u32[]{:S(2)}, u32[]{:S(2)}) %collective-permute-start.18) | collective-permute-done | bytes 262176 | tf_op jit(solution)/shard_map/ppermute | solution.py:66
  87.8 3.2 %collective-permute-done.13 = f32[1,64,2,512]{3,1,2,0:T(8,128)S(1)} collective-permute-done((f32[1,64,2,512]{3,1,2,0:T(8,128)S(1)}, f32[1,64,2,512]{3,1,2,0:T(8,128)S(1)}, u32[]{:S(2)}, u32[]{:S(2)}) %collective-permute-start.13) | collective-permute-done | bytes 262176 | tf_op jit(solution)/shard_map/ppermute | solution.py:66
  91.2 1.6 %collective-permute-start.14 = (f32[64,512]{1,0:T(8,128)S(1)}, f32[64,512]{1,0:T(8,128)S(1)}, u32[]{:S(2)}, u32[]{:S(2)}) collective-permute-start(f32[64,512]{1,0:T(8,128)S(1)} %get-tuple-element.16), channel_id=1, source_target_pairs={{0,8},{8,0},{16,24},{24,16},{1,9},{9,1},{17,25},{25,17},{2,10},{10... | collective-permute-start | bytes 393224 | tf_op jit(solution)/shard_map/ppermute | solution.py:171
  92.8 1.5 %collective-permute-start.15 = (f32[64,512]{1,0:T(8,128)S(1)}, f32[64,512]{1,0:T(8,128)S(1)}, u32[]{:S(2)}, u32[]{:S(2)}) collective-permute-start(f32[64,512]{1,0:T(8,128)S(1)} %get-tuple-element.17), channel_id=1, source_target_pairs={{0,16},{8,24},{16,0},{24,8},{1,17},{9,25},{17,1},{25,9},{2,18},{10... | collective-permute-start | bytes 393224 | tf_op jit(solution)/shard_map/ppermute | solution.py:171
  94.7 3.1 %collective-permute-done.19 = f32[1,64,512]{2,1,0:T(8,128)S(1)} collective-permute-done((f32[1,64,512]{2,1,0:T(8,128)S(1)}, f32[1,64,512]{2,1,0:T(8,128)S(1)}, u32[]{:S(2)}, u32[]{:S(2)}) %collective-permute-start.19) | collective-permute-done | bytes 131104 | tf_op jit(solution)/shard_map/ppermute | solution.py:66
  97.9 0.7 dynamic-slice_add_fusion.1
  98.5 1.6 %collective-permute-done.16 = f32[64,512]{1,0:T(8,128)S(1)} collective-permute-done((f32[64,512]{1,0:T(8,128)S(1)}, f32[64,512]{1,0:T(8,128)S(1)}, u32[]{:S(2)}, u32[]{:S(2)}) %collective-permute-start.16) | collective-permute-done | bytes 131104 | tf_op jit(solution)/shard_map/ppermute | solution.py:171
  100.1 0.7 fusion.26
  (66 shorter events, 6.4 us)
Async XLA Ops:
  0.6 22.6 %copy-start.1 = (bf16[1,1280,1024]{2,1,0:T(8,128)(2,1)S(1)}, bf16[1,1280,1024]{2,1,0:T(8,128)(2,1)}, u32[]{:S(2)}) copy-start(bf16[1,1280,1024]{2,1,0:T(8,128)(2,1)} %param.11) | copy-start | bytes 7864324
  1.5 5.0 %collective-permute-start = (bf16[1,64,128]{2,0,1:T(2,128)(2,1)S(1)}, bf16[1,64,128]{2,0,1:T(2,128)(2,1)S(1)}, u32[]{:S(2)}, u32[]{:S(2)}) collective-permute-start(bf16[1,64,128]{2,0,1:T(2,128)(2,1)S(1)} %copy.33), channel_id=1, source_target_pairs={{0,16},{8,24},{16,0},{24,8},{1,17},{9,25},{17,1},{25,9},{2,18},{10... | collective-permute-start | bytes 49160 | tf_op jit(solution)/shard_map/ppermute | solution.py:40
  6.6 4.0 %collective-permute-start.1 = (bf16[2,64,128]{2,0,1:T(2,128)(2,1)S(1)}, bf16[2,64,128]{2,0,1:T(2,128)(2,1)S(1)}, u32[]{:S(2)}, u32[]{:S(2)}) collective-permute-start(bf16[2,64,128]{2,0,1:T(2,128)(2,1)S(1)} %pad_maximum_fusion.5), channel_id=1, source_target_pairs={{0,8},{8,0},{16,24},{24,16},{1,9},{9,1},{17,25},{25,17},{2,10},{10... | collective-permute-start | bytes 98312 | tf_op jit(solution)/shard_map/ppermute | solution.py:40
  10.8 5.2 %collective-permute-start.2 = (bf16[2,64,128]{2,0,1:T(2,128)(2,1)S(1)}, bf16[2,64,128]{2,0,1:T(2,128)(2,1)S(1)}, u32[]{:S(2)}, u32[]{:S(2)}) collective-permute-start(bf16[2,64,128]{2,0,1:T(2,128)(2,1)S(1)} %convolution_convert_fusion), channel_id=1, source_target_pairs={{0,4},{1,5},{2,6},{3,7},{4,0},{5,1},{6,2},{7,3},{8,12},{9,13},{10,... | collective-permute-start | bytes 98312 | tf_op jit(solution)/shard_map/ppermute | solution.py:40
  16.0 4.3 %collective-permute-start.3 = (bf16[2,128,128]{2,0,1:T(2,128)(2,1)S(1)}, bf16[2,128,128]{2,0,1:T(2,128)(2,1)S(1)}, u32[]{:S(2)}, u32[]{:S(2)}) collective-permute-start(bf16[2,128,128]{2,0,1:T(2,128)(2,1)S(1)} %pad_maximum_fusion.4), channel_id=1, source_target_pairs={{0,2},{1,3},{2,0},{3,1},{4,6},{5,7},{6,4},{7,5},{8,10},{9,11},{10,... | collective-permute-start | bytes 196616 | tf_op jit(solution)/shard_map/ppermute | solution.py:40
  20.6 1.5 %collective-permute-start.4 = (bf16[2,256,128]{2,0,1:T(2,128)(2,1)S(1)}, bf16[2,256,128]{2,0,1:T(2,128)(2,1)S(1)}, u32[]{:S(2)}, u32[]{:S(2)}) collective-permute-start(bf16[2,256,128]{2,0,1:T(2,128)(2,1)S(1)} %pad_maximum_fusion.1), channel_id=1, source_target_pairs={{0,1},{1,0},{2,3},{3,2},{4,5},{5,4},{6,7},{7,6},{8,9},{9,8},{10,11... | collective-permute-start | bytes 393224 | tf_op jit(solution)/shard_map/ppermute | solution.py:40
  23.2 1.6 %copy-start.4 = (f32[1,1280]{1,0:T(1,128)S(1)}, f32[1,1280]{1,0:T(1,128)}, u32[]{:S(2)}) copy-start(f32[1,1280]{1,0:T(1,128)} %param.17) | copy-start | bytes 15364
  23.2 2.5 %copy-start = (bf16[1,1280,2048]{2,1,0:T(8,128)(2,1)S(1)}, bf16[1,1280,2048]{2,1,0:T(8,128)(2,1)}, u32[]{:S(2)}) copy-start(bf16[1,1280,2048]{2,1,0:T(8,128)(2,1)} %param.12) | copy-start | bytes 15728644
  25.7 12.3 %copy-start.2 = (f32[1,256,2048]{2,1,0:T(8,128)S(1)}, f32[1,256,2048]{2,1,0:T(8,128)}, u32[]{:S(2)}) copy-start(f32[1,256,2048]{2,1,0:T(8,128)} %param.18) | copy-start | bytes 6291460
  27.9 1.4 %collective-permute-start.5 = (f32[2,2176]{1,0:T(2,128)S(1)}, f32[2,2176]{1,0:T(2,128)S(1)}, u32[]{:S(2)}, u32[]{:S(2)}) collective-permute-start(f32[2,2176]{1,0:T(2,128)S(1)} %pad_maximum_fusion.6), channel_id=1, source_target_pairs={{0,1},{1,0},{2,3},{3,2},{4,5},{5,4},{6,7},{7,6},{8,9},{9,8},{10,11... | collective-permute-start | bytes 52232 | tf_op jit(solution)/shard_map/ppermute | solution.py:27
  29.4 3.8 %collective-permute-start.6 = (f32[2,2176]{1,0:T(2,128)S(1)}, f32[2,2176]{1,0:T(2,128)S(1)}, u32[]{:S(2)}, u32[]{:S(2)}) collective-permute-start(f32[2,2176]{1,0:T(2,128)S(1)} %fusion.47), channel_id=1, source_target_pairs={{0,2},{1,3},{2,0},{3,1},{4,6},{5,7},{6,4},{7,5},{8,10},{9,11},{10,... | collective-permute-start | bytes 52232 | tf_op jit(solution)/shard_map/ppermute | solution.py:27
  33.2 4.8 %collective-permute-start.7 = (f32[2,2176]{1,0:T(2,128)S(1)}, f32[2,2176]{1,0:T(2,128)S(1)}, u32[]{:S(2)}, u32[]{:S(2)}) collective-permute-start(f32[2,2176]{1,0:T(2,128)S(1)} %add.132), channel_id=1, source_target_pairs={{0,4},{1,5},{2,6},{3,7},{4,0},{5,1},{6,2},{7,3},{8,12},{9,13},{10,... | collective-permute-start | bytes 52232 | tf_op jit(solution)/shard_map/ppermute | solution.py:27
  38.3 4.5 %collective-permute-start.8 = (f32[256]{0:T(256)S(1)}, f32[256]{0:T(256)S(1)}, u32[]{:S(2)}, u32[]{:S(2)}) collective-permute-start(f32[256]{0:T(256)S(1)} %fusion.2), channel_id=1, source_target_pairs={{0,4},{1,5},{2,6},{3,7},{4,0},{5,1},{6,2},{7,3},{8,12},{9,13},{10,... | collective-permute-start | bytes 3080 | tf_op jit(solution)/shard_map/ppermute | solution.py:40
  42.8 3.6 %collective-permute-start.9 = (f32[512]{0:T(512)S(1)}, f32[512]{0:T(512)S(1)}, u32[]{:S(2)}, u32[]{:S(2)}) collective-permute-start(f32[512]{0:T(512)S(1)} %pad_maximum_fusion.10), channel_id=1, source_target_pairs={{0,2},{1,3},{2,0},{3,1},{4,6},{5,7},{6,4},{7,5},{8,10},{9,11},{10,... | collective-permute-start | bytes 6152 | tf_op jit(solution)/shard_map/ppermute | solution.py:40
  46.4 1.2 %collective-permute-start.10 = (f32[1024]{0:T(1024)S(1)}, f32[1024]{0:T(1024)S(1)}, u32[]{:S(2)}, u32[]{:S(2)}) collective-permute-start(f32[1024]{0:T(1024)S(1)} %pad_maximum_fusion.9), channel_id=1, source_target_pairs={{0,1},{1,0},{2,3},{3,2},{4,5},{5,4},{6,7},{7,6},{8,9},{9,8},{10,11... | collective-permute-start | bytes 12296 | tf_op jit(solution)/shard_map/ppermute | solution.py:40
  57.0 2.7 %collective-permute-start.11 = (f32[4,64,2,512]{3,1,2,0:T(8,128)S(1)}, f32[4,64,2,512]{3,1,2,0:T(8,128)S(1)}, u32[]{:S(2)}, u32[]{:S(2)}) collective-permute-start(f32[4,64,2,512]{3,1,2,0:T(8,128)S(1)} %bitcast.91), channel_id=1, source_target_pairs={{0,1},{1,0},{2,3},{3,2},{4,5},{5,4},{6,7},{7,6},{8,9},{9,8},{10,11... | collective-permute-start | bytes 3145736 | tf_op jit(solution)/shard_map/ppermute | solution.py:66
  58.1 1.8 %copy-start.3 = (f32[512,512]{1,0:T(8,128)}, f32[512,512]{1,0:T(8,128)S(1)}, u32[]{:S(2)}) copy-start(f32[512,512]{1,0:T(8,128)S(1)} %fusion.8) | copy-start | bytes 3145732
  60.0 2.1 %collective-permute-start.17 = (f32[4,64,512]{2,1,0:T(8,128)S(1)}, f32[4,64,512]{2,1,0:T(8,128)S(1)}, u32[]{:S(2)}, u32[]{:S(2)}) collective-permute-start(f32[4,64,512]{2,1,0:T(8,128)S(1)} %dynamic-slice_bitcast_fusion), channel_id=1, source_target_pairs={{0,1},{1,0},{2,3},{3,2},{4,5},{5,4},{6,7},{7,6},{8,9},{9,8},{10,11... | collective-permute-start | bytes 1572872 | tf_op jit(solution)/shard_map/ppermute | solution.py:66
  60.2 19.2 %copy-start.5 = (s32[1,2]{1,0:T(1,128)S(1)}, s32[1,2]{1,0:T(1,128)}, u32[]{:S(2)}) copy-start(s32[1,2]{1,0:T(1,128)} %param.15) | copy-start | bytes 28
  60.2 14.2 %collective-permute-start.12 = (f32[2,64,2,512]{3,1,2,0:T(8,128)S(1)}, f32[2,64,2,512]{3,1,2,0:T(8,128)S(1)}, u32[]{:S(2)}, u32[]{:S(2)}) collective-permute-start(f32[2,64,2,512]{3,1,2,0:T(8,128)S(1)} %dynamic-slice_bitcast_fusion.1), channel_id=1, source_target_pairs={{0,2},{1,3},{2,0},{3,1},{4,6},{5,7},{6,4},{7,5},{8,10},{9,11},{10,... | collective-permute-start | bytes 1572872 | tf_op jit(solution)/shard_map/ppermute | solution.py:66
  74.6 13.1 %collective-permute-start.18 = (f32[2,64,512]{2,1,0:T(8,128)S(1)}, f32[2,64,512]{2,1,0:T(8,128)S(1)}, u32[]{:S(2)}, u32[]{:S(2)}) collective-permute-start(f32[2,64,512]{2,1,0:T(8,128)S(1)} %dynamic-slice_bitcast_fusion.2), channel_id=1, source_target_pairs={{0,2},{1,3},{2,0},{3,1},{4,6},{5,7},{6,4},{7,5},{8,10},{9,11},{10,... | collective-permute-start | bytes 786440 | tf_op jit(solution)/shard_map/ppermute | solution.py:66
  76.4 14.5 %collective-permute-start.13 = (f32[1,64,2,512]{3,1,2,0:T(8,128)S(1)}, f32[1,64,2,512]{3,1,2,0:T(8,128)S(1)}, u32[]{:S(2)}, u32[]{:S(2)}) collective-permute-start(f32[1,64,2,512]{3,1,2,0:T(8,128)S(1)} %constant_dynamic-slice_fusion.1), channel_id=1, source_target_pairs={{0,4},{1,5},{2,6},{3,7},{4,0},{5,1},{6,2},{7,3},{8,12},{9,13},{10,... | collective-permute-start | bytes 786440 | tf_op jit(solution)/shard_map/ppermute | solution.py:66
  91.0 6.8 %collective-permute-start.19 = (f32[1,64,512]{2,1,0:T(8,128)S(1)}, f32[1,64,512]{2,1,0:T(8,128)S(1)}, u32[]{:S(2)}, u32[]{:S(2)}) collective-permute-start(f32[1,64,512]{2,1,0:T(8,128)S(1)} %constant_dynamic-slice_fusion), channel_id=1, source_target_pairs={{0,4},{1,5},{2,6},{3,7},{4,0},{5,1},{6,2},{7,3},{8,12},{9,13},{10,... | collective-permute-start | bytes 393224 | tf_op jit(solution)/shard_map/ppermute | solution.py:66
  91.2 7.4 %collective-permute-start.14 = (f32[64,512]{1,0:T(8,128)S(1)}, f32[64,512]{1,0:T(8,128)S(1)}, u32[]{:S(2)}, u32[]{:S(2)}) collective-permute-start(f32[64,512]{1,0:T(8,128)S(1)} %get-tuple-element.16), channel_id=1, source_target_pairs={{0,8},{8,0},{16,24},{24,16},{1,9},{9,1},{17,25},{25,17},{2,10},{10... | collective-permute-start | bytes 393224 | tf_op jit(solution)/shard_map/ppermute | solution.py:171
  92.8 5.8 %collective-permute-start.15 = (f32[64,512]{1,0:T(8,128)S(1)}, f32[64,512]{1,0:T(8,128)S(1)}, u32[]{:S(2)}, u32[]{:S(2)}) collective-permute-start(f32[64,512]{1,0:T(8,128)S(1)} %get-tuple-element.17), channel_id=1, source_target_pairs={{0,16},{8,24},{16,0},{24,8},{1,17},{9,25},{17,1},{25,9},{2,18},{10... | collective-permute-start | bytes 393224 | tf_op jit(solution)/shard_map/ppermute | solution.py:171
  94.3 5.9 %collective-permute-start.16 = (f32[64,512]{1,0:T(8,128)S(1)}, f32[64,512]{1,0:T(8,128)S(1)}, u32[]{:S(2)}, u32[]{:S(2)}) collective-permute-start(f32[64,512]{1,0:T(8,128)S(1)} %get-tuple-element.18), channel_id=1, source_target_pairs={{0,24},{8,16},{16,8},{24,0},{1,25},{9,17},{17,9},{25,1},{2,26},{10... | collective-permute-start | bytes 393224 | tf_op jit(solution)/shard_map/ppermute | solution.py:171

commit v19 on v15

--- a/solution.py
+++ b/solution.py
@@ -22,10 +22,10 @@
     size = lax.axis_size(axis)
     if size & (size - 1):
         return lax.psum(value, axis)
-    step = 1
-    while step < size:
+    step = size // 2
+    while step:
         value = value + lax.ppermute(value, axis, [(i, i ^ step) for i in range(size)])
-        step *= 2
+        step //= 2
     return value
 
 

time: 101 us -> 101 us (level)
  no operation moved by 1% of the time
where the time goes in v19:
time: 101 us
  waiting for transfers between devices  38.5 us (38%)
  starting transfers between devices  30.5 us (30%)
  other arithmetic  14.1 us (14%)
  between operations  8.75 us (9%)
  matrix products  4.56 us (5%)
  local copies, waits for them, and re-layouts  4.35 us (4%)
    ppermute x6, waiting for transfers between devices, scatter_step(): lax.ppermute(send, axis, [(i, i ^ 1 << bit) for i in range(size)])  21.8 us
    ppermute x8, starting transfers between devices, xor_gather(): other = lax.ppermute(value, axis, [(i, i ^ 1 << bit) for i in range(size)])  14.9 us
    ppermute x8, waiting for transfers between devices, xor_gather(): other = lax.ppermute(value, axis, [(i, i ^ 1 << bit) for i in range(size)])  10.1 us
    ppermute x6, starting transfers between devices, scatter_step(): lax.ppermute(send, axis, [(i, i ^ 1 << bit) for i in range(size)])  7.07 us
    ppermute x3, starting transfers between devices, xor_sum(): lax.ppermute(value, axis, [(i, i ^ step) for i in range(size)])  4.92 us
    ppermute x3, waiting for transfers between devices, xor_sum(): lax.ppermute(value, axis, [(i, i ^ step) for i in range(size)])  4.92 us
    reduce_sum x1, other arithmetic, shards(): jnp.sum(aux_block.astype(jnp.float32) * coefficients[None, :], axis=1)  3.59 us
    ppermute x3, starting transfers between devices, shards(): frag_fock = frag_fock + lax.ppermute(piece(dest), 'dimer', pairs)  3.55 us
  transfers between devices with their start and end apart: 20, of which 16 were waited for; matrix products, arithmetic and copies ran while one was open for 7% of the time, Pallas kernels for 0%

profile of v19, /device:TPU:0, one launch (start us, length us, event | category | flops | bytes accessed | tf_op | source)
XLA Modules:
  0.0 100.7 jit_solution(3250129458178297114)
XLA Ops:
  0.6 0.9 copy.33
  1.5 3.1 %collective-permute-start = (bf16[1,64,128]{2,0,1:T(2,128)(2,1)S(1)}, bf16[1,64,128]{2,0,1:T(2,128)(2,1)S(1)}, u32[]{:S(2)}, u32[]{:S(2)}) collective-permute-start(bf16[1,64,128]{2,0,1:T(2,128)(2,1)S(1)} %copy.33), channel_id=1, source_target_pairs={{0,16},{8,24},{16,0},{24,8},{1,17},{9,25},{17,1},{25,9},{2,18},{10... | collective-permute-start | bytes 49160 | tf_op jit(solution)/shard_map/ppermute | solution.py:40
  4.6 0.7 broadcast_xor_fusion
  5.3 1.2 %collective-permute-done = bf16[1,64,128]{2,0,1:T(2,128)(2,1)S(1)} collective-permute-done((bf16[1,64,128]{2,0,1:T(2,128)(2,1)S(1)}, bf16[1,64,128]{2,0,1:T(2,128)(2,1)S(1)}, u32[]{:S(2)}, u32[]{:S(2)}) %collective-permute-start) | collective-permute-done | bytes 16416 | tf_op jit(solution)/shard_map/ppermute | solution.py:40
  6.6 2.1 %collective-permute-start.1 = (bf16[2,64,128]{2,0,1:T(2,128)(2,1)S(1)}, bf16[2,64,128]{2,0,1:T(2,128)(2,1)S(1)}, u32[]{:S(2)}, u32[]{:S(2)}) collective-permute-start(bf16[2,64,128]{2,0,1:T(2,128)(2,1)S(1)} %pad_maximum_fusion.5), channel_id=1, source_target_pairs={{0,8},{8,0},{16,24},{24,16},{1,9},{9,1},{17,25},{25,17},{2,10},{10... | collective-permute-start | bytes 98312 | tf_op jit(solution)/shard_map/ppermute | solution.py:40
  8.6 0.9 fusion.38
  9.5 1.1 %collective-permute-done.1 = bf16[2,64,128]{2,0,1:T(2,128)(2,1)S(1)} collective-permute-done((bf16[2,64,128]{2,0,1:T(2,128)(2,1)S(1)}, bf16[2,64,128]{2,0,1:T(2,128)(2,1)S(1)}, u32[]{:S(2)}, u32[]{:S(2)}) %collective-permute-start.1) | collective-permute-done | bytes 32800 | tf_op jit(solution)/shard_map/ppermute | solution.py:40
  10.8 3.2 %collective-permute-start.2 = (bf16[2,64,128]{2,0,1:T(2,128)(2,1)S(1)}, bf16[2,64,128]{2,0,1:T(2,128)(2,1)S(1)}, u32[]{:S(2)}, u32[]{:S(2)}) collective-permute-start(bf16[2,64,128]{2,0,1:T(2,128)(2,1)S(1)} %convolution_convert_fusion), channel_id=1, source_target_pairs={{0,4},{1,5},{2,6},{3,7},{4,0},{5,1},{6,2},{7,3},{8,12},{9,13},{10,... | collective-permute-start | bytes 98312 | tf_op jit(solution)/shard_map/ppermute | solution.py:40
  13.9 2.0 %collective-permute-done.2 = bf16[2,64,128]{2,0,1:T(2,128)(2,1)S(1)} collective-permute-done((bf16[2,64,128]{2,0,1:T(2,128)(2,1)S(1)}, bf16[2,64,128]{2,0,1:T(2,128)(2,1)S(1)}, u32[]{:S(2)}, u32[]{:S(2)}) %collective-permute-start.2) | collective-permute-done | bytes 32800 | tf_op jit(solution)/shard_map/ppermute | solution.py:40
  16.0 1.9 %collective-permute-start.3 = (bf16[2,128,128]{2,0,1:T(2,128)(2,1)S(1)}, bf16[2,128,128]{2,0,1:T(2,128)(2,1)S(1)}, u32[]{:S(2)}, u32[]{:S(2)}) collective-permute-start(bf16[2,128,128]{2,0,1:T(2,128)(2,1)S(1)} %pad_maximum_fusion.4), channel_id=1, source_target_pairs={{0,2},{1,3},{2,0},{3,1},{4,6},{5,7},{6,4},{7,5},{8,10},{9,11},{10,... | collective-permute-start | bytes 196616 | tf_op jit(solution)/shard_map/ppermute | solution.py:40
  17.9 0.7 compare_and_fusion
  18.6 1.8 %collective-permute-done.3 = bf16[2,128,128]{2,0,1:T(2,128)(2,1)S(1)} collective-permute-done((bf16[2,128,128]{2,0,1:T(2,128)(2,1)S(1)}, bf16[2,128,128]{2,0,1:T(2,128)(2,1)S(1)}, u32[]{:S(2)}, u32[]{:S(2)}) %collective-permute-start.3) | collective-permute-done | bytes 65568 | tf_op jit(solution)/shard_map/ppermute | solution.py:40
  21.3 0.7 reduce.2
  22.5 0.6 gather_fusion
  23.2 0.9 fusion.7
  24.1 0.7 multiply_reduce_fusion.2
  24.9 0.8 copy-done
  25.7 0.8 fusion
  26.5 1.3 %pad_maximum_fusion.11 = f32[2]{0:T(128)S(1)} fusion(f32[1]{0:T(128)} %bitcast.12, f32[1]{0:T(128)} %bitcast.11), kind=kLoop, calls=%fused_computation.93 | loop fusion | flops 2 | bytes 16 | tf_op jit(solution)/shard_map/stack | solution.py:124
  27.9 3.1 %collective-permute-start.5 = (f32[2,2176]{1,0:T(2,128)S(1)}, f32[2,2176]{1,0:T(2,128)S(1)}, u32[]{:S(2)}, u32[]{:S(2)}) collective-permute-start(f32[2,2176]{1,0:T(2,128)S(1)} %pad_maximum_fusion.6), channel_id=1, source_target_pairs={{0,4},{1,5},{2,6},{3,7},{4,0},{5,1},{6,2},{7,3},{8,12},{9,13},{10,... | collective-permute-start | bytes 52232 | tf_op jit(solution)/shard_map/ppermute | solution.py:27
  31.0 1.7 %collective-permute-done.5 = f32[2,2176]{1,0:T(2,128)S(1)} collective-permute-done((f32[2,2176]{1,0:T(2,128)S(1)}, f32[2,2176]{1,0:T(2,128)S(1)}, u32[]{:S(2)}, u32[]{:S(2)}) %collective-permute-start.5) | collective-permute-done | bytes 17440 | tf_op jit(solution)/shard_map/ppermute | solution.py:27
  32.8 1.8 %collective-permute-start.6 = (f32[2,2176]{1,0:T(2,128)S(1)}, f32[2,2176]{1,0:T(2,128)S(1)}, u32[]{:S(2)}, u32[]{:S(2)}) collective-permute-start(f32[2,2176]{1,0:T(2,128)S(1)} %fusion.47), channel_id=1, source_target_pairs={{0,2},{1,3},{2,0},{3,1},{4,6},{5,7},{6,4},{7,5},{8,10},{9,11},{10,... | collective-permute-start | bytes 52232 | tf_op jit(solution)/shard_map/ppermute | solution.py:27
  34.6 2.0 %collective-permute-done.6 = f32[2,2176]{1,0:T(2,128)S(1)} collective-permute-done((f32[2,2176]{1,0:T(2,128)S(1)}, f32[2,2176]{1,0:T(2,128)S(1)}, u32[]{:S(2)}, u32[]{:S(2)}) %collective-permute-start.6) | collective-permute-done | bytes 17440 | tf_op jit(solution)/shard_map/ppermute | solution.py:27
  36.7 1.2 %collective-permute-done.7 = f32[2,2176]{1,0:T(2,128)S(1)} collective-permute-done((f32[2,2176]{1,0:T(2,128)S(1)}, f32[2,2176]{1,0:T(2,128)S(1)}, u32[]{:S(2)}, u32[]{:S(2)}) %collective-permute-start.7) | collective-permute-done | bytes 17440 | tf_op jit(solution)/shard_map/ppermute | solution.py:27
  38.1 3.0 %collective-permute-start.8 = (f32[256]{0:T(256)S(1)}, f32[256]{0:T(256)S(1)}, u32[]{:S(2)}, u32[]{:S(2)}) collective-permute-start(f32[256]{0:T(256)S(1)} %fusion.2), channel_id=1, source_target_pairs={{0,4},{1,5},{2,6},{3,7},{4,0},{5,1},{6,2},{7,3},{8,12},{9,13},{10,... | collective-permute-start | bytes 3080 | tf_op jit(solution)/shard_map/ppermute | solution.py:40
  41.1 1.6 %collective-permute-done.8 = f32[256]{0:T(256)S(1)} collective-permute-done((f32[256]{0:T(256)S(1)}, f32[256]{0:T(256)S(1)}, u32[]{:S(2)}, u32[]{:S(2)}) %collective-permute-start.8) | collective-permute-done | bytes 1056 | tf_op jit(solution)/shard_map/ppermute | solution.py:40
  42.7 1.7 %collective-permute-start.9 = (f32[512]{0:T(512)S(1)}, f32[512]{0:T(512)S(1)}, u32[]{:S(2)}, u32[]{:S(2)}) collective-permute-start(f32[512]{0:T(512)S(1)} %pad_maximum_fusion.10), channel_id=1, source_target_pairs={{0,2},{1,3},{2,0},{3,1},{4,6},{5,7},{6,4},{7,5},{8,10},{9,11},{10,... | collective-permute-start | bytes 6152 | tf_op jit(solution)/shard_map/ppermute | solution.py:40
  44.4 1.9 %collective-permute-done.9 = f32[512]{0:T(512)S(1)} collective-permute-done((f32[512]{0:T(512)S(1)}, f32[512]{0:T(512)S(1)}, u32[]{:S(2)}, u32[]{:S(2)}) %collective-permute-start.9) | collective-permute-done | bytes 2080 | tf_op jit(solution)/shard_map/ppermute | solution.py:40
  46.3 0.6 fusion.49
  48.1 3.6 %multiply_reduce_fusion = f32[1280]{0:T(1024)S(1)} fusion(bf16[1,1280,2048]{2,1,0:T(8,128)(2,1)} %param.12, f32[2048]{0:T(1024)S(1)} %bitcast.97), kind=kLoop, calls=%fused_computation.2 | loop fusion | flops 7863040 | bytes 5256192 | tf_op jit(solution)/shard_map/reduce_sum | solution.py:136
  51.7 0.6 multiply_reduce_fusion.1
  54.7 0.9 fusion.3
  55.6 0.9 fusion.5
  57.1 0.9 fusion.8
  57.9 1.6 %collective-permute-done.11 = f32[4,64,2,512]{3,1,2,0:T(8,128)S(1)} collective-permute-done((f32[4,64,2,512]{3,1,2,0:T(8,128)S(1)}, f32[4,64,2,512]{3,1,2,0:T(8,128)S(1)}, u32[]{:S(2)}, u32[]{:S(2)}) %collective-permute-start.11) | collective-permute-done | bytes 1048608 | tf_op jit(solution)/shard_map/ppermute | solution.py:66
  60.1 1.8 %collective-permute-start.12 = (f32[2,64,2,512]{3,1,2,0:T(8,128)S(1)}, f32[2,64,2,512]{3,1,2,0:T(8,128)S(1)}, u32[]{:S(2)}, u32[]{:S(2)}) collective-permute-start(f32[2,64,2,512]{3,1,2,0:T(8,128)S(1)} %dynamic-slice_bitcast_fusion.1), channel_id=1, source_target_pairs={{0,2},{1,3},{2,0},{3,1},{4,6},{5,7},{6,4},{7,5},{8,10},{9,11},{10,... | collective-permute-start | bytes 1572872 | tf_op jit(solution)/shard_map/ppermute | solution.py:66
  61.9 1.1 %bitcast_add_fusion.1 = f32[4,64,512]{2,1,0:T(8,128)S(1)} fusion(f32[4,64,512]{2,1,0:T(8,128)S(1)} %collective-permute-done.17, f32[4,2,64,512]{3,2,1,0:T(8,128)} %bitcast.94, s32[]{:T(128)S(6)} %select_n.150), kind=kLoop, calls=%fused_computation.36 | loop fusion | flops 131072 | bytes 1572868 | tf_op jit(solution)/shard_map/add | solution.py:66
  63.0 11.3 %collective-permute-done.12 = f32[2,64,2,512]{3,1,2,0:T(8,128)S(1)} collective-permute-done((f32[2,64,2,512]{3,1,2,0:T(8,128)S(1)}, f32[2,64,2,512]{3,1,2,0:T(8,128)S(1)}, u32[]{:S(2)}, u32[]{:S(2)}) %collective-permute-start.12) | collective-permute-done | bytes 524320 | tf_op jit(solution)/shard_map/ppermute | solution.py:66
  74.5 1.8 %collective-permute-start.18 = (f32[2,64,512]{2,1,0:T(8,128)S(1)}, f32[2,64,512]{2,1,0:T(8,128)S(1)}, u32[]{:S(2)}, u32[]{:S(2)}) collective-permute-start(f32[2,64,512]{2,1,0:T(8,128)S(1)} %dynamic-slice_bitcast_fusion.2), channel_id=1, source_target_pairs={{0,2},{1,3},{2,0},{3,1},{4,6},{5,7},{6,4},{7,5},{8,10},{9,11},{10,... | collective-permute-start | bytes 786440 | tf_op jit(solution)/shard_map/ppermute | solution.py:66
  76.3 3.0 %collective-permute-start.13 = (f32[1,64,2,512]{3,1,2,0:T(8,128)S(1)}, f32[1,64,2,512]{3,1,2,0:T(8,128)S(1)}, u32[]{:S(2)}, u32[]{:S(2)}) collective-permute-start(f32[1,64,2,512]{3,1,2,0:T(8,128)S(1)} %constant_dynamic-slice_fusion.1), channel_id=1, source_target_pairs={{0,4},{1,5},{2,6},{3,7},{4,0},{5,1},{6,2},{7,3},{8,12},{9,13},{10,... | collective-permute-start | bytes 786440 | tf_op jit(solution)/shard_map/ppermute | solution.py:66
  85.0 2.6 %collective-permute-done.18 = f32[2,64,512]{2,1,0:T(8,128)S(1)} collective-permute-done((f32[2,64,512]{2,1,0:T(8,128)S(1)}, f32[2,64,512]{2,1,0:T(8,128)S(1)}, u32[]{:S(2)}, u32[]{:S(2)}) %collective-permute-start.18) | collective-permute-done | bytes 262176 | tf_op jit(solution)/shard_map/ppermute | solution.py:66
  87.6 3.2 %collective-permute-done.13 = f32[1,64,2,512]{3,1,2,0:T(8,128)S(1)} collective-permute-done((f32[1,64,2,512]{3,1,2,0:T(8,128)S(1)}, f32[1,64,2,512]{3,1,2,0:T(8,128)S(1)}, u32[]{:S(2)}, u32[]{:S(2)}) %collective-permute-start.13) | collective-permute-done | bytes 262176 | tf_op jit(solution)/shard_map/ppermute | solution.py:66
  91.1 1.5 %collective-permute-start.14 = (f32[64,512]{1,0:T(8,128)S(1)}, f32[64,512]{1,0:T(8,128)S(1)}, u32[]{:S(2)}, u32[]{:S(2)}) collective-permute-start(f32[64,512]{1,0:T(8,128)S(1)} %get-tuple-element.16), channel_id=1, source_target_pairs={{0,8},{8,0},{16,24},{24,16},{1,9},{9,1},{17,25},{25,17},{2,10},{10... | collective-permute-start | bytes 393224 | tf_op jit(solution)/shard_map/ppermute | solution.py:170
  92.6 1.5 %collective-permute-start.15 = (f32[64,512]{1,0:T(8,128)S(1)}, f32[64,512]{1,0:T(8,128)S(1)}, u32[]{:S(2)}, u32[]{:S(2)}) collective-permute-start(f32[64,512]{1,0:T(8,128)S(1)} %get-tuple-element.17), channel_id=1, source_target_pairs={{0,16},{8,24},{16,0},{24,8},{1,17},{9,25},{17,1},{25,9},{2,18},{10... | collective-permute-start | bytes 393224 | tf_op jit(solution)/shard_map/ppermute | solution.py:170
  94.6 3.1 %collective-permute-done.19 = f32[1,64,512]{2,1,0:T(8,128)S(1)} collective-permute-done((f32[1,64,512]{2,1,0:T(8,128)S(1)}, f32[1,64,512]{2,1,0:T(8,128)S(1)}, u32[]{:S(2)}, u32[]{:S(2)}) %collective-permute-start.19) | collective-permute-done | bytes 131104 | tf_op jit(solution)/shard_map/ppermute | solution.py:66
  97.7 0.7 dynamic-slice_add_fusion.1
  98.4 1.6 %collective-permute-done.16 = f32[64,512]{1,0:T(8,128)S(1)} collective-permute-done((f32[64,512]{1,0:T(8,128)S(1)}, f32[64,512]{1,0:T(8,128)S(1)}, u32[]{:S(2)}, u32[]{:S(2)}) %collective-permute-start.16) | collective-permute-done | bytes 131104 | tf_op jit(solution)/shard_map/ppermute | solution.py:170
  100.0 0.7 fusion.26
  (66 shorter events, 5.9 us)
Async XLA Ops:
  0.6 22.6 %copy-start.1 = (bf16[1,1280,1024]{2,1,0:T(8,128)(2,1)S(1)}, bf16[1,1280,1024]{2,1,0:T(8,128)(2,1)}, u32[]{:S(2)}) copy-start(bf16[1,1280,1024]{2,1,0:T(8,128)(2,1)} %param.11) | copy-start | bytes 7864324
  1.5 5.0 %collective-permute-start = (bf16[1,64,128]{2,0,1:T(2,128)(2,1)S(1)}, bf16[1,64,128]{2,0,1:T(2,128)(2,1)S(1)}, u32[]{:S(2)}, u32[]{:S(2)}) collective-permute-start(bf16[1,64,128]{2,0,1:T(2,128)(2,1)S(1)} %copy.33), channel_id=1, source_target_pairs={{0,16},{8,24},{16,0},{24,8},{1,17},{9,25},{17,1},{25,9},{2,18},{10... | collective-permute-start | bytes 49160 | tf_op jit(solution)/shard_map/ppermute | solution.py:40
  6.6 4.0 %collective-permute-start.1 = (bf16[2,64,128]{2,0,1:T(2,128)(2,1)S(1)}, bf16[2,64,128]{2,0,1:T(2,128)(2,1)S(1)}, u32[]{:S(2)}, u32[]{:S(2)}) collective-permute-start(bf16[2,64,128]{2,0,1:T(2,128)(2,1)S(1)} %pad_maximum_fusion.5), channel_id=1, source_target_pairs={{0,8},{8,0},{16,24},{24,16},{1,9},{9,1},{17,25},{25,17},{2,10},{10... | collective-permute-start | bytes 98312 | tf_op jit(solution)/shard_map/ppermute | solution.py:40
  10.8 5.2 %collective-permute-start.2 = (bf16[2,64,128]{2,0,1:T(2,128)(2,1)S(1)}, bf16[2,64,128]{2,0,1:T(2,128)(2,1)S(1)}, u32[]{:S(2)}, u32[]{:S(2)}) collective-permute-start(bf16[2,64,128]{2,0,1:T(2,128)(2,1)S(1)} %convolution_convert_fusion), channel_id=1, source_target_pairs={{0,4},{1,5},{2,6},{3,7},{4,0},{5,1},{6,2},{7,3},{8,12},{9,13},{10,... | collective-permute-start | bytes 98312 | tf_op jit(solution)/shard_map/ppermute | solution.py:40
  16.0 4.3 %collective-permute-start.3 = (bf16[2,128,128]{2,0,1:T(2,128)(2,1)S(1)}, bf16[2,128,128]{2,0,1:T(2,128)(2,1)S(1)}, u32[]{:S(2)}, u32[]{:S(2)}) collective-permute-start(bf16[2,128,128]{2,0,1:T(2,128)(2,1)S(1)} %pad_maximum_fusion.4), channel_id=1, source_target_pairs={{0,2},{1,3},{2,0},{3,1},{4,6},{5,7},{6,4},{7,5},{8,10},{9,11},{10,... | collective-permute-start | bytes 196616 | tf_op jit(solution)/shard_map/ppermute | solution.py:40
  20.6 1.5 %collective-permute-start.4 = (bf16[2,256,128]{2,0,1:T(2,128)(2,1)S(1)}, bf16[2,256,128]{2,0,1:T(2,128)(2,1)S(1)}, u32[]{:S(2)}, u32[]{:S(2)}) collective-permute-start(bf16[2,256,128]{2,0,1:T(2,128)(2,1)S(1)} %pad_maximum_fusion.1), channel_id=1, source_target_pairs={{0,1},{1,0},{2,3},{3,2},{4,5},{5,4},{6,7},{7,6},{8,9},{9,8},{10,11... | collective-permute-start | bytes 393224 | tf_op jit(solution)/shard_map/ppermute | solution.py:40
  23.2 1.6 %copy-start.4 = (f32[1,1280]{1,0:T(1,128)S(1)}, f32[1,1280]{1,0:T(1,128)}, u32[]{:S(2)}) copy-start(f32[1,1280]{1,0:T(1,128)} %param.17) | copy-start | bytes 15364
  23.2 2.5 %copy-start = (bf16[1,1280,2048]{2,1,0:T(8,128)(2,1)S(1)}, bf16[1,1280,2048]{2,1,0:T(8,128)(2,1)}, u32[]{:S(2)}) copy-start(bf16[1,1280,2048]{2,1,0:T(8,128)(2,1)} %param.12) | copy-start | bytes 15728644
  25.7 12.2 %copy-start.2 = (f32[1,256,2048]{2,1,0:T(8,128)S(1)}, f32[1,256,2048]{2,1,0:T(8,128)}, u32[]{:S(2)}) copy-start(f32[1,256,2048]{2,1,0:T(8,128)} %param.18) | copy-start | bytes 6291460
  27.9 4.8 %collective-permute-start.5 = (f32[2,2176]{1,0:T(2,128)S(1)}, f32[2,2176]{1,0:T(2,128)S(1)}, u32[]{:S(2)}, u32[]{:S(2)}) collective-permute-start(f32[2,2176]{1,0:T(2,128)S(1)} %pad_maximum_fusion.6), channel_id=1, source_target_pairs={{0,4},{1,5},{2,6},{3,7},{4,0},{5,1},{6,2},{7,3},{8,12},{9,13},{10,... | collective-permute-start | bytes 52232 | tf_op jit(solution)/shard_map/ppermute | solution.py:27
  32.8 3.8 %collective-permute-start.6 = (f32[2,2176]{1,0:T(2,128)S(1)}, f32[2,2176]{1,0:T(2,128)S(1)}, u32[]{:S(2)}, u32[]{:S(2)}) collective-permute-start(f32[2,2176]{1,0:T(2,128)S(1)} %fusion.47), channel_id=1, source_target_pairs={{0,2},{1,3},{2,0},{3,1},{4,6},{5,7},{6,4},{7,5},{8,10},{9,11},{10,... | collective-permute-start | bytes 52232 | tf_op jit(solution)/shard_map/ppermute | solution.py:27
  36.6 1.3 %collective-permute-start.7 = (f32[2,2176]{1,0:T(2,128)S(1)}, f32[2,2176]{1,0:T(2,128)S(1)}, u32[]{:S(2)}, u32[]{:S(2)}) collective-permute-start(f32[2,2176]{1,0:T(2,128)S(1)} %add.132), channel_id=1, source_target_pairs={{0,1},{1,0},{2,3},{3,2},{4,5},{5,4},{6,7},{7,6},{8,9},{9,8},{10,11... | collective-permute-start | bytes 52232 | tf_op jit(solution)/shard_map/ppermute | solution.py:27
  38.1 4.5 %collective-permute-start.8 = (f32[256]{0:T(256)S(1)}, f32[256]{0:T(256)S(1)}, u32[]{:S(2)}, u32[]{:S(2)}) collective-permute-start(f32[256]{0:T(256)S(1)} %fusion.2), channel_id=1, source_target_pairs={{0,4},{1,5},{2,6},{3,7},{4,0},{5,1},{6,2},{7,3},{8,12},{9,13},{10,... | collective-permute-start | bytes 3080 | tf_op jit(solution)/shard_map/ppermute | solution.py:40
  42.7 3.6 %collective-permute-start.9 = (f32[512]{0:T(512)S(1)}, f32[512]{0:T(512)S(1)}, u32[]{:S(2)}, u32[]{:S(2)}) collective-permute-start(f32[512]{0:T(512)S(1)} %pad_maximum_fusion.10), channel_id=1, source_target_pairs={{0,2},{1,3},{2,0},{3,1},{4,6},{5,7},{6,4},{7,5},{8,10},{9,11},{10,... | collective-permute-start | bytes 6152 | tf_op jit(solution)/shard_map/ppermute | solution.py:40
  46.2 1.2 %collective-permute-start.10 = (f32[1024]{0:T(1024)S(1)}, f32[1024]{0:T(1024)S(1)}, u32[]{:S(2)}, u32[]{:S(2)}) collective-permute-start(f32[1024]{0:T(1024)S(1)} %pad_maximum_fusion.9), channel_id=1, source_target_pairs={{0,1},{1,0},{2,3},{3,2},{4,5},{5,4},{6,7},{7,6},{8,9},{9,8},{10,11... | collective-permute-start | bytes 12296 | tf_op jit(solution)/shard_map/ppermute | solution.py:40
  56.8 2.7 %collective-permute-start.11 = (f32[4,64,2,512]{3,1,2,0:T(8,128)S(1)}, f32[4,64,2,512]{3,1,2,0:T(8,128)S(1)}, u32[]{:S(2)}, u32[]{:S(2)}) collective-permute-start(f32[4,64,2,512]{3,1,2,0:T(8,128)S(1)} %bitcast.91), channel_id=1, source_target_pairs={{0,1},{1,0},{2,3},{3,2},{4,5},{5,4},{6,7},{7,6},{8,9},{9,8},{10,11... | collective-permute-start | bytes 3145736 | tf_op jit(solution)/shard_map/ppermute | solution.py:66
  57.9 1.8 %copy-start.3 = (f32[512,512]{1,0:T(8,128)}, f32[512,512]{1,0:T(8,128)S(1)}, u32[]{:S(2)}) copy-start(f32[512,512]{1,0:T(8,128)S(1)} %fusion.8) | copy-start | bytes 3145732
  59.8 2.1 %collective-permute-start.17 = (f32[4,64,512]{2,1,0:T(8,128)S(1)}, f32[4,64,512]{2,1,0:T(8,128)S(1)}, u32[]{:S(2)}, u32[]{:S(2)}) collective-permute-start(f32[4,64,512]{2,1,0:T(8,128)S(1)} %dynamic-slice_bitcast_fusion), channel_id=1, source_target_pairs={{0,1},{1,0},{2,3},{3,2},{4,5},{5,4},{6,7},{7,6},{8,9},{9,8},{10,11... | collective-permute-start | bytes 1572872 | tf_op jit(solution)/shard_map/ppermute | solution.py:66
  60.1 19.2 %copy-start.5 = (s32[1,2]{1,0:T(1,128)S(1)}, s32[1,2]{1,0:T(1,128)}, u32[]{:S(2)}) copy-start(s32[1,2]{1,0:T(1,128)} %param.15) | copy-start | bytes 28
  60.1 14.2 %collective-permute-start.12 = (f32[2,64,2,512]{3,1,2,0:T(8,128)S(1)}, f32[2,64,2,512]{3,1,2,0:T(8,128)S(1)}, u32[]{:S(2)}, u32[]{:S(2)}) collective-permute-start(f32[2,64,2,512]{3,1,2,0:T(8,128)S(1)} %dynamic-slice_bitcast_fusion.1), channel_id=1, source_target_pairs={{0,2},{1,3},{2,0},{3,1},{4,6},{5,7},{6,4},{7,5},{8,10},{9,11},{10,... | collective-permute-start | bytes 1572872 | tf_op jit(solution)/shard_map/ppermute | solution.py:66
  74.5 13.1 %collective-permute-start.18 = (f32[2,64,512]{2,1,0:T(8,128)S(1)}, f32[2,64,512]{2,1,0:T(8,128)S(1)}, u32[]{:S(2)}, u32[]{:S(2)}) collective-permute-start(f32[2,64,512]{2,1,0:T(8,128)S(1)} %dynamic-slice_bitcast_fusion.2), channel_id=1, source_target_pairs={{0,2},{1,3},{2,0},{3,1},{4,6},{5,7},{6,4},{7,5},{8,10},{9,11},{10,... | collective-permute-start | bytes 786440 | tf_op jit(solution)/shard_map/ppermute | solution.py:66
  76.3 14.6 %collective-permute-start.13 = (f32[1,64,2,512]{3,1,2,0:T(8,128)S(1)}, f32[1,64,2,512]{3,1,2,0:T(8,128)S(1)}, u32[]{:S(2)}, u32[]{:S(2)}) collective-permute-start(f32[1,64,2,512]{3,1,2,0:T(8,128)S(1)} %constant_dynamic-slice_fusion.1), channel_id=1, source_target_pairs={{0,4},{1,5},{2,6},{3,7},{4,0},{5,1},{6,2},{7,3},{8,12},{9,13},{10,... | collective-permute-start | bytes 786440 | tf_op jit(solution)/shard_map/ppermute | solution.py:66
  90.9 6.8 %collective-permute-start.19 = (f32[1,64,512]{2,1,0:T(8,128)S(1)}, f32[1,64,512]{2,1,0:T(8,128)S(1)}, u32[]{:S(2)}, u32[]{:S(2)}) collective-permute-start(f32[1,64,512]{2,1,0:T(8,128)S(1)} %constant_dynamic-slice_fusion), channel_id=1, source_target_pairs={{0,4},{1,5},{2,6},{3,7},{4,0},{5,1},{6,2},{7,3},{8,12},{9,13},{10,... | collective-permute-start | bytes 393224 | tf_op jit(solution)/shard_map/ppermute | solution.py:66
  91.1 7.3 %collective-permute-start.14 = (f32[64,512]{1,0:T(8,128)S(1)}, f32[64,512]{1,0:T(8,128)S(1)}, u32[]{:S(2)}, u32[]{:S(2)}) collective-permute-start(f32[64,512]{1,0:T(8,128)S(1)} %get-tuple-element.16), channel_id=1, source_target_pairs={{0,8},{8,0},{16,24},{24,16},{1,9},{9,1},{17,25},{25,17},{2,10},{10... | collective-permute-start | bytes 393224 | tf_op jit(solution)/shard_map/ppermute | solution.py:170
  92.6 5.8 %collective-permute-start.15 = (f32[64,512]{1,0:T(8,128)S(1)}, f32[64,512]{1,0:T(8,128)S(1)}, u32[]{:S(2)}, u32[]{:S(2)}) collective-permute-start(f32[64,512]{1,0:T(8,128)S(1)} %get-tuple-element.17), channel_id=1, source_target_pairs={{0,16},{8,24},{16,0},{24,8},{1,17},{9,25},{17,1},{25,9},{2,18},{10... | collective-permute-start | bytes 393224 | tf_op jit(solution)/shard_map/ppermute | solution.py:170
  94.1 5.9 %collective-permute-start.16 = (f32[64,512]{1,0:T(8,128)S(1)}, f32[64,512]{1,0:T(8,128)S(1)}, u32[]{:S(2)}, u32[]{:S(2)}) collective-permute-start(f32[64,512]{1,0:T(8,128)S(1)} %get-tuple-element.18), channel_id=1, source_target_pairs={{0,24},{8,16},{16,8},{24,0},{1,25},{9,17},{17,9},{25,1},{2,26},{10... | collective-permute-start | bytes 393224 | tf_op jit(solution)/shard_map/ppermute | solution.py:170
